TPU v7x, 512 devices: a whole 4x8x8 slice. The times are simulated.
512 devices in a mesh: px: 32 (over y, x), py: 16 (over z, core).
Axes of the slice: x: 4, y: 8, z: 8, core: 2. Of those that a mesh axis runs over, the one named last changes fastest.
Arguments:
- solution: float32 [32, 16, 16, 136], P('px', 'py'), may hold values from -6 to 6
- residual: float32 [32, 16, 16, 136], P('px', 'py')
- direction: float32 [32, 16, 16, 136], P('px', 'py'), may hold values from -6 to 6
- rz_previous: float32 [16], replicated, may hold values from 34816 to 278528
- dual_inverse: bfloat16 [32, 16, 272, 272], P('px', 'py'), as said below
- dual_schur: bfloat16 [32, 16, 272, 272], P('px', 'py'), as said below
- coupling: bfloat16 [32, 16, 8, 272], P('px', 'py'), may hold values from -0.375 to 0.375
- coarse_inverse: float32 [32, 16, 2, 2], P('px', 'py'), as said below
- matching: int32 [32, 16, 2, 68], P('px', 'py'), may hold values from 0 to 67, as said below
- patch_counts: int32 [32, 16], P('px', 'py'), may hold values from 1 to 1, as said below
Outputs:
- new_solution: float32 [32, 16, 16, 136], P('px', 'py')
- new_residual: float32 [32, 16, 16, 136], P('px', 'py')
- new_direction: float32 [32, 16, 16, 136], P('px', 'py')
- rz_current: float32 [16], replicated
- residual_sq: float32 [16], replicated
Inputs may be any that keep to these rules, and one draw needn't show every extreme that they name: `matching`: each row is 0 to 67 in order, or with the order of its 34 node pairs reversed (components kept). `patch_counts`: some device holds 1 active patches. `dual_inverse`: each block symmetric positive definite. `dual_schur`: each block symmetric positive definite. `coarse_inverse`: each 2 x 2 block symmetric positive definite.
All inputs are finite; a program needn't handle non-finite values.
Results may differ from a plain program's by a relative error of at most 0.0016.
Values sent between devices are 32-bit elements; how exact they have to be, the bound alone decides.
No kernel may reach another device: no remote copies, remote signals or barrier semaphores. Data moves between devices by JAX's collectives and lax.ppermute only.
A program may use at most 64 MiB of HBM per device.

v0:
```python
import jax
import jax.numpy as jnp
from jax import lax
from jax.sharding import PartitionSpec as P

SIDE = 68


def passed_along(value, axis, by):
    peers = lax.axis_size(axis)
    pairs = [(i, i + by) for i in range(peers) if 0 <= i + by < peers]
    return lax.ppermute(value, axis, pairs)


def permute_side(values, order):
    return jnp.take_along_axis(values, jnp.broadcast_to(order[:, :, None, :], values.shape), axis=3)


def on_device(
    solution,
    residual,
    direction,
    rz_previous,
    dual_inverse,
    dual_schur,
    coupling,
    coarse_inverse,
    matching,
    patch_counts,
):
    rows_here = solution.shape[0]
    cols_here = solution.shape[1]
    total_rows = rows_here * lax.axis_size("px")
    total_cols = cols_here * lax.axis_size("py")
    grid_row = lax.axis_index("px") * rows_here + jnp.arange(rows_here)
    grid_col = lax.axis_index("py") * cols_here + jnp.arange(cols_here)
    local_slot = jnp.arange(rows_here)[:, None] * cols_here + jnp.arange(cols_here)[None, :]
    count_here = patch_counts[0, 0]
    active = (local_slot < count_here).astype(jnp.float32)[:, :, None, None]
    edge_index = jnp.arange(2 * SIDE)
    edge_ok = jnp.where(
        edge_index[None, None, :] < SIDE,
        (grid_col < total_cols - 1)[None, :, None] & (grid_row >= 0)[:, None, None],
        (grid_row < total_rows - 1)[:, None, None] & (grid_col >= 0)[None, :, None],
    )
    edge_mask = active * edge_ok[:, :, None, :].astype(jnp.float32)
    vertex_mask = ((grid_row >= 1)[:, None] & (grid_col >= 1)[None, :]).astype(jnp.float32)[
        :, :, None, None
    ]
    east_order = matching[:, :, 0]
    north_order = matching[:, :, 1]

    def spread_b(vector):
        east_part = vector[..., :SIDE]
        north_part = vector[..., SIDE:]
        east_perm = permute_side(east_part, east_order)
        north_perm = permute_side(north_part, north_order)
        west_edge = passed_along(east_perm, "py", 1)
        from_west = jnp.concatenate([west_edge, east_perm[:, :-1]], 1)
        south_edge = passed_along(north_perm, "px", 1)
        from_south = jnp.concatenate([south_edge, north_perm[:-1]], 0)
        return jnp.concatenate([east_part, north_part, -from_west, -from_south], 3)

    def jump_b(side_values):
        west_side = side_values[..., 2 * SIDE : 3 * SIDE]
        south_side = side_values[..., 3 * SIDE :]
        east_edge = passed_along(west_side, "py", -1)
        from_east = jnp.concatenate([west_side[:, 1:], east_edge], 1)
        north_edge = passed_along(south_side, "px", -1)
        from_north = jnp.concatenate([south_side[1:], north_edge], 0)
        east_term = permute_side(from_east, east_order)
        north_term = permute_side(from_north, north_order)
        joined = jnp.concatenate(
            [side_values[..., :SIDE] - east_term, side_values[..., SIDE : 2 * SIDE] - north_term], 3
        )
        return joined * edge_mask

    def patch_products(matrices, vectors):
        return (
            jnp.einsum("rpab,rpcb->rpca", matrices, vectors, preferred_element_type=jnp.float32)
            * active
        )

    start_sol = solution * edge_mask
    start_res = residual * edge_mask
    start_dir = direction * edge_mask
    spread = spread_b(0.5 * start_res).astype(jnp.bfloat16)
    side_values = patch_products(dual_schur, spread)
    precond = 0.5 * jump_b(side_values)
    rz_current = lax.psum(jnp.sum(start_res * precond, axis=(0, 1, 3)), ("px", "py"))
    step_ratio = rz_current / rz_previous
    new_direction = precond + step_ratio[None, None, :, None] * start_dir
    spread = spread_b(new_direction).astype(jnp.bfloat16)
    inner_part = patch_products(dual_inverse, spread)
    corner = (
        jnp.einsum("rpkb,rpcb->rpck", coupling, spread, preferred_element_type=jnp.float32) * active
    )
    flat_corner = corner.reshape(rows_here, cols_here, -1)
    west_column = passed_along(flat_corner, "py", 1)
    with_west = jnp.concatenate([west_column, flat_corner], 1)
    south_row = passed_along(with_west, "px", 1)
    extended = jnp.concatenate([south_row, with_west], 0)
    extended = extended.reshape(rows_here + 1, cols_here + 1, corner.shape[2], corner.shape[3])
    assembled = (
        extended[1:, 1:, :, 0:2]
        + extended[1:, :-1, :, 2:4]
        + extended[:-1, 1:, :, 4:6]
        + extended[:-1, :-1, :, 6:8]
    ) * vertex_mask
    coarse = jnp.einsum(
        "rpxy,rpcy->rpcx", coarse_inverse, assembled, precision=lax.Precision.HIGHEST
    )
    flat_coarse = coarse.reshape(rows_here, cols_here, -1)
    east_column = passed_along(flat_coarse, "py", -1)
    with_east = jnp.concatenate([flat_coarse, east_column], 1)
    north_row = passed_along(with_east, "px", -1)
    beside_all = jnp.concatenate([with_east, north_row], 0)
    beside_all = beside_all.reshape(rows_here + 1, cols_here + 1, coarse.shape[2], 2)
    corners_back = jnp.concatenate(
        [beside_all[:-1, :-1], beside_all[:-1, 1:], beside_all[1:, :-1], beside_all[1:, 1:]], 3
    )
    correction = jnp.einsum(
        "rpkb,rpck->rpcb",
        coupling.astype(jnp.float32),
        corners_back,
        precision=lax.Precision.HIGHEST,
    )
    image = jump_b((inner_part + correction) * active)
    curvature = lax.psum(jnp.sum(new_direction * image, axis=(0, 1, 3)), ("px", "py"))
    step_length = rz_current / curvature
    new_solution = start_sol + step_length[None, None, :, None] * new_direction
    new_residual = start_res - step_length[None, None, :, None] * image
    residual_sq = lax.psum(jnp.sum(new_residual * new_residual, axis=(0, 1, 3)), ("px", "py"))
    return (new_solution, new_residual, new_direction, rz_current, residual_sq)


def solution(mesh):
    in_specs = (
        P("px", "py", None, None),
        P("px", "py", None, None),
        P("px", "py", None, None),
        P(),
        P("px", "py", None, None),
        P("px", "py", None, None),
        P("px", "py", None, None),
        P("px", "py", None, None),
        P("px", "py", None, None),
        P("px", "py"),
    )
    out_specs = (
        P("px", "py", None, None),
        P("px", "py", None, None),
        P("px", "py", None, None),
        P(),
        P(),
    )
    return jax.shard_map(
        on_device, mesh=mesh, in_specs=in_specs, out_specs=out_specs, check_vma=False
    )
```

profile of v0, /device:TPU:1, one launch (start us, length us, event | category | flops | bytes accessed | tf_op | source)
XLA Modules:
  0.0 426.3 jit_solution(13344961360590823993)
XLA Ops:
  0.7 0.7 copy-done.6
  2.2 0.1 reshape.501
  2.3 6.9 %gather_fusion = f32[1088]{0:T(1024)S(1)} fusion(f32[16,68]{1,0:T(8,128)S(1)} %get-tuple-element.22, s32[1088]{0:T(1024)S(1)} %reshape.501), kind=kCustom, calls=%fused_computation.clone | custom fusion | bytes 17408 | tf_op jit(solution)/shard_map/jit(take_along_axis)/gather | solution.py:16
  9.3 5.4 %collective-permute-start = (f32[1,1,16,68]{3,2,1,0:T(8,128)S(1)}, f32[1,1,16,68]{3,2,1,0:T(8,128)S(1)}, u32[]{:S(2)}, u32[]{:S(2)}) collective-permute-start(f32[1,1,16,68]{3,2,1,0:T(8,128)S(1)} %broadcast_select_fusion.3), channel_id=1, source_target_pairs={{0,1},{1,2},{2,3},{3,4},{4,5},{5,6},{6,7},{7,8},{8,9},{9,10},{10,1... | collective-permute-start | bytes 13064 | tf_op jit(solution)/shard_map/ppermute | solution.py:12
  14.8 6.9 %gather_fusion.1 = f32[1088]{0:T(1024)S(1)} fusion(f32[16,68]{1,0:T(8,128)S(1)} %get-tuple-element.23, s32[1088]{0:T(1024)S(1)} %reshape.507), kind=kCustom, calls=%fused_computation.1.clone | custom fusion | bytes 17408 | tf_op jit(solution)/shard_map/jit(take_along_axis)/gather | solution.py:16
  21.7 3.1 collective-permute-start.1
  24.9 0.8 collective-permute-done.1
  25.6 0.2 fusion.2
  25.9 3.4 collective-permute-start.2
  29.3 1.5 collective-permute-done.2
  30.9 6.9 %gather_fusion.2 = f32[1088]{0:T(1024)S(1)} fusion(f32[16,68]{1,0:T(8,128)S(1)} %bitcast.83, s32[1088]{0:T(1024)S(1)} %reshape.501), kind=kCustom, calls=%fused_computation.2.clone | custom fusion | bytes 17408 | tf_op jit(solution)/shard_map/jit(take_along_axis)/gather | solution.py:16
  37.9 1.3 collective-permute-start.3
  39.2 3.4 collective-permute-done.3
  42.5 6.9 %gather_fusion.3 = f32[1088]{0:T(1024)S(1)} fusion(f32[16,68]{1,0:T(8,128)S(1)} %bitcast.84, s32[1088]{0:T(1024)S(1)} %reshape.507), kind=kCustom, calls=%fused_computation.3.clone | custom fusion | bytes 17408 | tf_op jit(solution)/shard_map/jit(take_along_axis)/gather | solution.py:16
  49.6 0.2 multiply_reduce_fusion.2
  49.8 105.7 %psum.21 = f32[16]{0:T(128)S(1)} all-reduce(f32[16]{0:T(128)S(1)} %multiply_reduce_fusion.2), channel_id=1, replica_groups=mesh['px'=32,'py'=16] {'px','py'}, use_global_device_ids=true, to_apply=%region_1.3 | all-reduce | flops 16 | bytes 128 | tf_op jit(solution)/shard_map/psum | solution.py:90
  155.7 6.9 %gather_fusion.4 = f32[1088]{0:T(1024)S(1)} fusion(f32[16,68]{1,0:T(8,128)S(1)} %get-tuple-element.20, s32[1088]{0:T(1024)S(1)} %reshape.501), kind=kCustom, calls=%fused_computation.4.clone | custom fusion | bytes 17408 | tf_op jit(solution)/shard_map/jit(take_along_axis)/gather | solution.py:16
  162.6 2.8 collective-permute-start.4
  165.5 6.9 %gather_fusion.5 = f32[1088]{0:T(1024)S(1)} fusion(f32[16,68]{1,0:T(8,128)S(1)} %get-tuple-element.21, s32[1088]{0:T(1024)S(1)} %reshape.507), kind=kCustom, calls=%fused_computation.5.clone | custom fusion | bytes 17408 | tf_op jit(solution)/shard_map/jit(take_along_axis)/gather | solution.py:16
  172.5 2.7 collective-permute-start.5
  175.2 0.7 collective-permute-done.5
  176.0 0.2 convolution_multiply_fusion.2
  176.3 0.1 reshape.340
  176.4 2.8 collective-permute-start.6
  179.1 0.7 collective-permute-done.6
  179.8 3.9 collective-permute-start.7
  183.8 0.7 collective-permute-done.7
  184.5 0.1 reshape.341
  184.6 0.6 copy-done.8
  185.1 0.2 fusion.19
  185.4 0.1 reshape.344
  185.4 2.3 collective-permute-start.8
  187.8 3.9 collective-permute-done.8
  191.7 1.3 collective-permute-start.9
  193.0 0.2 convolution_multiply_fusion
  193.2 3.3 collective-permute-done.9
  196.5 0.1 reshape.345
  196.6 0.2 fusion.1
  196.9 1.9 collective-permute-start.10
  198.9 3.0 collective-permute-done.10
  201.9 6.9 %gather_fusion.6 = f32[1088]{0:T(1024)S(1)} fusion(f32[16,68]{1,0:T(8,128)S(1)} %bitcast.81, s32[1088]{0:T(1024)S(1)} %reshape.501), kind=kCustom, calls=%fused_computation.6.clone | custom fusion | bytes 17408 | tf_op jit(solution)/shard_map/jit(take_along_axis)/gather | solution.py:16
  208.9 1.3 collective-permute-start.11
  210.2 3.1 collective-permute-done.11
  213.3 6.9 %gather_fusion.7 = f32[1088]{0:T(1024)S(1)} fusion(f32[16,68]{1,0:T(8,128)S(1)} %bitcast.82, s32[1088]{0:T(1024)S(1)} %reshape.507), kind=kCustom, calls=%fused_computation.7.clone | custom fusion | bytes 17408 | tf_op jit(solution)/shard_map/jit(take_along_axis)/gather | solution.py:16
  220.3 0.2 multiply_reduce_fusion.1
  220.5 110.4 %psum.22 = f32[16]{0:T(128)S(1)} all-reduce(f32[16]{0:T(128)S(1)} %multiply_reduce_fusion.1), channel_id=1, replica_groups=mesh['px'=32,'py'=16] {'px','py'}, use_global_device_ids=true, to_apply=%region_3.5 | all-reduce | flops 16 | bytes 128 | tf_op jit(solution)/shard_map/psum | solution.py:129
  330.9 0.8 multiply_reduce_fusion
  331.7 94.6 %psum.23 = f32[16]{0:T(128)} all-reduce(f32[16]{0:T(128)S(1)} %get-tuple-element.6), channel_id=1, replica_groups=mesh['px'=32,'py'=16] {'px','py'}, use_global_device_ids=true, to_apply=%region_5.7 | all-reduce | flops 16 | bytes 128 | tf_op jit(solution)/shard_map/psum | solution.py:133
  (63 shorter events, 1.7 us)
Async XLA Ops:
  0.6 25.0 %copy-start = (bf16[1,1,272,272]{3,2,1,0:T(8,128)(2,1)S(1)}, bf16[1,1,272,272]{3,2,1,0:T(8,128)(2,1)}, u32[]{:S(2)}) copy-start(bf16[1,1,272,272]{3,2,1,0:T(8,128)(2,1)} %param.17) | copy-start | bytes 443908
  0.6 0.7 copy-start.6
  1.4 0.7 copy-start.3
  9.3 15.6 %collective-permute-start = (f32[1,1,16,68]{3,2,1,0:T(8,128)S(1)}, f32[1,1,16,68]{3,2,1,0:T(8,128)S(1)}, u32[]{:S(2)}, u32[]{:S(2)}) collective-permute-start(f32[1,1,16,68]{3,2,1,0:T(8,128)S(1)} %broadcast_select_fusion.3), channel_id=1, source_target_pairs={{0,1},{1,2},{2,3},{3,4},{4,5},{5,6},{6,7},{7,8},{8,9},{9,10},{10,1... | collective-permute-start | bytes 13064 | tf_op jit(solution)/shard_map/ppermute | solution.py:12
  21.7 3.9 collective-permute-start.1
  25.9 5.0 %collective-permute-start.2 = (f32[1,1,16,68]{3,2,1,0:T(8,128)S(1)}, f32[1,1,16,68]{3,2,1,0:T(8,128)S(1)}, u32[]{:S(2)}, u32[]{:S(2)}) collective-permute-start(f32[1,1,16,68]{3,2,1,0:T(8,128)S(1)} %slice.109), channel_id=1, source_target_pairs={{1,0},{2,1},{3,2},{4,3},{5,4},{6,5},{7,6},{8,7},{9,8},{10,9},{11,1... | collective-permute-start | bytes 13064 | tf_op jit(solution)/shard_map/ppermute | solution.py:12
  37.9 4.6 %collective-permute-start.3 = (f32[1,1,16,68]{3,2,1,0:T(8,128)S(1)}, f32[1,1,16,68]{3,2,1,0:T(8,128)S(1)}, u32[]{:S(2)}, u32[]{:S(2)}) collective-permute-start(f32[1,1,16,68]{3,2,1,0:T(8,128)S(1)} %get-tuple-element.19), channel_id=1, source_target_pairs={{16,0},{32,16},{48,32},{64,48},{80,64},{96,80},{112,96},{128,112},... | collective-permute-start | bytes 13064 | tf_op jit(solution)/shard_map/ppermute | solution.py:12
  49.6 105.9 %copy-start.4 = (f32[1,1,16,136]{3,2,1,0:T(8,128)S(1)}, f32[1,1,16,136]{3,2,1,0:T(8,128)}, u32[]{:S(2)}) copy-start(f32[1,1,16,136]{3,2,1,0:T(8,128)} %param.14) | copy-start | bytes 26116
  49.8 105.7 %copy-start.9 = (f32[16]{0:T(128)S(1)}, f32[16]{0:T(128)}, u32[]{:S(2)}) copy-start(f32[16]{0:T(128)} %param.15) | copy-start | bytes 196
  155.5 175.4 %copy-start.10 = (f32[16]{0:T(128)}, f32[16]{0:T(128)S(1)}, u32[]{:S(2)}) copy-start(f32[16]{0:T(128)S(1)} %psum.21) | copy-start | bytes 196
  155.6 175.3 %copy-start.1 = (f32[1,1,16,136]{3,2,1,0:T(8,128)}, f32[1,1,16,136]{3,2,1,0:T(8,128)S(1)}, u32[]{:S(2)}) copy-start(f32[1,1,16,136]{3,2,1,0:T(8,128)S(1)} %get-tuple-element.9) | copy-start | bytes 26116
  162.6 12.6 %collective-permute-start.4 = (f32[1,1,16,68]{3,2,1,0:T(8,128)S(1)}, f32[1,1,16,68]{3,2,1,0:T(8,128)S(1)}, u32[]{:S(2)}, u32[]{:S(2)}) collective-permute-start(f32[1,1,16,68]{3,2,1,0:T(8,128)S(1)} %broadcast_select_fusion.1), channel_id=1, source_target_pairs={{0,1},{1,2},{2,3},{3,4},{4,5},{5,6},{6,7},{7,8},{8,9},{9,10},{10,1... | collective-permute-start | bytes 13064 | tf_op jit(solution)/shard_map/ppermute | solution.py:12
  165.5 27.5 %copy-start.2 = (bf16[1,1,272,272]{3,2,1,0:T(8,128)(2,1)S(1)}, bf16[1,1,272,272]{3,2,1,0:T(8,128)(2,1)}, u32[]{:S(2)}) copy-start(bf16[1,1,272,272]{3,2,1,0:T(8,128)(2,1)} %param.16) | copy-start | bytes 443908
  172.5 3.5 collective-permute-start.5
  175.2 0.8 copy-start.7
  176.4 3.5 collective-permute-start.6
  179.8 4.6 %collective-permute-start.7 = (f32[1,2,128]{2,1,0:T(2,128)S(1)}, f32[1,2,128]{2,1,0:T(2,128)S(1)}, u32[]{:S(2)}, u32[]{:S(2)}) collective-permute-start(f32[1,2,128]{2,1,0:T(2,128)S(1)} %pad_maximum_fusion.4), channel_id=1, source_target_pairs={{0,16},{16,32},{32,48},{48,64},{64,80},{80,96},{96,112},{112,128},... | collective-permute-start | bytes 3080 | tf_op jit(solution)/shard_map/ppermute | solution.py:12
  184.5 0.7 copy-start.8
  185.4 6.2 %collective-permute-start.8 = (f32[1,1,32]{2,1,0:T(1,128)S(1)}, f32[1,1,32]{2,1,0:T(1,128)S(1)}, u32[]{:S(2)}, u32[]{:S(2)}) collective-permute-start(f32[1,1,32]{2,1,0:T(1,128)S(1)} %reshape.344), channel_id=1, source_target_pairs={{1,0},{2,1},{3,2},{4,3},{5,4},{6,5},{7,6},{8,7},{9,8},{10,9},{11,1... | collective-permute-start | bytes 392 | tf_op jit(solution)/shard_map/ppermute | solution.py:12
  191.7 4.8 %collective-permute-start.9 = (f32[1,2,32]{2,1,0:T(2,128)S(1)}, f32[1,2,32]{2,1,0:T(2,128)S(1)}, u32[]{:S(2)}, u32[]{:S(2)}) collective-permute-start(f32[1,2,32]{2,1,0:T(2,128)S(1)} %pad_maximum_fusion.5), channel_id=1, source_target_pairs={{16,0},{32,16},{48,32},{64,48},{80,64},{96,80},{112,96},{128,112},... | collective-permute-start | bytes 776 | tf_op jit(solution)/shard_map/ppermute | solution.py:12
  196.9 5.0 %collective-permute-start.10 = (f32[1,1,16,68]{3,2,1,0:T(8,128)S(1)}, f32[1,1,16,68]{3,2,1,0:T(8,128)S(1)}, u32[]{:S(2)}, u32[]{:S(2)}) collective-permute-start(f32[1,1,16,68]{3,2,1,0:T(8,128)S(1)} %slice.123), channel_id=1, source_target_pairs={{1,0},{2,1},{3,2},{4,3},{5,4},{6,5},{7,6},{8,7},{9,8},{10,9},{11,1... | collective-permute-start | bytes 13064 | tf_op jit(solution)/shard_map/ppermute | solution.py:12
  208.9 4.4 %collective-permute-start.11 = (f32[1,1,16,68]{3,2,1,0:T(8,128)S(1)}, f32[1,1,16,68]{3,2,1,0:T(8,128)S(1)}, u32[]{:S(2)}, u32[]{:S(2)}) collective-permute-start(f32[1,1,16,68]{3,2,1,0:T(8,128)S(1)} %get-tuple-element.17), channel_id=1, source_target_pairs={{16,0},{32,16},{48,32},{64,48},{80,64},{96,80},{112,96},{128,112},... | collective-permute-start | bytes 13064 | tf_op jit(solution)/shard_map/ppermute | solution.py:12
  220.3 110.6 %copy-start.5 = (f32[1,1,16,136]{3,2,1,0:T(8,128)S(1)}, f32[1,1,16,136]{3,2,1,0:T(8,128)}, u32[]{:S(2)}) copy-start(f32[1,1,16,136]{3,2,1,0:T(8,128)} %param.12) | copy-start | bytes 26116
where the time goes:
time: 427 us; the launch traced here: 426 us
  blocking collectives  311 us (73%)
  local copies, waits for them, and re-layouts  57.8 us (14%)
  starting transfers between devices  32.2 us (8%)
  waiting for transfers between devices  21.2 us (5%)
    psum x1, blocking collectives, on_device(): lax.psum(jnp.sum(new_direction * image, axis=(0, 1, 3)), ('px', 'py'))  110 us
    psum x1, blocking collectives, on_device(): lax.psum(jnp.sum(start_res * precond, axis=(0, 1, 3)), ('px', 'py'))  106 us
    psum x1, blocking collectives, on_device(): lax.psum(jnp.sum(new_residual * new_residual, axis=(0, 1, 3)), ('px', 'py'))  94.6 us
    gather x18, local copies, waits for them, and re-layouts, permute_side(): jnp.take_along_axis(values, jnp.broadcast_to(order[:, :, None, :], values...  55.7 us
    ppermute x12, starting transfers between devices, passed_along(): return lax.ppermute(value, axis, pairs)  32.2 us
    ppermute x12, waiting for transfers between devices, passed_along(): return lax.ppermute(value, axis, pairs)  21.2 us
  transfers between devices with their start and end apart: 12, of which 10 were waited for; matrix products, arithmetic and copies ran while one was open for 3% of the time, Pallas kernels for 0%

commit v1 on v0

--- a/solution.py
+++ b/solution.py
@@ -12,8 +12,24 @@
     return lax.ppermute(value, axis, pairs)
 
 
-def permute_side(values, order):
-    return jnp.take_along_axis(values, jnp.broadcast_to(order[:, :, None, :], values.shape), axis=3)
+def all_sum(value):
+    for axis in ("py", "px"):
+        peers = lax.axis_size(axis)
+        if peers & (peers - 1):
+            value = lax.psum(value, axis)
+            continue
+        step = 1
+        while step < peers:
+            value = value + lax.ppermute(value, axis, [(i, i ^ step) for i in range(peers)])
+            step *= 2
+    return value
+
+
+def permute_side(values, flip):
+    shape = values.shape
+    pairs = values.reshape(shape[:-1] + (shape[-1] // 2, 2))
+    reversed_pairs = jnp.flip(pairs, axis=-2).reshape(shape)
+    return jnp.where(flip[:, :, None, None], reversed_pairs, values)
 
 
 def on_device(
@@ -47,18 +63,22 @@
     vertex_mask = ((grid_row >= 1)[:, None] & (grid_col >= 1)[None, :]).astype(jnp.float32)[
         :, :, None, None
     ]
-    east_order = matching[:, :, 0]
-    north_order = matching[:, :, 1]
+    east_flip = matching[:, :, 0, 0] != 0
+    north_flip = matching[:, :, 1, 0] != 0
 
-    def spread_b(vector):
+    def spread_parts(vector):
         east_part = vector[..., :SIDE]
         north_part = vector[..., SIDE:]
-        east_perm = permute_side(east_part, east_order)
-        north_perm = permute_side(north_part, north_order)
+        east_perm = permute_side(east_part, east_flip)
+        north_perm = permute_side(north_part, north_flip)
         west_edge = passed_along(east_perm, "py", 1)
         from_west = jnp.concatenate([west_edge, east_perm[:, :-1]], 1)
         south_edge = passed_along(north_perm, "px", 1)
         from_south = jnp.concatenate([south_edge, north_perm[:-1]], 0)
+        return east_part, north_part, from_west, from_south
+
+    def spread_of(parts):
+        east_part, north_part, from_west, from_south = parts
         return jnp.concatenate([east_part, north_part, -from_west, -from_south], 3)
 
     def jump_b(side_values):
@@ -68,8 +88,8 @@
         from_east = jnp.concatenate([west_side[:, 1:], east_edge], 1)
         north_edge = passed_along(south_side, "px", -1)
         from_north = jnp.concatenate([south_side[1:], north_edge], 0)
-        east_term = permute_side(from_east, east_order)
-        north_term = permute_side(from_north, north_order)
+        east_term = permute_side(from_east, east_flip)
+        north_term = permute_side(from_north, north_flip)
         joined = jnp.concatenate(
             [side_values[..., :SIDE] - east_term, side_values[..., SIDE : 2 * SIDE] - north_term], 3
         )
@@ -84,13 +104,18 @@
     start_sol = solution * edge_mask
     start_res = residual * edge_mask
     start_dir = direction * edge_mask
-    spread = spread_b(0.5 * start_res).astype(jnp.bfloat16)
+    dir_parts = spread_parts(start_dir)
+    spread = spread_of(spread_parts(0.5 * start_res)).astype(jnp.bfloat16)
     side_values = patch_products(dual_schur, spread)
     precond = 0.5 * jump_b(side_values)
-    rz_current = lax.psum(jnp.sum(start_res * precond, axis=(0, 1, 3)), ("px", "py"))
+    precond_parts = spread_parts(precond)
+    rz_current = all_sum(jnp.sum(start_res * precond, axis=(0, 1, 3)))
     step_ratio = rz_current / rz_previous
-    new_direction = precond + step_ratio[None, None, :, None] * start_dir
-    spread = spread_b(new_direction).astype(jnp.bfloat16)
+    ratio = step_ratio[None, None, :, None]
+    new_direction = precond + ratio * start_dir
+    spread = spread_of(
+        tuple(p + ratio * d for p, d in zip(precond_parts, dir_parts))
+    ).astype(jnp.bfloat16)
     inner_part = patch_products(dual_inverse, spread)
     corner = (
         jnp.einsum("rpkb,rpcb->rpck", coupling, spread, preferred_element_type=jnp.float32) * active
@@ -126,11 +151,11 @@
         precision=lax.Precision.HIGHEST,
     )
     image = jump_b((inner_part + correction) * active)
-    curvature = lax.psum(jnp.sum(new_direction * image, axis=(0, 1, 3)), ("px", "py"))
+    curvature = all_sum(jnp.sum(new_direction * image, axis=(0, 1, 3)))
     step_length = rz_current / curvature
     new_solution = start_sol + step_length[None, None, :, None] * new_direction
     new_residual = start_res - step_length[None, None, :, None] * image
-    residual_sq = lax.psum(jnp.sum(new_residual * new_residual, axis=(0, 1, 3)), ("px", "py"))
+    residual_sq = all_sum(jnp.sum(new_residual * new_residual, axis=(0, 1, 3)))
     return (new_solution, new_residual, new_direction, rz_current, residual_sq)
 
 

time: 427 us -> 263 us (0.62)
  the two profiles are of different devices: /device:TPU:1 before, /device:TPU:30 now
where the time goes in v1:
time: 263 us; the launch traced here: 262 us
  waiting for transfers between devices  126 us (48%)
  starting transfers between devices  123 us (47%)
  local copies, waits for them, and re-layouts  5.11 us (2%)
  between operations  3.29 us (1%)
    ppermute x27, waiting for transfers between devices, all_sum(): lax.ppermute(value, axis, [(i, i ^ step) for i in range(peers)])  89.4 us
    ppermute x27, starting transfers between devices, all_sum(): lax.ppermute(value, axis, [(i, i ^ step) for i in range(peers)])  89.4 us
    ppermute x14, waiting for transfers between devices, passed_along(): return lax.ppermute(value, axis, pairs)  36.9 us
    ppermute x14, starting transfers between devices, passed_along(): return lax.ppermute(value, axis, pairs)  34.1 us
  transfers between devices with their start and end apart: 41, of which 37 were waited for; matrix products, arithmetic and copies ran while one was open for 0% of the time, Pallas kernels for 0%

profile of v1, /device:TPU:30, one launch (start us, length us, event | category | flops | bytes accessed | tf_op | source)
XLA Modules:
  0.0 261.6 jit_solution(12209118855814680407)
XLA Ops:
  6.1 4.6 %collective-permute-start.1 = (f32[1,1,16,68]{3,2,1,0:T(8,128)S(1)}, f32[1,1,16,68]{3,2,1,0:T(8,128)S(1)}, u32[]{:S(2)}, u32[]{:S(2)}) collective-permute-start(f32[1,1,16,68]{3,2,1,0:T(8,128)S(1)} %get-tuple-element.34), channel_id=1, source_target_pairs={{0,16},{16,32},{32,48},{48,64},{64,80},{80,96},{96,112},{112,128},... | collective-permute-start | bytes 13064 | tf_op jit(solution)/shard_map/ppermute | solution.py:12
  13.7 3.1 %collective-permute-done.2 = f32[1,1,16,68]{3,2,1,0:T(8,128)S(1)} collective-permute-done((f32[1,1,16,68]{3,2,1,0:T(8,128)S(1)}, f32[1,1,16,68]{3,2,1,0:T(8,128)S(1)}, u32[]{:S(2)}, u32[]{:S(2)}) %collective-permute-start.2) | collective-permute-done | bytes 4384 | tf_op jit(solution)/shard_map/ppermute | solution.py:12
  17.0 2.0 collective-permute-start.3
  19.4 6.5 %collective-permute-done.3 = f32[1,1,16,68]{3,2,1,0:T(8,128)S(1)} collective-permute-done((f32[1,1,16,68]{3,2,1,0:T(8,128)S(1)}, f32[1,1,16,68]{3,2,1,0:T(8,128)S(1)}, u32[]{:S(2)}, u32[]{:S(2)}) %collective-permute-start.3) | collective-permute-done | bytes 4384 | tf_op jit(solution)/shard_map/ppermute | solution.py:12
  26.3 3.4 %collective-permute-start.4 = (f32[16]{0:T(128)S(1)}, f32[16]{0:T(128)S(1)}, u32[]{:S(2)}, u32[]{:S(2)}) collective-permute-start(f32[16]{0:T(128)S(1)} %get-tuple-element.11), channel_id=1, source_target_pairs={{0,1},{1,0},{2,3},{3,2},{4,5},{5,4},{6,7},{7,6},{8,9},{9,8},{10,11... | collective-permute-start | bytes 200 | tf_op jit(solution)/shard_map/ppermute | solution.py:23
  30.6 4.3 %collective-permute-start.5 = (f32[16]{0:T(128)S(1)}, f32[16]{0:T(128)S(1)}, u32[]{:S(2)}, u32[]{:S(2)}) collective-permute-start(f32[16]{0:T(128)S(1)} %add.114), channel_id=1, source_target_pairs={{0,2},{1,3},{2,0},{3,1},{4,6},{5,7},{6,4},{7,5},{8,10},{9,11},{10,... | collective-permute-start | bytes 200 | tf_op jit(solution)/shard_map/ppermute | solution.py:23
  36.3 8.5 %collective-permute-start.6 = (f32[16]{0:T(128)S(1)}, f32[16]{0:T(128)S(1)}, u32[]{:S(2)}, u32[]{:S(2)}) collective-permute-start(f32[16]{0:T(128)S(1)} %add.115), channel_id=1, source_target_pairs={{0,4},{1,5},{2,6},{3,7},{4,0},{5,1},{6,2},{7,3},{8,12},{9,13},{10,... | collective-permute-start | bytes 200 | tf_op jit(solution)/shard_map/ppermute | solution.py:23
  46.4 6.8 %collective-permute-start.7 = (f32[16]{0:T(128)S(1)}, f32[16]{0:T(128)S(1)}, u32[]{:S(2)}, u32[]{:S(2)}) collective-permute-start(f32[16]{0:T(128)S(1)} %add.116), channel_id=1, source_target_pairs={{0,8},{1,9},{2,10},{3,11},{4,12},{5,13},{6,14},{7,15},{8,0},{9,1},... | collective-permute-start | bytes 200 | tf_op jit(solution)/shard_map/ppermute | solution.py:23
  53.3 2.4 collective-permute-done.7
  57.6 3.5 %collective-permute-done.8 = f32[16]{0:T(128)S(1)} collective-permute-done((f32[16]{0:T(128)S(1)}, f32[16]{0:T(128)S(1)}, u32[]{:S(2)}, u32[]{:S(2)}) %collective-permute-start.8) | collective-permute-done | bytes 96 | tf_op jit(solution)/shard_map/ppermute | solution.py:23
  63.1 4.9 %collective-permute-done.9 = f32[16]{0:T(128)S(1)} collective-permute-done((f32[16]{0:T(128)S(1)}, f32[16]{0:T(128)S(1)}, u32[]{:S(2)}, u32[]{:S(2)}) %collective-permute-start.9) | collective-permute-done | bytes 96 | tf_op jit(solution)/shard_map/ppermute | solution.py:23
  70.1 3.4 %collective-permute-done.10 = f32[16]{0:T(128)S(1)} collective-permute-done((f32[16]{0:T(128)S(1)}, f32[16]{0:T(128)S(1)}, u32[]{:S(2)}, u32[]{:S(2)}) %collective-permute-start.10) | collective-permute-done | bytes 96 | tf_op jit(solution)/shard_map/ppermute | solution.py:23
  75.4 4.4 %collective-permute-done.11 = f32[16]{0:T(128)S(1)} collective-permute-done((f32[16]{0:T(128)S(1)}, f32[16]{0:T(128)S(1)}, u32[]{:S(2)}, u32[]{:S(2)}) %collective-permute-start.11) | collective-permute-done | bytes 96 | tf_op jit(solution)/shard_map/ppermute | solution.py:23
  79.8 2.2 collective-permute-start.12
  82.1 7.1 %collective-permute-done.12 = f32[16]{0:T(128)S(1)} collective-permute-done((f32[16]{0:T(128)S(1)}, f32[16]{0:T(128)S(1)}, u32[]{:S(2)}, u32[]{:S(2)}) %collective-permute-start.12) | collective-permute-done | bytes 96 | tf_op jit(solution)/shard_map/ppermute | solution.py:23
  90.5 4.7 %collective-permute-start.14 = (f32[1,1,16,68]{3,2,1,0:T(8,128)S(1)}, f32[1,1,16,68]{3,2,1,0:T(8,128)S(1)}, u32[]{:S(2)}, u32[]{:S(2)}) collective-permute-start(f32[1,1,16,68]{3,2,1,0:T(8,128)S(1)} %get-tuple-element.27), channel_id=1, source_target_pairs={{0,1},{1,2},{2,3},{3,4},{4,5},{5,6},{6,7},{7,8},{8,9},{9,10},{10,1... | collective-permute-start | bytes 13064 | tf_op jit(solution)/shard_map/ppermute | solution.py:12
  95.2 3.6 %collective-permute-start.15 = (f32[1,1,16,68]{3,2,1,0:T(8,128)S(1)}, f32[1,1,16,68]{3,2,1,0:T(8,128)S(1)}, u32[]{:S(2)}, u32[]{:S(2)}) collective-permute-start(f32[1,1,16,68]{3,2,1,0:T(8,128)S(1)} %get-tuple-element.26), channel_id=1, source_target_pairs={{0,16},{16,32},{32,48},{48,64},{64,80},{80,96},{96,112},{112,128},... | collective-permute-start | bytes 13064 | tf_op jit(solution)/shard_map/ppermute | solution.py:12
  98.8 1.9 collective-permute-start.16
  100.8 3.6 %collective-permute-done.16 = f32[1,1,16,68]{3,2,1,0:T(8,128)S(1)} collective-permute-done((f32[1,1,16,68]{3,2,1,0:T(8,128)S(1)}, f32[1,1,16,68]{3,2,1,0:T(8,128)S(1)}, u32[]{:S(2)}, u32[]{:S(2)}) %collective-permute-start.16) | collective-permute-done | bytes 4384 | tf_op jit(solution)/shard_map/ppermute | solution.py:12
  107.6 5.3 %collective-permute-start.18 = (f32[1,2,128]{2,1,0:T(2,128)S(1)}, f32[1,2,128]{2,1,0:T(2,128)S(1)}, u32[]{:S(2)}, u32[]{:S(2)}) collective-permute-start(f32[1,2,128]{2,1,0:T(2,128)S(1)} %pad_maximum_fusion.2), channel_id=1, source_target_pairs={{0,16},{16,32},{32,48},{48,64},{64,80},{80,96},{96,112},{112,128},... | collective-permute-start | bytes 3080 | tf_op jit(solution)/shard_map/ppermute | solution.py:12
  116.4 2.5 collective-permute-done.19
  118.9 1.9 collective-permute-start.20
  121.1 6.6 %collective-permute-done.20 = f32[1,2,32]{2,1,0:T(2,128)S(1)} collective-permute-done((f32[1,2,32]{2,1,0:T(2,128)S(1)}, f32[1,2,32]{2,1,0:T(2,128)S(1)}, u32[]{:S(2)}, u32[]{:S(2)}) %collective-permute-start.20) | collective-permute-done | bytes 288 | tf_op jit(solution)/shard_map/ppermute | solution.py:12
  129.4 4.4 %collective-permute-done.21 = f32[1,1,16,68]{3,2,1,0:T(8,128)S(1)} collective-permute-done((f32[1,1,16,68]{3,2,1,0:T(8,128)S(1)}, f32[1,1,16,68]{3,2,1,0:T(8,128)S(1)}, u32[]{:S(2)}, u32[]{:S(2)}) %collective-permute-start.21) | collective-permute-done | bytes 4384 | tf_op jit(solution)/shard_map/ppermute | solution.py:12
  134.0 1.9 collective-permute-start.22
  135.9 6.9 %collective-permute-done.22 = f32[1,1,16,68]{3,2,1,0:T(8,128)S(1)} collective-permute-done((f32[1,1,16,68]{3,2,1,0:T(8,128)S(1)}, f32[1,1,16,68]{3,2,1,0:T(8,128)S(1)}, u32[]{:S(2)}, u32[]{:S(2)}) %collective-permute-start.22) | collective-permute-done | bytes 4384 | tf_op jit(solution)/shard_map/ppermute | solution.py:12
  143.4 3.3 %collective-permute-start.23 = (f32[16]{0:T(128)S(1)}, f32[16]{0:T(128)S(1)}, u32[]{:S(2)}, u32[]{:S(2)}) collective-permute-start(f32[16]{0:T(128)S(1)} %get-tuple-element.7), channel_id=1, source_target_pairs={{0,1},{1,0},{2,3},{3,2},{4,5},{5,4},{6,7},{7,6},{8,9},{9,8},{10,11... | collective-permute-start | bytes 200 | tf_op jit(solution)/shard_map/ppermute | solution.py:23
  147.5 3.9 %collective-permute-start.24 = (f32[16]{0:T(128)S(1)}, f32[16]{0:T(128)S(1)}, u32[]{:S(2)}, u32[]{:S(2)}) collective-permute-start(f32[16]{0:T(128)S(1)} %add.132), channel_id=1, source_target_pairs={{0,2},{1,3},{2,0},{3,1},{4,6},{5,7},{6,4},{7,5},{8,10},{9,11},{10,... | collective-permute-start | bytes 200 | tf_op jit(solution)/shard_map/ppermute | solution.py:23
  152.9 5.5 %collective-permute-start.25 = (f32[16]{0:T(128)S(1)}, f32[16]{0:T(128)S(1)}, u32[]{:S(2)}, u32[]{:S(2)}) collective-permute-start(f32[16]{0:T(128)S(1)} %add.133), channel_id=1, source_target_pairs={{0,4},{1,5},{2,6},{3,7},{4,0},{5,1},{6,2},{7,3},{8,12},{9,13},{10,... | collective-permute-start | bytes 200 | tf_op jit(solution)/shard_map/ppermute | solution.py:23
  159.9 7.1 %collective-permute-start.26 = (f32[16]{0:T(128)S(1)}, f32[16]{0:T(128)S(1)}, u32[]{:S(2)}, u32[]{:S(2)}) collective-permute-start(f32[16]{0:T(128)S(1)} %add.134), channel_id=1, source_target_pairs={{0,8},{1,9},{2,10},{3,11},{4,12},{5,13},{6,14},{7,15},{8,0},{9,1},... | collective-permute-start | bytes 200 | tf_op jit(solution)/shard_map/ppermute | solution.py:23
  167.0 2.3 collective-permute-done.26
  171.1 3.5 %collective-permute-done.27 = f32[16]{0:T(128)S(1)} collective-permute-done((f32[16]{0:T(128)S(1)}, f32[16]{0:T(128)S(1)}, u32[]{:S(2)}, u32[]{:S(2)}) %collective-permute-start.27) | collective-permute-done | bytes 96 | tf_op jit(solution)/shard_map/ppermute | solution.py:23
  176.6 5.0 %collective-permute-done.28 = f32[16]{0:T(128)S(1)} collective-permute-done((f32[16]{0:T(128)S(1)}, f32[16]{0:T(128)S(1)}, u32[]{:S(2)}, u32[]{:S(2)}) %collective-permute-start.28) | collective-permute-done | bytes 96 | tf_op jit(solution)/shard_map/ppermute | solution.py:23
  181.6 1.9 collective-permute-start.29
  183.5 3.5 %collective-permute-done.29 = f32[16]{0:T(128)S(1)} collective-permute-done((f32[16]{0:T(128)S(1)}, f32[16]{0:T(128)S(1)}, u32[]{:S(2)}, u32[]{:S(2)}) %collective-permute-start.29) | collective-permute-done | bytes 96 | tf_op jit(solution)/shard_map/ppermute | solution.py:23
  187.0 1.9 collective-permute-start.30
  188.9 4.4 %collective-permute-done.30 = f32[16]{0:T(128)S(1)} collective-permute-done((f32[16]{0:T(128)S(1)}, f32[16]{0:T(128)S(1)}, u32[]{:S(2)}, u32[]{:S(2)}) %collective-permute-start.30) | collective-permute-done | bytes 96 | tf_op jit(solution)/shard_map/ppermute | solution.py:23
  195.3 7.4 %collective-permute-done.31 = f32[16]{0:T(128)S(1)} collective-permute-done((f32[16]{0:T(128)S(1)}, f32[16]{0:T(128)S(1)}, u32[]{:S(2)}, u32[]{:S(2)}) %collective-permute-start.31) | collective-permute-done | bytes 96 | tf_op jit(solution)/shard_map/ppermute | solution.py:23
  203.5 1.9 collective-permute-start.32
  206.5 3.9 %collective-permute-start.33 = (f32[16]{0:T(128)S(1)}, f32[16]{0:T(128)S(1)}, u32[]{:S(2)}, u32[]{:S(2)}) collective-permute-start(f32[16]{0:T(128)S(1)} %add.142), channel_id=1, source_target_pairs={{0,2},{1,3},{2,0},{3,1},{4,6},{5,7},{6,4},{7,5},{8,10},{9,11},{10,... | collective-permute-start | bytes 200 | tf_op jit(solution)/shard_map/ppermute | solution.py:23
  211.9 4.8 %collective-permute-start.34 = (f32[16]{0:T(128)S(1)}, f32[16]{0:T(128)S(1)}, u32[]{:S(2)}, u32[]{:S(2)}) collective-permute-start(f32[16]{0:T(128)S(1)} %add.143), channel_id=1, source_target_pairs={{0,4},{1,5},{2,6},{3,7},{4,0},{5,1},{6,2},{7,3},{8,12},{9,13},{10,... | collective-permute-start | bytes 200 | tf_op jit(solution)/shard_map/ppermute | solution.py:23
  218.3 7.1 %collective-permute-start.35 = (f32[16]{0:T(128)S(1)}, f32[16]{0:T(128)S(1)}, u32[]{:S(2)}, u32[]{:S(2)}) collective-permute-start(f32[16]{0:T(128)S(1)} %add.144), channel_id=1, source_target_pairs={{0,8},{1,9},{2,10},{3,11},{4,12},{5,13},{6,14},{7,15},{8,0},{9,1},... | collective-permute-start | bytes 200 | tf_op jit(solution)/shard_map/ppermute | solution.py:23
  225.3 2.3 collective-permute-done.35
  229.5 3.5 %collective-permute-done.36 = f32[16]{0:T(128)S(1)} collective-permute-done((f32[16]{0:T(128)S(1)}, f32[16]{0:T(128)S(1)}, u32[]{:S(2)}, u32[]{:S(2)}) %collective-permute-start.36) | collective-permute-done | bytes 96 | tf_op jit(solution)/shard_map/ppermute | solution.py:23
  234.9 5.0 %collective-permute-done.37 = f32[16]{0:T(128)S(1)} collective-permute-done((f32[16]{0:T(128)S(1)}, f32[16]{0:T(128)S(1)}, u32[]{:S(2)}, u32[]{:S(2)}) %collective-permute-start.37) | collective-permute-done | bytes 96 | tf_op jit(solution)/shard_map/ppermute | solution.py:23
  241.9 3.5 %collective-permute-done.38 = f32[16]{0:T(128)S(1)} collective-permute-done((f32[16]{0:T(128)S(1)}, f32[16]{0:T(128)S(1)}, u32[]{:S(2)}, u32[]{:S(2)}) %collective-permute-start.38) | collective-permute-done | bytes 96 | tf_op jit(solution)/shard_map/ppermute | solution.py:23
  247.3 4.4 %collective-permute-done.39 = f32[16]{0:T(128)S(1)} collective-permute-done((f32[16]{0:T(128)S(1)}, f32[16]{0:T(128)S(1)}, u32[]{:S(2)}, u32[]{:S(2)}) %collective-permute-start.39) | collective-permute-done | bytes 96 | tf_op jit(solution)/shard_map/ppermute | solution.py:23
  253.6 7.4 %collective-permute-done.40 = f32[16]{0:T(128)S(1)} collective-permute-done((f32[16]{0:T(128)S(1)}, f32[16]{0:T(128)S(1)}, u32[]{:S(2)}, u32[]{:S(2)}) %collective-permute-start.40) | collective-permute-done | bytes 96 | tf_op jit(solution)/shard_map/ppermute | solution.py:23
  (148 shorter events, 54.5 us)
Async XLA Ops:
  0.6 11.5 %copy-start = (bf16[1,1,272,272]{3,2,1,0:T(8,128)(2,1)S(1)}, bf16[1,1,272,272]{3,2,1,0:T(8,128)(2,1)}, u32[]{:S(2)}) copy-start(bf16[1,1,272,272]{3,2,1,0:T(8,128)(2,1)} %param.15) | copy-start | bytes 443908
  0.7 0.8 copy-start.5
  4.4 6.4 %collective-permute-start = (f32[1,1,16,68]{3,2,1,0:T(8,128)S(1)}, f32[1,1,16,68]{3,2,1,0:T(8,128)S(1)}, u32[]{:S(2)}, u32[]{:S(2)}) collective-permute-start(f32[1,1,16,68]{3,2,1,0:T(8,128)S(1)} %get-tuple-element.33), channel_id=1, source_target_pairs={{0,1},{1,2},{2,3},{3,4},{4,5},{5,6},{6,7},{7,8},{8,9},{9,10},{10,1... | collective-permute-start | bytes 13064 | tf_op jit(solution)/shard_map/ppermute | solution.py:12
  6.1 6.0 %collective-permute-start.1 = (f32[1,1,16,68]{3,2,1,0:T(8,128)S(1)}, f32[1,1,16,68]{3,2,1,0:T(8,128)S(1)}, u32[]{:S(2)}, u32[]{:S(2)}) collective-permute-start(f32[1,1,16,68]{3,2,1,0:T(8,128)S(1)} %get-tuple-element.34), channel_id=1, source_target_pairs={{0,16},{16,32},{32,48},{48,64},{64,80},{80,96},{96,112},{112,128},... | collective-permute-start | bytes 13064 | tf_op jit(solution)/shard_map/ppermute | solution.py:12
  12.4 4.4 %collective-permute-start.2 = (f32[1,1,16,68]{3,2,1,0:T(8,128)S(1)}, f32[1,1,16,68]{3,2,1,0:T(8,128)S(1)}, u32[]{:S(2)}, u32[]{:S(2)}) collective-permute-start(f32[1,1,16,68]{3,2,1,0:T(8,128)S(1)} %slice.100), channel_id=1, source_target_pairs={{1,0},{2,1},{3,2},{4,3},{5,4},{6,5},{7,6},{8,7},{9,8},{10,9},{11,1... | collective-permute-start | bytes 13064 | tf_op jit(solution)/shard_map/ppermute | solution.py:12
  17.0 8.9 %collective-permute-start.3 = (f32[1,1,16,68]{3,2,1,0:T(8,128)S(1)}, f32[1,1,16,68]{3,2,1,0:T(8,128)S(1)}, u32[]{:S(2)}, u32[]{:S(2)}) collective-permute-start(f32[1,1,16,68]{3,2,1,0:T(8,128)S(1)} %get-tuple-element.24), channel_id=1, source_target_pairs={{16,0},{32,16},{48,32},{64,48},{80,64},{96,80},{112,96},{128,112},... | collective-permute-start | bytes 13064 | tf_op jit(solution)/shard_map/ppermute | solution.py:12
  26.3 4.2 %collective-permute-start.4 = (f32[16]{0:T(128)S(1)}, f32[16]{0:T(128)S(1)}, u32[]{:S(2)}, u32[]{:S(2)}) collective-permute-start(f32[16]{0:T(128)S(1)} %get-tuple-element.11), channel_id=1, source_target_pairs={{0,1},{1,0},{2,3},{3,2},{4,5},{5,4},{6,7},{7,6},{8,9},{9,8},{10,11... | collective-permute-start | bytes 200 | tf_op jit(solution)/shard_map/ppermute | solution.py:23
  30.6 5.8 %collective-permute-start.5 = (f32[16]{0:T(128)S(1)}, f32[16]{0:T(128)S(1)}, u32[]{:S(2)}, u32[]{:S(2)}) collective-permute-start(f32[16]{0:T(128)S(1)} %add.114), channel_id=1, source_target_pairs={{0,2},{1,3},{2,0},{3,1},{4,6},{5,7},{6,4},{7,5},{8,10},{9,11},{10,... | collective-permute-start | bytes 200 | tf_op jit(solution)/shard_map/ppermute | solution.py:23
  36.3 10.0 %collective-permute-start.6 = (f32[16]{0:T(128)S(1)}, f32[16]{0:T(128)S(1)}, u32[]{:S(2)}, u32[]{:S(2)}) collective-permute-start(f32[16]{0:T(128)S(1)} %add.115), channel_id=1, source_target_pairs={{0,4},{1,5},{2,6},{3,7},{4,0},{5,1},{6,2},{7,3},{8,12},{9,13},{10,... | collective-permute-start | bytes 200 | tf_op jit(solution)/shard_map/ppermute | solution.py:23
  46.4 9.3 %collective-permute-start.7 = (f32[16]{0:T(128)S(1)}, f32[16]{0:T(128)S(1)}, u32[]{:S(2)}, u32[]{:S(2)}) collective-permute-start(f32[16]{0:T(128)S(1)} %add.116), channel_id=1, source_target_pairs={{0,8},{1,9},{2,10},{3,11},{4,12},{5,13},{6,14},{7,15},{8,0},{9,1},... | collective-permute-start | bytes 200 | tf_op jit(solution)/shard_map/ppermute | solution.py:23
  55.7 5.4 %collective-permute-start.8 = (f32[16]{0:T(128)S(1)}, f32[16]{0:T(128)S(1)}, u32[]{:S(2)}, u32[]{:S(2)}) collective-permute-start(f32[16]{0:T(128)S(1)} %add.117), channel_id=1, source_target_pairs={{0,16},{16,0},{32,48},{48,32},{64,80},{80,64},{96,112},{112,96},{1... | collective-permute-start | bytes 200 | tf_op jit(solution)/shard_map/ppermute | solution.py:23
  61.1 6.9 %collective-permute-start.9 = (f32[16]{0:T(128)S(1)}, f32[16]{0:T(128)S(1)}, u32[]{:S(2)}, u32[]{:S(2)}) collective-permute-start(f32[16]{0:T(128)S(1)} %add.118), channel_id=1, source_target_pairs={{0,32},{16,48},{32,0},{48,16},{64,96},{80,112},{96,64},{112,80},{1... | collective-permute-start | bytes 200 | tf_op jit(solution)/shard_map/ppermute | solution.py:23
  68.0 5.4 %collective-permute-start.10 = (f32[16]{0:T(128)S(1)}, f32[16]{0:T(128)S(1)}, u32[]{:S(2)}, u32[]{:S(2)}) collective-permute-start(f32[16]{0:T(128)S(1)} %add.119), channel_id=1, source_target_pairs={{0,64},{16,80},{32,96},{48,112},{64,0},{80,16},{96,32},{112,48},{1... | collective-permute-start | bytes 200 | tf_op jit(solution)/shard_map/ppermute | solution.py:23
  70.0 19.2 %copy-start.10 = (f32[16]{0:T(128)S(1)}, f32[16]{0:T(128)}, u32[]{:S(2)}) copy-start(f32[16]{0:T(128)} %param.13) | copy-start | bytes 196
  73.5 6.3 %collective-permute-start.11 = (f32[16]{0:T(128)S(1)}, f32[16]{0:T(128)S(1)}, u32[]{:S(2)}, u32[]{:S(2)}) collective-permute-start(f32[16]{0:T(128)S(1)} %add.120), channel_id=1, source_target_pairs={{0,128},{16,144},{32,160},{48,176},{64,192},{80,208},{96,224},{112... | collective-permute-start | bytes 200 | tf_op jit(solution)/shard_map/ppermute | solution.py:23
  75.4 45.4 %copy-start.1 = (bf16[1,1,272,272]{3,2,1,0:T(8,128)(2,1)S(1)}, bf16[1,1,272,272]{3,2,1,0:T(8,128)(2,1)}, u32[]{:S(2)}) copy-start(bf16[1,1,272,272]{3,2,1,0:T(8,128)(2,1)} %param.14) | copy-start | bytes 443908
  79.8 9.3 %collective-permute-start.12 = (f32[16]{0:T(128)S(1)}, f32[16]{0:T(128)S(1)}, u32[]{:S(2)}, u32[]{:S(2)}) collective-permute-start(f32[16]{0:T(128)S(1)} %add.121), channel_id=1, source_target_pairs={{0,256},{16,272},{32,288},{48,304},{64,320},{80,336},{96,352},{112... | collective-permute-start | bytes 200 | tf_op jit(solution)/shard_map/ppermute | solution.py:23
  89.1 113.5 %copy-start.7 = (f32[16]{0:T(128)}, f32[16]{0:T(128)S(1)}, u32[]{:S(2)}) copy-start(f32[16]{0:T(128)S(1)} %get-tuple-element.10) | copy-start | bytes 196
  89.2 11.6 %collective-permute-start.13 = (f32[1,1,16,68]{3,2,1,0:T(8,128)S(1)}, f32[1,1,16,68]{3,2,1,0:T(8,128)S(1)}, u32[]{:S(2)}, u32[]{:S(2)}) collective-permute-start(f32[1,1,16,68]{3,2,1,0:T(8,128)S(1)} %get-tuple-element.25), channel_id=1, source_target_pairs={{0,1},{1,2},{2,3},{3,4},{4,5},{5,6},{6,7},{7,8},{8,9},{9,10},{10,1... | collective-permute-start | bytes 13064 | tf_op jit(solution)/shard_map/ppermute | solution.py:12
  90.5 10.3 %collective-permute-start.14 = (f32[1,1,16,68]{3,2,1,0:T(8,128)S(1)}, f32[1,1,16,68]{3,2,1,0:T(8,128)S(1)}, u32[]{:S(2)}, u32[]{:S(2)}) collective-permute-start(f32[1,1,16,68]{3,2,1,0:T(8,128)S(1)} %get-tuple-element.27), channel_id=1, source_target_pairs={{0,1},{1,2},{2,3},{3,4},{4,5},{5,6},{6,7},{7,8},{8,9},{9,10},{10,1... | collective-permute-start | bytes 13064 | tf_op jit(solution)/shard_map/ppermute | solution.py:12
  95.2 5.6 %collective-permute-start.15 = (f32[1,1,16,68]{3,2,1,0:T(8,128)S(1)}, f32[1,1,16,68]{3,2,1,0:T(8,128)S(1)}, u32[]{:S(2)}, u32[]{:S(2)}) collective-permute-start(f32[1,1,16,68]{3,2,1,0:T(8,128)S(1)} %get-tuple-element.26), channel_id=1, source_target_pairs={{0,16},{16,32},{32,48},{48,64},{64,80},{80,96},{96,112},{112,128},... | collective-permute-start | bytes 13064 | tf_op jit(solution)/shard_map/ppermute | solution.py:12
  98.8 5.5 %collective-permute-start.16 = (f32[1,1,16,68]{3,2,1,0:T(8,128)S(1)}, f32[1,1,16,68]{3,2,1,0:T(8,128)S(1)}, u32[]{:S(2)}, u32[]{:S(2)}) collective-permute-start(f32[1,1,16,68]{3,2,1,0:T(8,128)S(1)} %get-tuple-element.28), channel_id=1, source_target_pairs={{0,16},{16,32},{32,48},{48,64},{64,80},{80,96},{96,112},{112,128},... | collective-permute-start | bytes 13064 | tf_op jit(solution)/shard_map/ppermute | solution.py:12
  105.5 2.1 collective-permute-start.17
  107.6 6.5 %collective-permute-start.18 = (f32[1,2,128]{2,1,0:T(2,128)S(1)}, f32[1,2,128]{2,1,0:T(2,128)S(1)}, u32[]{:S(2)}, u32[]{:S(2)}) collective-permute-start(f32[1,2,128]{2,1,0:T(2,128)S(1)} %pad_maximum_fusion.2), channel_id=1, source_target_pairs={{0,16},{16,32},{32,48},{48,64},{64,80},{80,96},{96,112},{112,128},... | collective-permute-start | bytes 3080 | tf_op jit(solution)/shard_map/ppermute | solution.py:12
  115.1 3.8 %collective-permute-start.19 = (f32[1,1,32]{2,1,0:T(1,128)S(1)}, f32[1,1,32]{2,1,0:T(1,128)S(1)}, u32[]{:S(2)}, u32[]{:S(2)}) collective-permute-start(f32[1,1,32]{2,1,0:T(1,128)S(1)} %reshape.421), channel_id=1, source_target_pairs={{1,0},{2,1},{3,2},{4,3},{5,4},{6,5},{7,6},{8,7},{9,8},{10,9},{11,1... | collective-permute-start | bytes 392 | tf_op jit(solution)/shard_map/ppermute | solution.py:12
  118.9 8.8 %collective-permute-start.20 = (f32[1,2,32]{2,1,0:T(2,128)S(1)}, f32[1,2,32]{2,1,0:T(2,128)S(1)}, u32[]{:S(2)}, u32[]{:S(2)}) collective-permute-start(f32[1,2,32]{2,1,0:T(2,128)S(1)} %pad_maximum_fusion.3), channel_id=1, source_target_pairs={{16,0},{32,16},{48,32},{64,48},{80,64},{96,80},{112,96},{128,112},... | collective-permute-start | bytes 776 | tf_op jit(solution)/shard_map/ppermute | solution.py:12
  128.1 5.7 %collective-permute-start.21 = (f32[1,1,16,68]{3,2,1,0:T(8,128)S(1)}, f32[1,1,16,68]{3,2,1,0:T(8,128)S(1)}, u32[]{:S(2)}, u32[]{:S(2)}) collective-permute-start(f32[1,1,16,68]{3,2,1,0:T(8,128)S(1)} %slice.116), channel_id=1, source_target_pairs={{1,0},{2,1},{3,2},{4,3},{5,4},{6,5},{7,6},{8,7},{9,8},{10,9},{11,1... | collective-permute-start | bytes 13064 | tf_op jit(solution)/shard_map/ppermute | solution.py:12
  134.0 8.9 %collective-permute-start.22 = (f32[1,1,16,68]{3,2,1,0:T(8,128)S(1)}, f32[1,1,16,68]{3,2,1,0:T(8,128)S(1)}, u32[]{:S(2)}, u32[]{:S(2)}) collective-permute-start(f32[1,1,16,68]{3,2,1,0:T(8,128)S(1)} %get-tuple-element.22), channel_id=1, source_target_pairs={{16,0},{32,16},{48,32},{64,48},{80,64},{96,80},{112,96},{128,112},... | collective-permute-start | bytes 13064 | tf_op jit(solution)/shard_map/ppermute | solution.py:12
  143.3 60.2 %copy-start.3 = (f32[1,1,16,136]{3,2,1,0:T(8,128)}, f32[1,1,16,136]{3,2,1,0:T(8,128)S(1)}, u32[]{:S(2)}) copy-start(f32[1,1,16,136]{3,2,1,0:T(8,128)S(1)} %get-tuple-element.8) | copy-start | bytes 26116
  143.3 59.3 %copy-start.4 = (f32[1,1,16,136]{3,2,1,0:T(8,128)S(1)}, f32[1,1,16,136]{3,2,1,0:T(8,128)}, u32[]{:S(2)}) copy-start(f32[1,1,16,136]{3,2,1,0:T(8,128)} %param.10) | copy-start | bytes 26116
  143.4 4.1 %collective-permute-start.23 = (f32[16]{0:T(128)S(1)}, f32[16]{0:T(128)S(1)}, u32[]{:S(2)}, u32[]{:S(2)}) collective-permute-start(f32[16]{0:T(128)S(1)} %get-tuple-element.7), channel_id=1, source_target_pairs={{0,1},{1,0},{2,3},{3,2},{4,5},{5,4},{6,7},{7,6},{8,9},{9,8},{10,11... | collective-permute-start | bytes 200 | tf_op jit(solution)/shard_map/ppermute | solution.py:23
  147.5 5.4 %collective-permute-start.24 = (f32[16]{0:T(128)S(1)}, f32[16]{0:T(128)S(1)}, u32[]{:S(2)}, u32[]{:S(2)}) collective-permute-start(f32[16]{0:T(128)S(1)} %add.132), channel_id=1, source_target_pairs={{0,2},{1,3},{2,0},{3,1},{4,6},{5,7},{6,4},{7,5},{8,10},{9,11},{10,... | collective-permute-start | bytes 200 | tf_op jit(solution)/shard_map/ppermute | solution.py:23
  152.9 7.0 %collective-permute-start.25 = (f32[16]{0:T(128)S(1)}, f32[16]{0:T(128)S(1)}, u32[]{:S(2)}, u32[]{:S(2)}) collective-permute-start(f32[16]{0:T(128)S(1)} %add.133), channel_id=1, source_target_pairs={{0,4},{1,5},{2,6},{3,7},{4,0},{5,1},{6,2},{7,3},{8,12},{9,13},{10,... | collective-permute-start | bytes 200 | tf_op jit(solution)/shard_map/ppermute | solution.py:23
  159.9 9.3 %collective-permute-start.26 = (f32[16]{0:T(128)S(1)}, f32[16]{0:T(128)S(1)}, u32[]{:S(2)}, u32[]{:S(2)}) collective-permute-start(f32[16]{0:T(128)S(1)} %add.134), channel_id=1, source_target_pairs={{0,8},{1,9},{2,10},{3,11},{4,12},{5,13},{6,14},{7,15},{8,0},{9,1},... | collective-permute-start | bytes 200 | tf_op jit(solution)/shard_map/ppermute | solution.py:23
  169.2 5.4 %collective-permute-start.27 = (f32[16]{0:T(128)S(1)}, f32[16]{0:T(128)S(1)}, u32[]{:S(2)}, u32[]{:S(2)}) collective-permute-start(f32[16]{0:T(128)S(1)} %add.135), channel_id=1, source_target_pairs={{0,16},{16,0},{32,48},{48,32},{64,80},{80,64},{96,112},{112,96},{1... | collective-permute-start | bytes 200 | tf_op jit(solution)/shard_map/ppermute | solution.py:23
  174.7 6.9 %collective-permute-start.28 = (f32[16]{0:T(128)S(1)}, f32[16]{0:T(128)S(1)}, u32[]{:S(2)}, u32[]{:S(2)}) collective-permute-start(f32[16]{0:T(128)S(1)} %add.136), channel_id=1, source_target_pairs={{0,32},{16,48},{32,0},{48,16},{64,96},{80,112},{96,64},{112,80},{1... | collective-permute-start | bytes 200 | tf_op jit(solution)/shard_map/ppermute | solution.py:23
  181.6 5.4 %collective-permute-start.29 = (f32[16]{0:T(128)S(1)}, f32[16]{0:T(128)S(1)}, u32[]{:S(2)}, u32[]{:S(2)}) collective-permute-start(f32[16]{0:T(128)S(1)} %add.137), channel_id=1, source_target_pairs={{0,64},{16,80},{32,96},{48,112},{64,0},{80,16},{96,32},{112,48},{1... | collective-permute-start | bytes 200 | tf_op jit(solution)/shard_map/ppermute | solution.py:23
  187.0 6.3 %collective-permute-start.30 = (f32[16]{0:T(128)S(1)}, f32[16]{0:T(128)S(1)}, u32[]{:S(2)}, u32[]{:S(2)}) collective-permute-start(f32[16]{0:T(128)S(1)} %add.138), channel_id=1, source_target_pairs={{0,128},{16,144},{32,160},{48,176},{64,192},{80,208},{96,224},{112... | collective-permute-start | bytes 200 | tf_op jit(solution)/shard_map/ppermute | solution.py:23
  193.3 9.3 %collective-permute-start.31 = (f32[16]{0:T(128)S(1)}, f32[16]{0:T(128)S(1)}, u32[]{:S(2)}, u32[]{:S(2)}) collective-permute-start(f32[16]{0:T(128)S(1)} %add.139), channel_id=1, source_target_pairs={{0,256},{16,272},{32,288},{48,304},{64,320},{80,336},{96,352},{112... | collective-permute-start | bytes 200 | tf_op jit(solution)/shard_map/ppermute | solution.py:23
  203.5 3.0 %collective-permute-start.32 = (f32[16]{0:T(128)S(1)}, f32[16]{0:T(128)S(1)}, u32[]{:S(2)}, u32[]{:S(2)}) collective-permute-start(f32[16]{0:T(128)S(1)} %get-tuple-element.5), channel_id=1, source_target_pairs={{0,1},{1,0},{2,3},{3,2},{4,5},{5,4},{6,7},{7,6},{8,9},{9,8},{10,11... | collective-permute-start | bytes 200 | tf_op jit(solution)/shard_map/ppermute | solution.py:23
  206.5 5.4 %collective-permute-start.33 = (f32[16]{0:T(128)S(1)}, f32[16]{0:T(128)S(1)}, u32[]{:S(2)}, u32[]{:S(2)}) collective-permute-start(f32[16]{0:T(128)S(1)} %add.142), channel_id=1, source_target_pairs={{0,2},{1,3},{2,0},{3,1},{4,6},{5,7},{6,4},{7,5},{8,10},{9,11},{10,... | collective-permute-start | bytes 200 | tf_op jit(solution)/shard_map/ppermute | solution.py:23
  211.9 6.3 %collective-permute-start.34 = (f32[16]{0:T(128)S(1)}, f32[16]{0:T(128)S(1)}, u32[]{:S(2)}, u32[]{:S(2)}) collective-permute-start(f32[16]{0:T(128)S(1)} %add.143), channel_id=1, source_target_pairs={{0,4},{1,5},{2,6},{3,7},{4,0},{5,1},{6,2},{7,3},{8,12},{9,13},{10,... | collective-permute-start | bytes 200 | tf_op jit(solution)/shard_map/ppermute | solution.py:23
  218.3 9.3 %collective-permute-start.35 = (f32[16]{0:T(128)S(1)}, f32[16]{0:T(128)S(1)}, u32[]{:S(2)}, u32[]{:S(2)}) collective-permute-start(f32[16]{0:T(128)S(1)} %add.144), channel_id=1, source_target_pairs={{0,8},{1,9},{2,10},{3,11},{4,12},{5,13},{6,14},{7,15},{8,0},{9,1},... | collective-permute-start | bytes 200 | tf_op jit(solution)/shard_map/ppermute | solution.py:23
  227.6 5.4 %collective-permute-start.36 = (f32[16]{0:T(128)S(1)}, f32[16]{0:T(128)S(1)}, u32[]{:S(2)}, u32[]{:S(2)}) collective-permute-start(f32[16]{0:T(128)S(1)} %add.145), channel_id=1, source_target_pairs={{0,16},{16,0},{32,48},{48,32},{64,80},{80,64},{96,112},{112,96},{1... | collective-permute-start | bytes 200 | tf_op jit(solution)/shard_map/ppermute | solution.py:23
  233.0 6.9 %collective-permute-start.37 = (f32[16]{0:T(128)S(1)}, f32[16]{0:T(128)S(1)}, u32[]{:S(2)}, u32[]{:S(2)}) collective-permute-start(f32[16]{0:T(128)S(1)} %add.146), channel_id=1, source_target_pairs={{0,32},{16,48},{32,0},{48,16},{64,96},{80,112},{96,64},{112,80},{1... | collective-permute-start | bytes 200 | tf_op jit(solution)/shard_map/ppermute | solution.py:23
  240.0 5.4 %collective-permute-start.38 = (f32[16]{0:T(128)S(1)}, f32[16]{0:T(128)S(1)}, u32[]{:S(2)}, u32[]{:S(2)}) collective-permute-start(f32[16]{0:T(128)S(1)} %add.147), channel_id=1, source_target_pairs={{0,64},{16,80},{32,96},{48,112},{64,0},{80,16},{96,32},{112,48},{1... | collective-permute-start | bytes 200 | tf_op jit(solution)/shard_map/ppermute | solution.py:23
  245.4 6.3 %collective-permute-start.39 = (f32[16]{0:T(128)S(1)}, f32[16]{0:T(128)S(1)}, u32[]{:S(2)}, u32[]{:S(2)}) collective-permute-start(f32[16]{0:T(128)S(1)} %add.148), channel_id=1, source_target_pairs={{0,128},{16,144},{32,160},{48,176},{64,192},{80,208},{96,224},{112... | collective-permute-start | bytes 200 | tf_op jit(solution)/shard_map/ppermute | solution.py:23
  251.7 9.3 %collective-permute-start.40 = (f32[16]{0:T(128)S(1)}, f32[16]{0:T(128)S(1)}, u32[]{:S(2)}, u32[]{:S(2)}) collective-permute-start(f32[16]{0:T(128)S(1)} %add.149), channel_id=1, source_target_pairs={{0,256},{16,272},{32,288},{48,304},{64,320},{80,336},{96,352},{112... | collective-permute-start | bytes 200 | tf_op jit(solution)/shard_map/ppermute | solution.py:23
  (4 other events, 2.8 us)

commit v2 on v1

--- a/solution.py
+++ b/solution.py
@@ -23,6 +23,68 @@
             value = value + lax.ppermute(value, axis, [(i, i ^ step) for i in range(peers)])
             step *= 2
     return value
+
+
+def two_sum(a, b):
+    total = a + b
+    back = total - a
+    return total, (a - (total - back)) + (b - back)
+
+
+def split_float(a):
+    scaled = 4097.0 * a
+    high = scaled - (scaled - a)
+    return high, a - high
+
+
+def two_prod(a, b):
+    product = a * b
+    a_high, a_low = split_float(a)
+    b_high, b_low = split_float(b)
+    error = ((a_high * b_high - product) + a_high * b_low + a_low * b_high) + a_low * b_low
+    return product, error
+
+
+def df_add(x, y):
+    total, error = two_sum(x[0], y[0])
+    error = error + (x[1] + y[1])
+    high = total + error
+    return high, error - (high - total)
+
+
+def df_scale(x, factor):
+    product, error = two_prod(x[0], factor)
+    error = error + x[1] * factor
+    high = product + error
+    return high, error - (high - product)
+
+
+def df_case_sums(a, b):
+    a = jnp.moveaxis(a, 2, 0).reshape(a.shape[2], -1)
+    b = jnp.moveaxis(b, 2, 0).reshape(b.shape[2], -1)
+    high, low = two_prod(a, b)
+    while high.shape[1] > 1:
+        if high.shape[1] % 2:
+            high = jnp.pad(high, ((0, 0), (0, 1)))
+            low = jnp.pad(low, ((0, 0), (0, 1)))
+        half = high.shape[1] // 2
+        high, low = df_add((high[:, :half], low[:, :half]), (high[:, half:], low[:, half:]))
+    return high[:, 0], low[:, 0]
+
+
+def all_sum_mixed(plain, pairs):
+    for axis in ("py", "px"):
+        peers = lax.axis_size(axis)
+        step = 1
+        while step < peers:
+            packed = jnp.stack([plain] + [part for pair in pairs for part in pair])
+            other = lax.ppermute(packed, axis, [(i, i ^ step) for i in range(peers)])
+            plain = plain + other[0]
+            pairs = [
+                df_add(pair, (other[1 + 2 * k], other[2 + 2 * k])) for k, pair in enumerate(pairs)
+            ]
+            step *= 2
+    return plain, pairs
 
 
 def permute_side(values, flip):
@@ -151,11 +213,24 @@
         precision=lax.Precision.HIGHEST,
     )
     image = jump_b((inner_part + correction) * active)
-    curvature = all_sum(jnp.sum(new_direction * image, axis=(0, 1, 3)))
+    curvature, (res_res, res_img, img_img) = all_sum_mixed(
+        jnp.sum(new_direction * image, axis=(0, 1, 3)),
+        [df_case_sums(start_res, start_res), df_case_sums(start_res, image), df_case_sums(image, image)],
+    )
     step_length = rz_current / curvature
     new_solution = start_sol + step_length[None, None, :, None] * new_direction
     new_residual = start_res - step_length[None, None, :, None] * image
-    residual_sq = all_sum(jnp.sum(new_residual * new_residual, axis=(0, 1, 3)))
+    cross = df_scale(res_img, -2.0 * step_length)
+    square = df_scale(df_scale(img_img, step_length), step_length)
+    merged = df_add(df_add(res_res, cross), square)
+    merged_sq = merged[0] + merged[1]
+    scale = res_res[0] + step_length * step_length * img_img[0]
+    trusted = jnp.all(jnp.isfinite(scale) & (merged_sq > 0) & (scale <= 1e7 * merged_sq))
+    residual_sq = lax.cond(
+        trusted,
+        lambda: merged_sq,
+        lambda: all_sum(jnp.sum(new_residual * new_residual, axis=(0, 1, 3))),
+    )
     return (new_solution, new_residual, new_direction, rz_current, residual_sq)
 
 

time: 263 us -> 209 us (0.79)
  waiting for transfers between devices: 126 us -> 96.4 us
  starting transfers between devices: 123 us -> 96.5 us
  other arithmetic: 2.37 us -> 5.01 us
    ppermute x27 -> x9, waiting for transfers between devices: 89.4 us -> 29.3 us  [all_sum(): lax.ppermute(value, axis, [(i, i ^ step) for i in range(peers)])]
    ppermute x27 -> x9, starting transfers between devices: 89.4 us -> 32.8 us  [all_sum(): lax.ppermute(value, axis, [(i, i ^ step) for i in range(peers)])]
    ppermute x0 -> x9, waiting for transfers between devices: none -> 30.4 us  [all_sum_mixed(): other = lax.ppermute(packed, axis, [(i, i ^ step) for i in range(peers)])]
    ppermute x0 -> x9, starting transfers between devices: none -> 29.3 us  [all_sum_mixed(): other = lax.ppermute(packed, axis, [(i, i ^ step) for i in range(peers)])]
    sub x0 -> x39, other arithmetic: none -> 3.15 us  [the longest x38 2.46 us: df_add(): return (high, error - (high - total))]
  transfers between devices with their start and end apart: 41 -> 32, of which waited for: 37 -> 28; matrix products, arithmetic and copies ran while one was open for 0% -> 1% of each run, Pallas kernels for 0% -> 0%
where the time goes in v2:
time: 209 us; the launch traced here: 208 us
  starting transfers between devices  96.5 us (46%)
  waiting for transfers between devices  96.4 us (46%)
  local copies, waits for them, and re-layouts  5.2 us (2%)
  other arithmetic  5.01 us (2%)
  between operations  4.02 us (2%)
    ppermute x14, waiting for transfers between devices, passed_along(): return lax.ppermute(value, axis, pairs)  36.6 us
    ppermute x14, starting transfers between devices, passed_along(): return lax.ppermute(value, axis, pairs)  34.3 us
    ppermute x9, starting transfers between devices, all_sum(): lax.ppermute(value, axis, [(i, i ^ step) for i in range(peers)])  32.8 us
    ppermute x9, waiting for transfers between devices, all_sum_mixed(): other = lax.ppermute(packed, axis, [(i, i ^ step) for i in range(peers)])  30.4 us
    ppermute x9, waiting for transfers between devices, all_sum(): lax.ppermute(value, axis, [(i, i ^ step) for i in range(peers)])  29.3 us
    ppermute x9, starting transfers between devices, all_sum_mixed(): other = lax.ppermute(packed, axis, [(i, i ^ step) for i in range(peers)])  29.3 us
  transfers between devices with their start and end apart: 32, of which 28 were waited for; matrix products, arithmetic and copies ran while one was open for 1% of the time, Pallas kernels for 0%

profile of v2, /device:TPU:30, one launch (start us, length us, event | category | flops | bytes accessed | tf_op | source)
XLA Modules:
  0.0 208.0 jit_solution(7579673073701213400)
XLA Ops:
  3.8 1.7 collective-permute-start.9
  5.5 4.6 %collective-permute-start.10 = (f32[1,1,16,68]{3,2,1,0:T(8,128)S(1)}, f32[1,1,16,68]{3,2,1,0:T(8,128)S(1)}, u32[]{:S(2)}, u32[]{:S(2)}) collective-permute-start(f32[1,1,16,68]{3,2,1,0:T(8,128)S(1)} %get-tuple-element.144), channel_id=1, source_target_pairs={{0,16},{16,32},{32,48},{48,64},{64,80},{80,96},{96,112},{112,128},... | collective-permute-start | bytes 13064 | tf_op jit(solution)/shard_map/ppermute | solution.py:12
  13.1 3.1 %collective-permute-done.11 = f32[1,1,16,68]{3,2,1,0:T(8,128)S(1)} collective-permute-done((f32[1,1,16,68]{3,2,1,0:T(8,128)S(1)}, f32[1,1,16,68]{3,2,1,0:T(8,128)S(1)}, u32[]{:S(2)}, u32[]{:S(2)}) %collective-permute-start.11) | collective-permute-done | bytes 4384 | tf_op jit(solution)/shard_map/ppermute | solution.py:12
  16.4 2.0 collective-permute-start.12
  18.8 6.5 %collective-permute-done.12 = f32[1,1,16,68]{3,2,1,0:T(8,128)S(1)} collective-permute-done((f32[1,1,16,68]{3,2,1,0:T(8,128)S(1)}, f32[1,1,16,68]{3,2,1,0:T(8,128)S(1)}, u32[]{:S(2)}, u32[]{:S(2)}) %collective-permute-start.12) | collective-permute-done | bytes 4384 | tf_op jit(solution)/shard_map/ppermute | solution.py:12
  25.7 3.4 %collective-permute-start.13 = (f32[16]{0:T(128)S(1)}, f32[16]{0:T(128)S(1)}, u32[]{:S(2)}, u32[]{:S(2)}) collective-permute-start(f32[16]{0:T(128)S(1)} %get-tuple-element.113), channel_id=1, source_target_pairs={{0,1},{1,0},{2,3},{3,2},{4,5},{5,4},{6,7},{7,6},{8,9},{9,8},{10,11... | collective-permute-start | bytes 200 | tf_op jit(solution)/shard_map/ppermute | solution.py:23
  29.9 4.3 %collective-permute-start.14 = (f32[16]{0:T(128)S(1)}, f32[16]{0:T(128)S(1)}, u32[]{:S(2)}, u32[]{:S(2)}) collective-permute-start(f32[16]{0:T(128)S(1)} %add.2410), channel_id=1, source_target_pairs={{0,2},{1,3},{2,0},{3,1},{4,6},{5,7},{6,4},{7,5},{8,10},{9,11},{10,... | collective-permute-start | bytes 200 | tf_op jit(solution)/shard_map/ppermute | solution.py:23
  35.7 8.5 %collective-permute-start.15 = (f32[16]{0:T(128)S(1)}, f32[16]{0:T(128)S(1)}, u32[]{:S(2)}, u32[]{:S(2)}) collective-permute-start(f32[16]{0:T(128)S(1)} %add.2411), channel_id=1, source_target_pairs={{0,4},{1,5},{2,6},{3,7},{4,0},{5,1},{6,2},{7,3},{8,12},{9,13},{10,... | collective-permute-start | bytes 200 | tf_op jit(solution)/shard_map/ppermute | solution.py:23
  45.7 6.8 %collective-permute-start.16 = (f32[16]{0:T(128)S(1)}, f32[16]{0:T(128)S(1)}, u32[]{:S(2)}, u32[]{:S(2)}) collective-permute-start(f32[16]{0:T(128)S(1)} %add.2412), channel_id=1, source_target_pairs={{0,8},{1,9},{2,10},{3,11},{4,12},{5,13},{6,14},{7,15},{8,0},{9,1},... | collective-permute-start | bytes 200 | tf_op jit(solution)/shard_map/ppermute | solution.py:23
  52.7 2.4 %collective-permute-done.16 = f32[16]{0:T(128)S(1)} collective-permute-done((f32[16]{0:T(128)S(1)}, f32[16]{0:T(128)S(1)}, u32[]{:S(2)}, u32[]{:S(2)}) %collective-permute-start.16) | collective-permute-done | bytes 96 | tf_op jit(solution)/shard_map/ppermute | solution.py:23
  55.1 1.9 collective-permute-start.17
  57.0 3.5 %collective-permute-done.17 = f32[16]{0:T(128)S(1)} collective-permute-done((f32[16]{0:T(128)S(1)}, f32[16]{0:T(128)S(1)}, u32[]{:S(2)}, u32[]{:S(2)}) %collective-permute-start.17) | collective-permute-done | bytes 96 | tf_op jit(solution)/shard_map/ppermute | solution.py:23
  60.5 1.9 collective-permute-start.18
  62.5 4.9 %collective-permute-done.18 = f32[16]{0:T(128)S(1)} collective-permute-done((f32[16]{0:T(128)S(1)}, f32[16]{0:T(128)S(1)}, u32[]{:S(2)}, u32[]{:S(2)}) %collective-permute-start.18) | collective-permute-done | bytes 96 | tf_op jit(solution)/shard_map/ppermute | solution.py:23
  67.4 1.9 collective-permute-start.19
  69.5 3.4 %collective-permute-done.19 = f32[16]{0:T(128)S(1)} collective-permute-done((f32[16]{0:T(128)S(1)}, f32[16]{0:T(128)S(1)}, u32[]{:S(2)}, u32[]{:S(2)}) %collective-permute-start.19) | collective-permute-done | bytes 96 | tf_op jit(solution)/shard_map/ppermute | solution.py:23
  72.9 1.9 collective-permute-start.20
  74.8 4.4 %collective-permute-done.20 = f32[16]{0:T(128)S(1)} collective-permute-done((f32[16]{0:T(128)S(1)}, f32[16]{0:T(128)S(1)}, u32[]{:S(2)}, u32[]{:S(2)}) %collective-permute-start.20) | collective-permute-done | bytes 96 | tf_op jit(solution)/shard_map/ppermute | solution.py:23
  79.2 2.2 %collective-permute-start.21 = (f32[16]{0:T(128)S(1)}, f32[16]{0:T(128)S(1)}, u32[]{:S(2)}, u32[]{:S(2)}) collective-permute-start(f32[16]{0:T(128)S(1)} %add.2417), channel_id=1, source_target_pairs={{0,256},{16,272},{32,288},{48,304},{64,320},{80,336},{96,352},{112... | collective-permute-start | bytes 200 | tf_op jit(solution)/shard_map/ppermute | solution.py:23
  81.5 7.1 %collective-permute-done.21 = f32[16]{0:T(128)S(1)} collective-permute-done((f32[16]{0:T(128)S(1)}, f32[16]{0:T(128)S(1)}, u32[]{:S(2)}, u32[]{:S(2)}) %collective-permute-start.21) | collective-permute-done | bytes 96 | tf_op jit(solution)/shard_map/ppermute | solution.py:23
  89.9 3.6 %collective-permute-start.24 = (f32[1,1,16,68]{3,2,1,0:T(8,128)S(1)}, f32[1,1,16,68]{3,2,1,0:T(8,128)S(1)}, u32[]{:S(2)}, u32[]{:S(2)}) collective-permute-start(f32[1,1,16,68]{3,2,1,0:T(8,128)S(1)} %get-tuple-element.136), channel_id=1, source_target_pairs={{0,16},{16,32},{32,48},{48,64},{64,80},{80,96},{96,112},{112,128},... | collective-permute-start | bytes 13064 | tf_op jit(solution)/shard_map/ppermute | solution.py:12
  93.6 4.4 %collective-permute-start.23 = (f32[1,1,16,68]{3,2,1,0:T(8,128)S(1)}, f32[1,1,16,68]{3,2,1,0:T(8,128)S(1)}, u32[]{:S(2)}, u32[]{:S(2)}) collective-permute-start(f32[1,1,16,68]{3,2,1,0:T(8,128)S(1)} %get-tuple-element.137), channel_id=1, source_target_pairs={{0,1},{1,2},{2,3},{3,4},{4,5},{5,6},{6,7},{7,8},{8,9},{9,10},{10,1... | collective-permute-start | bytes 13064 | tf_op jit(solution)/shard_map/ppermute | solution.py:12
  97.9 2.2 %collective-permute-start.25 = (f32[1,1,16,68]{3,2,1,0:T(8,128)S(1)}, f32[1,1,16,68]{3,2,1,0:T(8,128)S(1)}, u32[]{:S(2)}, u32[]{:S(2)}) collective-permute-start(f32[1,1,16,68]{3,2,1,0:T(8,128)S(1)} %get-tuple-element.138), channel_id=1, source_target_pairs={{0,16},{16,32},{32,48},{48,64},{64,80},{80,96},{96,112},{112,128},... | collective-permute-start | bytes 13064 | tf_op jit(solution)/shard_map/ppermute | solution.py:12
  100.2 3.3 %collective-permute-done.25 = f32[1,1,16,68]{3,2,1,0:T(8,128)S(1)} collective-permute-done((f32[1,1,16,68]{3,2,1,0:T(8,128)S(1)}, f32[1,1,16,68]{3,2,1,0:T(8,128)S(1)}, u32[]{:S(2)}, u32[]{:S(2)}) %collective-permute-start.25) | collective-permute-done | bytes 4384 | tf_op jit(solution)/shard_map/ppermute | solution.py:12
  106.7 5.5 %collective-permute-start.27 = (f32[1,2,128]{2,1,0:T(2,128)S(1)}, f32[1,2,128]{2,1,0:T(2,128)S(1)}, u32[]{:S(2)}, u32[]{:S(2)}) collective-permute-start(f32[1,2,128]{2,1,0:T(2,128)S(1)} %pad_maximum_fusion.2), channel_id=1, source_target_pairs={{0,16},{16,32},{32,48},{48,64},{64,80},{80,96},{96,112},{112,128},... | collective-permute-start | bytes 3080 | tf_op jit(solution)/shard_map/ppermute | solution.py:12
  115.8 2.5 %collective-permute-done.28 = f32[1,1,32]{2,1,0:T(1,128)S(1)} collective-permute-done((f32[1,1,32]{2,1,0:T(1,128)S(1)}, f32[1,1,32]{2,1,0:T(1,128)S(1)}, u32[]{:S(2)}, u32[]{:S(2)}) %collective-permute-start.28) | collective-permute-done | bytes 160 | tf_op jit(solution)/shard_map/ppermute | solution.py:12
  118.3 1.9 collective-permute-start.29
  120.4 6.6 %collective-permute-done.29 = f32[1,2,32]{2,1,0:T(2,128)S(1)} collective-permute-done((f32[1,2,32]{2,1,0:T(2,128)S(1)}, f32[1,2,32]{2,1,0:T(2,128)S(1)}, u32[]{:S(2)}, u32[]{:S(2)}) %collective-permute-start.29) | collective-permute-done | bytes 288 | tf_op jit(solution)/shard_map/ppermute | solution.py:12
  128.8 4.4 %collective-permute-done.30 = f32[1,1,16,68]{3,2,1,0:T(8,128)S(1)} collective-permute-done((f32[1,1,16,68]{3,2,1,0:T(8,128)S(1)}, f32[1,1,16,68]{3,2,1,0:T(8,128)S(1)}, u32[]{:S(2)}, u32[]{:S(2)}) %collective-permute-start.30) | collective-permute-done | bytes 4384 | tf_op jit(solution)/shard_map/ppermute | solution.py:12
  133.4 1.9 collective-permute-start.31
  135.3 6.9 %collective-permute-done.31 = f32[1,1,16,68]{3,2,1,0:T(8,128)S(1)} collective-permute-done((f32[1,1,16,68]{3,2,1,0:T(8,128)S(1)}, f32[1,1,16,68]{3,2,1,0:T(8,128)S(1)}, u32[]{:S(2)}, u32[]{:S(2)}) %collective-permute-start.31) | collective-permute-done | bytes 4384 | tf_op jit(solution)/shard_map/ppermute | solution.py:12
  145.2 3.2 %collective-permute-start.32 = (f32[7,16]{1,0:T(8,128)S(1)}, f32[7,16]{1,0:T(8,128)S(1)}, u32[]{:S(2)}, u32[]{:S(2)}) collective-permute-start(f32[7,16]{1,0:T(8,128)S(1)} %stack.21), channel_id=1, source_target_pairs={{0,1},{1,0},{2,3},{3,2},{4,5},{5,4},{6,7},{7,6},{8,9},{9,8},{10,11... | collective-permute-start | bytes 1352 | tf_op jit(solution)/shard_map/ppermute | solution.py:81
  149.2 3.9 %collective-permute-start.33 = (f32[7,16]{1,0:T(8,128)S(1)}, f32[7,16]{1,0:T(8,128)S(1)}, u32[]{:S(2)}, u32[]{:S(2)}) collective-permute-start(f32[7,16]{1,0:T(8,128)S(1)} %stack.22), channel_id=1, source_target_pairs={{0,2},{1,3},{2,0},{3,1},{4,6},{5,7},{6,4},{7,5},{8,10},{9,11},{10,... | collective-permute-start | bytes 1352 | tf_op jit(solution)/shard_map/ppermute | solution.py:81
  153.1 1.6 collective-permute-done.33
  154.7 5.5 %collective-permute-start.34 = (f32[7,16]{1,0:T(8,128)S(1)}, f32[7,16]{1,0:T(8,128)S(1)}, u32[]{:S(2)}, u32[]{:S(2)}) collective-permute-start(f32[7,16]{1,0:T(8,128)S(1)} %stack.23), channel_id=1, source_target_pairs={{0,4},{1,5},{2,6},{3,7},{4,0},{5,1},{6,2},{7,3},{8,12},{9,13},{10,... | collective-permute-start | bytes 1352 | tf_op jit(solution)/shard_map/ppermute | solution.py:81
  160.3 1.6 collective-permute-done.34
  161.9 7.1 %collective-permute-start.35 = (f32[7,16]{1,0:T(8,128)S(1)}, f32[7,16]{1,0:T(8,128)S(1)}, u32[]{:S(2)}, u32[]{:S(2)}) collective-permute-start(f32[7,16]{1,0:T(8,128)S(1)} %stack.24), channel_id=1, source_target_pairs={{0,8},{1,9},{2,10},{3,11},{4,12},{5,13},{6,14},{7,15},{8,0},{9,1},... | collective-permute-start | bytes 1352 | tf_op jit(solution)/shard_map/ppermute | solution.py:81
  169.0 2.3 %collective-permute-done.35 = f32[7,16]{1,0:T(8,128)S(1)} collective-permute-done((f32[7,16]{1,0:T(8,128)S(1)}, f32[7,16]{1,0:T(8,128)S(1)}, u32[]{:S(2)}, u32[]{:S(2)}) %collective-permute-start.35) | collective-permute-done | bytes 480 | tf_op jit(solution)/shard_map/ppermute | solution.py:81
  171.3 1.9 collective-permute-start.36
  173.3 3.6 %collective-permute-done.36 = f32[7,16]{1,0:T(8,128)S(1)} collective-permute-done((f32[7,16]{1,0:T(8,128)S(1)}, f32[7,16]{1,0:T(8,128)S(1)}, u32[]{:S(2)}, u32[]{:S(2)}) %collective-permute-start.36) | collective-permute-done | bytes 480 | tf_op jit(solution)/shard_map/ppermute | solution.py:81
  176.9 1.9 collective-permute-start.37
  178.8 5.1 %collective-permute-done.37 = f32[7,16]{1,0:T(8,128)S(1)} collective-permute-done((f32[7,16]{1,0:T(8,128)S(1)}, f32[7,16]{1,0:T(8,128)S(1)}, u32[]{:S(2)}, u32[]{:S(2)}) %collective-permute-start.37) | collective-permute-done | bytes 480 | tf_op jit(solution)/shard_map/ppermute | solution.py:81
  184.0 1.9 collective-permute-start.38
  185.9 3.6 %collective-permute-done.38 = f32[7,16]{1,0:T(8,128)S(1)} collective-permute-done((f32[7,16]{1,0:T(8,128)S(1)}, f32[7,16]{1,0:T(8,128)S(1)}, u32[]{:S(2)}, u32[]{:S(2)}) %collective-permute-start.38) | collective-permute-done | bytes 480 | tf_op jit(solution)/shard_map/ppermute | solution.py:81
  189.5 1.9 collective-permute-start.39
  191.5 4.5 %collective-permute-done.39 = f32[7,16]{1,0:T(8,128)S(1)} collective-permute-done((f32[7,16]{1,0:T(8,128)S(1)}, f32[7,16]{1,0:T(8,128)S(1)}, u32[]{:S(2)}, u32[]{:S(2)}) %collective-permute-start.39) | collective-permute-done | bytes 480 | tf_op jit(solution)/shard_map/ppermute | solution.py:81
  196.0 1.9 collective-permute-start.40
  197.9 7.5 %collective-permute-done.40 = f32[7,16]{1,0:T(8,128)S(1)} collective-permute-done((f32[7,16]{1,0:T(8,128)S(1)}, f32[7,16]{1,0:T(8,128)S(1)}, u32[]{:S(2)}, u32[]{:S(2)}) %collective-permute-start.40) | collective-permute-done | bytes 480 | tf_op jit(solution)/shard_map/ppermute | solution.py:81
  (166 shorter events, 25.5 us)
Async XLA Ops:
  0.6 10.9 %copy-start = (bf16[1,1,272,272]{3,2,1,0:T(8,128)(2,1)S(1)}, bf16[1,1,272,272]{3,2,1,0:T(8,128)(2,1)}, u32[]{:S(2)}) copy-start(bf16[1,1,272,272]{3,2,1,0:T(8,128)(2,1)} %param.17) | copy-start | bytes 443908
  0.7 0.7 copy-start.9
  0.7 2.6 %copy-start.1 = (f32[1,1,16,136]{3,2,1,0:T(8,128)S(1)}, f32[1,1,16,136]{3,2,1,0:T(8,128)}, u32[]{:S(2)}) copy-start(f32[1,1,16,136]{3,2,1,0:T(8,128)} %param.13) | copy-start | bytes 26116
  0.7 2.6 %copy-start.5 = (f32[1,1,16,136]{3,2,1,0:T(8,128)S(1)}, f32[1,1,16,136]{3,2,1,0:T(8,128)}, u32[]{:S(2)}) copy-start(f32[1,1,16,136]{3,2,1,0:T(8,128)} %param.14) | copy-start | bytes 26116
  3.8 6.4 %collective-permute-start.9 = (f32[1,1,16,68]{3,2,1,0:T(8,128)S(1)}, f32[1,1,16,68]{3,2,1,0:T(8,128)S(1)}, u32[]{:S(2)}, u32[]{:S(2)}) collective-permute-start(f32[1,1,16,68]{3,2,1,0:T(8,128)S(1)} %get-tuple-element.143), channel_id=1, source_target_pairs={{0,1},{1,2},{2,3},{3,4},{4,5},{5,6},{6,7},{7,8},{8,9},{9,10},{10,1... | collective-permute-start | bytes 13064 | tf_op jit(solution)/shard_map/ppermute | solution.py:12
  5.5 6.0 %collective-permute-start.10 = (f32[1,1,16,68]{3,2,1,0:T(8,128)S(1)}, f32[1,1,16,68]{3,2,1,0:T(8,128)S(1)}, u32[]{:S(2)}, u32[]{:S(2)}) collective-permute-start(f32[1,1,16,68]{3,2,1,0:T(8,128)S(1)} %get-tuple-element.144), channel_id=1, source_target_pairs={{0,16},{16,32},{32,48},{48,64},{64,80},{80,96},{96,112},{112,128},... | collective-permute-start | bytes 13064 | tf_op jit(solution)/shard_map/ppermute | solution.py:12
  11.8 4.4 %collective-permute-start.11 = (f32[1,1,16,68]{3,2,1,0:T(8,128)S(1)}, f32[1,1,16,68]{3,2,1,0:T(8,128)S(1)}, u32[]{:S(2)}, u32[]{:S(2)}) collective-permute-start(f32[1,1,16,68]{3,2,1,0:T(8,128)S(1)} %slice.760), channel_id=1, source_target_pairs={{1,0},{2,1},{3,2},{4,3},{5,4},{6,5},{7,6},{8,7},{9,8},{10,9},{11,1... | collective-permute-start | bytes 13064 | tf_op jit(solution)/shard_map/ppermute | solution.py:12
  16.4 8.9 %collective-permute-start.12 = (f32[1,1,16,68]{3,2,1,0:T(8,128)S(1)}, f32[1,1,16,68]{3,2,1,0:T(8,128)S(1)}, u32[]{:S(2)}, u32[]{:S(2)}) collective-permute-start(f32[1,1,16,68]{3,2,1,0:T(8,128)S(1)} %get-tuple-element.128), channel_id=1, source_target_pairs={{16,0},{32,16},{48,32},{64,48},{80,64},{96,80},{112,96},{128,112},... | collective-permute-start | bytes 13064 | tf_op jit(solution)/shard_map/ppermute | solution.py:12
  25.7 4.2 %collective-permute-start.13 = (f32[16]{0:T(128)S(1)}, f32[16]{0:T(128)S(1)}, u32[]{:S(2)}, u32[]{:S(2)}) collective-permute-start(f32[16]{0:T(128)S(1)} %get-tuple-element.113), channel_id=1, source_target_pairs={{0,1},{1,0},{2,3},{3,2},{4,5},{5,4},{6,7},{7,6},{8,9},{9,8},{10,11... | collective-permute-start | bytes 200 | tf_op jit(solution)/shard_map/ppermute | solution.py:23
  29.9 5.8 %collective-permute-start.14 = (f32[16]{0:T(128)S(1)}, f32[16]{0:T(128)S(1)}, u32[]{:S(2)}, u32[]{:S(2)}) collective-permute-start(f32[16]{0:T(128)S(1)} %add.2410), channel_id=1, source_target_pairs={{0,2},{1,3},{2,0},{3,1},{4,6},{5,7},{6,4},{7,5},{8,10},{9,11},{10,... | collective-permute-start | bytes 200 | tf_op jit(solution)/shard_map/ppermute | solution.py:23
  35.7 10.0 %collective-permute-start.15 = (f32[16]{0:T(128)S(1)}, f32[16]{0:T(128)S(1)}, u32[]{:S(2)}, u32[]{:S(2)}) collective-permute-start(f32[16]{0:T(128)S(1)} %add.2411), channel_id=1, source_target_pairs={{0,4},{1,5},{2,6},{3,7},{4,0},{5,1},{6,2},{7,3},{8,12},{9,13},{10,... | collective-permute-start | bytes 200 | tf_op jit(solution)/shard_map/ppermute | solution.py:23
  45.7 9.3 %collective-permute-start.16 = (f32[16]{0:T(128)S(1)}, f32[16]{0:T(128)S(1)}, u32[]{:S(2)}, u32[]{:S(2)}) collective-permute-start(f32[16]{0:T(128)S(1)} %add.2412), channel_id=1, source_target_pairs={{0,8},{1,9},{2,10},{3,11},{4,12},{5,13},{6,14},{7,15},{8,0},{9,1},... | collective-permute-start | bytes 200 | tf_op jit(solution)/shard_map/ppermute | solution.py:23
  55.1 5.4 %collective-permute-start.17 = (f32[16]{0:T(128)S(1)}, f32[16]{0:T(128)S(1)}, u32[]{:S(2)}, u32[]{:S(2)}) collective-permute-start(f32[16]{0:T(128)S(1)} %add.2413), channel_id=1, source_target_pairs={{0,16},{16,0},{32,48},{48,32},{64,80},{80,64},{96,112},{112,96},{1... | collective-permute-start | bytes 200 | tf_op jit(solution)/shard_map/ppermute | solution.py:23
  60.5 6.9 %collective-permute-start.18 = (f32[16]{0:T(128)S(1)}, f32[16]{0:T(128)S(1)}, u32[]{:S(2)}, u32[]{:S(2)}) collective-permute-start(f32[16]{0:T(128)S(1)} %add.2414), channel_id=1, source_target_pairs={{0,32},{16,48},{32,0},{48,16},{64,96},{80,112},{96,64},{112,80},{1... | collective-permute-start | bytes 200 | tf_op jit(solution)/shard_map/ppermute | solution.py:23
  67.4 5.4 %collective-permute-start.19 = (f32[16]{0:T(128)S(1)}, f32[16]{0:T(128)S(1)}, u32[]{:S(2)}, u32[]{:S(2)}) collective-permute-start(f32[16]{0:T(128)S(1)} %add.2415), channel_id=1, source_target_pairs={{0,64},{16,80},{32,96},{48,112},{64,0},{80,16},{96,32},{112,48},{1... | collective-permute-start | bytes 200 | tf_op jit(solution)/shard_map/ppermute | solution.py:23
  69.4 19.2 %copy-start.11 = (f32[16]{0:T(128)S(1)}, f32[16]{0:T(128)}, u32[]{:S(2)}) copy-start(f32[16]{0:T(128)} %param.15) | copy-start | bytes 196
  72.9 6.3 %collective-permute-start.20 = (f32[16]{0:T(128)S(1)}, f32[16]{0:T(128)S(1)}, u32[]{:S(2)}, u32[]{:S(2)}) collective-permute-start(f32[16]{0:T(128)S(1)} %add.2416), channel_id=1, source_target_pairs={{0,128},{16,144},{32,160},{48,176},{64,192},{80,208},{96,224},{112... | collective-permute-start | bytes 200 | tf_op jit(solution)/shard_map/ppermute | solution.py:23
  74.8 45.4 %copy-start.2 = (bf16[1,1,272,272]{3,2,1,0:T(8,128)(2,1)S(1)}, bf16[1,1,272,272]{3,2,1,0:T(8,128)(2,1)}, u32[]{:S(2)}) copy-start(bf16[1,1,272,272]{3,2,1,0:T(8,128)(2,1)} %param.16) | copy-start | bytes 443908
  79.2 9.3 %collective-permute-start.21 = (f32[16]{0:T(128)S(1)}, f32[16]{0:T(128)S(1)}, u32[]{:S(2)}, u32[]{:S(2)}) collective-permute-start(f32[16]{0:T(128)S(1)} %add.2417), channel_id=1, source_target_pairs={{0,256},{16,272},{32,288},{48,304},{64,320},{80,336},{96,352},{112... | collective-permute-start | bytes 200 | tf_op jit(solution)/shard_map/ppermute | solution.py:23
  88.5 116.9 %copy-start.7 = (f32[16]{0:T(128)}, f32[16]{0:T(128)S(1)}, u32[]{:S(2)}) copy-start(f32[16]{0:T(128)S(1)} %get-tuple-element.112) | copy-start | bytes 196
  88.6 11.5 %collective-permute-start.22 = (f32[1,1,16,68]{3,2,1,0:T(8,128)S(1)}, f32[1,1,16,68]{3,2,1,0:T(8,128)S(1)}, u32[]{:S(2)}, u32[]{:S(2)}) collective-permute-start(f32[1,1,16,68]{3,2,1,0:T(8,128)S(1)} %get-tuple-element.135), channel_id=1, source_target_pairs={{0,1},{1,2},{2,3},{3,4},{4,5},{5,6},{6,7},{7,8},{8,9},{9,10},{10,1... | collective-permute-start | bytes 13064 | tf_op jit(solution)/shard_map/ppermute | solution.py:12
  89.9 10.3 %collective-permute-start.24 = (f32[1,1,16,68]{3,2,1,0:T(8,128)S(1)}, f32[1,1,16,68]{3,2,1,0:T(8,128)S(1)}, u32[]{:S(2)}, u32[]{:S(2)}) collective-permute-start(f32[1,1,16,68]{3,2,1,0:T(8,128)S(1)} %get-tuple-element.136), channel_id=1, source_target_pairs={{0,16},{16,32},{32,48},{48,64},{64,80},{80,96},{96,112},{112,128},... | collective-permute-start | bytes 13064 | tf_op jit(solution)/shard_map/ppermute | solution.py:12
  93.6 6.6 %collective-permute-start.23 = (f32[1,1,16,68]{3,2,1,0:T(8,128)S(1)}, f32[1,1,16,68]{3,2,1,0:T(8,128)S(1)}, u32[]{:S(2)}, u32[]{:S(2)}) collective-permute-start(f32[1,1,16,68]{3,2,1,0:T(8,128)S(1)} %get-tuple-element.137), channel_id=1, source_target_pairs={{0,1},{1,2},{2,3},{3,4},{4,5},{5,6},{6,7},{7,8},{8,9},{9,10},{10,1... | collective-permute-start | bytes 13064 | tf_op jit(solution)/shard_map/ppermute | solution.py:12
  97.9 5.5 %collective-permute-start.25 = (f32[1,1,16,68]{3,2,1,0:T(8,128)S(1)}, f32[1,1,16,68]{3,2,1,0:T(8,128)S(1)}, u32[]{:S(2)}, u32[]{:S(2)}) collective-permute-start(f32[1,1,16,68]{3,2,1,0:T(8,128)S(1)} %get-tuple-element.138), channel_id=1, source_target_pairs={{0,16},{16,32},{32,48},{48,64},{64,80},{80,96},{96,112},{112,128},... | collective-permute-start | bytes 13064 | tf_op jit(solution)/shard_map/ppermute | solution.py:12
  103.6 0.7 copy-start.6
  104.6 2.1 %collective-permute-start.26 = (f32[1,1,128]{2,1,0:T(1,128)S(1)}, f32[1,1,128]{2,1,0:T(1,128)S(1)}, u32[]{:S(2)}, u32[]{:S(2)}) collective-permute-start(f32[1,1,128]{2,1,0:T(1,128)S(1)} %reshape.529), channel_id=1, source_target_pairs={{0,1},{1,2},{2,3},{3,4},{4,5},{5,6},{6,7},{7,8},{8,9},{9,10},{10,1... | collective-permute-start | bytes 1544 | tf_op jit(solution)/shard_map/ppermute | solution.py:12
  106.7 6.8 %collective-permute-start.27 = (f32[1,2,128]{2,1,0:T(2,128)S(1)}, f32[1,2,128]{2,1,0:T(2,128)S(1)}, u32[]{:S(2)}, u32[]{:S(2)}) collective-permute-start(f32[1,2,128]{2,1,0:T(2,128)S(1)} %pad_maximum_fusion.2), channel_id=1, source_target_pairs={{0,16},{16,32},{32,48},{48,64},{64,80},{80,96},{96,112},{112,128},... | collective-permute-start | bytes 3080 | tf_op jit(solution)/shard_map/ppermute | solution.py:12
  113.5 0.7 copy-start.8
  114.5 3.8 %collective-permute-start.28 = (f32[1,1,32]{2,1,0:T(1,128)S(1)}, f32[1,1,32]{2,1,0:T(1,128)S(1)}, u32[]{:S(2)}, u32[]{:S(2)}) collective-permute-start(f32[1,1,32]{2,1,0:T(1,128)S(1)} %reshape.533), channel_id=1, source_target_pairs={{1,0},{2,1},{3,2},{4,3},{5,4},{6,5},{7,6},{8,7},{9,8},{10,9},{11,1... | collective-permute-start | bytes 392 | tf_op jit(solution)/shard_map/ppermute | solution.py:12
  118.3 8.8 %collective-permute-start.29 = (f32[1,2,32]{2,1,0:T(2,128)S(1)}, f32[1,2,32]{2,1,0:T(2,128)S(1)}, u32[]{:S(2)}, u32[]{:S(2)}) collective-permute-start(f32[1,2,32]{2,1,0:T(2,128)S(1)} %pad_maximum_fusion.3), channel_id=1, source_target_pairs={{16,0},{32,16},{48,32},{64,48},{80,64},{96,80},{112,96},{128,112},... | collective-permute-start | bytes 776 | tf_op jit(solution)/shard_map/ppermute | solution.py:12
  127.5 5.7 %collective-permute-start.30 = (f32[1,1,16,68]{3,2,1,0:T(8,128)S(1)}, f32[1,1,16,68]{3,2,1,0:T(8,128)S(1)}, u32[]{:S(2)}, u32[]{:S(2)}) collective-permute-start(f32[1,1,16,68]{3,2,1,0:T(8,128)S(1)} %slice.776), channel_id=1, source_target_pairs={{1,0},{2,1},{3,2},{4,3},{5,4},{6,5},{7,6},{8,7},{9,8},{10,9},{11,1... | collective-permute-start | bytes 13064 | tf_op jit(solution)/shard_map/ppermute | solution.py:12
  133.4 8.9 %collective-permute-start.31 = (f32[1,1,16,68]{3,2,1,0:T(8,128)S(1)}, f32[1,1,16,68]{3,2,1,0:T(8,128)S(1)}, u32[]{:S(2)}, u32[]{:S(2)}) collective-permute-start(f32[1,1,16,68]{3,2,1,0:T(8,128)S(1)} %get-tuple-element.126), channel_id=1, source_target_pairs={{16,0},{32,16},{48,32},{64,48},{80,64},{96,80},{112,96},{128,112},... | collective-permute-start | bytes 13064 | tf_op jit(solution)/shard_map/ppermute | solution.py:12
  142.7 64.1 %copy-start.3 = (f32[1,1,16,136]{3,2,1,0:T(8,128)}, f32[1,1,16,136]{3,2,1,0:T(8,128)S(1)}, u32[]{:S(2)}) copy-start(f32[1,1,16,136]{3,2,1,0:T(8,128)S(1)} %get-tuple-element.110) | copy-start | bytes 26116
  145.2 4.0 %collective-permute-start.32 = (f32[7,16]{1,0:T(8,128)S(1)}, f32[7,16]{1,0:T(8,128)S(1)}, u32[]{:S(2)}, u32[]{:S(2)}) collective-permute-start(f32[7,16]{1,0:T(8,128)S(1)} %stack.21), channel_id=1, source_target_pairs={{0,1},{1,0},{2,3},{3,2},{4,5},{5,4},{6,7},{7,6},{8,9},{9,8},{10,11... | collective-permute-start | bytes 1352 | tf_op jit(solution)/shard_map/ppermute | solution.py:81
  149.2 5.5 %collective-permute-start.33 = (f32[7,16]{1,0:T(8,128)S(1)}, f32[7,16]{1,0:T(8,128)S(1)}, u32[]{:S(2)}, u32[]{:S(2)}) collective-permute-start(f32[7,16]{1,0:T(8,128)S(1)} %stack.22), channel_id=1, source_target_pairs={{0,2},{1,3},{2,0},{3,1},{4,6},{5,7},{6,4},{7,5},{8,10},{9,11},{10,... | collective-permute-start | bytes 1352 | tf_op jit(solution)/shard_map/ppermute | solution.py:81
  154.7 7.1 %collective-permute-start.34 = (f32[7,16]{1,0:T(8,128)S(1)}, f32[7,16]{1,0:T(8,128)S(1)}, u32[]{:S(2)}, u32[]{:S(2)}) collective-permute-start(f32[7,16]{1,0:T(8,128)S(1)} %stack.23), channel_id=1, source_target_pairs={{0,4},{1,5},{2,6},{3,7},{4,0},{5,1},{6,2},{7,3},{8,12},{9,13},{10,... | collective-permute-start | bytes 1352 | tf_op jit(solution)/shard_map/ppermute | solution.py:81
  161.9 9.4 %collective-permute-start.35 = (f32[7,16]{1,0:T(8,128)S(1)}, f32[7,16]{1,0:T(8,128)S(1)}, u32[]{:S(2)}, u32[]{:S(2)}) collective-permute-start(f32[7,16]{1,0:T(8,128)S(1)} %stack.24), channel_id=1, source_target_pairs={{0,8},{1,9},{2,10},{3,11},{4,12},{5,13},{6,14},{7,15},{8,0},{9,1},... | collective-permute-start | bytes 1352 | tf_op jit(solution)/shard_map/ppermute | solution.py:81
  171.3 5.5 %collective-permute-start.36 = (f32[7,16]{1,0:T(8,128)S(1)}, f32[7,16]{1,0:T(8,128)S(1)}, u32[]{:S(2)}, u32[]{:S(2)}) collective-permute-start(f32[7,16]{1,0:T(8,128)S(1)} %stack.25), channel_id=1, source_target_pairs={{0,16},{16,0},{32,48},{48,32},{64,80},{80,64},{96,112},{112,96},{1... | collective-permute-start | bytes 1352 | tf_op jit(solution)/shard_map/ppermute | solution.py:81
  176.9 7.0 %collective-permute-start.37 = (f32[7,16]{1,0:T(8,128)S(1)}, f32[7,16]{1,0:T(8,128)S(1)}, u32[]{:S(2)}, u32[]{:S(2)}) collective-permute-start(f32[7,16]{1,0:T(8,128)S(1)} %stack.26), channel_id=1, source_target_pairs={{0,32},{16,48},{32,0},{48,16},{64,96},{80,112},{96,64},{112,80},{1... | collective-permute-start | bytes 1352 | tf_op jit(solution)/shard_map/ppermute | solution.py:81
  184.0 5.5 %collective-permute-start.38 = (f32[7,16]{1,0:T(8,128)S(1)}, f32[7,16]{1,0:T(8,128)S(1)}, u32[]{:S(2)}, u32[]{:S(2)}) collective-permute-start(f32[7,16]{1,0:T(8,128)S(1)} %stack.27), channel_id=1, source_target_pairs={{0,64},{16,80},{32,96},{48,112},{64,0},{80,16},{96,32},{112,48},{1... | collective-permute-start | bytes 1352 | tf_op jit(solution)/shard_map/ppermute | solution.py:81
  189.5 6.4 %collective-permute-start.39 = (f32[7,16]{1,0:T(8,128)S(1)}, f32[7,16]{1,0:T(8,128)S(1)}, u32[]{:S(2)}, u32[]{:S(2)}) collective-permute-start(f32[7,16]{1,0:T(8,128)S(1)} %stack.28), channel_id=1, source_target_pairs={{0,128},{16,144},{32,160},{48,176},{64,192},{80,208},{96,224},{112... | collective-permute-start | bytes 1352 | tf_op jit(solution)/shard_map/ppermute | solution.py:81
  196.0 9.4 %collective-permute-start.40 = (f32[7,16]{1,0:T(8,128)S(1)}, f32[7,16]{1,0:T(8,128)S(1)}, u32[]{:S(2)}, u32[]{:S(2)}) collective-permute-start(f32[7,16]{1,0:T(8,128)S(1)} %stack.29), channel_id=1, source_target_pairs={{0,256},{16,272},{32,288},{48,304},{64,320},{80,336},{96,352},{112... | collective-permute-start | bytes 1352 | tf_op jit(solution)/shard_map/ppermute | solution.py:81
  205.4 1.4 copy-start.4
  207.5 0.5 copy-start.10

commit v3 on v2

--- a/solution.py
+++ b/solution.py
@@ -163,14 +163,55 @@
             * active
         )
 
+    def spread_pair(first, second):
+        east_perm = jnp.stack(
+            [permute_side(first[..., :SIDE], east_flip), permute_side(second[..., :SIDE], east_flip)]
+        )
+        north_perm = jnp.stack(
+            [permute_side(first[..., SIDE:], north_flip), permute_side(second[..., SIDE:], north_flip)]
+        )
+        west_edge = passed_along(east_perm, "py", 1)
+        from_west = jnp.concatenate([west_edge, east_perm[:, :, :-1]], 2)
+        south_edge = passed_along(north_perm, "px", 1)
+        from_south = jnp.concatenate([south_edge, north_perm[:, :-1]], 1)
+        return [
+            (field[..., :SIDE], field[..., SIDE:], from_west[k], from_south[k])
+            for k, field in enumerate((first, second))
+        ]
+
+    def jump_and_spread(side_values):
+        east_side = side_values[..., :SIDE]
+        north_side = side_values[..., SIDE : 2 * SIDE]
+        west_side = side_values[..., 2 * SIDE : 3 * SIDE]
+        south_side = side_values[..., 3 * SIDE :]
+        ones = jnp.broadcast_to(active, east_side.shape)
+        east_edge = passed_along(west_side, "py", -1)
+        from_east = jnp.concatenate([west_side[:, 1:], east_edge], 1)
+        north_edge = passed_along(south_side, "px", -1)
+        from_north = jnp.concatenate([south_side[1:], north_edge], 0)
+        east_perm_side = permute_side(east_side, east_flip)
+        north_perm_side = permute_side(north_side, north_flip)
+        west_sent = passed_along(jnp.stack([east_perm_side, ones]), "py", 1)
+        south_sent = passed_along(jnp.stack([north_perm_side, ones]), "px", 1)
+        east_term = permute_side(from_east, east_flip)
+        north_term = permute_side(from_north, north_flip)
+        joined = jnp.concatenate([east_side - east_term, north_side - north_term], 3)
+        half_jump = 0.5 * (joined * edge_mask)
+        west_edge = 0.5 * ((west_sent[0] - west_side[:, :1]) * west_sent[1])
+        south_edge = 0.5 * ((south_sent[0] - south_side[:1]) * south_sent[1])
+        local_east = permute_side(half_jump[..., :SIDE], east_flip)
+        local_north = permute_side(half_jump[..., SIDE:], north_flip)
+        from_west = jnp.concatenate([west_edge, local_east[:, :-1]], 1)
+        from_south = jnp.concatenate([south_edge, local_north[:-1]], 0)
+        return half_jump, (half_jump[..., :SIDE], half_jump[..., SIDE:], from_west, from_south)
+
     start_sol = solution * edge_mask
     start_res = residual * edge_mask
     start_dir = direction * edge_mask
-    dir_parts = spread_parts(start_dir)
-    spread = spread_of(spread_parts(0.5 * start_res)).astype(jnp.bfloat16)
+    res_parts, dir_parts = spread_pair(0.5 * start_res, start_dir)
+    spread = spread_of(res_parts).astype(jnp.bfloat16)
     side_values = patch_products(dual_schur, spread)
-    precond = 0.5 * jump_b(side_values)
-    precond_parts = spread_parts(precond)
+    precond, precond_parts = jump_and_spread(side_values)
     rz_current = all_sum(jnp.sum(start_res * precond, axis=(0, 1, 3)))
     step_ratio = rz_current / rz_previous
     ratio = step_ratio[None, None, :, None]

time: 209 us -> 196 us (0.938)
  waiting for transfers between devices: 96.4 us -> 89.4 us
  starting transfers between devices: 96.5 us -> 89.9 us
    ppermute x14 -> x12, starting transfers between devices: 34.3 us -> 27.4 us  [passed_along(): return lax.ppermute(value, axis, pairs)]
    ppermute x14 -> x12, waiting for transfers between devices: 36.6 us -> 32.7 us  [passed_along(): return lax.ppermute(value, axis, pairs)]
    ppermute x9, waiting for transfers between devices: 29.3 us -> 25.7 us  [all_sum(): lax.ppermute(value, axis, [(i, i ^ step) for i in range(peers)])]
  transfers between devices with their start and end apart: 32 -> 30, of which waited for: 28 -> 27; matrix products, arithmetic and copies ran while one was open for 1% -> 0% of each run, Pallas kernels for 0% -> 0%
where the time goes in v3:
time: 196 us; the launch traced here: 195 us
  starting transfers between devices  89.9 us (46%)
  waiting for transfers between devices  89.4 us (46%)
  local copies, waits for them, and re-layouts  5.79 us (3%)
  other arithmetic  4.96 us (3%)
  between operations  3.97 us (2%)
    ppermute x9, starting transfers between devices, all_sum(): lax.ppermute(value, axis, [(i, i ^ step) for i in range(peers)])  33.1 us
    ppermute x12, waiting for transfers between devices, passed_along(): return lax.ppermute(value, axis, pairs)  32.7 us
    ppermute x9, waiting for transfers between devices, all_sum_mixed(): other = lax.ppermute(packed, axis, [(i, i ^ step) for i in range(peers)])  30.9 us
    ppermute x9, starting transfers between devices, all_sum_mixed(): other = lax.ppermute(packed, axis, [(i, i ^ step) for i in range(peers)])  29.3 us
    ppermute x12, starting transfers between devices, passed_along(): return lax.ppermute(value, axis, pairs)  27.4 us
    ppermute x9, waiting for transfers between devices, all_sum(): lax.ppermute(value, axis, [(i, i ^ step) for i in range(peers)])  25.7 us
  transfers between devices with their start and end apart: 30, of which 27 were waited for; matrix products, arithmetic and copies ran while one was open for 0% of the time, Pallas kernels for 0%

profile of v3, /device:TPU:30, one launch (start us, length us, event | category | flops | bytes accessed | tf_op | source)
XLA Modules:
  0.0 195.1 jit_solution(8875485997380286503)
XLA Ops:
  4.9 1.7 collective-permute-start.9
  6.6 4.6 %collective-permute-start.10 = (f32[2,1,1,16,68]{4,3,2,1,0:T(8,128)S(1)}, f32[2,1,1,16,68]{4,3,2,1,0:T(8,128)S(1)}, u32[]{:S(2)}, u32[]{:S(2)}) collective-permute-start(f32[2,1,1,16,68]{4,3,2,1,0:T(8,128)S(1)} %pad_maximum_fusion.1), channel_id=1, source_target_pairs={{0,16},{16,32},{32,48},{48,64},{64,80},{80,96},{96,112},{112,128},... | collective-permute-start | bytes 26120 | tf_op jit(solution)/shard_map/ppermute | solution.py:12
  11.3 1.4 collective-permute-done.10
  12.9 2.3 %collective-permute-start.12 = (f32[1,1,16,68]{3,2,1,0:T(8,128)S(1)}, f32[1,1,16,68]{3,2,1,0:T(8,128)S(1)}, u32[]{:S(2)}, u32[]{:S(2)}) collective-permute-start(f32[1,1,16,68]{3,2,1,0:T(8,128)S(1)} %get-tuple-element.134), channel_id=1, source_target_pairs={{16,0},{32,16},{48,32},{64,48},{80,64},{96,80},{112,96},{128,112},... | collective-permute-start | bytes 13064 | tf_op jit(solution)/shard_map/ppermute | solution.py:12
  15.7 6.4 %collective-permute-done.12 = f32[1,1,16,68]{3,2,1,0:T(8,128)S(1)} collective-permute-done((f32[1,1,16,68]{3,2,1,0:T(8,128)S(1)}, f32[1,1,16,68]{3,2,1,0:T(8,128)S(1)}, u32[]{:S(2)}, u32[]{:S(2)}) %collective-permute-start.12) | collective-permute-done | bytes 4384 | tf_op jit(solution)/shard_map/ppermute | solution.py:12
  23.6 1.9 collective-permute-done.11
  25.9 4.6 %collective-permute-start.13 = (f32[16]{0:T(128)S(1)}, f32[16]{0:T(128)S(1)}, u32[]{:S(2)}, u32[]{:S(2)}) collective-permute-start(f32[16]{0:T(128)S(1)} %get-tuple-element.113), channel_id=1, source_target_pairs={{0,1},{1,0},{2,3},{3,2},{4,5},{5,4},{6,7},{7,6},{8,9},{9,8},{10,11... | collective-permute-start | bytes 200 | tf_op jit(solution)/shard_map/ppermute | solution.py:23
  31.4 4.3 %collective-permute-start.14 = (f32[16]{0:T(128)S(1)}, f32[16]{0:T(128)S(1)}, u32[]{:S(2)}, u32[]{:S(2)}) collective-permute-start(f32[16]{0:T(128)S(1)} %add.2414), channel_id=1, source_target_pairs={{0,2},{1,3},{2,0},{3,1},{4,6},{5,7},{6,4},{7,5},{8,10},{9,11},{10,... | collective-permute-start | bytes 200 | tf_op jit(solution)/shard_map/ppermute | solution.py:23
  35.6 1.5 collective-permute-done.14
  37.1 8.2 %collective-permute-start.15 = (f32[16]{0:T(128)S(1)}, f32[16]{0:T(128)S(1)}, u32[]{:S(2)}, u32[]{:S(2)}) collective-permute-start(f32[16]{0:T(128)S(1)} %add.2415), channel_id=1, source_target_pairs={{0,4},{1,5},{2,6},{3,7},{4,0},{5,1},{6,2},{7,3},{8,12},{9,13},{10,... | collective-permute-start | bytes 200 | tf_op jit(solution)/shard_map/ppermute | solution.py:23
  45.4 1.5 collective-permute-done.15
  46.9 6.3 %collective-permute-start.16 = (f32[16]{0:T(128)S(1)}, f32[16]{0:T(128)S(1)}, u32[]{:S(2)}, u32[]{:S(2)}) collective-permute-start(f32[16]{0:T(128)S(1)} %add.2416), channel_id=1, source_target_pairs={{0,8},{1,9},{2,10},{3,11},{4,12},{5,13},{6,14},{7,15},{8,0},{9,1},... | collective-permute-start | bytes 200 | tf_op jit(solution)/shard_map/ppermute | solution.py:23
  53.1 3.1 %collective-permute-done.16 = f32[16]{0:T(128)S(1)} collective-permute-done((f32[16]{0:T(128)S(1)}, f32[16]{0:T(128)S(1)}, u32[]{:S(2)}, u32[]{:S(2)}) %collective-permute-start.16) | collective-permute-done | bytes 96 | tf_op jit(solution)/shard_map/ppermute | solution.py:23
  56.2 1.9 collective-permute-start.17
  58.1 3.5 %collective-permute-done.17 = f32[16]{0:T(128)S(1)} collective-permute-done((f32[16]{0:T(128)S(1)}, f32[16]{0:T(128)S(1)}, u32[]{:S(2)}, u32[]{:S(2)}) %collective-permute-start.17) | collective-permute-done | bytes 96 | tf_op jit(solution)/shard_map/ppermute | solution.py:23
  61.6 1.9 collective-permute-start.18
  63.6 5.0 %collective-permute-done.18 = f32[16]{0:T(128)S(1)} collective-permute-done((f32[16]{0:T(128)S(1)}, f32[16]{0:T(128)S(1)}, u32[]{:S(2)}, u32[]{:S(2)}) %collective-permute-start.18) | collective-permute-done | bytes 96 | tf_op jit(solution)/shard_map/ppermute | solution.py:23
  68.6 1.9 collective-permute-start.19
  71.8 2.2 %collective-permute-done.19 = f32[16]{0:T(128)S(1)} collective-permute-done((f32[16]{0:T(128)S(1)}, f32[16]{0:T(128)S(1)}, u32[]{:S(2)}, u32[]{:S(2)}) %collective-permute-start.19) | collective-permute-done | bytes 96 | tf_op jit(solution)/shard_map/ppermute | solution.py:23
  74.0 1.9 collective-permute-start.20
  75.9 4.4 %collective-permute-done.20 = f32[16]{0:T(128)S(1)} collective-permute-done((f32[16]{0:T(128)S(1)}, f32[16]{0:T(128)S(1)}, u32[]{:S(2)}, u32[]{:S(2)}) %collective-permute-start.20) | collective-permute-done | bytes 96 | tf_op jit(solution)/shard_map/ppermute | solution.py:23
  80.3 2.2 %collective-permute-start.21 = (f32[16]{0:T(128)S(1)}, f32[16]{0:T(128)S(1)}, u32[]{:S(2)}, u32[]{:S(2)}) collective-permute-start(f32[16]{0:T(128)S(1)} %add.2421), channel_id=1, source_target_pairs={{0,256},{16,272},{32,288},{48,304},{64,320},{80,336},{96,352},{112... | collective-permute-start | bytes 200 | tf_op jit(solution)/shard_map/ppermute | solution.py:23
  82.5 3.4 %collective-permute-start.23 = (f32[2,1,1,16,68]{4,3,2,1,0:T(8,128)S(1)}, f32[2,1,1,16,68]{4,3,2,1,0:T(8,128)S(1)}, u32[]{:S(2)}, u32[]{:S(2)}) collective-permute-start(f32[2,1,1,16,68]{4,3,2,1,0:T(8,128)S(1)} %stack.49), channel_id=1, source_target_pairs={{0,16},{16,32},{32,48},{48,64},{64,80},{80,96},{96,112},{112,128},... | collective-permute-start | bytes 26120 | tf_op jit(solution)/shard_map/ppermute | solution.py:12
  85.9 3.8 %collective-permute-done.21 = f32[16]{0:T(128)S(1)} collective-permute-done((f32[16]{0:T(128)S(1)}, f32[16]{0:T(128)S(1)}, u32[]{:S(2)}, u32[]{:S(2)}) %collective-permute-start.21) | collective-permute-done | bytes 96 | tf_op jit(solution)/shard_map/ppermute | solution.py:23
  92.9 5.1 %collective-permute-start.25 = (f32[1,2,128]{2,1,0:T(2,128)S(1)}, f32[1,2,128]{2,1,0:T(2,128)S(1)}, u32[]{:S(2)}, u32[]{:S(2)}) collective-permute-start(f32[1,2,128]{2,1,0:T(2,128)S(1)} %pad_maximum_fusion.4), channel_id=1, source_target_pairs={{0,16},{16,32},{32,48},{48,64},{64,80},{80,96},{96,112},{112,128},... | collective-permute-start | bytes 3080 | tf_op jit(solution)/shard_map/ppermute | solution.py:12
  101.6 3.0 %collective-permute-done.26 = f32[1,1,32]{2,1,0:T(1,128)S(1)} collective-permute-done((f32[1,1,32]{2,1,0:T(1,128)S(1)}, f32[1,1,32]{2,1,0:T(1,128)S(1)}, u32[]{:S(2)}, u32[]{:S(2)}) %collective-permute-start.26) | collective-permute-done | bytes 160 | tf_op jit(solution)/shard_map/ppermute | solution.py:12
  104.7 1.9 collective-permute-start.27
  106.8 6.6 %collective-permute-done.27 = f32[1,2,32]{2,1,0:T(2,128)S(1)} collective-permute-done((f32[1,2,32]{2,1,0:T(2,128)S(1)}, f32[1,2,32]{2,1,0:T(2,128)S(1)}, u32[]{:S(2)}, u32[]{:S(2)}) %collective-permute-start.27) | collective-permute-done | bytes 288 | tf_op jit(solution)/shard_map/ppermute | solution.py:12
  115.1 4.4 %collective-permute-done.28 = f32[1,1,16,68]{3,2,1,0:T(8,128)S(1)} collective-permute-done((f32[1,1,16,68]{3,2,1,0:T(8,128)S(1)}, f32[1,1,16,68]{3,2,1,0:T(8,128)S(1)}, u32[]{:S(2)}, u32[]{:S(2)}) %collective-permute-start.28) | collective-permute-done | bytes 4384 | tf_op jit(solution)/shard_map/ppermute | solution.py:12
  119.8 1.9 collective-permute-start.29
  121.7 6.9 %collective-permute-done.29 = f32[1,1,16,68]{3,2,1,0:T(8,128)S(1)} collective-permute-done((f32[1,1,16,68]{3,2,1,0:T(8,128)S(1)}, f32[1,1,16,68]{3,2,1,0:T(8,128)S(1)}, u32[]{:S(2)}, u32[]{:S(2)}) %collective-permute-start.29) | collective-permute-done | bytes 4384 | tf_op jit(solution)/shard_map/ppermute | solution.py:12
  131.6 3.2 %collective-permute-start.30 = (f32[7,16]{1,0:T(8,128)S(1)}, f32[7,16]{1,0:T(8,128)S(1)}, u32[]{:S(2)}, u32[]{:S(2)}) collective-permute-start(f32[7,16]{1,0:T(8,128)S(1)} %stack.51), channel_id=1, source_target_pairs={{0,1},{1,0},{2,3},{3,2},{4,5},{5,4},{6,7},{7,6},{8,9},{9,8},{10,11... | collective-permute-start | bytes 1352 | tf_op jit(solution)/shard_map/ppermute | solution.py:81
  135.6 3.4 %collective-permute-start.31 = (f32[7,16]{1,0:T(8,128)S(1)}, f32[7,16]{1,0:T(8,128)S(1)}, u32[]{:S(2)}, u32[]{:S(2)}) collective-permute-start(f32[7,16]{1,0:T(8,128)S(1)} %stack.52), channel_id=1, source_target_pairs={{0,2},{1,3},{2,0},{3,1},{4,6},{5,7},{6,4},{7,5},{8,10},{9,11},{10,... | collective-permute-start | bytes 1352 | tf_op jit(solution)/shard_map/ppermute | solution.py:81
  139.0 2.1 %collective-permute-done.31 = f32[7,16]{1,0:T(8,128)S(1)} collective-permute-done((f32[7,16]{1,0:T(8,128)S(1)}, f32[7,16]{1,0:T(8,128)S(1)}, u32[]{:S(2)}, u32[]{:S(2)}) %collective-permute-start.31) | collective-permute-done | bytes 480 | tf_op jit(solution)/shard_map/ppermute | solution.py:81
  141.2 6.1 %collective-permute-start.32 = (f32[7,16]{1,0:T(8,128)S(1)}, f32[7,16]{1,0:T(8,128)S(1)}, u32[]{:S(2)}, u32[]{:S(2)}) collective-permute-start(f32[7,16]{1,0:T(8,128)S(1)} %stack.53), channel_id=1, source_target_pairs={{0,4},{1,5},{2,6},{3,7},{4,0},{5,1},{6,2},{7,3},{8,12},{9,13},{10,... | collective-permute-start | bytes 1352 | tf_op jit(solution)/shard_map/ppermute | solution.py:81
  147.3 1.6 collective-permute-done.32
  148.9 7.1 %collective-permute-start.33 = (f32[7,16]{1,0:T(8,128)S(1)}, f32[7,16]{1,0:T(8,128)S(1)}, u32[]{:S(2)}, u32[]{:S(2)}) collective-permute-start(f32[7,16]{1,0:T(8,128)S(1)} %stack.54), channel_id=1, source_target_pairs={{0,8},{1,9},{2,10},{3,11},{4,12},{5,13},{6,14},{7,15},{8,0},{9,1},... | collective-permute-start | bytes 1352 | tf_op jit(solution)/shard_map/ppermute | solution.py:81
  156.0 2.3 %collective-permute-done.33 = f32[7,16]{1,0:T(8,128)S(1)} collective-permute-done((f32[7,16]{1,0:T(8,128)S(1)}, f32[7,16]{1,0:T(8,128)S(1)}, u32[]{:S(2)}, u32[]{:S(2)}) %collective-permute-start.33) | collective-permute-done | bytes 480 | tf_op jit(solution)/shard_map/ppermute | solution.py:81
  158.4 1.9 collective-permute-start.34
  160.3 3.6 %collective-permute-done.34 = f32[7,16]{1,0:T(8,128)S(1)} collective-permute-done((f32[7,16]{1,0:T(8,128)S(1)}, f32[7,16]{1,0:T(8,128)S(1)}, u32[]{:S(2)}, u32[]{:S(2)}) %collective-permute-start.34) | collective-permute-done | bytes 480 | tf_op jit(solution)/shard_map/ppermute | solution.py:81
  163.9 1.9 collective-permute-start.35
  165.8 5.1 %collective-permute-done.35 = f32[7,16]{1,0:T(8,128)S(1)} collective-permute-done((f32[7,16]{1,0:T(8,128)S(1)}, f32[7,16]{1,0:T(8,128)S(1)}, u32[]{:S(2)}, u32[]{:S(2)}) %collective-permute-start.35) | collective-permute-done | bytes 480 | tf_op jit(solution)/shard_map/ppermute | solution.py:81
  171.0 1.9 collective-permute-start.36
  172.9 3.6 %collective-permute-done.36 = f32[7,16]{1,0:T(8,128)S(1)} collective-permute-done((f32[7,16]{1,0:T(8,128)S(1)}, f32[7,16]{1,0:T(8,128)S(1)}, u32[]{:S(2)}, u32[]{:S(2)}) %collective-permute-start.36) | collective-permute-done | bytes 480 | tf_op jit(solution)/shard_map/ppermute | solution.py:81
  176.5 1.9 collective-permute-start.37
  178.5 4.5 %collective-permute-done.37 = f32[7,16]{1,0:T(8,128)S(1)} collective-permute-done((f32[7,16]{1,0:T(8,128)S(1)}, f32[7,16]{1,0:T(8,128)S(1)}, u32[]{:S(2)}, u32[]{:S(2)}) %collective-permute-start.37) | collective-permute-done | bytes 480 | tf_op jit(solution)/shard_map/ppermute | solution.py:81
  183.0 1.9 collective-permute-start.38
  184.9 7.5 %collective-permute-done.38 = f32[7,16]{1,0:T(8,128)S(1)} collective-permute-done((f32[7,16]{1,0:T(8,128)S(1)}, f32[7,16]{1,0:T(8,128)S(1)}, u32[]{:S(2)}, u32[]{:S(2)}) %collective-permute-start.38) | collective-permute-done | bytes 480 | tf_op jit(solution)/shard_map/ppermute | solution.py:81
  (165 shorter events, 21.9 us)
Async XLA Ops:
  0.6 12.0 %copy-start = (bf16[1,1,272,272]{3,2,1,0:T(8,128)(2,1)S(1)}, bf16[1,1,272,272]{3,2,1,0:T(8,128)(2,1)}, u32[]{:S(2)}) copy-start(bf16[1,1,272,272]{3,2,1,0:T(8,128)(2,1)} %param.17) | copy-start | bytes 443908
  0.6 0.8 copy-start.1
  0.7 0.8 copy-start.5
  2.3 0.7 copy-start.9
  4.9 6.4 %collective-permute-start.9 = (f32[2,1,1,16,68]{4,3,2,1,0:T(8,128)S(1)}, f32[2,1,1,16,68]{4,3,2,1,0:T(8,128)S(1)}, u32[]{:S(2)}, u32[]{:S(2)}) collective-permute-start(f32[2,1,1,16,68]{4,3,2,1,0:T(8,128)S(1)} %pad_maximum_fusion), channel_id=1, source_target_pairs={{0,1},{1,2},{2,3},{3,4},{4,5},{5,6},{6,7},{7,8},{8,9},{9,10},{10,1... | collective-permute-start | bytes 26120 | tf_op jit(solution)/shard_map/ppermute | solution.py:12
  6.6 6.0 %collective-permute-start.10 = (f32[2,1,1,16,68]{4,3,2,1,0:T(8,128)S(1)}, f32[2,1,1,16,68]{4,3,2,1,0:T(8,128)S(1)}, u32[]{:S(2)}, u32[]{:S(2)}) collective-permute-start(f32[2,1,1,16,68]{4,3,2,1,0:T(8,128)S(1)} %pad_maximum_fusion.1), channel_id=1, source_target_pairs={{0,16},{16,32},{32,48},{48,64},{64,80},{80,96},{96,112},{112,128},... | collective-permute-start | bytes 26120 | tf_op jit(solution)/shard_map/ppermute | solution.py:12
  12.9 9.1 %collective-permute-start.12 = (f32[1,1,16,68]{3,2,1,0:T(8,128)S(1)}, f32[1,1,16,68]{3,2,1,0:T(8,128)S(1)}, u32[]{:S(2)}, u32[]{:S(2)}) collective-permute-start(f32[1,1,16,68]{3,2,1,0:T(8,128)S(1)} %get-tuple-element.134), channel_id=1, source_target_pairs={{16,0},{32,16},{48,32},{64,48},{80,64},{96,80},{112,96},{128,112},... | collective-permute-start | bytes 13064 | tf_op jit(solution)/shard_map/ppermute | solution.py:12
  22.3 3.2 %collective-permute-start.11 = (f32[1,1,16,68]{3,2,1,0:T(8,128)S(1)}, f32[1,1,16,68]{3,2,1,0:T(8,128)S(1)}, u32[]{:S(2)}, u32[]{:S(2)}) collective-permute-start(f32[1,1,16,68]{3,2,1,0:T(8,128)S(1)} %get-tuple-element.132), channel_id=1, source_target_pairs={{1,0},{2,1},{3,2},{4,3},{5,4},{6,5},{7,6},{8,7},{9,8},{10,9},{11,1... | collective-permute-start | bytes 13064 | tf_op jit(solution)/shard_map/ppermute | solution.py:12
  25.7 63.9 %copy-start.11 = (f32[16]{0:T(128)S(1)}, f32[16]{0:T(128)}, u32[]{:S(2)}) copy-start(f32[16]{0:T(128)} %param.15) | copy-start | bytes 196
  25.7 80.8 %copy-start.2 = (bf16[1,1,272,272]{3,2,1,0:T(8,128)(2,1)S(1)}, bf16[1,1,272,272]{3,2,1,0:T(8,128)(2,1)}, u32[]{:S(2)}) copy-start(bf16[1,1,272,272]{3,2,1,0:T(8,128)(2,1)} %param.16) | copy-start | bytes 443908
  25.9 5.4 %collective-permute-start.13 = (f32[16]{0:T(128)S(1)}, f32[16]{0:T(128)S(1)}, u32[]{:S(2)}, u32[]{:S(2)}) collective-permute-start(f32[16]{0:T(128)S(1)} %get-tuple-element.113), channel_id=1, source_target_pairs={{0,1},{1,0},{2,3},{3,2},{4,5},{5,4},{6,7},{7,6},{8,9},{9,8},{10,11... | collective-permute-start | bytes 200 | tf_op jit(solution)/shard_map/ppermute | solution.py:23
  31.4 5.8 %collective-permute-start.14 = (f32[16]{0:T(128)S(1)}, f32[16]{0:T(128)S(1)}, u32[]{:S(2)}, u32[]{:S(2)}) collective-permute-start(f32[16]{0:T(128)S(1)} %add.2414), channel_id=1, source_target_pairs={{0,2},{1,3},{2,0},{3,1},{4,6},{5,7},{6,4},{7,5},{8,10},{9,11},{10,... | collective-permute-start | bytes 200 | tf_op jit(solution)/shard_map/ppermute | solution.py:23
  37.1 9.7 %collective-permute-start.15 = (f32[16]{0:T(128)S(1)}, f32[16]{0:T(128)S(1)}, u32[]{:S(2)}, u32[]{:S(2)}) collective-permute-start(f32[16]{0:T(128)S(1)} %add.2415), channel_id=1, source_target_pairs={{0,4},{1,5},{2,6},{3,7},{4,0},{5,1},{6,2},{7,3},{8,12},{9,13},{10,... | collective-permute-start | bytes 200 | tf_op jit(solution)/shard_map/ppermute | solution.py:23
  46.9 9.3 %collective-permute-start.16 = (f32[16]{0:T(128)S(1)}, f32[16]{0:T(128)S(1)}, u32[]{:S(2)}, u32[]{:S(2)}) collective-permute-start(f32[16]{0:T(128)S(1)} %add.2416), channel_id=1, source_target_pairs={{0,8},{1,9},{2,10},{3,11},{4,12},{5,13},{6,14},{7,15},{8,0},{9,1},... | collective-permute-start | bytes 200 | tf_op jit(solution)/shard_map/ppermute | solution.py:23
  56.2 5.4 %collective-permute-start.17 = (f32[16]{0:T(128)S(1)}, f32[16]{0:T(128)S(1)}, u32[]{:S(2)}, u32[]{:S(2)}) collective-permute-start(f32[16]{0:T(128)S(1)} %add.2417), channel_id=1, source_target_pairs={{0,16},{16,0},{32,48},{48,32},{64,80},{80,64},{96,112},{112,96},{1... | collective-permute-start | bytes 200 | tf_op jit(solution)/shard_map/ppermute | solution.py:23
  61.6 6.9 %collective-permute-start.18 = (f32[16]{0:T(128)S(1)}, f32[16]{0:T(128)S(1)}, u32[]{:S(2)}, u32[]{:S(2)}) collective-permute-start(f32[16]{0:T(128)S(1)} %add.2418), channel_id=1, source_target_pairs={{0,32},{16,48},{32,0},{48,16},{64,96},{80,112},{96,64},{112,80},{1... | collective-permute-start | bytes 200 | tf_op jit(solution)/shard_map/ppermute | solution.py:23
  68.6 5.4 %collective-permute-start.19 = (f32[16]{0:T(128)S(1)}, f32[16]{0:T(128)S(1)}, u32[]{:S(2)}, u32[]{:S(2)}) collective-permute-start(f32[16]{0:T(128)S(1)} %add.2419), channel_id=1, source_target_pairs={{0,64},{16,80},{32,96},{48,112},{64,0},{80,16},{96,32},{112,48},{1... | collective-permute-start | bytes 200 | tf_op jit(solution)/shard_map/ppermute | solution.py:23
  70.5 19.2 %collective-permute-start.22 = (f32[2,1,1,16,68]{4,3,2,1,0:T(8,128)S(1)}, f32[2,1,1,16,68]{4,3,2,1,0:T(8,128)S(1)}, u32[]{:S(2)}, u32[]{:S(2)}) collective-permute-start(f32[2,1,1,16,68]{4,3,2,1,0:T(8,128)S(1)} %stack.47), channel_id=1, source_target_pairs={{0,1},{1,2},{2,3},{3,4},{4,5},{5,6},{6,7},{7,8},{8,9},{9,10},{10,1... | collective-permute-start | bytes 26120 | tf_op jit(solution)/shard_map/ppermute | solution.py:12
  74.0 6.3 %collective-permute-start.20 = (f32[16]{0:T(128)S(1)}, f32[16]{0:T(128)S(1)}, u32[]{:S(2)}, u32[]{:S(2)}) collective-permute-start(f32[16]{0:T(128)S(1)} %add.2420), channel_id=1, source_target_pairs={{0,128},{16,144},{32,160},{48,176},{64,192},{80,208},{96,224},{112... | collective-permute-start | bytes 200 | tf_op jit(solution)/shard_map/ppermute | solution.py:23
  80.3 9.3 %collective-permute-start.21 = (f32[16]{0:T(128)S(1)}, f32[16]{0:T(128)S(1)}, u32[]{:S(2)}, u32[]{:S(2)}) collective-permute-start(f32[16]{0:T(128)S(1)} %add.2421), channel_id=1, source_target_pairs={{0,256},{16,272},{32,288},{48,304},{64,320},{80,336},{96,352},{112... | collective-permute-start | bytes 200 | tf_op jit(solution)/shard_map/ppermute | solution.py:23
  82.5 7.2 %collective-permute-start.23 = (f32[2,1,1,16,68]{4,3,2,1,0:T(8,128)S(1)}, f32[2,1,1,16,68]{4,3,2,1,0:T(8,128)S(1)}, u32[]{:S(2)}, u32[]{:S(2)}) collective-permute-start(f32[2,1,1,16,68]{4,3,2,1,0:T(8,128)S(1)} %stack.49), channel_id=1, source_target_pairs={{0,16},{16,32},{32,48},{48,64},{64,80},{80,96},{96,112},{112,128},... | collective-permute-start | bytes 26120 | tf_op jit(solution)/shard_map/ppermute | solution.py:12
  89.6 102.8 %copy-start.7 = (f32[16]{0:T(128)}, f32[16]{0:T(128)S(1)}, u32[]{:S(2)}) copy-start(f32[16]{0:T(128)S(1)} %get-tuple-element.112) | copy-start | bytes 196
  89.8 0.7 copy-start.6
  90.8 2.1 %collective-permute-start.24 = (f32[1,1,128]{2,1,0:T(1,128)S(1)}, f32[1,1,128]{2,1,0:T(1,128)S(1)}, u32[]{:S(2)}, u32[]{:S(2)}) collective-permute-start(f32[1,1,128]{2,1,0:T(1,128)S(1)} %reshape.602), channel_id=1, source_target_pairs={{0,1},{1,2},{2,3},{3,4},{4,5},{5,6},{6,7},{7,8},{8,9},{9,10},{10,1... | collective-permute-start | bytes 1544 | tf_op jit(solution)/shard_map/ppermute | solution.py:12
  92.9 6.4 %collective-permute-start.25 = (f32[1,2,128]{2,1,0:T(2,128)S(1)}, f32[1,2,128]{2,1,0:T(2,128)S(1)}, u32[]{:S(2)}, u32[]{:S(2)}) collective-permute-start(f32[1,2,128]{2,1,0:T(2,128)S(1)} %pad_maximum_fusion.4), channel_id=1, source_target_pairs={{0,16},{16,32},{32,48},{48,64},{64,80},{80,96},{96,112},{112,128},... | collective-permute-start | bytes 3080 | tf_op jit(solution)/shard_map/ppermute | solution.py:12
  99.4 0.7 copy-start.8
  100.3 4.3 %collective-permute-start.26 = (f32[1,1,32]{2,1,0:T(1,128)S(1)}, f32[1,1,32]{2,1,0:T(1,128)S(1)}, u32[]{:S(2)}, u32[]{:S(2)}) collective-permute-start(f32[1,1,32]{2,1,0:T(1,128)S(1)} %reshape.606), channel_id=1, source_target_pairs={{1,0},{2,1},{3,2},{4,3},{5,4},{6,5},{7,6},{8,7},{9,8},{10,9},{11,1... | collective-permute-start | bytes 392 | tf_op jit(solution)/shard_map/ppermute | solution.py:12
  104.7 8.8 %collective-permute-start.27 = (f32[1,2,32]{2,1,0:T(2,128)S(1)}, f32[1,2,32]{2,1,0:T(2,128)S(1)}, u32[]{:S(2)}, u32[]{:S(2)}) collective-permute-start(f32[1,2,32]{2,1,0:T(2,128)S(1)} %pad_maximum_fusion.5), channel_id=1, source_target_pairs={{16,0},{32,16},{48,32},{64,48},{80,64},{96,80},{112,96},{128,112},... | collective-permute-start | bytes 776 | tf_op jit(solution)/shard_map/ppermute | solution.py:12
  113.8 5.7 %collective-permute-start.28 = (f32[1,1,16,68]{3,2,1,0:T(8,128)S(1)}, f32[1,1,16,68]{3,2,1,0:T(8,128)S(1)}, u32[]{:S(2)}, u32[]{:S(2)}) collective-permute-start(f32[1,1,16,68]{3,2,1,0:T(8,128)S(1)} %slice.822), channel_id=1, source_target_pairs={{1,0},{2,1},{3,2},{4,3},{5,4},{6,5},{7,6},{8,7},{9,8},{10,9},{11,1... | collective-permute-start | bytes 13064 | tf_op jit(solution)/shard_map/ppermute | solution.py:12
  119.8 8.9 %collective-permute-start.29 = (f32[1,1,16,68]{3,2,1,0:T(8,128)S(1)}, f32[1,1,16,68]{3,2,1,0:T(8,128)S(1)}, u32[]{:S(2)}, u32[]{:S(2)}) collective-permute-start(f32[1,1,16,68]{3,2,1,0:T(8,128)S(1)} %get-tuple-element.128), channel_id=1, source_target_pairs={{16,0},{32,16},{48,32},{64,48},{80,64},{96,80},{112,96},{128,112},... | collective-permute-start | bytes 13064 | tf_op jit(solution)/shard_map/ppermute | solution.py:12
  129.1 64.8 %copy-start.3 = (f32[1,1,16,136]{3,2,1,0:T(8,128)}, f32[1,1,16,136]{3,2,1,0:T(8,128)S(1)}, u32[]{:S(2)}) copy-start(f32[1,1,16,136]{3,2,1,0:T(8,128)S(1)} %get-tuple-element.110) | copy-start | bytes 26116
  131.6 4.0 %collective-permute-start.30 = (f32[7,16]{1,0:T(8,128)S(1)}, f32[7,16]{1,0:T(8,128)S(1)}, u32[]{:S(2)}, u32[]{:S(2)}) collective-permute-start(f32[7,16]{1,0:T(8,128)S(1)} %stack.51), channel_id=1, source_target_pairs={{0,1},{1,0},{2,3},{3,2},{4,5},{5,4},{6,7},{7,6},{8,9},{9,8},{10,11... | collective-permute-start | bytes 1352 | tf_op jit(solution)/shard_map/ppermute | solution.py:81
  135.6 5.5 %collective-permute-start.31 = (f32[7,16]{1,0:T(8,128)S(1)}, f32[7,16]{1,0:T(8,128)S(1)}, u32[]{:S(2)}, u32[]{:S(2)}) collective-permute-start(f32[7,16]{1,0:T(8,128)S(1)} %stack.52), channel_id=1, source_target_pairs={{0,2},{1,3},{2,0},{3,1},{4,6},{5,7},{6,4},{7,5},{8,10},{9,11},{10,... | collective-permute-start | bytes 1352 | tf_op jit(solution)/shard_map/ppermute | solution.py:81
  141.2 7.6 %collective-permute-start.32 = (f32[7,16]{1,0:T(8,128)S(1)}, f32[7,16]{1,0:T(8,128)S(1)}, u32[]{:S(2)}, u32[]{:S(2)}) collective-permute-start(f32[7,16]{1,0:T(8,128)S(1)} %stack.53), channel_id=1, source_target_pairs={{0,4},{1,5},{2,6},{3,7},{4,0},{5,1},{6,2},{7,3},{8,12},{9,13},{10,... | collective-permute-start | bytes 1352 | tf_op jit(solution)/shard_map/ppermute | solution.py:81
  148.9 9.4 %collective-permute-start.33 = (f32[7,16]{1,0:T(8,128)S(1)}, f32[7,16]{1,0:T(8,128)S(1)}, u32[]{:S(2)}, u32[]{:S(2)}) collective-permute-start(f32[7,16]{1,0:T(8,128)S(1)} %stack.54), channel_id=1, source_target_pairs={{0,8},{1,9},{2,10},{3,11},{4,12},{5,13},{6,14},{7,15},{8,0},{9,1},... | collective-permute-start | bytes 1352 | tf_op jit(solution)/shard_map/ppermute | solution.py:81
  158.4 5.5 %collective-permute-start.34 = (f32[7,16]{1,0:T(8,128)S(1)}, f32[7,16]{1,0:T(8,128)S(1)}, u32[]{:S(2)}, u32[]{:S(2)}) collective-permute-start(f32[7,16]{1,0:T(8,128)S(1)} %stack.55), channel_id=1, source_target_pairs={{0,16},{16,0},{32,48},{48,32},{64,80},{80,64},{96,112},{112,96},{1... | collective-permute-start | bytes 1352 | tf_op jit(solution)/shard_map/ppermute | solution.py:81
  163.9 7.0 %collective-permute-start.35 = (f32[7,16]{1,0:T(8,128)S(1)}, f32[7,16]{1,0:T(8,128)S(1)}, u32[]{:S(2)}, u32[]{:S(2)}) collective-permute-start(f32[7,16]{1,0:T(8,128)S(1)} %stack.56), channel_id=1, source_target_pairs={{0,32},{16,48},{32,0},{48,16},{64,96},{80,112},{96,64},{112,80},{1... | collective-permute-start | bytes 1352 | tf_op jit(solution)/shard_map/ppermute | solution.py:81
  171.0 5.5 %collective-permute-start.36 = (f32[7,16]{1,0:T(8,128)S(1)}, f32[7,16]{1,0:T(8,128)S(1)}, u32[]{:S(2)}, u32[]{:S(2)}) collective-permute-start(f32[7,16]{1,0:T(8,128)S(1)} %stack.57), channel_id=1, source_target_pairs={{0,64},{16,80},{32,96},{48,112},{64,0},{80,16},{96,32},{112,48},{1... | collective-permute-start | bytes 1352 | tf_op jit(solution)/shard_map/ppermute | solution.py:81
  176.5 6.4 %collective-permute-start.37 = (f32[7,16]{1,0:T(8,128)S(1)}, f32[7,16]{1,0:T(8,128)S(1)}, u32[]{:S(2)}, u32[]{:S(2)}) collective-permute-start(f32[7,16]{1,0:T(8,128)S(1)} %stack.58), channel_id=1, source_target_pairs={{0,128},{16,144},{32,160},{48,176},{64,192},{80,208},{96,224},{112... | collective-permute-start | bytes 1352 | tf_op jit(solution)/shard_map/ppermute | solution.py:81
  183.0 9.4 %collective-permute-start.38 = (f32[7,16]{1,0:T(8,128)S(1)}, f32[7,16]{1,0:T(8,128)S(1)}, u32[]{:S(2)}, u32[]{:S(2)}) collective-permute-start(f32[7,16]{1,0:T(8,128)S(1)} %stack.59), channel_id=1, source_target_pairs={{0,256},{16,272},{32,288},{48,304},{64,320},{80,336},{96,352},{112... | collective-permute-start | bytes 1352 | tf_op jit(solution)/shard_map/ppermute | solution.py:81
  192.4 1.4 copy-start.4
  194.5 0.5 copy-start.10

commit v4 on v3

--- a/solution.py
+++ b/solution.py
@@ -10,6 +10,12 @@
     peers = lax.axis_size(axis)
     pairs = [(i, i + by) for i in range(peers) if 0 <= i + by < peers]
     return lax.ppermute(value, axis, pairs)
+
+
+def exchanged_together(moves):
+    values = lax.optimization_barrier(tuple(value for value, _, _ in moves))
+    received = tuple(passed_along(value, axis, by) for value, (_, axis, by) in zip(values, moves))
+    return lax.optimization_barrier(received)
 
 
 def all_sum(value):
@@ -146,9 +152,10 @@
     def jump_b(side_values):
         west_side = side_values[..., 2 * SIDE : 3 * SIDE]
         south_side = side_values[..., 3 * SIDE :]
-        east_edge = passed_along(west_side, "py", -1)
+        east_edge, north_edge = exchanged_together(
+            [(west_side, "py", -1), (south_side, "px", -1)]
+        )
         from_east = jnp.concatenate([west_side[:, 1:], east_edge], 1)
-        north_edge = passed_along(south_side, "px", -1)
         from_north = jnp.concatenate([south_side[1:], north_edge], 0)
         east_term = permute_side(from_east, east_flip)
         north_term = permute_side(from_north, north_flip)
@@ -185,9 +192,10 @@
         west_side = side_values[..., 2 * SIDE : 3 * SIDE]
         south_side = side_values[..., 3 * SIDE :]
         ones = jnp.broadcast_to(active, east_side.shape)
-        east_edge = passed_along(west_side, "py", -1)
+        east_edge, north_edge = exchanged_together(
+            [(west_side, "py", -1), (south_side, "px", -1)]
+        )
         from_east = jnp.concatenate([west_side[:, 1:], east_edge], 1)
-        north_edge = passed_along(south_side, "px", -1)
         from_north = jnp.concatenate([south_side[1:], north_edge], 0)
         east_perm_side = permute_side(east_side, east_flip)
         north_perm_side = permute_side(north_side, north_flip)

time: 196 us -> 192 us (0.980)
  waiting for transfers between devices: 89.4 us -> 82.3 us
  starting transfers between devices: 89.9 us -> 93.3 us
    ppermute x9, starting transfers between devices: 29.3 us -> 35.2 us  [all_sum_mixed(): other = lax.ppermute(packed, axis, [(i, i ^ step) for i in range(peers)])]
    ppermute x12, waiting for transfers between devices: 32.7 us -> 27 us  [passed_along(): return lax.ppermute(value, axis, pairs)]
    ppermute x12, starting transfers between devices: 27.4 us -> 22.1 us  [passed_along(): return lax.ppermute(value, axis, pairs)]
    ppermute x9, starting transfers between devices: 33.1 us -> 36 us  [all_sum(): lax.ppermute(value, axis, [(i, i ^ step) for i in range(peers)])]
where the time goes in v4:
time: 192 us; the launch traced here: 191 us
  starting transfers between devices  93.3 us (49%)
  waiting for transfers between devices  82.3 us (43%)
  local copies, waits for them, and re-layouts  5.14 us (3%)
  other arithmetic  4.88 us (3%)
  between operations  4.01 us (2%)
    ppermute x9, starting transfers between devices, all_sum(): lax.ppermute(value, axis, [(i, i ^ step) for i in range(peers)])  36 us
    ppermute x9, starting transfers between devices, all_sum_mixed(): other = lax.ppermute(packed, axis, [(i, i ^ step) for i in range(peers)])  35.2 us
    ppermute x9, waiting for transfers between devices, all_sum_mixed(): other = lax.ppermute(packed, axis, [(i, i ^ step) for i in range(peers)])  29.4 us
    ppermute x12, waiting for transfers between devices, passed_along(): return lax.ppermute(value, axis, pairs)  27 us
    ppermute x9, waiting for transfers between devices, all_sum(): lax.ppermute(value, axis, [(i, i ^ step) for i in range(peers)])  25.9 us
    ppermute x12, starting transfers between devices, passed_along(): return lax.ppermute(value, axis, pairs)  22.1 us
  transfers between devices with their start and end apart: 30, of which 27 were waited for; matrix products, arithmetic and copies ran while one was open for 0% of the time, Pallas kernels for 0%

profile of v4, /device:TPU:30, one launch (start us, length us, event | category | flops | bytes accessed | tf_op | source)
XLA Modules:
  0.0 190.6 jit_solution(2660928284909197951)
XLA Ops:
  4.3 4.6 %collective-permute-start.10 = (f32[2,1,1,16,68]{4,3,2,1,0:T(8,128)S(1)}, f32[2,1,1,16,68]{4,3,2,1,0:T(8,128)S(1)}, u32[]{:S(2)}, u32[]{:S(2)}) collective-permute-start(f32[2,1,1,16,68]{4,3,2,1,0:T(8,128)S(1)} %pad_maximum_fusion.1), channel_id=1, source_target_pairs={{0,16},{16,32},{32,48},{48,64},{64,80},{80,96},{96,112},{112,128},... | collective-permute-start | bytes 26120 | tf_op jit(solution)/shard_map/ppermute | solution.py:12
  8.9 1.5 collective-permute-start.9
  12.8 1.9 %collective-permute-start.12 = (f32[1,1,16,68]{3,2,1,0:T(8,128)S(1)}, f32[1,1,16,68]{3,2,1,0:T(8,128)S(1)}, u32[]{:S(2)}, u32[]{:S(2)}) collective-permute-start(f32[1,1,16,68]{3,2,1,0:T(8,128)S(1)} %get-tuple-element.19), channel_id=1, source_target_pairs={{16,0},{32,16},{48,32},{64,48},{80,64},{96,80},{112,96},{128,112},... | collective-permute-start | bytes 13064 | tf_op jit(solution)/shard_map/ppermute | solution.py:12
  15.1 1.9 %collective-permute-done.11 = f32[1,1,16,68]{3,2,1,0:T(8,128)S(1)} collective-permute-done((f32[1,1,16,68]{3,2,1,0:T(8,128)S(1)}, f32[1,1,16,68]{3,2,1,0:T(8,128)S(1)}, u32[]{:S(2)}, u32[]{:S(2)}) %collective-permute-start.11) | collective-permute-done | bytes 4384 | tf_op jit(solution)/shard_map/ppermute | solution.py:12
  17.0 4.6 %collective-permute-done.12 = f32[1,1,16,68]{3,2,1,0:T(8,128)S(1)} collective-permute-done((f32[1,1,16,68]{3,2,1,0:T(8,128)S(1)}, f32[1,1,16,68]{3,2,1,0:T(8,128)S(1)}, u32[]{:S(2)}, u32[]{:S(2)}) %collective-permute-start.12) | collective-permute-done | bytes 4384 | tf_op jit(solution)/shard_map/ppermute | solution.py:12
  22.3 4.4 %collective-permute-start.13 = (f32[16]{0:T(128)S(1)}, f32[16]{0:T(128)S(1)}, u32[]{:S(2)}, u32[]{:S(2)}) collective-permute-start(f32[16]{0:T(128)S(1)} %get-tuple-element.129), channel_id=1, source_target_pairs={{0,1},{1,0},{2,3},{3,2},{4,5},{5,4},{6,7},{7,6},{8,9},{9,8},{10,11... | collective-permute-start | bytes 200 | tf_op jit(solution)/shard_map/ppermute | solution.py:29
  27.4 5.5 %collective-permute-start.14 = (f32[16]{0:T(128)S(1)}, f32[16]{0:T(128)S(1)}, u32[]{:S(2)}, u32[]{:S(2)}) collective-permute-start(f32[16]{0:T(128)S(1)} %add.2414), channel_id=1, source_target_pairs={{0,2},{1,3},{2,0},{3,1},{4,6},{5,7},{6,4},{7,5},{8,10},{9,11},{10,... | collective-permute-start | bytes 200 | tf_op jit(solution)/shard_map/ppermute | solution.py:29
  33.0 1.5 collective-permute-done.14
  34.5 6.1 %collective-permute-start.15 = (f32[16]{0:T(128)S(1)}, f32[16]{0:T(128)S(1)}, u32[]{:S(2)}, u32[]{:S(2)}) collective-permute-start(f32[16]{0:T(128)S(1)} %add.2415), channel_id=1, source_target_pairs={{0,4},{1,5},{2,6},{3,7},{4,0},{5,1},{6,2},{7,3},{8,12},{9,13},{10,... | collective-permute-start | bytes 200 | tf_op jit(solution)/shard_map/ppermute | solution.py:29
  40.6 1.5 collective-permute-done.15
  42.1 10.5 %collective-permute-start.16 = (f32[16]{0:T(128)S(1)}, f32[16]{0:T(128)S(1)}, u32[]{:S(2)}, u32[]{:S(2)}) collective-permute-start(f32[16]{0:T(128)S(1)} %add.2416), channel_id=1, source_target_pairs={{0,8},{1,9},{2,10},{3,11},{4,12},{5,13},{6,14},{7,15},{8,0},{9,1},... | collective-permute-start | bytes 200 | tf_op jit(solution)/shard_map/ppermute | solution.py:29
  52.6 1.5 collective-permute-done.16
  54.1 1.9 %collective-permute-start.17 = (f32[16]{0:T(128)S(1)}, f32[16]{0:T(128)S(1)}, u32[]{:S(2)}, u32[]{:S(2)}) collective-permute-start(f32[16]{0:T(128)S(1)} %add.2417), channel_id=1, source_target_pairs={{0,16},{16,0},{32,48},{48,32},{64,80},{80,64},{96,112},{112,96},{1... | collective-permute-start | bytes 200 | tf_op jit(solution)/shard_map/ppermute | solution.py:29
  56.0 3.5 %collective-permute-done.17 = f32[16]{0:T(128)S(1)} collective-permute-done((f32[16]{0:T(128)S(1)}, f32[16]{0:T(128)S(1)}, u32[]{:S(2)}, u32[]{:S(2)}) %collective-permute-start.17) | collective-permute-done | bytes 96 | tf_op jit(solution)/shard_map/ppermute | solution.py:29
  59.5 1.9 %collective-permute-start.18 = (f32[16]{0:T(128)S(1)}, f32[16]{0:T(128)S(1)}, u32[]{:S(2)}, u32[]{:S(2)}) collective-permute-start(f32[16]{0:T(128)S(1)} %add.2418), channel_id=1, source_target_pairs={{0,32},{16,48},{32,0},{48,16},{64,96},{80,112},{96,64},{112,80},{1... | collective-permute-start | bytes 200 | tf_op jit(solution)/shard_map/ppermute | solution.py:29
  61.4 5.0 %collective-permute-done.18 = f32[16]{0:T(128)S(1)} collective-permute-done((f32[16]{0:T(128)S(1)}, f32[16]{0:T(128)S(1)}, u32[]{:S(2)}, u32[]{:S(2)}) %collective-permute-start.18) | collective-permute-done | bytes 96 | tf_op jit(solution)/shard_map/ppermute | solution.py:29
  66.4 1.9 %collective-permute-start.19 = (f32[16]{0:T(128)S(1)}, f32[16]{0:T(128)S(1)}, u32[]{:S(2)}, u32[]{:S(2)}) collective-permute-start(f32[16]{0:T(128)S(1)} %add.2419), channel_id=1, source_target_pairs={{0,64},{16,80},{32,96},{48,112},{64,0},{80,16},{96,32},{112,48},{1... | collective-permute-start | bytes 200 | tf_op jit(solution)/shard_map/ppermute | solution.py:29
  68.4 3.5 %collective-permute-done.19 = f32[16]{0:T(128)S(1)} collective-permute-done((f32[16]{0:T(128)S(1)}, f32[16]{0:T(128)S(1)}, u32[]{:S(2)}, u32[]{:S(2)}) %collective-permute-start.19) | collective-permute-done | bytes 96 | tf_op jit(solution)/shard_map/ppermute | solution.py:29
  71.9 1.9 %collective-permute-start.20 = (f32[16]{0:T(128)S(1)}, f32[16]{0:T(128)S(1)}, u32[]{:S(2)}, u32[]{:S(2)}) collective-permute-start(f32[16]{0:T(128)S(1)} %add.2420), channel_id=1, source_target_pairs={{0,128},{16,144},{32,160},{48,176},{64,192},{80,208},{96,224},{112... | collective-permute-start | bytes 200 | tf_op jit(solution)/shard_map/ppermute | solution.py:29
  73.8 1.9 %collective-permute-start.23 = (f32[2,1,1,16,68]{4,3,2,1,0:T(8,128)S(1)}, f32[2,1,1,16,68]{4,3,2,1,0:T(8,128)S(1)}, u32[]{:S(2)}, u32[]{:S(2)}) collective-permute-start(f32[2,1,1,16,68]{4,3,2,1,0:T(8,128)S(1)} %stack.49), channel_id=1, source_target_pairs={{0,16},{16,32},{32,48},{48,64},{64,80},{80,96},{96,112},{112,128},... | collective-permute-start | bytes 26120 | tf_op jit(solution)/shard_map/ppermute | solution.py:12
  75.7 2.5 %collective-permute-done.20 = f32[16]{0:T(128)S(1)} collective-permute-done((f32[16]{0:T(128)S(1)}, f32[16]{0:T(128)S(1)}, u32[]{:S(2)}, u32[]{:S(2)}) %collective-permute-start.20) | collective-permute-done | bytes 96 | tf_op jit(solution)/shard_map/ppermute | solution.py:29
  78.2 1.9 %collective-permute-start.21 = (f32[16]{0:T(128)S(1)}, f32[16]{0:T(128)S(1)}, u32[]{:S(2)}, u32[]{:S(2)}) collective-permute-start(f32[16]{0:T(128)S(1)} %add.2421), channel_id=1, source_target_pairs={{0,256},{16,272},{32,288},{48,304},{64,320},{80,336},{96,352},{112... | collective-permute-start | bytes 200 | tf_op jit(solution)/shard_map/ppermute | solution.py:29
  81.4 6.1 %collective-permute-done.21 = f32[16]{0:T(128)S(1)} collective-permute-done((f32[16]{0:T(128)S(1)}, f32[16]{0:T(128)S(1)}, u32[]{:S(2)}, u32[]{:S(2)}) %collective-permute-start.21) | collective-permute-done | bytes 96 | tf_op jit(solution)/shard_map/ppermute | solution.py:29
  90.8 1.9 %collective-permute-start.25 = (f32[1,2,128]{2,1,0:T(2,128)S(1)}, f32[1,2,128]{2,1,0:T(2,128)S(1)}, u32[]{:S(2)}, u32[]{:S(2)}) collective-permute-start(f32[1,2,128]{2,1,0:T(2,128)S(1)} %pad_maximum_fusion.4), channel_id=1, source_target_pairs={{0,16},{16,32},{32,48},{48,64},{64,80},{80,96},{96,112},{112,128},... | collective-permute-start | bytes 3080 | tf_op jit(solution)/shard_map/ppermute | solution.py:12
  92.7 3.5 %collective-permute-done.25 = f32[1,2,128]{2,1,0:T(2,128)S(1)} collective-permute-done((f32[1,2,128]{2,1,0:T(2,128)S(1)}, f32[1,2,128]{2,1,0:T(2,128)S(1)}, u32[]{:S(2)}, u32[]{:S(2)}) %collective-permute-start.25) | collective-permute-done | bytes 1056 | tf_op jit(solution)/shard_map/ppermute | solution.py:12
  98.5 1.7 collective-permute-done.26
  100.3 1.9 %collective-permute-start.27 = (f32[1,2,32]{2,1,0:T(2,128)S(1)}, f32[1,2,32]{2,1,0:T(2,128)S(1)}, u32[]{:S(2)}, u32[]{:S(2)}) collective-permute-start(f32[1,2,32]{2,1,0:T(2,128)S(1)} %pad_maximum_fusion.5), channel_id=1, source_target_pairs={{16,0},{32,16},{48,32},{64,48},{80,64},{96,80},{112,96},{128,112},... | collective-permute-start | bytes 776 | tf_op jit(solution)/shard_map/ppermute | solution.py:12
  102.4 6.6 %collective-permute-done.27 = f32[1,2,32]{2,1,0:T(2,128)S(1)} collective-permute-done((f32[1,2,32]{2,1,0:T(2,128)S(1)}, f32[1,2,32]{2,1,0:T(2,128)S(1)}, u32[]{:S(2)}, u32[]{:S(2)}) %collective-permute-start.27) | collective-permute-done | bytes 288 | tf_op jit(solution)/shard_map/ppermute | solution.py:12
  110.8 1.9 %collective-permute-start.29 = (f32[1,1,16,68]{3,2,1,0:T(8,128)S(1)}, f32[1,1,16,68]{3,2,1,0:T(8,128)S(1)}, u32[]{:S(2)}, u32[]{:S(2)}) collective-permute-start(f32[1,1,16,68]{3,2,1,0:T(8,128)S(1)} %get-tuple-element.23), channel_id=1, source_target_pairs={{16,0},{32,16},{48,32},{64,48},{80,64},{96,80},{112,96},{128,112},... | collective-permute-start | bytes 13064 | tf_op jit(solution)/shard_map/ppermute | solution.py:12
  112.7 1.4 collective-permute-done.28
  114.1 5.5 %collective-permute-done.29 = f32[1,1,16,68]{3,2,1,0:T(8,128)S(1)} collective-permute-done((f32[1,1,16,68]{3,2,1,0:T(8,128)S(1)}, f32[1,1,16,68]{3,2,1,0:T(8,128)S(1)}, u32[]{:S(2)}, u32[]{:S(2)}) %collective-permute-start.29) | collective-permute-done | bytes 4384 | tf_op jit(solution)/shard_map/ppermute | solution.py:12
  122.8 3.5 %collective-permute-start.30 = (f32[7,16]{1,0:T(8,128)S(1)}, f32[7,16]{1,0:T(8,128)S(1)}, u32[]{:S(2)}, u32[]{:S(2)}) collective-permute-start(f32[7,16]{1,0:T(8,128)S(1)} %stack.51), channel_id=1, source_target_pairs={{0,1},{1,0},{2,3},{3,2},{4,5},{5,4},{6,7},{7,6},{8,9},{9,8},{10,11... | collective-permute-start | bytes 1352 | tf_op jit(solution)/shard_map/ppermute | solution.py:87
  127.2 5.0 %collective-permute-start.31 = (f32[7,16]{1,0:T(8,128)S(1)}, f32[7,16]{1,0:T(8,128)S(1)}, u32[]{:S(2)}, u32[]{:S(2)}) collective-permute-start(f32[7,16]{1,0:T(8,128)S(1)} %stack.52), channel_id=1, source_target_pairs={{0,2},{1,3},{2,0},{3,1},{4,6},{5,7},{6,4},{7,5},{8,10},{9,11},{10,... | collective-permute-start | bytes 1352 | tf_op jit(solution)/shard_map/ppermute | solution.py:87
  132.2 1.6 collective-permute-done.31
  133.8 6.8 %collective-permute-start.32 = (f32[7,16]{1,0:T(8,128)S(1)}, f32[7,16]{1,0:T(8,128)S(1)}, u32[]{:S(2)}, u32[]{:S(2)}) collective-permute-start(f32[7,16]{1,0:T(8,128)S(1)} %stack.53), channel_id=1, source_target_pairs={{0,4},{1,5},{2,6},{3,7},{4,0},{5,1},{6,2},{7,3},{8,12},{9,13},{10,... | collective-permute-start | bytes 1352 | tf_op jit(solution)/shard_map/ppermute | solution.py:87
  140.6 1.6 collective-permute-done.32
  142.2 10.0 %collective-permute-start.33 = (f32[7,16]{1,0:T(8,128)S(1)}, f32[7,16]{1,0:T(8,128)S(1)}, u32[]{:S(2)}, u32[]{:S(2)}) collective-permute-start(f32[7,16]{1,0:T(8,128)S(1)} %stack.54), channel_id=1, source_target_pairs={{0,8},{1,9},{2,10},{3,11},{4,12},{5,13},{6,14},{7,15},{8,0},{9,1},... | collective-permute-start | bytes 1352 | tf_op jit(solution)/shard_map/ppermute | solution.py:87
  152.3 1.6 collective-permute-done.33
  153.9 1.9 %collective-permute-start.34 = (f32[7,16]{1,0:T(8,128)S(1)}, f32[7,16]{1,0:T(8,128)S(1)}, u32[]{:S(2)}, u32[]{:S(2)}) collective-permute-start(f32[7,16]{1,0:T(8,128)S(1)} %stack.55), channel_id=1, source_target_pairs={{0,16},{16,0},{32,48},{48,32},{64,80},{80,64},{96,112},{112,96},{1... | collective-permute-start | bytes 1352 | tf_op jit(solution)/shard_map/ppermute | solution.py:87
  155.8 3.6 %collective-permute-done.34 = f32[7,16]{1,0:T(8,128)S(1)} collective-permute-done((f32[7,16]{1,0:T(8,128)S(1)}, f32[7,16]{1,0:T(8,128)S(1)}, u32[]{:S(2)}, u32[]{:S(2)}) %collective-permute-start.34) | collective-permute-done | bytes 480 | tf_op jit(solution)/shard_map/ppermute | solution.py:87
  159.5 1.9 %collective-permute-start.35 = (f32[7,16]{1,0:T(8,128)S(1)}, f32[7,16]{1,0:T(8,128)S(1)}, u32[]{:S(2)}, u32[]{:S(2)}) collective-permute-start(f32[7,16]{1,0:T(8,128)S(1)} %stack.56), channel_id=1, source_target_pairs={{0,32},{16,48},{32,0},{48,16},{64,96},{80,112},{96,64},{112,80},{1... | collective-permute-start | bytes 1352 | tf_op jit(solution)/shard_map/ppermute | solution.py:87
  161.4 5.1 %collective-permute-done.35 = f32[7,16]{1,0:T(8,128)S(1)} collective-permute-done((f32[7,16]{1,0:T(8,128)S(1)}, f32[7,16]{1,0:T(8,128)S(1)}, u32[]{:S(2)}, u32[]{:S(2)}) %collective-permute-start.35) | collective-permute-done | bytes 480 | tf_op jit(solution)/shard_map/ppermute | solution.py:87
  166.5 1.9 %collective-permute-start.36 = (f32[7,16]{1,0:T(8,128)S(1)}, f32[7,16]{1,0:T(8,128)S(1)}, u32[]{:S(2)}, u32[]{:S(2)}) collective-permute-start(f32[7,16]{1,0:T(8,128)S(1)} %stack.57), channel_id=1, source_target_pairs={{0,64},{16,80},{32,96},{48,112},{64,0},{80,16},{96,32},{112,48},{1... | collective-permute-start | bytes 1352 | tf_op jit(solution)/shard_map/ppermute | solution.py:87
  168.5 3.6 %collective-permute-done.36 = f32[7,16]{1,0:T(8,128)S(1)} collective-permute-done((f32[7,16]{1,0:T(8,128)S(1)}, f32[7,16]{1,0:T(8,128)S(1)}, u32[]{:S(2)}, u32[]{:S(2)}) %collective-permute-start.36) | collective-permute-done | bytes 480 | tf_op jit(solution)/shard_map/ppermute | solution.py:87
  172.1 1.9 %collective-permute-start.37 = (f32[7,16]{1,0:T(8,128)S(1)}, f32[7,16]{1,0:T(8,128)S(1)}, u32[]{:S(2)}, u32[]{:S(2)}) collective-permute-start(f32[7,16]{1,0:T(8,128)S(1)} %stack.58), channel_id=1, source_target_pairs={{0,128},{16,144},{32,160},{48,176},{64,192},{80,208},{96,224},{112... | collective-permute-start | bytes 1352 | tf_op jit(solution)/shard_map/ppermute | solution.py:87
  174.0 4.5 %collective-permute-done.37 = f32[7,16]{1,0:T(8,128)S(1)} collective-permute-done((f32[7,16]{1,0:T(8,128)S(1)}, f32[7,16]{1,0:T(8,128)S(1)}, u32[]{:S(2)}, u32[]{:S(2)}) %collective-permute-start.37) | collective-permute-done | bytes 480 | tf_op jit(solution)/shard_map/ppermute | solution.py:87
  178.6 2.2 %collective-permute-start.38 = (f32[7,16]{1,0:T(8,128)S(1)}, f32[7,16]{1,0:T(8,128)S(1)}, u32[]{:S(2)}, u32[]{:S(2)}) collective-permute-start(f32[7,16]{1,0:T(8,128)S(1)} %stack.59), channel_id=1, source_target_pairs={{0,256},{16,272},{32,288},{48,304},{64,320},{80,336},{96,352},{112... | collective-permute-start | bytes 1352 | tf_op jit(solution)/shard_map/ppermute | solution.py:87
  180.8 7.2 %collective-permute-done.38 = f32[7,16]{1,0:T(8,128)S(1)} collective-permute-done((f32[7,16]{1,0:T(8,128)S(1)}, f32[7,16]{1,0:T(8,128)S(1)}, u32[]{:S(2)}, u32[]{:S(2)}) %collective-permute-start.38) | collective-permute-done | bytes 480 | tf_op jit(solution)/shard_map/ppermute | solution.py:87
  (163 shorter events, 20.7 us)
Async XLA Ops:
  0.6 10.5 %copy-start = (bf16[1,1,272,272]{3,2,1,0:T(8,128)(2,1)S(1)}, bf16[1,1,272,272]{3,2,1,0:T(8,128)(2,1)}, u32[]{:S(2)}) copy-start(bf16[1,1,272,272]{3,2,1,0:T(8,128)(2,1)} %param.17) | copy-start | bytes 443908
  0.7 0.7 copy-start.9
  0.7 2.6 %copy-start.1 = (f32[1,1,16,136]{3,2,1,0:T(8,128)S(1)}, f32[1,1,16,136]{3,2,1,0:T(8,128)}, u32[]{:S(2)}) copy-start(f32[1,1,16,136]{3,2,1,0:T(8,128)} %param.13) | copy-start | bytes 26116
  0.7 2.6 %copy-start.5 = (f32[1,1,16,136]{3,2,1,0:T(8,128)S(1)}, f32[1,1,16,136]{3,2,1,0:T(8,128)}, u32[]{:S(2)}) copy-start(f32[1,1,16,136]{3,2,1,0:T(8,128)} %param.14) | copy-start | bytes 26116
  4.3 6.1 %collective-permute-start.10 = (f32[2,1,1,16,68]{4,3,2,1,0:T(8,128)S(1)}, f32[2,1,1,16,68]{4,3,2,1,0:T(8,128)S(1)}, u32[]{:S(2)}, u32[]{:S(2)}) collective-permute-start(f32[2,1,1,16,68]{4,3,2,1,0:T(8,128)S(1)} %pad_maximum_fusion.1), channel_id=1, source_target_pairs={{0,16},{16,32},{32,48},{48,64},{64,80},{80,96},{96,112},{112,128},... | collective-permute-start | bytes 26120 | tf_op jit(solution)/shard_map/ppermute | solution.py:12
  8.9 2.3 %collective-permute-start.9 = (f32[2,1,1,16,68]{4,3,2,1,0:T(8,128)S(1)}, f32[2,1,1,16,68]{4,3,2,1,0:T(8,128)S(1)}, u32[]{:S(2)}, u32[]{:S(2)}) collective-permute-start(f32[2,1,1,16,68]{4,3,2,1,0:T(8,128)S(1)} %pad_maximum_fusion), channel_id=1, source_target_pairs={{0,1},{1,2},{2,3},{3,4},{4,5},{5,6},{6,7},{7,8},{8,9},{9,10},{10,1... | collective-permute-start | bytes 26120 | tf_op jit(solution)/shard_map/ppermute | solution.py:12
  11.5 5.5 %collective-permute-start.11 = (f32[1,1,16,68]{3,2,1,0:T(8,128)S(1)}, f32[1,1,16,68]{3,2,1,0:T(8,128)S(1)}, u32[]{:S(2)}, u32[]{:S(2)}) collective-permute-start(f32[1,1,16,68]{3,2,1,0:T(8,128)S(1)} %get-tuple-element.18), channel_id=1, source_target_pairs={{1,0},{2,1},{3,2},{4,3},{5,4},{6,5},{7,6},{8,7},{9,8},{10,9},{11,1... | collective-permute-start | bytes 13064 | tf_op jit(solution)/shard_map/ppermute | solution.py:12
  12.8 8.9 %collective-permute-start.12 = (f32[1,1,16,68]{3,2,1,0:T(8,128)S(1)}, f32[1,1,16,68]{3,2,1,0:T(8,128)S(1)}, u32[]{:S(2)}, u32[]{:S(2)}) collective-permute-start(f32[1,1,16,68]{3,2,1,0:T(8,128)S(1)} %get-tuple-element.19), channel_id=1, source_target_pairs={{16,0},{32,16},{48,32},{64,48},{80,64},{96,80},{112,96},{128,112},... | collective-permute-start | bytes 13064 | tf_op jit(solution)/shard_map/ppermute | solution.py:12
  22.0 65.5 %copy-start.11 = (f32[16]{0:T(128)S(1)}, f32[16]{0:T(128)}, u32[]{:S(2)}) copy-start(f32[16]{0:T(128)} %param.15) | copy-start | bytes 196
  22.1 80.1 %copy-start.2 = (bf16[1,1,272,272]{3,2,1,0:T(8,128)(2,1)S(1)}, bf16[1,1,272,272]{3,2,1,0:T(8,128)(2,1)}, u32[]{:S(2)}) copy-start(bf16[1,1,272,272]{3,2,1,0:T(8,128)(2,1)} %param.16) | copy-start | bytes 443908
  22.3 5.2 %collective-permute-start.13 = (f32[16]{0:T(128)S(1)}, f32[16]{0:T(128)S(1)}, u32[]{:S(2)}, u32[]{:S(2)}) collective-permute-start(f32[16]{0:T(128)S(1)} %get-tuple-element.129), channel_id=1, source_target_pairs={{0,1},{1,0},{2,3},{3,2},{4,5},{5,4},{6,7},{7,6},{8,9},{9,8},{10,11... | collective-permute-start | bytes 200 | tf_op jit(solution)/shard_map/ppermute | solution.py:29
  27.4 7.0 %collective-permute-start.14 = (f32[16]{0:T(128)S(1)}, f32[16]{0:T(128)S(1)}, u32[]{:S(2)}, u32[]{:S(2)}) collective-permute-start(f32[16]{0:T(128)S(1)} %add.2414), channel_id=1, source_target_pairs={{0,2},{1,3},{2,0},{3,1},{4,6},{5,7},{6,4},{7,5},{8,10},{9,11},{10,... | collective-permute-start | bytes 200 | tf_op jit(solution)/shard_map/ppermute | solution.py:29
  34.5 7.6 %collective-permute-start.15 = (f32[16]{0:T(128)S(1)}, f32[16]{0:T(128)S(1)}, u32[]{:S(2)}, u32[]{:S(2)}) collective-permute-start(f32[16]{0:T(128)S(1)} %add.2415), channel_id=1, source_target_pairs={{0,4},{1,5},{2,6},{3,7},{4,0},{5,1},{6,2},{7,3},{8,12},{9,13},{10,... | collective-permute-start | bytes 200 | tf_op jit(solution)/shard_map/ppermute | solution.py:29
  42.1 12.0 %collective-permute-start.16 = (f32[16]{0:T(128)S(1)}, f32[16]{0:T(128)S(1)}, u32[]{:S(2)}, u32[]{:S(2)}) collective-permute-start(f32[16]{0:T(128)S(1)} %add.2416), channel_id=1, source_target_pairs={{0,8},{1,9},{2,10},{3,11},{4,12},{5,13},{6,14},{7,15},{8,0},{9,1},... | collective-permute-start | bytes 200 | tf_op jit(solution)/shard_map/ppermute | solution.py:29
  54.1 5.4 %collective-permute-start.17 = (f32[16]{0:T(128)S(1)}, f32[16]{0:T(128)S(1)}, u32[]{:S(2)}, u32[]{:S(2)}) collective-permute-start(f32[16]{0:T(128)S(1)} %add.2417), channel_id=1, source_target_pairs={{0,16},{16,0},{32,48},{48,32},{64,80},{80,64},{96,112},{112,96},{1... | collective-permute-start | bytes 200 | tf_op jit(solution)/shard_map/ppermute | solution.py:29
  59.5 6.9 %collective-permute-start.18 = (f32[16]{0:T(128)S(1)}, f32[16]{0:T(128)S(1)}, u32[]{:S(2)}, u32[]{:S(2)}) collective-permute-start(f32[16]{0:T(128)S(1)} %add.2418), channel_id=1, source_target_pairs={{0,32},{16,48},{32,0},{48,16},{64,96},{80,112},{96,64},{112,80},{1... | collective-permute-start | bytes 200 | tf_op jit(solution)/shard_map/ppermute | solution.py:29
  66.4 5.4 %collective-permute-start.19 = (f32[16]{0:T(128)S(1)}, f32[16]{0:T(128)S(1)}, u32[]{:S(2)}, u32[]{:S(2)}) collective-permute-start(f32[16]{0:T(128)S(1)} %add.2419), channel_id=1, source_target_pairs={{0,64},{16,80},{32,96},{48,112},{64,0},{80,16},{96,32},{112,48},{1... | collective-permute-start | bytes 200 | tf_op jit(solution)/shard_map/ppermute | solution.py:29
  71.9 6.3 %collective-permute-start.20 = (f32[16]{0:T(128)S(1)}, f32[16]{0:T(128)S(1)}, u32[]{:S(2)}, u32[]{:S(2)}) collective-permute-start(f32[16]{0:T(128)S(1)} %add.2420), channel_id=1, source_target_pairs={{0,128},{16,144},{32,160},{48,176},{64,192},{80,208},{96,224},{112... | collective-permute-start | bytes 200 | tf_op jit(solution)/shard_map/ppermute | solution.py:29
  73.8 13.8 %collective-permute-start.23 = (f32[2,1,1,16,68]{4,3,2,1,0:T(8,128)S(1)}, f32[2,1,1,16,68]{4,3,2,1,0:T(8,128)S(1)}, u32[]{:S(2)}, u32[]{:S(2)}) collective-permute-start(f32[2,1,1,16,68]{4,3,2,1,0:T(8,128)S(1)} %stack.49), channel_id=1, source_target_pairs={{0,16},{16,32},{32,48},{48,64},{64,80},{80,96},{96,112},{112,128},... | collective-permute-start | bytes 26120 | tf_op jit(solution)/shard_map/ppermute | solution.py:12
  78.2 9.3 %collective-permute-start.21 = (f32[16]{0:T(128)S(1)}, f32[16]{0:T(128)S(1)}, u32[]{:S(2)}, u32[]{:S(2)}) collective-permute-start(f32[16]{0:T(128)S(1)} %add.2421), channel_id=1, source_target_pairs={{0,256},{16,272},{32,288},{48,304},{64,320},{80,336},{96,352},{112... | collective-permute-start | bytes 200 | tf_op jit(solution)/shard_map/ppermute | solution.py:29
  80.1 7.4 %collective-permute-start.22 = (f32[2,1,1,16,68]{4,3,2,1,0:T(8,128)S(1)}, f32[2,1,1,16,68]{4,3,2,1,0:T(8,128)S(1)}, u32[]{:S(2)}, u32[]{:S(2)}) collective-permute-start(f32[2,1,1,16,68]{4,3,2,1,0:T(8,128)S(1)} %stack.47), channel_id=1, source_target_pairs={{0,1},{1,2},{2,3},{3,4},{4,5},{5,6},{6,7},{7,8},{8,9},{9,10},{10,1... | collective-permute-start | bytes 26120 | tf_op jit(solution)/shard_map/ppermute | solution.py:12
  87.5 100.5 %copy-start.7 = (f32[16]{0:T(128)}, f32[16]{0:T(128)S(1)}, u32[]{:S(2)}) copy-start(f32[16]{0:T(128)S(1)} %get-tuple-element.128) | copy-start | bytes 196
  87.6 0.7 copy-start.6
  88.7 2.1 %collective-permute-start.24 = (f32[1,1,128]{2,1,0:T(1,128)S(1)}, f32[1,1,128]{2,1,0:T(1,128)S(1)}, u32[]{:S(2)}, u32[]{:S(2)}) collective-permute-start(f32[1,1,128]{2,1,0:T(1,128)S(1)} %reshape.602), channel_id=1, source_target_pairs={{0,1},{1,2},{2,3},{3,4},{4,5},{5,6},{6,7},{7,8},{8,9},{9,10},{10,1... | collective-permute-start | bytes 1544 | tf_op jit(solution)/shard_map/ppermute | solution.py:12
  90.8 5.5 %collective-permute-start.25 = (f32[1,2,128]{2,1,0:T(2,128)S(1)}, f32[1,2,128]{2,1,0:T(2,128)S(1)}, u32[]{:S(2)}, u32[]{:S(2)}) collective-permute-start(f32[1,2,128]{2,1,0:T(2,128)S(1)} %pad_maximum_fusion.4), channel_id=1, source_target_pairs={{0,16},{16,32},{32,48},{48,64},{64,80},{80,96},{96,112},{112,128},... | collective-permute-start | bytes 3080 | tf_op jit(solution)/shard_map/ppermute | solution.py:12
  96.3 0.7 copy-start.8
  97.2 3.0 %collective-permute-start.26 = (f32[1,1,32]{2,1,0:T(1,128)S(1)}, f32[1,1,32]{2,1,0:T(1,128)S(1)}, u32[]{:S(2)}, u32[]{:S(2)}) collective-permute-start(f32[1,1,32]{2,1,0:T(1,128)S(1)} %reshape.606), channel_id=1, source_target_pairs={{1,0},{2,1},{3,2},{4,3},{5,4},{6,5},{7,6},{8,7},{9,8},{10,9},{11,1... | collective-permute-start | bytes 392 | tf_op jit(solution)/shard_map/ppermute | solution.py:12
  100.3 8.8 %collective-permute-start.27 = (f32[1,2,32]{2,1,0:T(2,128)S(1)}, f32[1,2,32]{2,1,0:T(2,128)S(1)}, u32[]{:S(2)}, u32[]{:S(2)}) collective-permute-start(f32[1,2,32]{2,1,0:T(2,128)S(1)} %pad_maximum_fusion.5), channel_id=1, source_target_pairs={{16,0},{32,16},{48,32},{64,48},{80,64},{96,80},{112,96},{128,112},... | collective-permute-start | bytes 776 | tf_op jit(solution)/shard_map/ppermute | solution.py:12
  109.5 4.7 %collective-permute-start.28 = (f32[1,1,16,68]{3,2,1,0:T(8,128)S(1)}, f32[1,1,16,68]{3,2,1,0:T(8,128)S(1)}, u32[]{:S(2)}, u32[]{:S(2)}) collective-permute-start(f32[1,1,16,68]{3,2,1,0:T(8,128)S(1)} %get-tuple-element.22), channel_id=1, source_target_pairs={{1,0},{2,1},{3,2},{4,3},{5,4},{6,5},{7,6},{8,7},{9,8},{10,9},{11,1... | collective-permute-start | bytes 13064 | tf_op jit(solution)/shard_map/ppermute | solution.py:12
  110.8 8.9 %collective-permute-start.29 = (f32[1,1,16,68]{3,2,1,0:T(8,128)S(1)}, f32[1,1,16,68]{3,2,1,0:T(8,128)S(1)}, u32[]{:S(2)}, u32[]{:S(2)}) collective-permute-start(f32[1,1,16,68]{3,2,1,0:T(8,128)S(1)} %get-tuple-element.23), channel_id=1, source_target_pairs={{16,0},{32,16},{48,32},{64,48},{80,64},{96,80},{112,96},{128,112},... | collective-permute-start | bytes 13064 | tf_op jit(solution)/shard_map/ppermute | solution.py:12
  120.3 69.1 %copy-start.3 = (f32[1,1,16,136]{3,2,1,0:T(8,128)}, f32[1,1,16,136]{3,2,1,0:T(8,128)S(1)}, u32[]{:S(2)}) copy-start(f32[1,1,16,136]{3,2,1,0:T(8,128)S(1)} %get-tuple-element.126) | copy-start | bytes 26116
  122.8 4.3 %collective-permute-start.30 = (f32[7,16]{1,0:T(8,128)S(1)}, f32[7,16]{1,0:T(8,128)S(1)}, u32[]{:S(2)}, u32[]{:S(2)}) collective-permute-start(f32[7,16]{1,0:T(8,128)S(1)} %stack.51), channel_id=1, source_target_pairs={{0,1},{1,0},{2,3},{3,2},{4,5},{5,4},{6,7},{7,6},{8,9},{9,8},{10,11... | collective-permute-start | bytes 1352 | tf_op jit(solution)/shard_map/ppermute | solution.py:87
  127.2 6.6 %collective-permute-start.31 = (f32[7,16]{1,0:T(8,128)S(1)}, f32[7,16]{1,0:T(8,128)S(1)}, u32[]{:S(2)}, u32[]{:S(2)}) collective-permute-start(f32[7,16]{1,0:T(8,128)S(1)} %stack.52), channel_id=1, source_target_pairs={{0,2},{1,3},{2,0},{3,1},{4,6},{5,7},{6,4},{7,5},{8,10},{9,11},{10,... | collective-permute-start | bytes 1352 | tf_op jit(solution)/shard_map/ppermute | solution.py:87
  133.8 8.4 %collective-permute-start.32 = (f32[7,16]{1,0:T(8,128)S(1)}, f32[7,16]{1,0:T(8,128)S(1)}, u32[]{:S(2)}, u32[]{:S(2)}) collective-permute-start(f32[7,16]{1,0:T(8,128)S(1)} %stack.53), channel_id=1, source_target_pairs={{0,4},{1,5},{2,6},{3,7},{4,0},{5,1},{6,2},{7,3},{8,12},{9,13},{10,... | collective-permute-start | bytes 1352 | tf_op jit(solution)/shard_map/ppermute | solution.py:87
  142.2 11.6 %collective-permute-start.33 = (f32[7,16]{1,0:T(8,128)S(1)}, f32[7,16]{1,0:T(8,128)S(1)}, u32[]{:S(2)}, u32[]{:S(2)}) collective-permute-start(f32[7,16]{1,0:T(8,128)S(1)} %stack.54), channel_id=1, source_target_pairs={{0,8},{1,9},{2,10},{3,11},{4,12},{5,13},{6,14},{7,15},{8,0},{9,1},... | collective-permute-start | bytes 1352 | tf_op jit(solution)/shard_map/ppermute | solution.py:87
  153.9 5.5 %collective-permute-start.34 = (f32[7,16]{1,0:T(8,128)S(1)}, f32[7,16]{1,0:T(8,128)S(1)}, u32[]{:S(2)}, u32[]{:S(2)}) collective-permute-start(f32[7,16]{1,0:T(8,128)S(1)} %stack.55), channel_id=1, source_target_pairs={{0,16},{16,0},{32,48},{48,32},{64,80},{80,64},{96,112},{112,96},{1... | collective-permute-start | bytes 1352 | tf_op jit(solution)/shard_map/ppermute | solution.py:87
  159.5 7.0 %collective-permute-start.35 = (f32[7,16]{1,0:T(8,128)S(1)}, f32[7,16]{1,0:T(8,128)S(1)}, u32[]{:S(2)}, u32[]{:S(2)}) collective-permute-start(f32[7,16]{1,0:T(8,128)S(1)} %stack.56), channel_id=1, source_target_pairs={{0,32},{16,48},{32,0},{48,16},{64,96},{80,112},{96,64},{112,80},{1... | collective-permute-start | bytes 1352 | tf_op jit(solution)/shard_map/ppermute | solution.py:87
  166.5 5.5 %collective-permute-start.36 = (f32[7,16]{1,0:T(8,128)S(1)}, f32[7,16]{1,0:T(8,128)S(1)}, u32[]{:S(2)}, u32[]{:S(2)}) collective-permute-start(f32[7,16]{1,0:T(8,128)S(1)} %stack.57), channel_id=1, source_target_pairs={{0,64},{16,80},{32,96},{48,112},{64,0},{80,16},{96,32},{112,48},{1... | collective-permute-start | bytes 1352 | tf_op jit(solution)/shard_map/ppermute | solution.py:87
  172.1 6.4 %collective-permute-start.37 = (f32[7,16]{1,0:T(8,128)S(1)}, f32[7,16]{1,0:T(8,128)S(1)}, u32[]{:S(2)}, u32[]{:S(2)}) collective-permute-start(f32[7,16]{1,0:T(8,128)S(1)} %stack.58), channel_id=1, source_target_pairs={{0,128},{16,144},{32,160},{48,176},{64,192},{80,208},{96,224},{112... | collective-permute-start | bytes 1352 | tf_op jit(solution)/shard_map/ppermute | solution.py:87
  178.6 9.4 %collective-permute-start.38 = (f32[7,16]{1,0:T(8,128)S(1)}, f32[7,16]{1,0:T(8,128)S(1)}, u32[]{:S(2)}, u32[]{:S(2)}) collective-permute-start(f32[7,16]{1,0:T(8,128)S(1)} %stack.59), channel_id=1, source_target_pairs={{0,256},{16,272},{32,288},{48,304},{64,320},{80,336},{96,352},{112... | collective-permute-start | bytes 1352 | tf_op jit(solution)/shard_map/ppermute | solution.py:87
  188.0 1.4 copy-start.4
  190.1 0.5 copy-start.10

commit v5 on v4

--- a/solution.py
+++ b/solution.py
@@ -16,6 +16,31 @@
     values = lax.optimization_barrier(tuple(value for value, _, _ in moves))
     received = tuple(passed_along(value, axis, by) for value, (_, axis, by) in zip(values, moves))
     return lax.optimization_barrier(received)
+
+
+INNER = {"py": 2, "px": 4}
+
+
+def butterfly_rounds(axis):
+    peers = lax.axis_size(axis)
+    inner = INNER.get(axis, peers)
+    if peers % inner or inner & (inner - 1) or (peers // inner) & (peers // inner - 1):
+        inner = peers
+    rounds = []
+    step = 1
+    while step < inner:
+        rounds.append([(i, i ^ step) for i in range(peers)])
+        step *= 2
+    outer = peers // inner
+    gray = [k ^ (k >> 1) for k in range(outer)]
+    place = {g: k for k, g in enumerate(gray)}
+    step = 1
+    while step < outer:
+        rounds.append(
+            [(i, place[gray[i // inner] ^ step] * inner + i % inner) for i in range(peers)]
+        )
+        step *= 2
+    return rounds
 
 
 def all_sum(value):
@@ -24,10 +49,8 @@
         if peers & (peers - 1):
             value = lax.psum(value, axis)
             continue
-        step = 1
-        while step < peers:
-            value = value + lax.ppermute(value, axis, [(i, i ^ step) for i in range(peers)])
-            step *= 2
+        for pairs in butterfly_rounds(axis):
+            value = value + lax.ppermute(value, axis, pairs)
     return value
 
 
@@ -80,16 +103,13 @@
 
 def all_sum_mixed(plain, pairs):
     for axis in ("py", "px"):
-        peers = lax.axis_size(axis)
-        step = 1
-        while step < peers:
+        for partners in butterfly_rounds(axis):
             packed = jnp.stack([plain] + [part for pair in pairs for part in pair])
-            other = lax.ppermute(packed, axis, [(i, i ^ step) for i in range(peers)])
+            other = lax.ppermute(packed, axis, partners)
             plain = plain + other[0]
             pairs = [
                 df_add(pair, (other[1 + 2 * k], other[2 + 2 * k])) for k, pair in enumerate(pairs)
             ]
-            step *= 2
     return plain, pairs
 
 

time: 192 us -> 185 us (0.964)
  waiting for transfers between devices: 82.3 us -> 78.1 us
    ppermute x18, waiting for transfers between devices: 55.3 us -> 51.3 us  [the longest x9 27.2 us: all_sum_mixed(): other = lax.ppermute(packed, axis, partners)]
    ppermute x18, starting transfers between devices: 71.2 us -> 69.1 us  [the longest x9 35.7 us: all_sum(): value = value + lax.ppermute(value, axis, pairs)]
where the time goes in v5:
time: 185 us; the launch traced here: 184 us
  starting transfers between devices  91.4 us (49%)
  waiting for transfers between devices  78.1 us (42%)
  local copies, waits for them, and re-layouts  5.14 us (3%)
  other arithmetic  4.88 us (3%)
  between operations  4.01 us (2%)
    ppermute x9, starting transfers between devices, all_sum(): value = value + lax.ppermute(value, axis, pairs)  35.7 us
    ppermute x9, starting transfers between devices, all_sum_mixed(): other = lax.ppermute(packed, axis, partners)  33.4 us
    ppermute x9, waiting for transfers between devices, all_sum_mixed(): other = lax.ppermute(packed, axis, partners)  27.2 us
    ppermute x12, waiting for transfers between devices, passed_along(): return lax.ppermute(value, axis, pairs)  26.8 us
    ppermute x9, waiting for transfers between devices, all_sum(): value = value + lax.ppermute(value, axis, pairs)  24.1 us
    ppermute x12, starting transfers between devices, passed_along(): return lax.ppermute(value, axis, pairs)  22.3 us
  transfers between devices with their start and end apart: 30, of which 27 were waited for; matrix products, arithmetic and copies ran while one was open for 0% of the time, Pallas kernels for 0%

profile of v5, /device:TPU:30, one launch (start us, length us, event | category | flops | bytes accessed | tf_op | source)
XLA Modules:
  0.0 184.5 jit_solution(16329346807789270570)
XLA Ops:
  4.3 4.6 %collective-permute-start.10 = (f32[2,1,1,16,68]{4,3,2,1,0:T(8,128)S(1)}, f32[2,1,1,16,68]{4,3,2,1,0:T(8,128)S(1)}, u32[]{:S(2)}, u32[]{:S(2)}) collective-permute-start(f32[2,1,1,16,68]{4,3,2,1,0:T(8,128)S(1)} %pad_maximum_fusion.1), channel_id=1, source_target_pairs={{0,16},{16,32},{32,48},{48,64},{64,80},{80,96},{96,112},{112,128},... | collective-permute-start | bytes 26120 | tf_op jit(solution)/shard_map/ppermute | solution.py:12
  8.9 1.5 collective-permute-start.9
  12.8 1.9 %collective-permute-start.12 = (f32[1,1,16,68]{3,2,1,0:T(8,128)S(1)}, f32[1,1,16,68]{3,2,1,0:T(8,128)S(1)}, u32[]{:S(2)}, u32[]{:S(2)}) collective-permute-start(f32[1,1,16,68]{3,2,1,0:T(8,128)S(1)} %get-tuple-element.19), channel_id=1, source_target_pairs={{16,0},{32,16},{48,32},{64,48},{80,64},{96,80},{112,96},{128,112},... | collective-permute-start | bytes 13064 | tf_op jit(solution)/shard_map/ppermute | solution.py:12
  15.1 1.9 %collective-permute-done.11 = f32[1,1,16,68]{3,2,1,0:T(8,128)S(1)} collective-permute-done((f32[1,1,16,68]{3,2,1,0:T(8,128)S(1)}, f32[1,1,16,68]{3,2,1,0:T(8,128)S(1)}, u32[]{:S(2)}, u32[]{:S(2)}) %collective-permute-start.11) | collective-permute-done | bytes 4384 | tf_op jit(solution)/shard_map/ppermute | solution.py:12
  17.0 4.6 %collective-permute-done.12 = f32[1,1,16,68]{3,2,1,0:T(8,128)S(1)} collective-permute-done((f32[1,1,16,68]{3,2,1,0:T(8,128)S(1)}, f32[1,1,16,68]{3,2,1,0:T(8,128)S(1)}, u32[]{:S(2)}, u32[]{:S(2)}) %collective-permute-start.12) | collective-permute-done | bytes 4384 | tf_op jit(solution)/shard_map/ppermute | solution.py:12
  22.3 4.4 %collective-permute-start.13 = (f32[16]{0:T(128)S(1)}, f32[16]{0:T(128)S(1)}, u32[]{:S(2)}, u32[]{:S(2)}) collective-permute-start(f32[16]{0:T(128)S(1)} %get-tuple-element.129), channel_id=1, source_target_pairs={{0,1},{1,0},{2,3},{3,2},{4,5},{5,4},{6,7},{7,6},{8,9},{9,8},{10,11... | collective-permute-start | bytes 200 | tf_op jit(solution)/shard_map/ppermute | solution.py:53
  27.4 5.5 %collective-permute-start.14 = (f32[16]{0:T(128)S(1)}, f32[16]{0:T(128)S(1)}, u32[]{:S(2)}, u32[]{:S(2)}) collective-permute-start(f32[16]{0:T(128)S(1)} %add.2414), channel_id=1, source_target_pairs={{0,2},{1,3},{2,0},{3,1},{4,6},{5,7},{6,4},{7,5},{8,10},{9,11},{10,... | collective-permute-start | bytes 200 | tf_op jit(solution)/shard_map/ppermute | solution.py:53
  33.0 1.5 collective-permute-done.14
  34.5 7.5 %collective-permute-start.15 = (f32[16]{0:T(128)S(1)}, f32[16]{0:T(128)S(1)}, u32[]{:S(2)}, u32[]{:S(2)}) collective-permute-start(f32[16]{0:T(128)S(1)} %add.2415), channel_id=1, source_target_pairs={{0,6},{1,7},{2,4},{3,5},{4,2},{5,3},{6,0},{7,1},{8,14},{9,15},{10,... | collective-permute-start | bytes 200 | tf_op jit(solution)/shard_map/ppermute | solution.py:53
  42.0 1.5 collective-permute-done.15
  43.5 8.8 %collective-permute-start.16 = (f32[16]{0:T(128)S(1)}, f32[16]{0:T(128)S(1)}, u32[]{:S(2)}, u32[]{:S(2)}) collective-permute-start(f32[16]{0:T(128)S(1)} %add.2416), channel_id=1, source_target_pairs={{0,14},{1,15},{2,12},{3,13},{4,10},{5,11},{6,8},{7,9},{8,6},{9,7},... | collective-permute-start | bytes 200 | tf_op jit(solution)/shard_map/ppermute | solution.py:53
  52.3 1.5 collective-permute-done.16
  53.8 1.9 %collective-permute-start.17 = (f32[16]{0:T(128)S(1)}, f32[16]{0:T(128)S(1)}, u32[]{:S(2)}, u32[]{:S(2)}) collective-permute-start(f32[16]{0:T(128)S(1)} %add.2417), channel_id=1, source_target_pairs={{0,16},{16,0},{32,48},{48,32},{64,80},{80,64},{96,112},{112,96},{1... | collective-permute-start | bytes 200 | tf_op jit(solution)/shard_map/ppermute | solution.py:53
  55.7 3.5 %collective-permute-done.17 = f32[16]{0:T(128)S(1)} collective-permute-done((f32[16]{0:T(128)S(1)}, f32[16]{0:T(128)S(1)}, u32[]{:S(2)}, u32[]{:S(2)}) %collective-permute-start.17) | collective-permute-done | bytes 96 | tf_op jit(solution)/shard_map/ppermute | solution.py:53
  59.2 1.9 %collective-permute-start.18 = (f32[16]{0:T(128)S(1)}, f32[16]{0:T(128)S(1)}, u32[]{:S(2)}, u32[]{:S(2)}) collective-permute-start(f32[16]{0:T(128)S(1)} %add.2418), channel_id=1, source_target_pairs={{0,32},{16,48},{32,0},{48,16},{64,96},{80,112},{96,64},{112,80},{1... | collective-permute-start | bytes 200 | tf_op jit(solution)/shard_map/ppermute | solution.py:53
  61.1 5.0 %collective-permute-done.18 = f32[16]{0:T(128)S(1)} collective-permute-done((f32[16]{0:T(128)S(1)}, f32[16]{0:T(128)S(1)}, u32[]{:S(2)}, u32[]{:S(2)}) %collective-permute-start.18) | collective-permute-done | bytes 96 | tf_op jit(solution)/shard_map/ppermute | solution.py:53
  66.1 1.9 %collective-permute-start.19 = (f32[16]{0:T(128)S(1)}, f32[16]{0:T(128)S(1)}, u32[]{:S(2)}, u32[]{:S(2)}) collective-permute-start(f32[16]{0:T(128)S(1)} %add.2419), channel_id=1, source_target_pairs={{0,64},{16,80},{32,96},{48,112},{64,0},{80,16},{96,32},{112,48},{1... | collective-permute-start | bytes 200 | tf_op jit(solution)/shard_map/ppermute | solution.py:53
  68.1 3.5 %collective-permute-done.19 = f32[16]{0:T(128)S(1)} collective-permute-done((f32[16]{0:T(128)S(1)}, f32[16]{0:T(128)S(1)}, u32[]{:S(2)}, u32[]{:S(2)}) %collective-permute-start.19) | collective-permute-done | bytes 96 | tf_op jit(solution)/shard_map/ppermute | solution.py:53
  71.6 1.9 %collective-permute-start.20 = (f32[16]{0:T(128)S(1)}, f32[16]{0:T(128)S(1)}, u32[]{:S(2)}, u32[]{:S(2)}) collective-permute-start(f32[16]{0:T(128)S(1)} %add.2420), channel_id=1, source_target_pairs={{0,192},{16,208},{32,224},{48,240},{64,128},{80,144},{96,160},{112... | collective-permute-start | bytes 200 | tf_op jit(solution)/shard_map/ppermute | solution.py:53
  73.5 1.9 %collective-permute-start.23 = (f32[2,1,1,16,68]{4,3,2,1,0:T(8,128)S(1)}, f32[2,1,1,16,68]{4,3,2,1,0:T(8,128)S(1)}, u32[]{:S(2)}, u32[]{:S(2)}) collective-permute-start(f32[2,1,1,16,68]{4,3,2,1,0:T(8,128)S(1)} %stack.49), channel_id=1, source_target_pairs={{0,16},{16,32},{32,48},{48,64},{64,80},{80,96},{96,112},{112,128},... | collective-permute-start | bytes 26120 | tf_op jit(solution)/shard_map/ppermute | solution.py:12
  75.4 3.4 %collective-permute-done.20 = f32[16]{0:T(128)S(1)} collective-permute-done((f32[16]{0:T(128)S(1)}, f32[16]{0:T(128)S(1)}, u32[]{:S(2)}, u32[]{:S(2)}) %collective-permute-start.20) | collective-permute-done | bytes 96 | tf_op jit(solution)/shard_map/ppermute | solution.py:53
  78.8 1.9 %collective-permute-start.21 = (f32[16]{0:T(128)S(1)}, f32[16]{0:T(128)S(1)}, u32[]{:S(2)}, u32[]{:S(2)}) collective-permute-start(f32[16]{0:T(128)S(1)} %add.2421), channel_id=1, source_target_pairs={{0,448},{16,464},{32,480},{48,496},{64,384},{80,400},{96,416},{112... | collective-permute-start | bytes 200 | tf_op jit(solution)/shard_map/ppermute | solution.py:53
  82.0 3.4 %collective-permute-done.21 = f32[16]{0:T(128)S(1)} collective-permute-done((f32[16]{0:T(128)S(1)}, f32[16]{0:T(128)S(1)}, u32[]{:S(2)}, u32[]{:S(2)}) %collective-permute-start.21) | collective-permute-done | bytes 96 | tf_op jit(solution)/shard_map/ppermute | solution.py:53
  88.7 2.1 %collective-permute-start.25 = (f32[1,2,128]{2,1,0:T(2,128)S(1)}, f32[1,2,128]{2,1,0:T(2,128)S(1)}, u32[]{:S(2)}, u32[]{:S(2)}) collective-permute-start(f32[1,2,128]{2,1,0:T(2,128)S(1)} %pad_maximum_fusion.4), channel_id=1, source_target_pairs={{0,16},{16,32},{32,48},{48,64},{64,80},{80,96},{96,112},{112,128},... | collective-permute-start | bytes 3080 | tf_op jit(solution)/shard_map/ppermute | solution.py:12
  90.9 3.3 %collective-permute-done.25 = f32[1,2,128]{2,1,0:T(2,128)S(1)} collective-permute-done((f32[1,2,128]{2,1,0:T(2,128)S(1)}, f32[1,2,128]{2,1,0:T(2,128)S(1)}, u32[]{:S(2)}, u32[]{:S(2)}) %collective-permute-start.25) | collective-permute-done | bytes 1056 | tf_op jit(solution)/shard_map/ppermute | solution.py:12
  95.2 1.3 collective-permute-start.26
  96.5 1.7 collective-permute-done.26
  98.2 1.9 %collective-permute-start.27 = (f32[1,2,32]{2,1,0:T(2,128)S(1)}, f32[1,2,32]{2,1,0:T(2,128)S(1)}, u32[]{:S(2)}, u32[]{:S(2)}) collective-permute-start(f32[1,2,32]{2,1,0:T(2,128)S(1)} %pad_maximum_fusion.5), channel_id=1, source_target_pairs={{16,0},{32,16},{48,32},{64,48},{80,64},{96,80},{112,96},{128,112},... | collective-permute-start | bytes 776 | tf_op jit(solution)/shard_map/ppermute | solution.py:12
  100.3 6.6 %collective-permute-done.27 = f32[1,2,32]{2,1,0:T(2,128)S(1)} collective-permute-done((f32[1,2,32]{2,1,0:T(2,128)S(1)}, f32[1,2,32]{2,1,0:T(2,128)S(1)}, u32[]{:S(2)}, u32[]{:S(2)}) %collective-permute-start.27) | collective-permute-done | bytes 288 | tf_op jit(solution)/shard_map/ppermute | solution.py:12
  108.7 1.9 %collective-permute-start.29 = (f32[1,1,16,68]{3,2,1,0:T(8,128)S(1)}, f32[1,1,16,68]{3,2,1,0:T(8,128)S(1)}, u32[]{:S(2)}, u32[]{:S(2)}) collective-permute-start(f32[1,1,16,68]{3,2,1,0:T(8,128)S(1)} %get-tuple-element.23), channel_id=1, source_target_pairs={{16,0},{32,16},{48,32},{64,48},{80,64},{96,80},{112,96},{128,112},... | collective-permute-start | bytes 13064 | tf_op jit(solution)/shard_map/ppermute | solution.py:12
  111.8 5.7 %collective-permute-done.29 = f32[1,1,16,68]{3,2,1,0:T(8,128)S(1)} collective-permute-done((f32[1,1,16,68]{3,2,1,0:T(8,128)S(1)}, f32[1,1,16,68]{3,2,1,0:T(8,128)S(1)}, u32[]{:S(2)}, u32[]{:S(2)}) %collective-permute-start.29) | collective-permute-done | bytes 4384 | tf_op jit(solution)/shard_map/ppermute | solution.py:12
  120.7 3.3 %collective-permute-start.30 = (f32[7,16]{1,0:T(8,128)S(1)}, f32[7,16]{1,0:T(8,128)S(1)}, u32[]{:S(2)}, u32[]{:S(2)}) collective-permute-start(f32[7,16]{1,0:T(8,128)S(1)} %stack.51), channel_id=1, source_target_pairs={{0,1},{1,0},{2,3},{3,2},{4,5},{5,4},{6,7},{7,6},{8,9},{9,8},{10,11... | collective-permute-start | bytes 1352 | tf_op jit(solution)/shard_map/ppermute | solution.py:108
  124.9 5.0 %collective-permute-start.31 = (f32[7,16]{1,0:T(8,128)S(1)}, f32[7,16]{1,0:T(8,128)S(1)}, u32[]{:S(2)}, u32[]{:S(2)}) collective-permute-start(f32[7,16]{1,0:T(8,128)S(1)} %stack.52), channel_id=1, source_target_pairs={{0,2},{1,3},{2,0},{3,1},{4,6},{5,7},{6,4},{7,5},{8,10},{9,11},{10,... | collective-permute-start | bytes 1352 | tf_op jit(solution)/shard_map/ppermute | solution.py:108
  129.9 1.6 collective-permute-done.31
  131.5 8.5 %collective-permute-start.32 = (f32[7,16]{1,0:T(8,128)S(1)}, f32[7,16]{1,0:T(8,128)S(1)}, u32[]{:S(2)}, u32[]{:S(2)}) collective-permute-start(f32[7,16]{1,0:T(8,128)S(1)} %stack.53), channel_id=1, source_target_pairs={{0,6},{1,7},{2,4},{3,5},{4,2},{5,3},{6,0},{7,1},{8,14},{9,15},{10,... | collective-permute-start | bytes 1352 | tf_op jit(solution)/shard_map/ppermute | solution.py:108
  140.1 1.6 collective-permute-done.32
  141.7 6.2 %collective-permute-start.33 = (f32[7,16]{1,0:T(8,128)S(1)}, f32[7,16]{1,0:T(8,128)S(1)}, u32[]{:S(2)}, u32[]{:S(2)}) collective-permute-start(f32[7,16]{1,0:T(8,128)S(1)} %stack.54), channel_id=1, source_target_pairs={{0,14},{1,15},{2,12},{3,13},{4,10},{5,11},{6,8},{7,9},{8,6},{9,7},... | collective-permute-start | bytes 1352 | tf_op jit(solution)/shard_map/ppermute | solution.py:108
  147.9 1.6 collective-permute-done.33
  149.6 1.9 %collective-permute-start.34 = (f32[7,16]{1,0:T(8,128)S(1)}, f32[7,16]{1,0:T(8,128)S(1)}, u32[]{:S(2)}, u32[]{:S(2)}) collective-permute-start(f32[7,16]{1,0:T(8,128)S(1)} %stack.55), channel_id=1, source_target_pairs={{0,16},{16,0},{32,48},{48,32},{64,80},{80,64},{96,112},{112,96},{1... | collective-permute-start | bytes 1352 | tf_op jit(solution)/shard_map/ppermute | solution.py:108
  151.5 3.6 %collective-permute-done.34 = f32[7,16]{1,0:T(8,128)S(1)} collective-permute-done((f32[7,16]{1,0:T(8,128)S(1)}, f32[7,16]{1,0:T(8,128)S(1)}, u32[]{:S(2)}, u32[]{:S(2)}) %collective-permute-start.34) | collective-permute-done | bytes 480 | tf_op jit(solution)/shard_map/ppermute | solution.py:108
  155.1 1.9 %collective-permute-start.35 = (f32[7,16]{1,0:T(8,128)S(1)}, f32[7,16]{1,0:T(8,128)S(1)}, u32[]{:S(2)}, u32[]{:S(2)}) collective-permute-start(f32[7,16]{1,0:T(8,128)S(1)} %stack.56), channel_id=1, source_target_pairs={{0,32},{16,48},{32,0},{48,16},{64,96},{80,112},{96,64},{112,80},{1... | collective-permute-start | bytes 1352 | tf_op jit(solution)/shard_map/ppermute | solution.py:108
  157.1 5.1 %collective-permute-done.35 = f32[7,16]{1,0:T(8,128)S(1)} collective-permute-done((f32[7,16]{1,0:T(8,128)S(1)}, f32[7,16]{1,0:T(8,128)S(1)}, u32[]{:S(2)}, u32[]{:S(2)}) %collective-permute-start.35) | collective-permute-done | bytes 480 | tf_op jit(solution)/shard_map/ppermute | solution.py:108
  162.2 1.9 %collective-permute-start.36 = (f32[7,16]{1,0:T(8,128)S(1)}, f32[7,16]{1,0:T(8,128)S(1)}, u32[]{:S(2)}, u32[]{:S(2)}) collective-permute-start(f32[7,16]{1,0:T(8,128)S(1)} %stack.57), channel_id=1, source_target_pairs={{0,64},{16,80},{32,96},{48,112},{64,0},{80,16},{96,32},{112,48},{1... | collective-permute-start | bytes 1352 | tf_op jit(solution)/shard_map/ppermute | solution.py:108
  164.1 3.6 %collective-permute-done.36 = f32[7,16]{1,0:T(8,128)S(1)} collective-permute-done((f32[7,16]{1,0:T(8,128)S(1)}, f32[7,16]{1,0:T(8,128)S(1)}, u32[]{:S(2)}, u32[]{:S(2)}) %collective-permute-start.36) | collective-permute-done | bytes 480 | tf_op jit(solution)/shard_map/ppermute | solution.py:108
  167.7 1.9 %collective-permute-start.37 = (f32[7,16]{1,0:T(8,128)S(1)}, f32[7,16]{1,0:T(8,128)S(1)}, u32[]{:S(2)}, u32[]{:S(2)}) collective-permute-start(f32[7,16]{1,0:T(8,128)S(1)} %stack.58), channel_id=1, source_target_pairs={{0,192},{16,208},{32,224},{48,240},{64,128},{80,144},{96,160},{112... | collective-permute-start | bytes 1352 | tf_op jit(solution)/shard_map/ppermute | solution.py:108
  169.7 5.4 %collective-permute-done.37 = f32[7,16]{1,0:T(8,128)S(1)} collective-permute-done((f32[7,16]{1,0:T(8,128)S(1)}, f32[7,16]{1,0:T(8,128)S(1)}, u32[]{:S(2)}, u32[]{:S(2)}) %collective-permute-start.37) | collective-permute-done | bytes 480 | tf_op jit(solution)/shard_map/ppermute | solution.py:108
  175.1 2.6 %collective-permute-start.38 = (f32[7,16]{1,0:T(8,128)S(1)}, f32[7,16]{1,0:T(8,128)S(1)}, u32[]{:S(2)}, u32[]{:S(2)}) collective-permute-start(f32[7,16]{1,0:T(8,128)S(1)} %stack.59), channel_id=1, source_target_pairs={{0,448},{16,464},{32,480},{48,496},{64,384},{80,400},{96,416},{112... | collective-permute-start | bytes 1352 | tf_op jit(solution)/shard_map/ppermute | solution.py:108
  177.7 4.1 %collective-permute-done.38 = f32[7,16]{1,0:T(8,128)S(1)} collective-permute-done((f32[7,16]{1,0:T(8,128)S(1)}, f32[7,16]{1,0:T(8,128)S(1)}, u32[]{:S(2)}, u32[]{:S(2)}) %collective-permute-start.38) | collective-permute-done | bytes 480 | tf_op jit(solution)/shard_map/ppermute | solution.py:108
  (163 shorter events, 20.6 us)
Async XLA Ops:
  0.6 10.5 %copy-start = (bf16[1,1,272,272]{3,2,1,0:T(8,128)(2,1)S(1)}, bf16[1,1,272,272]{3,2,1,0:T(8,128)(2,1)}, u32[]{:S(2)}) copy-start(bf16[1,1,272,272]{3,2,1,0:T(8,128)(2,1)} %param.17) | copy-start | bytes 443908
  0.7 0.7 copy-start.9
  0.7 2.6 %copy-start.1 = (f32[1,1,16,136]{3,2,1,0:T(8,128)S(1)}, f32[1,1,16,136]{3,2,1,0:T(8,128)}, u32[]{:S(2)}) copy-start(f32[1,1,16,136]{3,2,1,0:T(8,128)} %param.13) | copy-start | bytes 26116
  0.7 2.6 %copy-start.5 = (f32[1,1,16,136]{3,2,1,0:T(8,128)S(1)}, f32[1,1,16,136]{3,2,1,0:T(8,128)}, u32[]{:S(2)}) copy-start(f32[1,1,16,136]{3,2,1,0:T(8,128)} %param.14) | copy-start | bytes 26116
  4.3 6.1 %collective-permute-start.10 = (f32[2,1,1,16,68]{4,3,2,1,0:T(8,128)S(1)}, f32[2,1,1,16,68]{4,3,2,1,0:T(8,128)S(1)}, u32[]{:S(2)}, u32[]{:S(2)}) collective-permute-start(f32[2,1,1,16,68]{4,3,2,1,0:T(8,128)S(1)} %pad_maximum_fusion.1), channel_id=1, source_target_pairs={{0,16},{16,32},{32,48},{48,64},{64,80},{80,96},{96,112},{112,128},... | collective-permute-start | bytes 26120 | tf_op jit(solution)/shard_map/ppermute | solution.py:12
  8.9 2.3 %collective-permute-start.9 = (f32[2,1,1,16,68]{4,3,2,1,0:T(8,128)S(1)}, f32[2,1,1,16,68]{4,3,2,1,0:T(8,128)S(1)}, u32[]{:S(2)}, u32[]{:S(2)}) collective-permute-start(f32[2,1,1,16,68]{4,3,2,1,0:T(8,128)S(1)} %pad_maximum_fusion), channel_id=1, source_target_pairs={{0,1},{1,2},{2,3},{3,4},{4,5},{5,6},{6,7},{7,8},{8,9},{9,10},{10,1... | collective-permute-start | bytes 26120 | tf_op jit(solution)/shard_map/ppermute | solution.py:12
  11.5 5.5 %collective-permute-start.11 = (f32[1,1,16,68]{3,2,1,0:T(8,128)S(1)}, f32[1,1,16,68]{3,2,1,0:T(8,128)S(1)}, u32[]{:S(2)}, u32[]{:S(2)}) collective-permute-start(f32[1,1,16,68]{3,2,1,0:T(8,128)S(1)} %get-tuple-element.18), channel_id=1, source_target_pairs={{1,0},{2,1},{3,2},{4,3},{5,4},{6,5},{7,6},{8,7},{9,8},{10,9},{11,1... | collective-permute-start | bytes 13064 | tf_op jit(solution)/shard_map/ppermute | solution.py:12
  12.8 8.9 %collective-permute-start.12 = (f32[1,1,16,68]{3,2,1,0:T(8,128)S(1)}, f32[1,1,16,68]{3,2,1,0:T(8,128)S(1)}, u32[]{:S(2)}, u32[]{:S(2)}) collective-permute-start(f32[1,1,16,68]{3,2,1,0:T(8,128)S(1)} %get-tuple-element.19), channel_id=1, source_target_pairs={{16,0},{32,16},{48,32},{64,48},{80,64},{96,80},{112,96},{128,112},... | collective-permute-start | bytes 13064 | tf_op jit(solution)/shard_map/ppermute | solution.py:12
  22.0 63.4 %copy-start.11 = (f32[16]{0:T(128)S(1)}, f32[16]{0:T(128)}, u32[]{:S(2)}) copy-start(f32[16]{0:T(128)} %param.15) | copy-start | bytes 196
  22.1 78.0 %copy-start.2 = (bf16[1,1,272,272]{3,2,1,0:T(8,128)(2,1)S(1)}, bf16[1,1,272,272]{3,2,1,0:T(8,128)(2,1)}, u32[]{:S(2)}) copy-start(bf16[1,1,272,272]{3,2,1,0:T(8,128)(2,1)} %param.16) | copy-start | bytes 443908
  22.3 5.2 %collective-permute-start.13 = (f32[16]{0:T(128)S(1)}, f32[16]{0:T(128)S(1)}, u32[]{:S(2)}, u32[]{:S(2)}) collective-permute-start(f32[16]{0:T(128)S(1)} %get-tuple-element.129), channel_id=1, source_target_pairs={{0,1},{1,0},{2,3},{3,2},{4,5},{5,4},{6,7},{7,6},{8,9},{9,8},{10,11... | collective-permute-start | bytes 200 | tf_op jit(solution)/shard_map/ppermute | solution.py:53
  27.4 7.0 %collective-permute-start.14 = (f32[16]{0:T(128)S(1)}, f32[16]{0:T(128)S(1)}, u32[]{:S(2)}, u32[]{:S(2)}) collective-permute-start(f32[16]{0:T(128)S(1)} %add.2414), channel_id=1, source_target_pairs={{0,2},{1,3},{2,0},{3,1},{4,6},{5,7},{6,4},{7,5},{8,10},{9,11},{10,... | collective-permute-start | bytes 200 | tf_op jit(solution)/shard_map/ppermute | solution.py:53
  34.5 9.0 %collective-permute-start.15 = (f32[16]{0:T(128)S(1)}, f32[16]{0:T(128)S(1)}, u32[]{:S(2)}, u32[]{:S(2)}) collective-permute-start(f32[16]{0:T(128)S(1)} %add.2415), channel_id=1, source_target_pairs={{0,6},{1,7},{2,4},{3,5},{4,2},{5,3},{6,0},{7,1},{8,14},{9,15},{10,... | collective-permute-start | bytes 200 | tf_op jit(solution)/shard_map/ppermute | solution.py:53
  43.5 10.3 %collective-permute-start.16 = (f32[16]{0:T(128)S(1)}, f32[16]{0:T(128)S(1)}, u32[]{:S(2)}, u32[]{:S(2)}) collective-permute-start(f32[16]{0:T(128)S(1)} %add.2416), channel_id=1, source_target_pairs={{0,14},{1,15},{2,12},{3,13},{4,10},{5,11},{6,8},{7,9},{8,6},{9,7},... | collective-permute-start | bytes 200 | tf_op jit(solution)/shard_map/ppermute | solution.py:53
  53.8 5.4 %collective-permute-start.17 = (f32[16]{0:T(128)S(1)}, f32[16]{0:T(128)S(1)}, u32[]{:S(2)}, u32[]{:S(2)}) collective-permute-start(f32[16]{0:T(128)S(1)} %add.2417), channel_id=1, source_target_pairs={{0,16},{16,0},{32,48},{48,32},{64,80},{80,64},{96,112},{112,96},{1... | collective-permute-start | bytes 200 | tf_op jit(solution)/shard_map/ppermute | solution.py:53
  59.2 6.9 %collective-permute-start.18 = (f32[16]{0:T(128)S(1)}, f32[16]{0:T(128)S(1)}, u32[]{:S(2)}, u32[]{:S(2)}) collective-permute-start(f32[16]{0:T(128)S(1)} %add.2418), channel_id=1, source_target_pairs={{0,32},{16,48},{32,0},{48,16},{64,96},{80,112},{96,64},{112,80},{1... | collective-permute-start | bytes 200 | tf_op jit(solution)/shard_map/ppermute | solution.py:53
  66.1 5.4 %collective-permute-start.19 = (f32[16]{0:T(128)S(1)}, f32[16]{0:T(128)S(1)}, u32[]{:S(2)}, u32[]{:S(2)}) collective-permute-start(f32[16]{0:T(128)S(1)} %add.2419), channel_id=1, source_target_pairs={{0,64},{16,80},{32,96},{48,112},{64,0},{80,16},{96,32},{112,48},{1... | collective-permute-start | bytes 200 | tf_op jit(solution)/shard_map/ppermute | solution.py:53
  71.6 7.2 %collective-permute-start.20 = (f32[16]{0:T(128)S(1)}, f32[16]{0:T(128)S(1)}, u32[]{:S(2)}, u32[]{:S(2)}) collective-permute-start(f32[16]{0:T(128)S(1)} %add.2420), channel_id=1, source_target_pairs={{0,192},{16,208},{32,224},{48,240},{64,128},{80,144},{96,160},{112... | collective-permute-start | bytes 200 | tf_op jit(solution)/shard_map/ppermute | solution.py:53
  73.5 12.0 %collective-permute-start.23 = (f32[2,1,1,16,68]{4,3,2,1,0:T(8,128)S(1)}, f32[2,1,1,16,68]{4,3,2,1,0:T(8,128)S(1)}, u32[]{:S(2)}, u32[]{:S(2)}) collective-permute-start(f32[2,1,1,16,68]{4,3,2,1,0:T(8,128)S(1)} %stack.49), channel_id=1, source_target_pairs={{0,16},{16,32},{32,48},{48,64},{64,80},{80,96},{96,112},{112,128},... | collective-permute-start | bytes 26120 | tf_op jit(solution)/shard_map/ppermute | solution.py:12
  78.8 6.6 %collective-permute-start.21 = (f32[16]{0:T(128)S(1)}, f32[16]{0:T(128)S(1)}, u32[]{:S(2)}, u32[]{:S(2)}) collective-permute-start(f32[16]{0:T(128)S(1)} %add.2421), channel_id=1, source_target_pairs={{0,448},{16,464},{32,480},{48,496},{64,384},{80,400},{96,416},{112... | collective-permute-start | bytes 200 | tf_op jit(solution)/shard_map/ppermute | solution.py:53
  80.7 4.8 %collective-permute-start.22 = (f32[2,1,1,16,68]{4,3,2,1,0:T(8,128)S(1)}, f32[2,1,1,16,68]{4,3,2,1,0:T(8,128)S(1)}, u32[]{:S(2)}, u32[]{:S(2)}) collective-permute-start(f32[2,1,1,16,68]{4,3,2,1,0:T(8,128)S(1)} %stack.47), channel_id=1, source_target_pairs={{0,1},{1,2},{2,3},{3,4},{4,5},{5,6},{6,7},{7,8},{8,9},{9,10},{10,1... | collective-permute-start | bytes 26120 | tf_op jit(solution)/shard_map/ppermute | solution.py:12
  85.4 96.4 %copy-start.7 = (f32[16]{0:T(128)}, f32[16]{0:T(128)S(1)}, u32[]{:S(2)}) copy-start(f32[16]{0:T(128)S(1)} %get-tuple-element.128) | copy-start | bytes 196
  85.6 0.7 copy-start.6
  86.6 2.1 %collective-permute-start.24 = (f32[1,1,128]{2,1,0:T(1,128)S(1)}, f32[1,1,128]{2,1,0:T(1,128)S(1)}, u32[]{:S(2)}, u32[]{:S(2)}) collective-permute-start(f32[1,1,128]{2,1,0:T(1,128)S(1)} %reshape.602), channel_id=1, source_target_pairs={{0,1},{1,2},{2,3},{3,4},{4,5},{5,6},{6,7},{7,8},{8,9},{9,10},{10,1... | collective-permute-start | bytes 1544 | tf_op jit(solution)/shard_map/ppermute | solution.py:12
  88.7 5.5 %collective-permute-start.25 = (f32[1,2,128]{2,1,0:T(2,128)S(1)}, f32[1,2,128]{2,1,0:T(2,128)S(1)}, u32[]{:S(2)}, u32[]{:S(2)}) collective-permute-start(f32[1,2,128]{2,1,0:T(2,128)S(1)} %pad_maximum_fusion.4), channel_id=1, source_target_pairs={{0,16},{16,32},{32,48},{48,64},{64,80},{80,96},{96,112},{112,128},... | collective-permute-start | bytes 3080 | tf_op jit(solution)/shard_map/ppermute | solution.py:12
  94.2 0.7 copy-start.8
  95.2 3.0 %collective-permute-start.26 = (f32[1,1,32]{2,1,0:T(1,128)S(1)}, f32[1,1,32]{2,1,0:T(1,128)S(1)}, u32[]{:S(2)}, u32[]{:S(2)}) collective-permute-start(f32[1,1,32]{2,1,0:T(1,128)S(1)} %reshape.606), channel_id=1, source_target_pairs={{1,0},{2,1},{3,2},{4,3},{5,4},{6,5},{7,6},{8,7},{9,8},{10,9},{11,1... | collective-permute-start | bytes 392 | tf_op jit(solution)/shard_map/ppermute | solution.py:12
  98.2 8.8 %collective-permute-start.27 = (f32[1,2,32]{2,1,0:T(2,128)S(1)}, f32[1,2,32]{2,1,0:T(2,128)S(1)}, u32[]{:S(2)}, u32[]{:S(2)}) collective-permute-start(f32[1,2,32]{2,1,0:T(2,128)S(1)} %pad_maximum_fusion.5), channel_id=1, source_target_pairs={{16,0},{32,16},{48,32},{64,48},{80,64},{96,80},{112,96},{128,112},... | collective-permute-start | bytes 776 | tf_op jit(solution)/shard_map/ppermute | solution.py:12
  107.4 4.4 %collective-permute-start.28 = (f32[1,1,16,68]{3,2,1,0:T(8,128)S(1)}, f32[1,1,16,68]{3,2,1,0:T(8,128)S(1)}, u32[]{:S(2)}, u32[]{:S(2)}) collective-permute-start(f32[1,1,16,68]{3,2,1,0:T(8,128)S(1)} %get-tuple-element.22), channel_id=1, source_target_pairs={{1,0},{2,1},{3,2},{4,3},{5,4},{6,5},{7,6},{8,7},{9,8},{10,9},{11,1... | collective-permute-start | bytes 13064 | tf_op jit(solution)/shard_map/ppermute | solution.py:12
  108.7 8.9 %collective-permute-start.29 = (f32[1,1,16,68]{3,2,1,0:T(8,128)S(1)}, f32[1,1,16,68]{3,2,1,0:T(8,128)S(1)}, u32[]{:S(2)}, u32[]{:S(2)}) collective-permute-start(f32[1,1,16,68]{3,2,1,0:T(8,128)S(1)} %get-tuple-element.23), channel_id=1, source_target_pairs={{16,0},{32,16},{48,32},{64,48},{80,64},{96,80},{112,96},{128,112},... | collective-permute-start | bytes 13064 | tf_op jit(solution)/shard_map/ppermute | solution.py:12
  118.2 65.0 %copy-start.3 = (f32[1,1,16,136]{3,2,1,0:T(8,128)}, f32[1,1,16,136]{3,2,1,0:T(8,128)S(1)}, u32[]{:S(2)}) copy-start(f32[1,1,16,136]{3,2,1,0:T(8,128)S(1)} %get-tuple-element.126) | copy-start | bytes 26116
  120.7 4.1 %collective-permute-start.30 = (f32[7,16]{1,0:T(8,128)S(1)}, f32[7,16]{1,0:T(8,128)S(1)}, u32[]{:S(2)}, u32[]{:S(2)}) collective-permute-start(f32[7,16]{1,0:T(8,128)S(1)} %stack.51), channel_id=1, source_target_pairs={{0,1},{1,0},{2,3},{3,2},{4,5},{5,4},{6,7},{7,6},{8,9},{9,8},{10,11... | collective-permute-start | bytes 1352 | tf_op jit(solution)/shard_map/ppermute | solution.py:108
  124.9 6.6 %collective-permute-start.31 = (f32[7,16]{1,0:T(8,128)S(1)}, f32[7,16]{1,0:T(8,128)S(1)}, u32[]{:S(2)}, u32[]{:S(2)}) collective-permute-start(f32[7,16]{1,0:T(8,128)S(1)} %stack.52), channel_id=1, source_target_pairs={{0,2},{1,3},{2,0},{3,1},{4,6},{5,7},{6,4},{7,5},{8,10},{9,11},{10,... | collective-permute-start | bytes 1352 | tf_op jit(solution)/shard_map/ppermute | solution.py:108
  131.5 10.1 %collective-permute-start.32 = (f32[7,16]{1,0:T(8,128)S(1)}, f32[7,16]{1,0:T(8,128)S(1)}, u32[]{:S(2)}, u32[]{:S(2)}) collective-permute-start(f32[7,16]{1,0:T(8,128)S(1)} %stack.53), channel_id=1, source_target_pairs={{0,6},{1,7},{2,4},{3,5},{4,2},{5,3},{6,0},{7,1},{8,14},{9,15},{10,... | collective-permute-start | bytes 1352 | tf_op jit(solution)/shard_map/ppermute | solution.py:108
  141.7 7.8 %collective-permute-start.33 = (f32[7,16]{1,0:T(8,128)S(1)}, f32[7,16]{1,0:T(8,128)S(1)}, u32[]{:S(2)}, u32[]{:S(2)}) collective-permute-start(f32[7,16]{1,0:T(8,128)S(1)} %stack.54), channel_id=1, source_target_pairs={{0,14},{1,15},{2,12},{3,13},{4,10},{5,11},{6,8},{7,9},{8,6},{9,7},... | collective-permute-start | bytes 1352 | tf_op jit(solution)/shard_map/ppermute | solution.py:108
  149.6 5.5 %collective-permute-start.34 = (f32[7,16]{1,0:T(8,128)S(1)}, f32[7,16]{1,0:T(8,128)S(1)}, u32[]{:S(2)}, u32[]{:S(2)}) collective-permute-start(f32[7,16]{1,0:T(8,128)S(1)} %stack.55), channel_id=1, source_target_pairs={{0,16},{16,0},{32,48},{48,32},{64,80},{80,64},{96,112},{112,96},{1... | collective-permute-start | bytes 1352 | tf_op jit(solution)/shard_map/ppermute | solution.py:108
  155.1 7.0 %collective-permute-start.35 = (f32[7,16]{1,0:T(8,128)S(1)}, f32[7,16]{1,0:T(8,128)S(1)}, u32[]{:S(2)}, u32[]{:S(2)}) collective-permute-start(f32[7,16]{1,0:T(8,128)S(1)} %stack.56), channel_id=1, source_target_pairs={{0,32},{16,48},{32,0},{48,16},{64,96},{80,112},{96,64},{112,80},{1... | collective-permute-start | bytes 1352 | tf_op jit(solution)/shard_map/ppermute | solution.py:108
  162.2 5.5 %collective-permute-start.36 = (f32[7,16]{1,0:T(8,128)S(1)}, f32[7,16]{1,0:T(8,128)S(1)}, u32[]{:S(2)}, u32[]{:S(2)}) collective-permute-start(f32[7,16]{1,0:T(8,128)S(1)} %stack.57), channel_id=1, source_target_pairs={{0,64},{16,80},{32,96},{48,112},{64,0},{80,16},{96,32},{112,48},{1... | collective-permute-start | bytes 1352 | tf_op jit(solution)/shard_map/ppermute | solution.py:108
  167.7 7.3 %collective-permute-start.37 = (f32[7,16]{1,0:T(8,128)S(1)}, f32[7,16]{1,0:T(8,128)S(1)}, u32[]{:S(2)}, u32[]{:S(2)}) collective-permute-start(f32[7,16]{1,0:T(8,128)S(1)} %stack.58), channel_id=1, source_target_pairs={{0,192},{16,208},{32,224},{48,240},{64,128},{80,144},{96,160},{112... | collective-permute-start | bytes 1352 | tf_op jit(solution)/shard_map/ppermute | solution.py:108
  175.1 6.7 %collective-permute-start.38 = (f32[7,16]{1,0:T(8,128)S(1)}, f32[7,16]{1,0:T(8,128)S(1)}, u32[]{:S(2)}, u32[]{:S(2)}) collective-permute-start(f32[7,16]{1,0:T(8,128)S(1)} %stack.59), channel_id=1, source_target_pairs={{0,448},{16,464},{32,480},{48,496},{64,384},{80,400},{96,416},{112... | collective-permute-start | bytes 1352 | tf_op jit(solution)/shard_map/ppermute | solution.py:108
  181.8 1.4 copy-start.4
  183.9 0.5 copy-start.10

commit v6 on v5

--- a/solution.py
+++ b/solution.py
@@ -251,29 +251,38 @@
     corner = (
         jnp.einsum("rpkb,rpcb->rpck", coupling, spread, preferred_element_type=jnp.float32) * active
     )
-    flat_corner = corner.reshape(rows_here, cols_here, -1)
-    west_column = passed_along(flat_corner, "py", 1)
-    with_west = jnp.concatenate([west_column, flat_corner], 1)
-    south_row = passed_along(with_west, "px", 1)
-    extended = jnp.concatenate([south_row, with_west], 0)
-    extended = extended.reshape(rows_here + 1, cols_here + 1, corner.shape[2], corner.shape[3])
+    corner_width = corner.shape[2] * corner.shape[3]
+    payload = jnp.concatenate(
+        [
+            corner.reshape(rows_here, cols_here, corner_width),
+            coarse_inverse.reshape(rows_here, cols_here, 4),
+        ],
+        2,
+    )
+    from_west_col, from_east_col = exchanged_together([(payload, "py", 1), (payload, "py", -1)])
+    row = jnp.concatenate([from_west_col[:, -1:], payload, from_east_col[:, :1]], 1)
+    from_south_row, from_north_row = exchanged_together([(row, "px", 1), (row, "px", -1)])
+    block = jnp.concatenate([from_south_row[-1:], row, from_north_row[:1]], 0)
+    corners = block[..., :corner_width].reshape(
+        rows_here + 2, cols_here + 2, corner.shape[2], corner.shape[3]
+    )
+    blocks = block[..., corner_width:].reshape(rows_here + 2, cols_here + 2, 2, 2)
+    vertex_row = lax.axis_index("px") * rows_here + jnp.arange(rows_here + 1)
+    vertex_col = lax.axis_index("py") * cols_here + jnp.arange(cols_here + 1)
+    vertex_ok = ((vertex_row >= 1)[:, None] & (vertex_col >= 1)[None, :]).astype(jnp.float32)[
+        :, :, None, None
+    ]
     assembled = (
-        extended[1:, 1:, :, 0:2]
-        + extended[1:, :-1, :, 2:4]
-        + extended[:-1, 1:, :, 4:6]
-        + extended[:-1, :-1, :, 6:8]
-    ) * vertex_mask
+        corners[1:, 1:, :, 0:2]
+        + corners[1:, :-1, :, 2:4]
+        + corners[:-1, 1:, :, 4:6]
+        + corners[:-1, :-1, :, 6:8]
+    ) * vertex_ok
     coarse = jnp.einsum(
-        "rpxy,rpcy->rpcx", coarse_inverse, assembled, precision=lax.Precision.HIGHEST
-    )
-    flat_coarse = coarse.reshape(rows_here, cols_here, -1)
-    east_column = passed_along(flat_coarse, "py", -1)
-    with_east = jnp.concatenate([flat_coarse, east_column], 1)
-    north_row = passed_along(with_east, "px", -1)
-    beside_all = jnp.concatenate([with_east, north_row], 0)
-    beside_all = beside_all.reshape(rows_here + 1, cols_here + 1, coarse.shape[2], 2)
+        "rpxy,rpcy->rpcx", blocks[1:, 1:], assembled, precision=lax.Precision.HIGHEST
+    )
     corners_back = jnp.concatenate(
-        [beside_all[:-1, :-1], beside_all[:-1, 1:], beside_all[1:, :-1], beside_all[1:, 1:]], 3
+        [coarse[:-1, :-1], coarse[:-1, 1:], coarse[1:, :-1], coarse[1:, 1:]], 3
     )
     correction = jnp.einsum(
         "rpkb,rpck->rpcb",

time: 185 us -> 184 us (level)
  waiting for transfers between devices: 78.1 us -> 74.3 us
    ppermute x12, waiting for transfers between devices: 26.8 us -> 22.6 us  [passed_along(): return lax.ppermute(value, axis, pairs)]
  transfers between devices with their start and end apart: 30 -> 30, of which waited for: 27 -> 25; matrix products, arithmetic and copies ran while one was open for 0% -> 0% of each run, Pallas kernels for 0% -> 0%
where the time goes in v6:
time: 184 us; the launch traced here: 183 us
  starting transfers between devices  91.7 us (50%)
  waiting for transfers between devices  74.3 us (40%)
  local copies, waits for them, and re-layouts  6.61 us (4%)
  other arithmetic  4.96 us (3%)
  between operations  4.01 us (2%)
    ppermute x9, starting transfers between devices, all_sum(): value = value + lax.ppermute(value, axis, pairs)  35.9 us
    ppermute x9, starting transfers between devices, all_sum_mixed(): other = lax.ppermute(packed, axis, partners)  31.7 us
    ppermute x9, waiting for transfers between devices, all_sum_mixed(): other = lax.ppermute(packed, axis, partners)  27.9 us
    ppermute x12, starting transfers between devices, passed_along(): return lax.ppermute(value, axis, pairs)  24.1 us
    ppermute x9, waiting for transfers between devices, all_sum(): value = value + lax.ppermute(value, axis, pairs)  23.8 us
    ppermute x12, waiting for transfers between devices, passed_along(): return lax.ppermute(value, axis, pairs)  22.6 us
  transfers between devices with their start and end apart: 30, of which 25 were waited for; matrix products, arithmetic and copies ran while one was open for 0% of the time, Pallas kernels for 0%

profile of v6, /device:TPU:30, one launch (start us, length us, event | category | flops | bytes accessed | tf_op | source)
XLA Modules:
  0.0 182.6 jit_solution(2637338024778231146)
XLA Ops:
  4.9 4.6 %collective-permute-start.10 = (f32[2,1,1,16,68]{4,3,2,1,0:T(8,128)S(1)}, f32[2,1,1,16,68]{4,3,2,1,0:T(8,128)S(1)}, u32[]{:S(2)}, u32[]{:S(2)}) collective-permute-start(f32[2,1,1,16,68]{4,3,2,1,0:T(8,128)S(1)} %pad_maximum_fusion.1), channel_id=1, source_target_pairs={{0,16},{16,32},{32,48},{48,64},{64,80},{80,96},{96,112},{112,128},... | collective-permute-start | bytes 26120 | tf_op jit(solution)/shard_map/ppermute | solution.py:12
  9.5 1.5 collective-permute-start.9
  13.4 1.9 %collective-permute-start.12 = (f32[1,1,16,68]{3,2,1,0:T(8,128)S(1)}, f32[1,1,16,68]{3,2,1,0:T(8,128)S(1)}, u32[]{:S(2)}, u32[]{:S(2)}) collective-permute-start(f32[1,1,16,68]{3,2,1,0:T(8,128)S(1)} %get-tuple-element.27), channel_id=1, source_target_pairs={{16,0},{32,16},{48,32},{64,48},{80,64},{96,80},{112,96},{128,112},... | collective-permute-start | bytes 13064 | tf_op jit(solution)/shard_map/ppermute | solution.py:12
  15.7 1.9 %collective-permute-done.11 = f32[1,1,16,68]{3,2,1,0:T(8,128)S(1)} collective-permute-done((f32[1,1,16,68]{3,2,1,0:T(8,128)S(1)}, f32[1,1,16,68]{3,2,1,0:T(8,128)S(1)}, u32[]{:S(2)}, u32[]{:S(2)}) %collective-permute-start.11) | collective-permute-done | bytes 4384 | tf_op jit(solution)/shard_map/ppermute | solution.py:12
  17.6 4.6 %collective-permute-done.12 = f32[1,1,16,68]{3,2,1,0:T(8,128)S(1)} collective-permute-done((f32[1,1,16,68]{3,2,1,0:T(8,128)S(1)}, f32[1,1,16,68]{3,2,1,0:T(8,128)S(1)}, u32[]{:S(2)}, u32[]{:S(2)}) %collective-permute-start.12) | collective-permute-done | bytes 4384 | tf_op jit(solution)/shard_map/ppermute | solution.py:12
  22.9 4.4 %collective-permute-start.13 = (f32[16]{0:T(128)S(1)}, f32[16]{0:T(128)S(1)}, u32[]{:S(2)}, u32[]{:S(2)}) collective-permute-start(f32[16]{0:T(128)S(1)} %get-tuple-element.145), channel_id=1, source_target_pairs={{0,1},{1,0},{2,3},{3,2},{4,5},{5,4},{6,7},{7,6},{8,9},{9,8},{10,11... | collective-permute-start | bytes 200 | tf_op jit(solution)/shard_map/ppermute | solution.py:53
  28.1 5.5 %collective-permute-start.14 = (f32[16]{0:T(128)S(1)}, f32[16]{0:T(128)S(1)}, u32[]{:S(2)}, u32[]{:S(2)}) collective-permute-start(f32[16]{0:T(128)S(1)} %add.2434), channel_id=1, source_target_pairs={{0,2},{1,3},{2,0},{3,1},{4,6},{5,7},{6,4},{7,5},{8,10},{9,11},{10,... | collective-permute-start | bytes 200 | tf_op jit(solution)/shard_map/ppermute | solution.py:53
  33.6 1.5 collective-permute-done.14
  35.1 7.5 %collective-permute-start.15 = (f32[16]{0:T(128)S(1)}, f32[16]{0:T(128)S(1)}, u32[]{:S(2)}, u32[]{:S(2)}) collective-permute-start(f32[16]{0:T(128)S(1)} %add.2435), channel_id=1, source_target_pairs={{0,6},{1,7},{2,4},{3,5},{4,2},{5,3},{6,0},{7,1},{8,14},{9,15},{10,... | collective-permute-start | bytes 200 | tf_op jit(solution)/shard_map/ppermute | solution.py:53
  42.6 1.5 collective-permute-done.15
  44.1 8.8 %collective-permute-start.16 = (f32[16]{0:T(128)S(1)}, f32[16]{0:T(128)S(1)}, u32[]{:S(2)}, u32[]{:S(2)}) collective-permute-start(f32[16]{0:T(128)S(1)} %add.2436), channel_id=1, source_target_pairs={{0,14},{1,15},{2,12},{3,13},{4,10},{5,11},{6,8},{7,9},{8,6},{9,7},... | collective-permute-start | bytes 200 | tf_op jit(solution)/shard_map/ppermute | solution.py:53
  52.9 1.5 collective-permute-done.16
  54.4 1.9 %collective-permute-start.17 = (f32[16]{0:T(128)S(1)}, f32[16]{0:T(128)S(1)}, u32[]{:S(2)}, u32[]{:S(2)}) collective-permute-start(f32[16]{0:T(128)S(1)} %add.2437), channel_id=1, source_target_pairs={{0,16},{16,0},{32,48},{48,32},{64,80},{80,64},{96,112},{112,96},{1... | collective-permute-start | bytes 200 | tf_op jit(solution)/shard_map/ppermute | solution.py:53
  56.4 3.4 %collective-permute-done.17 = f32[16]{0:T(128)S(1)} collective-permute-done((f32[16]{0:T(128)S(1)}, f32[16]{0:T(128)S(1)}, u32[]{:S(2)}, u32[]{:S(2)}) %collective-permute-start.17) | collective-permute-done | bytes 96 | tf_op jit(solution)/shard_map/ppermute | solution.py:53
  59.8 1.9 %collective-permute-start.18 = (f32[16]{0:T(128)S(1)}, f32[16]{0:T(128)S(1)}, u32[]{:S(2)}, u32[]{:S(2)}) collective-permute-start(f32[16]{0:T(128)S(1)} %add.2438), channel_id=1, source_target_pairs={{0,32},{16,48},{32,0},{48,16},{64,96},{80,112},{96,64},{112,80},{1... | collective-permute-start | bytes 200 | tf_op jit(solution)/shard_map/ppermute | solution.py:53
  61.8 5.0 %collective-permute-done.18 = f32[16]{0:T(128)S(1)} collective-permute-done((f32[16]{0:T(128)S(1)}, f32[16]{0:T(128)S(1)}, u32[]{:S(2)}, u32[]{:S(2)}) %collective-permute-start.18) | collective-permute-done | bytes 96 | tf_op jit(solution)/shard_map/ppermute | solution.py:53
  66.8 1.9 %collective-permute-start.19 = (f32[16]{0:T(128)S(1)}, f32[16]{0:T(128)S(1)}, u32[]{:S(2)}, u32[]{:S(2)}) collective-permute-start(f32[16]{0:T(128)S(1)} %add.2439), channel_id=1, source_target_pairs={{0,64},{16,80},{32,96},{48,112},{64,0},{80,16},{96,32},{112,48},{1... | collective-permute-start | bytes 200 | tf_op jit(solution)/shard_map/ppermute | solution.py:53
  68.7 1.9 %collective-permute-start.23 = (f32[2,1,1,16,68]{4,3,2,1,0:T(8,128)S(1)}, f32[2,1,1,16,68]{4,3,2,1,0:T(8,128)S(1)}, u32[]{:S(2)}, u32[]{:S(2)}) collective-permute-start(f32[2,1,1,16,68]{4,3,2,1,0:T(8,128)S(1)} %stack.49), channel_id=1, source_target_pairs={{0,16},{16,32},{32,48},{48,64},{64,80},{80,96},{96,112},{112,128},... | collective-permute-start | bytes 26120 | tf_op jit(solution)/shard_map/ppermute | solution.py:12
  70.6 1.6 collective-permute-done.19
  72.2 1.9 %collective-permute-start.20 = (f32[16]{0:T(128)S(1)}, f32[16]{0:T(128)S(1)}, u32[]{:S(2)}, u32[]{:S(2)}) collective-permute-start(f32[16]{0:T(128)S(1)} %add.2440), channel_id=1, source_target_pairs={{0,192},{16,208},{32,224},{48,240},{64,128},{80,144},{96,160},{112... | collective-permute-start | bytes 200 | tf_op jit(solution)/shard_map/ppermute | solution.py:53
  74.1 5.3 %collective-permute-done.20 = f32[16]{0:T(128)S(1)} collective-permute-done((f32[16]{0:T(128)S(1)}, f32[16]{0:T(128)S(1)}, u32[]{:S(2)}, u32[]{:S(2)}) %collective-permute-start.20) | collective-permute-done | bytes 96 | tf_op jit(solution)/shard_map/ppermute | solution.py:53
  79.4 2.1 %collective-permute-start.21 = (f32[16]{0:T(128)S(1)}, f32[16]{0:T(128)S(1)}, u32[]{:S(2)}, u32[]{:S(2)}) collective-permute-start(f32[16]{0:T(128)S(1)} %add.2441), channel_id=1, source_target_pairs={{0,448},{16,464},{32,480},{48,496},{64,384},{80,400},{96,416},{112... | collective-permute-start | bytes 200 | tf_op jit(solution)/shard_map/ppermute | solution.py:53
  81.5 1.3 collective-permute-start.22
  82.8 3.2 %collective-permute-done.21 = f32[16]{0:T(128)S(1)} collective-permute-done((f32[16]{0:T(128)S(1)}, f32[16]{0:T(128)S(1)}, u32[]{:S(2)}, u32[]{:S(2)}) %collective-permute-start.21) | collective-permute-done | bytes 96 | tf_op jit(solution)/shard_map/ppermute | solution.py:53
  88.6 1.3 collective-permute-start.25
  89.9 2.0 %collective-permute-done.25 = f32[1,1,132]{2,1,0:T(1,128)S(1)} collective-permute-done((f32[1,1,132]{2,1,0:T(1,128)S(1)}, f32[1,1,132]{2,1,0:T(1,128)S(1)}, u32[]{:S(2)}, u32[]{:S(2)}) %collective-permute-start.25) | collective-permute-done | bytes 560 | tf_op jit(solution)/shard_map/ppermute | solution.py:12
  92.0 3.6 %collective-permute-start.26 = (f32[1,3,132]{2,1,0:T(4,128)S(1)}, f32[1,3,132]{2,1,0:T(4,128)S(1)}, u32[]{:S(2)}, u32[]{:S(2)}) collective-permute-start(f32[1,3,132]{2,1,0:T(4,128)S(1)} %pad_maximum_fusion.4), channel_id=1, source_target_pairs={{0,16},{16,32},{32,48},{48,64},{64,80},{80,96},{96,112},{112,128},... | collective-permute-start | bytes 4760 | tf_op jit(solution)/shard_map/ppermute | solution.py:12
  95.5 2.3 %collective-permute-start.27 = (f32[1,3,132]{2,1,0:T(4,128)S(1)}, f32[1,3,132]{2,1,0:T(4,128)S(1)}, u32[]{:S(2)}, u32[]{:S(2)}) collective-permute-start(f32[1,3,132]{2,1,0:T(4,128)S(1)} %pad_maximum_fusion.4), channel_id=1, source_target_pairs={{16,0},{32,16},{48,32},{64,48},{80,64},{96,80},{112,96},{128,112},... | collective-permute-start | bytes 4760 | tf_op jit(solution)/shard_map/ppermute | solution.py:12
  98.1 6.3 %collective-permute-done.27 = f32[1,3,132]{2,1,0:T(4,128)S(1)} collective-permute-done((f32[1,3,132]{2,1,0:T(4,128)S(1)}, f32[1,3,132]{2,1,0:T(4,128)S(1)}, u32[]{:S(2)}, u32[]{:S(2)}) %collective-permute-start.27) | collective-permute-done | bytes 1616 | tf_op jit(solution)/shard_map/ppermute | solution.py:12
  107.8 1.9 %collective-permute-start.29 = (f32[1,1,16,68]{3,2,1,0:T(8,128)S(1)}, f32[1,1,16,68]{3,2,1,0:T(8,128)S(1)}, u32[]{:S(2)}, u32[]{:S(2)}) collective-permute-start(f32[1,1,16,68]{3,2,1,0:T(8,128)S(1)} %get-tuple-element.39), channel_id=1, source_target_pairs={{16,0},{32,16},{48,32},{64,48},{80,64},{96,80},{112,96},{128,112},... | collective-permute-start | bytes 13064 | tf_op jit(solution)/shard_map/ppermute | solution.py:12
  110.0 6.7 %collective-permute-done.29 = f32[1,1,16,68]{3,2,1,0:T(8,128)S(1)} collective-permute-done((f32[1,1,16,68]{3,2,1,0:T(8,128)S(1)}, f32[1,1,16,68]{3,2,1,0:T(8,128)S(1)}, u32[]{:S(2)}, u32[]{:S(2)}) %collective-permute-start.29) | collective-permute-done | bytes 4384 | tf_op jit(solution)/shard_map/ppermute | solution.py:12
  119.9 2.3 %collective-permute-start.30 = (f32[7,16]{1,0:T(8,128)S(1)}, f32[7,16]{1,0:T(8,128)S(1)}, u32[]{:S(2)}, u32[]{:S(2)}) collective-permute-start(f32[7,16]{1,0:T(8,128)S(1)} %stack.51), channel_id=1, source_target_pairs={{0,1},{1,0},{2,3},{3,2},{4,5},{5,4},{6,7},{7,6},{8,9},{9,8},{10,11... | collective-permute-start | bytes 1352 | tf_op jit(solution)/shard_map/ppermute | solution.py:108
  123.1 5.0 %collective-permute-start.31 = (f32[7,16]{1,0:T(8,128)S(1)}, f32[7,16]{1,0:T(8,128)S(1)}, u32[]{:S(2)}, u32[]{:S(2)}) collective-permute-start(f32[7,16]{1,0:T(8,128)S(1)} %stack.52), channel_id=1, source_target_pairs={{0,2},{1,3},{2,0},{3,1},{4,6},{5,7},{6,4},{7,5},{8,10},{9,11},{10,... | collective-permute-start | bytes 1352 | tf_op jit(solution)/shard_map/ppermute | solution.py:108
  128.1 1.6 collective-permute-done.31
  129.7 8.5 %collective-permute-start.32 = (f32[7,16]{1,0:T(8,128)S(1)}, f32[7,16]{1,0:T(8,128)S(1)}, u32[]{:S(2)}, u32[]{:S(2)}) collective-permute-start(f32[7,16]{1,0:T(8,128)S(1)} %stack.53), channel_id=1, source_target_pairs={{0,6},{1,7},{2,4},{3,5},{4,2},{5,3},{6,0},{7,1},{8,14},{9,15},{10,... | collective-permute-start | bytes 1352 | tf_op jit(solution)/shard_map/ppermute | solution.py:108
  138.3 1.6 collective-permute-done.32
  139.9 6.2 %collective-permute-start.33 = (f32[7,16]{1,0:T(8,128)S(1)}, f32[7,16]{1,0:T(8,128)S(1)}, u32[]{:S(2)}, u32[]{:S(2)}) collective-permute-start(f32[7,16]{1,0:T(8,128)S(1)} %stack.54), channel_id=1, source_target_pairs={{0,14},{1,15},{2,12},{3,13},{4,10},{5,11},{6,8},{7,9},{8,6},{9,7},... | collective-permute-start | bytes 1352 | tf_op jit(solution)/shard_map/ppermute | solution.py:108
  146.1 1.6 collective-permute-done.33
  147.8 1.9 %collective-permute-start.34 = (f32[7,16]{1,0:T(8,128)S(1)}, f32[7,16]{1,0:T(8,128)S(1)}, u32[]{:S(2)}, u32[]{:S(2)}) collective-permute-start(f32[7,16]{1,0:T(8,128)S(1)} %stack.55), channel_id=1, source_target_pairs={{0,16},{16,0},{32,48},{48,32},{64,80},{80,64},{96,112},{112,96},{1... | collective-permute-start | bytes 1352 | tf_op jit(solution)/shard_map/ppermute | solution.py:108
  149.7 3.6 %collective-permute-done.34 = f32[7,16]{1,0:T(8,128)S(1)} collective-permute-done((f32[7,16]{1,0:T(8,128)S(1)}, f32[7,16]{1,0:T(8,128)S(1)}, u32[]{:S(2)}, u32[]{:S(2)}) %collective-permute-start.34) | collective-permute-done | bytes 480 | tf_op jit(solution)/shard_map/ppermute | solution.py:108
  153.3 1.9 %collective-permute-start.35 = (f32[7,16]{1,0:T(8,128)S(1)}, f32[7,16]{1,0:T(8,128)S(1)}, u32[]{:S(2)}, u32[]{:S(2)}) collective-permute-start(f32[7,16]{1,0:T(8,128)S(1)} %stack.56), channel_id=1, source_target_pairs={{0,32},{16,48},{32,0},{48,16},{64,96},{80,112},{96,64},{112,80},{1... | collective-permute-start | bytes 1352 | tf_op jit(solution)/shard_map/ppermute | solution.py:108
  155.2 5.1 %collective-permute-done.35 = f32[7,16]{1,0:T(8,128)S(1)} collective-permute-done((f32[7,16]{1,0:T(8,128)S(1)}, f32[7,16]{1,0:T(8,128)S(1)}, u32[]{:S(2)}, u32[]{:S(2)}) %collective-permute-start.35) | collective-permute-done | bytes 480 | tf_op jit(solution)/shard_map/ppermute | solution.py:108
  160.4 1.9 %collective-permute-start.36 = (f32[7,16]{1,0:T(8,128)S(1)}, f32[7,16]{1,0:T(8,128)S(1)}, u32[]{:S(2)}, u32[]{:S(2)}) collective-permute-start(f32[7,16]{1,0:T(8,128)S(1)} %stack.57), channel_id=1, source_target_pairs={{0,64},{16,80},{32,96},{48,112},{64,0},{80,16},{96,32},{112,48},{1... | collective-permute-start | bytes 1352 | tf_op jit(solution)/shard_map/ppermute | solution.py:108
  162.3 3.6 %collective-permute-done.36 = f32[7,16]{1,0:T(8,128)S(1)} collective-permute-done((f32[7,16]{1,0:T(8,128)S(1)}, f32[7,16]{1,0:T(8,128)S(1)}, u32[]{:S(2)}, u32[]{:S(2)}) %collective-permute-start.36) | collective-permute-done | bytes 480 | tf_op jit(solution)/shard_map/ppermute | solution.py:108
  165.9 1.9 %collective-permute-start.37 = (f32[7,16]{1,0:T(8,128)S(1)}, f32[7,16]{1,0:T(8,128)S(1)}, u32[]{:S(2)}, u32[]{:S(2)}) collective-permute-start(f32[7,16]{1,0:T(8,128)S(1)} %stack.58), channel_id=1, source_target_pairs={{0,192},{16,208},{32,224},{48,240},{64,128},{80,144},{96,160},{112... | collective-permute-start | bytes 1352 | tf_op jit(solution)/shard_map/ppermute | solution.py:108
  167.9 5.4 %collective-permute-done.37 = f32[7,16]{1,0:T(8,128)S(1)} collective-permute-done((f32[7,16]{1,0:T(8,128)S(1)}, f32[7,16]{1,0:T(8,128)S(1)}, u32[]{:S(2)}, u32[]{:S(2)}) %collective-permute-start.37) | collective-permute-done | bytes 480 | tf_op jit(solution)/shard_map/ppermute | solution.py:108
  173.3 1.9 %collective-permute-start.38 = (f32[7,16]{1,0:T(8,128)S(1)}, f32[7,16]{1,0:T(8,128)S(1)}, u32[]{:S(2)}, u32[]{:S(2)}) collective-permute-start(f32[7,16]{1,0:T(8,128)S(1)} %stack.59), channel_id=1, source_target_pairs={{0,448},{16,464},{32,480},{48,496},{64,384},{80,400},{96,416},{112... | collective-permute-start | bytes 1352 | tf_op jit(solution)/shard_map/ppermute | solution.py:108
  175.2 4.8 %collective-permute-done.38 = f32[7,16]{1,0:T(8,128)S(1)} collective-permute-done((f32[7,16]{1,0:T(8,128)S(1)}, f32[7,16]{1,0:T(8,128)S(1)}, u32[]{:S(2)}, u32[]{:S(2)}) %collective-permute-start.38) | collective-permute-done | bytes 480 | tf_op jit(solution)/shard_map/ppermute | solution.py:108
  (172 shorter events, 19.2 us)
Async XLA Ops:
  0.6 11.2 %copy-start = (bf16[1,1,272,272]{3,2,1,0:T(8,128)(2,1)S(1)}, bf16[1,1,272,272]{3,2,1,0:T(8,128)(2,1)}, u32[]{:S(2)}) copy-start(bf16[1,1,272,272]{3,2,1,0:T(8,128)(2,1)} %param.17) | copy-start | bytes 443908
  0.6 0.8 copy-start.1
  0.7 0.8 copy-start.6
  1.6 0.7 copy-start.9
  4.9 6.1 %collective-permute-start.10 = (f32[2,1,1,16,68]{4,3,2,1,0:T(8,128)S(1)}, f32[2,1,1,16,68]{4,3,2,1,0:T(8,128)S(1)}, u32[]{:S(2)}, u32[]{:S(2)}) collective-permute-start(f32[2,1,1,16,68]{4,3,2,1,0:T(8,128)S(1)} %pad_maximum_fusion.1), channel_id=1, source_target_pairs={{0,16},{16,32},{32,48},{48,64},{64,80},{80,96},{96,112},{112,128},... | collective-permute-start | bytes 26120 | tf_op jit(solution)/shard_map/ppermute | solution.py:12
  9.5 2.3 %collective-permute-start.9 = (f32[2,1,1,16,68]{4,3,2,1,0:T(8,128)S(1)}, f32[2,1,1,16,68]{4,3,2,1,0:T(8,128)S(1)}, u32[]{:S(2)}, u32[]{:S(2)}) collective-permute-start(f32[2,1,1,16,68]{4,3,2,1,0:T(8,128)S(1)} %pad_maximum_fusion), channel_id=1, source_target_pairs={{0,1},{1,2},{2,3},{3,4},{4,5},{5,6},{6,7},{7,8},{8,9},{9,10},{10,1... | collective-permute-start | bytes 26120 | tf_op jit(solution)/shard_map/ppermute | solution.py:12
  12.1 5.5 %collective-permute-start.11 = (f32[1,1,16,68]{3,2,1,0:T(8,128)S(1)}, f32[1,1,16,68]{3,2,1,0:T(8,128)S(1)}, u32[]{:S(2)}, u32[]{:S(2)}) collective-permute-start(f32[1,1,16,68]{3,2,1,0:T(8,128)S(1)} %get-tuple-element.26), channel_id=1, source_target_pairs={{1,0},{2,1},{3,2},{4,3},{5,4},{6,5},{7,6},{8,7},{9,8},{10,9},{11,1... | collective-permute-start | bytes 13064 | tf_op jit(solution)/shard_map/ppermute | solution.py:12
  13.4 8.9 %collective-permute-start.12 = (f32[1,1,16,68]{3,2,1,0:T(8,128)S(1)}, f32[1,1,16,68]{3,2,1,0:T(8,128)S(1)}, u32[]{:S(2)}, u32[]{:S(2)}) collective-permute-start(f32[1,1,16,68]{3,2,1,0:T(8,128)S(1)} %get-tuple-element.27), channel_id=1, source_target_pairs={{16,0},{32,16},{48,32},{64,48},{80,64},{96,80},{112,96},{128,112},... | collective-permute-start | bytes 13064 | tf_op jit(solution)/shard_map/ppermute | solution.py:12
  22.5 33.8 %copy-start.12 = (f32[1,1,2,2]{3,2,1,0:T(2,128)S(1)}, f32[1,1,2,2]{3,2,1,0:T(2,128)}, u32[]{:S(2)}) copy-start(f32[1,1,2,2]{3,2,1,0:T(2,128)} %param.19) | copy-start | bytes 52
  22.6 75.2 %copy-start.2 = (bf16[1,1,272,272]{3,2,1,0:T(8,128)(2,1)S(1)}, bf16[1,1,272,272]{3,2,1,0:T(8,128)(2,1)}, u32[]{:S(2)}) copy-start(bf16[1,1,272,272]{3,2,1,0:T(8,128)(2,1)} %param.16) | copy-start | bytes 443908
  22.9 5.2 %collective-permute-start.13 = (f32[16]{0:T(128)S(1)}, f32[16]{0:T(128)S(1)}, u32[]{:S(2)}, u32[]{:S(2)}) collective-permute-start(f32[16]{0:T(128)S(1)} %get-tuple-element.145), channel_id=1, source_target_pairs={{0,1},{1,0},{2,3},{3,2},{4,5},{5,4},{6,7},{7,6},{8,9},{9,8},{10,11... | collective-permute-start | bytes 200 | tf_op jit(solution)/shard_map/ppermute | solution.py:53
  28.1 7.0 %collective-permute-start.14 = (f32[16]{0:T(128)S(1)}, f32[16]{0:T(128)S(1)}, u32[]{:S(2)}, u32[]{:S(2)}) collective-permute-start(f32[16]{0:T(128)S(1)} %add.2434), channel_id=1, source_target_pairs={{0,2},{1,3},{2,0},{3,1},{4,6},{5,7},{6,4},{7,5},{8,10},{9,11},{10,... | collective-permute-start | bytes 200 | tf_op jit(solution)/shard_map/ppermute | solution.py:53
  35.1 9.0 %collective-permute-start.15 = (f32[16]{0:T(128)S(1)}, f32[16]{0:T(128)S(1)}, u32[]{:S(2)}, u32[]{:S(2)}) collective-permute-start(f32[16]{0:T(128)S(1)} %add.2435), channel_id=1, source_target_pairs={{0,6},{1,7},{2,4},{3,5},{4,2},{5,3},{6,0},{7,1},{8,14},{9,15},{10,... | collective-permute-start | bytes 200 | tf_op jit(solution)/shard_map/ppermute | solution.py:53
  44.1 10.3 %collective-permute-start.16 = (f32[16]{0:T(128)S(1)}, f32[16]{0:T(128)S(1)}, u32[]{:S(2)}, u32[]{:S(2)}) collective-permute-start(f32[16]{0:T(128)S(1)} %add.2436), channel_id=1, source_target_pairs={{0,14},{1,15},{2,12},{3,13},{4,10},{5,11},{6,8},{7,9},{8,6},{9,7},... | collective-permute-start | bytes 200 | tf_op jit(solution)/shard_map/ppermute | solution.py:53
  54.4 5.4 %collective-permute-start.17 = (f32[16]{0:T(128)S(1)}, f32[16]{0:T(128)S(1)}, u32[]{:S(2)}, u32[]{:S(2)}) collective-permute-start(f32[16]{0:T(128)S(1)} %add.2437), channel_id=1, source_target_pairs={{0,16},{16,0},{32,48},{48,32},{64,80},{80,64},{96,112},{112,96},{1... | collective-permute-start | bytes 200 | tf_op jit(solution)/shard_map/ppermute | solution.py:53
  59.8 6.9 %collective-permute-start.18 = (f32[16]{0:T(128)S(1)}, f32[16]{0:T(128)S(1)}, u32[]{:S(2)}, u32[]{:S(2)}) collective-permute-start(f32[16]{0:T(128)S(1)} %add.2438), channel_id=1, source_target_pairs={{0,32},{16,48},{32,0},{48,16},{64,96},{80,112},{96,64},{112,80},{1... | collective-permute-start | bytes 200 | tf_op jit(solution)/shard_map/ppermute | solution.py:53
  66.8 5.4 %collective-permute-start.19 = (f32[16]{0:T(128)S(1)}, f32[16]{0:T(128)S(1)}, u32[]{:S(2)}, u32[]{:S(2)}) collective-permute-start(f32[16]{0:T(128)S(1)} %add.2439), channel_id=1, source_target_pairs={{0,64},{16,80},{32,96},{48,112},{64,0},{80,16},{96,32},{112,48},{1... | collective-permute-start | bytes 200 | tf_op jit(solution)/shard_map/ppermute | solution.py:53
  68.7 17.4 %collective-permute-start.23 = (f32[2,1,1,16,68]{4,3,2,1,0:T(8,128)S(1)}, f32[2,1,1,16,68]{4,3,2,1,0:T(8,128)S(1)}, u32[]{:S(2)}, u32[]{:S(2)}) collective-permute-start(f32[2,1,1,16,68]{4,3,2,1,0:T(8,128)S(1)} %stack.49), channel_id=1, source_target_pairs={{0,16},{16,32},{32,48},{48,64},{64,80},{80,96},{96,112},{112,128},... | collective-permute-start | bytes 26120 | tf_op jit(solution)/shard_map/ppermute | solution.py:12
  72.2 7.2 %collective-permute-start.20 = (f32[16]{0:T(128)S(1)}, f32[16]{0:T(128)S(1)}, u32[]{:S(2)}, u32[]{:S(2)}) collective-permute-start(f32[16]{0:T(128)S(1)} %add.2440), channel_id=1, source_target_pairs={{0,192},{16,208},{32,224},{48,240},{64,128},{80,144},{96,160},{112... | collective-permute-start | bytes 200 | tf_op jit(solution)/shard_map/ppermute | solution.py:53
  74.1 11.9 %copy-start.11 = (f32[16]{0:T(128)S(1)}, f32[16]{0:T(128)}, u32[]{:S(2)}) copy-start(f32[16]{0:T(128)} %param.15) | copy-start | bytes 196
  79.4 6.6 %collective-permute-start.21 = (f32[16]{0:T(128)S(1)}, f32[16]{0:T(128)S(1)}, u32[]{:S(2)}, u32[]{:S(2)}) collective-permute-start(f32[16]{0:T(128)S(1)} %add.2441), channel_id=1, source_target_pairs={{0,448},{16,464},{32,480},{48,496},{64,384},{80,400},{96,416},{112... | collective-permute-start | bytes 200 | tf_op jit(solution)/shard_map/ppermute | solution.py:53
  81.5 4.6 %collective-permute-start.22 = (f32[2,1,1,16,68]{4,3,2,1,0:T(8,128)S(1)}, f32[2,1,1,16,68]{4,3,2,1,0:T(8,128)S(1)}, u32[]{:S(2)}, u32[]{:S(2)}) collective-permute-start(f32[2,1,1,16,68]{4,3,2,1,0:T(8,128)S(1)} %stack.47), channel_id=1, source_target_pairs={{0,1},{1,2},{2,3},{3,4},{4,5},{5,6},{6,7},{7,8},{8,9},{9,10},{10,1... | collective-permute-start | bytes 26120 | tf_op jit(solution)/shard_map/ppermute | solution.py:12
  86.1 94.0 %copy-start.8 = (f32[16]{0:T(128)}, f32[16]{0:T(128)S(1)}, u32[]{:S(2)}) copy-start(f32[16]{0:T(128)S(1)} %get-tuple-element.144) | copy-start | bytes 196
  86.2 0.7 copy-start.7
  87.3 2.7 %collective-permute-start.24 = (f32[1,1,132]{2,1,0:T(1,128)S(1)}, f32[1,1,132]{2,1,0:T(1,128)S(1)}, u32[]{:S(2)}, u32[]{:S(2)}) collective-permute-start(f32[1,1,132]{2,1,0:T(1,128)S(1)} %constant_dynamic-update-slice_fusion), channel_id=1, source_target_pairs={{0,1},{1,2},{2,3},{3,4},{4,5},{5,6},{6,7},{7,8},{8,9},{9,10},{10,1... | collective-permute-start | bytes 1592 | tf_op jit(solution)/shard_map/ppermute | solution.py:12
  88.6 3.4 %collective-permute-start.25 = (f32[1,1,132]{2,1,0:T(1,128)S(1)}, f32[1,1,132]{2,1,0:T(1,128)S(1)}, u32[]{:S(2)}, u32[]{:S(2)}) collective-permute-start(f32[1,1,132]{2,1,0:T(1,128)S(1)} %constant_dynamic-update-slice_fusion), channel_id=1, source_target_pairs={{1,0},{2,1},{3,2},{4,3},{5,4},{6,5},{7,6},{8,7},{9,8},{10,9},{11,1... | collective-permute-start | bytes 1592 | tf_op jit(solution)/shard_map/ppermute | solution.py:12
  92.0 6.1 %collective-permute-start.26 = (f32[1,3,132]{2,1,0:T(4,128)S(1)}, f32[1,3,132]{2,1,0:T(4,128)S(1)}, u32[]{:S(2)}, u32[]{:S(2)}) collective-permute-start(f32[1,3,132]{2,1,0:T(4,128)S(1)} %pad_maximum_fusion.4), channel_id=1, source_target_pairs={{0,16},{16,32},{32,48},{48,64},{64,80},{80,96},{96,112},{112,128},... | collective-permute-start | bytes 4760 | tf_op jit(solution)/shard_map/ppermute | solution.py:12
  95.5 8.8 %collective-permute-start.27 = (f32[1,3,132]{2,1,0:T(4,128)S(1)}, f32[1,3,132]{2,1,0:T(4,128)S(1)}, u32[]{:S(2)}, u32[]{:S(2)}) collective-permute-start(f32[1,3,132]{2,1,0:T(4,128)S(1)} %pad_maximum_fusion.4), channel_id=1, source_target_pairs={{16,0},{32,16},{48,32},{64,48},{80,64},{96,80},{112,96},{128,112},... | collective-permute-start | bytes 4760 | tf_op jit(solution)/shard_map/ppermute | solution.py:12
  104.4 0.6 copy-start.4
  105.2 0.7 slice-start
  106.5 3.5 %collective-permute-start.28 = (f32[1,1,16,68]{3,2,1,0:T(8,128)S(1)}, f32[1,1,16,68]{3,2,1,0:T(8,128)S(1)}, u32[]{:S(2)}, u32[]{:S(2)}) collective-permute-start(f32[1,1,16,68]{3,2,1,0:T(8,128)S(1)} %get-tuple-element.38), channel_id=1, source_target_pairs={{1,0},{2,1},{3,2},{4,3},{5,4},{6,5},{7,6},{8,7},{9,8},{10,9},{11,1... | collective-permute-start | bytes 13064 | tf_op jit(solution)/shard_map/ppermute | solution.py:12
  107.8 8.9 %collective-permute-start.29 = (f32[1,1,16,68]{3,2,1,0:T(8,128)S(1)}, f32[1,1,16,68]{3,2,1,0:T(8,128)S(1)}, u32[]{:S(2)}, u32[]{:S(2)}) collective-permute-start(f32[1,1,16,68]{3,2,1,0:T(8,128)S(1)} %get-tuple-element.39), channel_id=1, source_target_pairs={{16,0},{32,16},{48,32},{64,48},{80,64},{96,80},{112,96},{128,112},... | collective-permute-start | bytes 13064 | tf_op jit(solution)/shard_map/ppermute | solution.py:12
  117.3 64.1 %copy-start.3 = (f32[1,1,16,136]{3,2,1,0:T(8,128)}, f32[1,1,16,136]{3,2,1,0:T(8,128)S(1)}, u32[]{:S(2)}) copy-start(f32[1,1,16,136]{3,2,1,0:T(8,128)S(1)} %get-tuple-element.142) | copy-start | bytes 26116
  119.9 3.1 %collective-permute-start.30 = (f32[7,16]{1,0:T(8,128)S(1)}, f32[7,16]{1,0:T(8,128)S(1)}, u32[]{:S(2)}, u32[]{:S(2)}) collective-permute-start(f32[7,16]{1,0:T(8,128)S(1)} %stack.51), channel_id=1, source_target_pairs={{0,1},{1,0},{2,3},{3,2},{4,5},{5,4},{6,7},{7,6},{8,9},{9,8},{10,11... | collective-permute-start | bytes 1352 | tf_op jit(solution)/shard_map/ppermute | solution.py:108
  123.1 6.6 %collective-permute-start.31 = (f32[7,16]{1,0:T(8,128)S(1)}, f32[7,16]{1,0:T(8,128)S(1)}, u32[]{:S(2)}, u32[]{:S(2)}) collective-permute-start(f32[7,16]{1,0:T(8,128)S(1)} %stack.52), channel_id=1, source_target_pairs={{0,2},{1,3},{2,0},{3,1},{4,6},{5,7},{6,4},{7,5},{8,10},{9,11},{10,... | collective-permute-start | bytes 1352 | tf_op jit(solution)/shard_map/ppermute | solution.py:108
  129.7 10.1 %collective-permute-start.32 = (f32[7,16]{1,0:T(8,128)S(1)}, f32[7,16]{1,0:T(8,128)S(1)}, u32[]{:S(2)}, u32[]{:S(2)}) collective-permute-start(f32[7,16]{1,0:T(8,128)S(1)} %stack.53), channel_id=1, source_target_pairs={{0,6},{1,7},{2,4},{3,5},{4,2},{5,3},{6,0},{7,1},{8,14},{9,15},{10,... | collective-permute-start | bytes 1352 | tf_op jit(solution)/shard_map/ppermute | solution.py:108
  139.9 7.8 %collective-permute-start.33 = (f32[7,16]{1,0:T(8,128)S(1)}, f32[7,16]{1,0:T(8,128)S(1)}, u32[]{:S(2)}, u32[]{:S(2)}) collective-permute-start(f32[7,16]{1,0:T(8,128)S(1)} %stack.54), channel_id=1, source_target_pairs={{0,14},{1,15},{2,12},{3,13},{4,10},{5,11},{6,8},{7,9},{8,6},{9,7},... | collective-permute-start | bytes 1352 | tf_op jit(solution)/shard_map/ppermute | solution.py:108
  147.8 5.5 %collective-permute-start.34 = (f32[7,16]{1,0:T(8,128)S(1)}, f32[7,16]{1,0:T(8,128)S(1)}, u32[]{:S(2)}, u32[]{:S(2)}) collective-permute-start(f32[7,16]{1,0:T(8,128)S(1)} %stack.55), channel_id=1, source_target_pairs={{0,16},{16,0},{32,48},{48,32},{64,80},{80,64},{96,112},{112,96},{1... | collective-permute-start | bytes 1352 | tf_op jit(solution)/shard_map/ppermute | solution.py:108
  153.3 7.0 %collective-permute-start.35 = (f32[7,16]{1,0:T(8,128)S(1)}, f32[7,16]{1,0:T(8,128)S(1)}, u32[]{:S(2)}, u32[]{:S(2)}) collective-permute-start(f32[7,16]{1,0:T(8,128)S(1)} %stack.56), channel_id=1, source_target_pairs={{0,32},{16,48},{32,0},{48,16},{64,96},{80,112},{96,64},{112,80},{1... | collective-permute-start | bytes 1352 | tf_op jit(solution)/shard_map/ppermute | solution.py:108
  160.4 5.5 %collective-permute-start.36 = (f32[7,16]{1,0:T(8,128)S(1)}, f32[7,16]{1,0:T(8,128)S(1)}, u32[]{:S(2)}, u32[]{:S(2)}) collective-permute-start(f32[7,16]{1,0:T(8,128)S(1)} %stack.57), channel_id=1, source_target_pairs={{0,64},{16,80},{32,96},{48,112},{64,0},{80,16},{96,32},{112,48},{1... | collective-permute-start | bytes 1352 | tf_op jit(solution)/shard_map/ppermute | solution.py:108
  165.9 7.3 %collective-permute-start.37 = (f32[7,16]{1,0:T(8,128)S(1)}, f32[7,16]{1,0:T(8,128)S(1)}, u32[]{:S(2)}, u32[]{:S(2)}) collective-permute-start(f32[7,16]{1,0:T(8,128)S(1)} %stack.58), channel_id=1, source_target_pairs={{0,192},{16,208},{32,224},{48,240},{64,128},{80,144},{96,160},{112... | collective-permute-start | bytes 1352 | tf_op jit(solution)/shard_map/ppermute | solution.py:108
  173.3 6.7 %collective-permute-start.38 = (f32[7,16]{1,0:T(8,128)S(1)}, f32[7,16]{1,0:T(8,128)S(1)}, u32[]{:S(2)}, u32[]{:S(2)}) collective-permute-start(f32[7,16]{1,0:T(8,128)S(1)} %stack.59), channel_id=1, source_target_pairs={{0,448},{16,464},{32,480},{48,496},{64,384},{80,400},{96,416},{112... | collective-permute-start | bytes 1352 | tf_op jit(solution)/shard_map/ppermute | solution.py:108
  180.0 1.4 copy-start.5
  182.1 0.5 copy-start.10

commit v7 on v6

--- a/solution.py
+++ b/solution.py
@@ -43,14 +43,15 @@
     return rounds
 
 
+def gathered(value, axis):
+    peers = lax.axis_size(axis)
+    copies = jnp.broadcast_to(value[None], (peers,) + value.shape)
+    return lax.all_to_all(copies, axis, 0, 0, tiled=False)
+
+
 def all_sum(value):
     for axis in ("py", "px"):
-        peers = lax.axis_size(axis)
-        if peers & (peers - 1):
-            value = lax.psum(value, axis)
-            continue
-        for pairs in butterfly_rounds(axis):
-            value = value + lax.ppermute(value, axis, pairs)
+        value = jnp.sum(gathered(value, axis), axis=0)
     return value
 
 
@@ -101,15 +102,22 @@
     return high[:, 0], low[:, 0]
 
 
+def df_tree_sum(high, low):
+    while high.shape[0] > 1:
+        if high.shape[0] % 2:
+            high = jnp.concatenate([high, jnp.zeros_like(high[:1])])
+            low = jnp.concatenate([low, jnp.zeros_like(low[:1])])
+        half = high.shape[0] // 2
+        high, low = df_add((high[:half], low[:half]), (high[half:], low[half:]))
+    return high[0], low[0]
+
+
 def all_sum_mixed(plain, pairs):
     for axis in ("py", "px"):
-        for partners in butterfly_rounds(axis):
-            packed = jnp.stack([plain] + [part for pair in pairs for part in pair])
-            other = lax.ppermute(packed, axis, partners)
-            plain = plain + other[0]
-            pairs = [
-                df_add(pair, (other[1 + 2 * k], other[2 + 2 * k])) for k, pair in enumerate(pairs)
-            ]
+        packed = jnp.stack([plain] + [part for pair in pairs for part in pair])
+        every = gathered(packed, axis)
+        plain = jnp.sum(every[:, 0], axis=0)
+        pairs = [df_tree_sum(every[:, 1 + 2 * k], every[:, 2 + 2 * k]) for k in range(len(pairs))]
     return plain, pairs
 
 

time: 184 us -> 133 us (0.72)
  the two profiles are of different devices: /device:TPU:30 before, /device:TPU:1 now
where the time goes in v7:
time: 133 us
  starting transfers between devices  55.7 us (42%)
  blocking collectives  38.2 us (29%)
  waiting for transfers between devices  21.4 us (16%)
  local copies, waits for them, and re-layouts  7.06 us (5%)
  other arithmetic  5.29 us (4%)
  between operations  3.97 us (3%)
    all_to_all x2, blocking collectives, gathered(): return lax.all_to_all(copies, axis, 0, 0, tiled=False)  38.2 us
    ppermute x12, starting transfers between devices, passed_along(): return lax.ppermute(value, axis, pairs)  31.8 us
    all_to_all x2, starting transfers between devices, gathered(): return lax.all_to_all(copies, axis, 0, 0, tiled=False)  23.9 us
    ppermute x12, waiting for transfers between devices, passed_along(): return lax.ppermute(value, axis, pairs)  13 us
    all_to_all x2, waiting for transfers between devices, gathered(): return lax.all_to_all(copies, axis, 0, 0, tiled=False)  8.4 us
    sub x48, other arithmetic, df_add(): return (high, error - (high - total))  2.69 us
  transfers between devices with their start and end apart: 14, of which 8 were waited for; matrix products, arithmetic and copies ran while one was open for 1% of the time, Pallas kernels for 0%

profile of v7, /device:TPU:1, one launch (start us, length us, event | category | flops | bytes accessed | tf_op | source)
XLA Modules:
  0.0 132.7 jit_solution(15253399470689806640)
XLA Ops:
  1.4 0.5 fusion.185
  3.6 0.1 copy.132
  4.3 3.9 %collective-permute-start.1 = (f32[2,1,1,16,68]{4,3,2,1,0:T(8,128)S(1)}, f32[2,1,1,16,68]{4,3,2,1,0:T(8,128)S(1)}, u32[]{:S(2)}, u32[]{:S(2)}) collective-permute-start(f32[2,1,1,16,68]{4,3,2,1,0:T(8,128)S(1)} %pad_maximum_fusion.1), channel_id=1, source_target_pairs={{0,16},{16,32},{32,48},{48,64},{64,80},{80,96},{96,112},{112,128},... | collective-permute-start | bytes 26120 | tf_op jit(solution)/shard_map/ppermute | solution.py:12
  8.2 4.8 %collective-permute-start = (f32[2,1,1,16,68]{4,3,2,1,0:T(8,128)S(1)}, f32[2,1,1,16,68]{4,3,2,1,0:T(8,128)S(1)}, u32[]{:S(2)}, u32[]{:S(2)}) collective-permute-start(f32[2,1,1,16,68]{4,3,2,1,0:T(8,128)S(1)} %pad_maximum_fusion), channel_id=1, source_target_pairs={{0,1},{1,2},{2,3},{3,4},{4,5},{5,6},{6,7},{7,8},{8,9},{9,10},{10,1... | collective-permute-start | bytes 26120 | tf_op jit(solution)/shard_map/ppermute | solution.py:12
  13.1 1.3 collective-permute-done
  14.4 0.2 fusion.2
  14.7 2.1 %collective-permute-start.2 = (f32[1,1,16,68]{3,2,1,0:T(8,128)S(1)}, f32[1,1,16,68]{3,2,1,0:T(8,128)S(1)}, u32[]{:S(2)}, u32[]{:S(2)}) collective-permute-start(f32[1,1,16,68]{3,2,1,0:T(8,128)S(1)} %get-tuple-element.26), channel_id=1, source_target_pairs={{1,0},{2,1},{3,2},{4,3},{5,4},{6,5},{7,6},{8,7},{9,8},{10,9},{11,1... | collective-permute-start | bytes 13064 | tf_op jit(solution)/shard_map/ppermute | solution.py:12
  16.8 1.3 collective-permute-start.3
  18.1 0.1 copy.146
  18.4 1.3 collective-permute-done.2
  19.7 1.6 %collective-permute-done.3 = f32[1,1,16,68]{3,2,1,0:T(8,128)S(1)} collective-permute-done((f32[1,1,16,68]{3,2,1,0:T(8,128)S(1)}, f32[1,1,16,68]{3,2,1,0:T(8,128)S(1)}, u32[]{:S(2)}, u32[]{:S(2)}) %collective-permute-start.3) | collective-permute-done | bytes 4384 | tf_op jit(solution)/shard_map/ppermute | solution.py:12
  21.8 0.2 multiply_reduce_fusion.2
  21.9 0.6 broadcast_in_dim.124
  22.6 12.2 %all-to-all-start.2 = ((f32[16,1,16]{2,1,0:T(1,128)}), f32[16,1,16]{2,1,0:T(1,128)S(1)}, u32[]{:S(2)}, u32[]{:S(2)}) async-start(f32[16,1,16]{2,1,0:T(1,128)} %broadcast_in_dim.124), calls=%async_computation.2 | async-start | bytes 16384 | tf_op jit(solution)/shard_map/all_to_all | solution.py:49
  34.8 3.1 %collective-permute-start.5 = (f32[2,1,1,16,68]{4,3,2,1,0:T(8,128)S(1)}, f32[2,1,1,16,68]{4,3,2,1,0:T(8,128)S(1)}, u32[]{:S(2)}, u32[]{:S(2)}) collective-permute-start(f32[2,1,1,16,68]{4,3,2,1,0:T(8,128)S(1)} %stack.51), channel_id=1, source_target_pairs={{0,16},{16,32},{32,48},{48,64},{64,80},{80,96},{96,112},{112,128},... | collective-permute-start | bytes 26120 | tf_op jit(solution)/shard_map/ppermute | solution.py:12
  37.9 3.8 %collective-permute-start.4 = (f32[2,1,1,16,68]{4,3,2,1,0:T(8,128)S(1)}, f32[2,1,1,16,68]{4,3,2,1,0:T(8,128)S(1)}, u32[]{:S(2)}, u32[]{:S(2)}) collective-permute-start(f32[2,1,1,16,68]{4,3,2,1,0:T(8,128)S(1)} %stack.49), channel_id=1, source_target_pairs={{0,1},{1,2},{2,3},{3,4},{4,5},{5,6},{6,7},{7,8},{8,9},{9,10},{10,1... | collective-permute-start | bytes 26120 | tf_op jit(solution)/shard_map/ppermute | solution.py:12
  41.8 0.6 broadcast_in_dim.125
  42.4 11.7 %all-to-all-start.3 = ((f32[32,1,16]{2,1,0:T(1,128)}), f32[32,1,16]{2,1,0:T(1,128)S(1)}, u32[]{:S(2)}, u32[]{:S(2)}) async-start(f32[32,1,16]{2,1,0:T(1,128)} %broadcast_in_dim.125), calls=%async_computation.3 | async-start | bytes 32768 | tf_op jit(solution)/shard_map/all_to_all | solution.py:49
  54.2 8.4 %all-to-all-done.3 = f32[32,1,16]{2,1,0:T(1,128)S(1)} async-done(((f32[32,1,16]{2,1,0:T(1,128)}), f32[32,1,16]{2,1,0:T(1,128)S(1)}, u32[]{:S(2)}, u32[]{:S(2)}) %all-to-all-start.3) | async-done | bytes 2080 | tf_op jit(solution)/shard_map/all_to_all | solution.py:49
  62.8 0.7 copy-done.7
  63.5 0.2 convolution_multiply_fusion.2
  63.9 4.1 %collective-permute-start.6 = (f32[1,1,132]{2,1,0:T(1,128)S(1)}, f32[1,1,132]{2,1,0:T(1,128)S(1)}, u32[]{:S(2)}, u32[]{:S(2)}) collective-permute-start(f32[1,1,132]{2,1,0:T(1,128)S(1)} %constant_dynamic-update-slice_fusion), channel_id=1, source_target_pairs={{0,1},{1,2},{2,3},{3,4},{4,5},{5,6},{6,7},{7,8},{8,9},{9,10},{10,1... | collective-permute-start | bytes 1592 | tf_op jit(solution)/shard_map/ppermute | solution.py:12
  68.0 1.9 %collective-permute-start.7 = (f32[1,1,132]{2,1,0:T(1,128)S(1)}, f32[1,1,132]{2,1,0:T(1,128)S(1)}, u32[]{:S(2)}, u32[]{:S(2)}) collective-permute-start(f32[1,1,132]{2,1,0:T(1,128)S(1)} %constant_dynamic-update-slice_fusion), channel_id=1, source_target_pairs={{1,0},{2,1},{3,2},{4,3},{5,4},{6,5},{7,6},{8,7},{9,8},{10,9},{11,1... | collective-permute-start | bytes 1592 | tf_op jit(solution)/shard_map/ppermute | solution.py:12
  70.0 2.9 %collective-permute-done.7 = f32[1,1,132]{2,1,0:T(1,128)S(1)} collective-permute-done((f32[1,1,132]{2,1,0:T(1,128)S(1)}, f32[1,1,132]{2,1,0:T(1,128)S(1)}, u32[]{:S(2)}, u32[]{:S(2)}) %collective-permute-start.7) | collective-permute-done | bytes 560 | tf_op jit(solution)/shard_map/ppermute | solution.py:12
  72.9 2.2 %collective-permute-start.8 = (f32[1,3,132]{2,1,0:T(4,128)S(1)}, f32[1,3,132]{2,1,0:T(4,128)S(1)}, u32[]{:S(2)}, u32[]{:S(2)}) collective-permute-start(f32[1,3,132]{2,1,0:T(4,128)S(1)} %pad_maximum_fusion.4), channel_id=1, source_target_pairs={{0,16},{16,32},{32,48},{48,64},{64,80},{80,96},{96,112},{112,128},... | collective-permute-start | bytes 4760 | tf_op jit(solution)/shard_map/ppermute | solution.py:12
  75.1 1.3 collective-permute-start.9
  76.4 0.2 convolution_multiply_fusion
  76.6 2.8 %collective-permute-done.9 = f32[1,3,132]{2,1,0:T(4,128)S(1)} collective-permute-done((f32[1,3,132]{2,1,0:T(4,128)S(1)}, f32[1,3,132]{2,1,0:T(4,128)S(1)}, u32[]{:S(2)}, u32[]{:S(2)}) %collective-permute-start.9) | collective-permute-done | bytes 1616 | tf_op jit(solution)/shard_map/ppermute | solution.py:12
  79.5 0.6 copy-done.4
  80.1 0.1 copy.151
  80.3 0.1 copy.179
  80.4 0.6 slice-done
  81.0 0.1 reshape.580
  81.1 0.3 fusion.6
  81.3 0.2 fusion.1
  81.6 1.9 %collective-permute-start.10 = (f32[1,1,16,68]{3,2,1,0:T(8,128)S(1)}, f32[1,1,16,68]{3,2,1,0:T(8,128)S(1)}, u32[]{:S(2)}, u32[]{:S(2)}) collective-permute-start(f32[1,1,16,68]{3,2,1,0:T(8,128)S(1)} %get-tuple-element.38), channel_id=1, source_target_pairs={{1,0},{2,1},{3,2},{4,3},{5,4},{6,5},{7,6},{8,7},{9,8},{10,9},{11,1... | collective-permute-start | bytes 13064 | tf_op jit(solution)/shard_map/ppermute | solution.py:12
  83.6 1.3 collective-permute-start.11
  84.9 1.7 %collective-permute-done.10 = f32[1,1,16,68]{3,2,1,0:T(8,128)S(1)} collective-permute-done((f32[1,1,16,68]{3,2,1,0:T(8,128)S(1)}, f32[1,1,16,68]{3,2,1,0:T(8,128)S(1)}, u32[]{:S(2)}, u32[]{:S(2)}) %collective-permute-start.10) | collective-permute-done | bytes 4384 | tf_op jit(solution)/shard_map/ppermute | solution.py:12
  86.6 1.4 %collective-permute-done.11 = f32[1,1,16,68]{3,2,1,0:T(8,128)S(1)} collective-permute-done((f32[1,1,16,68]{3,2,1,0:T(8,128)S(1)}, f32[1,1,16,68]{3,2,1,0:T(8,128)S(1)}, u32[]{:S(2)}, u32[]{:S(2)}) %collective-permute-start.11) | collective-permute-done | bytes 4384 | tf_op jit(solution)/shard_map/ppermute | solution.py:12
  88.4 0.2 multiply_reduce_fusion.1
  89.3 0.2 subtract_reduce_fusion
  90.1 0.2 subtract_reduce_fusion.1
  90.9 0.2 subtract_reduce_fusion.2
  91.1 17.7 %all_to_all.34 = f32[16,7,16]{2,1,0:T(8,128)S(1)} all-to-all(f32[16,7,16]{2,1,0:T(8,128)S(1)} %broadcast_in_dim.126), channel_id=1, replica_groups=mesh['px'=32,'py'=16] {'py'}, dimensions={0} | all-to-all | bytes 14336 | tf_op jit(solution)/shard_map/all_to_all | solution.py:49
  109.3 20.4 %all_to_all.35 = f32[32,7,16]{2,1,0:T(8,128)S(1)} all-to-all(f32[32,7,16]{2,1,0:T(8,128)S(1)} %broadcast_in_dim.127), channel_id=1, replica_groups=mesh['px'=32,'py'=16] {'px'}, dimensions={0} | all-to-all | bytes 28672 | tf_op jit(solution)/shard_map/all_to_all | solution.py:49
  130.1 0.7 and_reduce_fusion
  131.5 0.7 multiply_subtract_fusion
  132.2 0.5 copy-done.10
  (150 shorter events, 5.4 us)
Async XLA Ops:
  0.6 13.8 %copy-start = (bf16[1,1,272,272]{3,2,1,0:T(8,128)(2,1)S(1)}, bf16[1,1,272,272]{3,2,1,0:T(8,128)(2,1)}, u32[]{:S(2)}) copy-start(bf16[1,1,272,272]{3,2,1,0:T(8,128)(2,1)} %param.17) | copy-start | bytes 443908
  0.7 0.7 copy-start.9
  0.7 2.6 %copy-start.1 = (f32[1,1,16,136]{3,2,1,0:T(8,128)S(1)}, f32[1,1,16,136]{3,2,1,0:T(8,128)}, u32[]{:S(2)}) copy-start(f32[1,1,16,136]{3,2,1,0:T(8,128)} %param.13) | copy-start | bytes 26116
  0.7 2.6 %copy-start.6 = (f32[1,1,16,136]{3,2,1,0:T(8,128)S(1)}, f32[1,1,16,136]{3,2,1,0:T(8,128)}, u32[]{:S(2)}) copy-start(f32[1,1,16,136]{3,2,1,0:T(8,128)} %param.14) | copy-start | bytes 26116
  4.3 8.8 %collective-permute-start.1 = (f32[2,1,1,16,68]{4,3,2,1,0:T(8,128)S(1)}, f32[2,1,1,16,68]{4,3,2,1,0:T(8,128)S(1)}, u32[]{:S(2)}, u32[]{:S(2)}) collective-permute-start(f32[2,1,1,16,68]{4,3,2,1,0:T(8,128)S(1)} %pad_maximum_fusion.1), channel_id=1, source_target_pairs={{0,16},{16,32},{32,48},{48,64},{64,80},{80,96},{96,112},{112,128},... | collective-permute-start | bytes 26120 | tf_op jit(solution)/shard_map/ppermute | solution.py:12
  8.2 6.2 %collective-permute-start = (f32[2,1,1,16,68]{4,3,2,1,0:T(8,128)S(1)}, f32[2,1,1,16,68]{4,3,2,1,0:T(8,128)S(1)}, u32[]{:S(2)}, u32[]{:S(2)}) collective-permute-start(f32[2,1,1,16,68]{4,3,2,1,0:T(8,128)S(1)} %pad_maximum_fusion), channel_id=1, source_target_pairs={{0,1},{1,2},{2,3},{3,4},{4,5},{5,6},{6,7},{7,8},{8,9},{9,10},{10,1... | collective-permute-start | bytes 26120 | tf_op jit(solution)/shard_map/ppermute | solution.py:12
  14.7 5.0 %collective-permute-start.2 = (f32[1,1,16,68]{3,2,1,0:T(8,128)S(1)}, f32[1,1,16,68]{3,2,1,0:T(8,128)S(1)}, u32[]{:S(2)}, u32[]{:S(2)}) collective-permute-start(f32[1,1,16,68]{3,2,1,0:T(8,128)S(1)} %get-tuple-element.26), channel_id=1, source_target_pairs={{1,0},{2,1},{3,2},{4,3},{5,4},{6,5},{7,6},{8,7},{9,8},{10,9},{11,1... | collective-permute-start | bytes 13064 | tf_op jit(solution)/shard_map/ppermute | solution.py:12
  16.8 4.5 %collective-permute-start.3 = (f32[1,1,16,68]{3,2,1,0:T(8,128)S(1)}, f32[1,1,16,68]{3,2,1,0:T(8,128)S(1)}, u32[]{:S(2)}, u32[]{:S(2)}) collective-permute-start(f32[1,1,16,68]{3,2,1,0:T(8,128)S(1)} %get-tuple-element.27), channel_id=1, source_target_pairs={{16,0},{32,16},{48,32},{64,48},{80,64},{96,80},{112,96},{128,112},... | collective-permute-start | bytes 13064 | tf_op jit(solution)/shard_map/ppermute | solution.py:12
  21.7 32.4 %copy-start.11 = (f32[1,1,2,2]{3,2,1,0:T(2,128)S(1)}, f32[1,1,2,2]{3,2,1,0:T(2,128)}, u32[]{:S(2)}) copy-start(f32[1,1,2,2]{3,2,1,0:T(2,128)} %param.19) | copy-start | bytes 52
  21.8 54.7 %copy-start.2 = (bf16[1,1,272,272]{3,2,1,0:T(8,128)(2,1)S(1)}, bf16[1,1,272,272]{3,2,1,0:T(8,128)(2,1)}, u32[]{:S(2)}) copy-start(bf16[1,1,272,272]{3,2,1,0:T(8,128)(2,1)} %param.16) | copy-start | bytes 443908
  22.6 19.2 %all-to-all-start.2 = ((f32[16,1,16]{2,1,0:T(1,128)}), f32[16,1,16]{2,1,0:T(1,128)S(1)}, u32[]{:S(2)}, u32[]{:S(2)}) async-start(f32[16,1,16]{2,1,0:T(1,128)} %broadcast_in_dim.124), calls=%async_computation.2 | async-start | bytes 16384 | tf_op jit(solution)/shard_map/all_to_all | solution.py:49
  34.8 27.9 %collective-permute-start.5 = (f32[2,1,1,16,68]{4,3,2,1,0:T(8,128)S(1)}, f32[2,1,1,16,68]{4,3,2,1,0:T(8,128)S(1)}, u32[]{:S(2)}, u32[]{:S(2)}) collective-permute-start(f32[2,1,1,16,68]{4,3,2,1,0:T(8,128)S(1)} %stack.51), channel_id=1, source_target_pairs={{0,16},{16,32},{32,48},{48,64},{64,80},{80,96},{96,112},{112,128},... | collective-permute-start | bytes 26120 | tf_op jit(solution)/shard_map/ppermute | solution.py:12
  37.9 24.7 %collective-permute-start.4 = (f32[2,1,1,16,68]{4,3,2,1,0:T(8,128)S(1)}, f32[2,1,1,16,68]{4,3,2,1,0:T(8,128)S(1)}, u32[]{:S(2)}, u32[]{:S(2)}) collective-permute-start(f32[2,1,1,16,68]{4,3,2,1,0:T(8,128)S(1)} %stack.49), channel_id=1, source_target_pairs={{0,1},{1,2},{2,3},{3,4},{4,5},{5,6},{6,7},{7,8},{8,9},{9,10},{10,1... | collective-permute-start | bytes 26120 | tf_op jit(solution)/shard_map/ppermute | solution.py:12
  42.4 20.2 %all-to-all-start.3 = ((f32[32,1,16]{2,1,0:T(1,128)}), f32[32,1,16]{2,1,0:T(1,128)S(1)}, u32[]{:S(2)}, u32[]{:S(2)}) async-start(f32[32,1,16]{2,1,0:T(1,128)} %broadcast_in_dim.125), calls=%async_computation.3 | async-start | bytes 32768 | tf_op jit(solution)/shard_map/all_to_all | solution.py:49
  54.2 8.5 %copy-start.12 = (f32[16]{0:T(128)S(1)}, f32[16]{0:T(128)}, u32[]{:S(2)}) copy-start(f32[16]{0:T(128)} %param.15) | copy-start | bytes 196
  62.6 67.5 %copy-start.8 = (f32[16]{0:T(128)}, f32[16]{0:T(128)S(1)}, u32[]{:S(2)}) copy-start(f32[16]{0:T(128)S(1)} %reduce_sum.83) | copy-start | bytes 196
  62.8 0.7 copy-start.7
  63.9 6.1 %collective-permute-start.6 = (f32[1,1,132]{2,1,0:T(1,128)S(1)}, f32[1,1,132]{2,1,0:T(1,128)S(1)}, u32[]{:S(2)}, u32[]{:S(2)}) collective-permute-start(f32[1,1,132]{2,1,0:T(1,128)S(1)} %constant_dynamic-update-slice_fusion), channel_id=1, source_target_pairs={{0,1},{1,2},{2,3},{3,4},{4,5},{5,6},{6,7},{7,8},{8,9},{9,10},{10,1... | collective-permute-start | bytes 1592 | tf_op jit(solution)/shard_map/ppermute | solution.py:12
  68.0 4.9 %collective-permute-start.7 = (f32[1,1,132]{2,1,0:T(1,128)S(1)}, f32[1,1,132]{2,1,0:T(1,128)S(1)}, u32[]{:S(2)}, u32[]{:S(2)}) collective-permute-start(f32[1,1,132]{2,1,0:T(1,128)S(1)} %constant_dynamic-update-slice_fusion), channel_id=1, source_target_pairs={{1,0},{2,1},{3,2},{4,3},{5,4},{6,5},{7,6},{8,7},{9,8},{10,9},{11,1... | collective-permute-start | bytes 1592 | tf_op jit(solution)/shard_map/ppermute | solution.py:12
  72.9 3.7 %collective-permute-start.8 = (f32[1,3,132]{2,1,0:T(4,128)S(1)}, f32[1,3,132]{2,1,0:T(4,128)S(1)}, u32[]{:S(2)}, u32[]{:S(2)}) collective-permute-start(f32[1,3,132]{2,1,0:T(4,128)S(1)} %pad_maximum_fusion.4), channel_id=1, source_target_pairs={{0,16},{16,32},{32,48},{48,64},{64,80},{80,96},{96,112},{112,128},... | collective-permute-start | bytes 4760 | tf_op jit(solution)/shard_map/ppermute | solution.py:12
  75.1 4.4 %collective-permute-start.9 = (f32[1,3,132]{2,1,0:T(4,128)S(1)}, f32[1,3,132]{2,1,0:T(4,128)S(1)}, u32[]{:S(2)}, u32[]{:S(2)}) collective-permute-start(f32[1,3,132]{2,1,0:T(4,128)S(1)} %pad_maximum_fusion.4), channel_id=1, source_target_pairs={{16,0},{32,16},{48,32},{64,48},{80,64},{96,80},{112,96},{128,112},... | collective-permute-start | bytes 4760 | tf_op jit(solution)/shard_map/ppermute | solution.py:12
  79.5 0.6 copy-start.4
  80.3 0.7 slice-start
  81.6 5.0 %collective-permute-start.10 = (f32[1,1,16,68]{3,2,1,0:T(8,128)S(1)}, f32[1,1,16,68]{3,2,1,0:T(8,128)S(1)}, u32[]{:S(2)}, u32[]{:S(2)}) collective-permute-start(f32[1,1,16,68]{3,2,1,0:T(8,128)S(1)} %get-tuple-element.38), channel_id=1, source_target_pairs={{1,0},{2,1},{3,2},{4,3},{5,4},{6,5},{7,6},{8,7},{9,8},{10,9},{11,1... | collective-permute-start | bytes 13064 | tf_op jit(solution)/shard_map/ppermute | solution.py:12
  83.6 4.4 %collective-permute-start.11 = (f32[1,1,16,68]{3,2,1,0:T(8,128)S(1)}, f32[1,1,16,68]{3,2,1,0:T(8,128)S(1)}, u32[]{:S(2)}, u32[]{:S(2)}) collective-permute-start(f32[1,1,16,68]{3,2,1,0:T(8,128)S(1)} %get-tuple-element.39), channel_id=1, source_target_pairs={{16,0},{32,16},{48,32},{64,48},{80,64},{96,80},{112,96},{128,112},... | collective-permute-start | bytes 13064 | tf_op jit(solution)/shard_map/ppermute | solution.py:12
  88.6 42.8 %copy-start.3 = (f32[1,1,16,136]{3,2,1,0:T(8,128)}, f32[1,1,16,136]{3,2,1,0:T(8,128)S(1)}, u32[]{:S(2)}) copy-start(f32[1,1,16,136]{3,2,1,0:T(8,128)S(1)} %get-tuple-element.142) | copy-start | bytes 26116
  130.1 1.4 %copy-start.5 = (f32[1,1,16,136]{3,2,1,0:T(8,128)S(1)}, f32[1,1,16,136]{3,2,1,0:T(8,128)}, u32[]{:S(2)}) copy-start(f32[1,1,16,136]{3,2,1,0:T(8,128)} %param.12) | copy-start | bytes 26116
  132.2 0.5 copy-start.10

commit v8 on v7

--- a/solution.py
+++ b/solution.py
@@ -1,3 +1,5 @@
+import math
+
 import jax
 import jax.numpy as jnp
 from jax import lax
@@ -44,15 +46,13 @@
 
 
 def gathered(value, axis):
-    peers = lax.axis_size(axis)
+    peers = lax.axis_size(axis) if isinstance(axis, str) else math.prod(lax.axis_size(a) for a in axis)
     copies = jnp.broadcast_to(value[None], (peers,) + value.shape)
     return lax.all_to_all(copies, axis, 0, 0, tiled=False)
 
 
 def all_sum(value):
-    for axis in ("py", "px"):
-        value = jnp.sum(gathered(value, axis), axis=0)
-    return value
+    return jnp.sum(gathered(value, ("px", "py")), axis=0)
 
 
 def two_sum(a, b):
@@ -113,11 +113,10 @@
 
 
 def all_sum_mixed(plain, pairs):
-    for axis in ("py", "px"):
-        packed = jnp.stack([plain] + [part for pair in pairs for part in pair])
-        every = gathered(packed, axis)
-        plain = jnp.sum(every[:, 0], axis=0)
-        pairs = [df_tree_sum(every[:, 1 + 2 * k], every[:, 2 + 2 * k]) for k in range(len(pairs))]
+    packed = jnp.stack([plain] + [part for pair in pairs for part in pair])
+    every = gathered(packed, ("px", "py"))
+    plain = jnp.sum(every[:, 0], axis=0)
+    pairs = [df_tree_sum(every[:, 1 + 2 * k], every[:, 2 + 2 * k]) for k in range(len(pairs))]
     return plain, pairs
 
 

time: 133 us -> 188 us (1.41)
  blocking collectives: 38.2 us -> 74.9 us
  waiting for transfers between devices: 21.4 us -> 30.2 us
  local copies, waits for them, and re-layouts: 7.06 us -> 13.5 us
  other arithmetic: 5.29 us -> 10.1 us
  starting transfers between devices: 55.7 us -> 53.7 us
    all_to_all x2 -> x1, blocking collectives: 38.2 us -> 74.9 us  [gathered(): return lax.all_to_all(copies, axis, 0, 0, tiled=False)]
    all_to_all x2 -> x1, waiting for transfers between devices: 8.4 us -> 17.2 us  [gathered(): return lax.all_to_all(copies, axis, 0, 0, tiled=False)]
    unnamed x28 -> x34, local copies, waits for them, and re-layouts: 1.94 us -> 6.41 us
    slice x1, local copies, waits for them, and re-layouts: 0.04 us -> 2.15 us  [df_tree_sum(): high, low = df_add((high[:half], low[:half]), (high[half:], low[half:]))]
    all_to_all x2 -> x1, starting transfers between devices: 23.9 us -> 22.2 us  [gathered(): return lax.all_to_all(copies, axis, 0, 0, tiled=False)]
    sub x48 -> x45, other arithmetic: 2.69 us -> 3.92 us  [df_add(): return (high, error - (high - total))]
  transfers between devices with their start and end apart: 14 -> 13, of which waited for: 8 -> 8; matrix products, arithmetic and copies ran while one was open for 1% -> 1% of each run, Pallas kernels for 0% -> 0%
where the time goes in v8:
time: 188 us; the launch traced here: 187 us
  blocking collectives  74.9 us (40%)
  starting transfers between devices  53.7 us (29%)
  waiting for transfers between devices  30.2 us (16%)
  local copies, waits for them, and re-layouts  13.5 us (7%)
  other arithmetic  10.1 us (5%)
  between operations  3.97 us (2%)
    all_to_all x1, blocking collectives, gathered(): return lax.all_to_all(copies, axis, 0, 0, tiled=False)  74.9 us
    ppermute x12, starting transfers between devices, passed_along(): return lax.ppermute(value, axis, pairs)  31.5 us
    all_to_all x1, starting transfers between devices, gathered(): return lax.all_to_all(copies, axis, 0, 0, tiled=False)  22.2 us
    all_to_all x1, waiting for transfers between devices, gathered(): return lax.all_to_all(copies, axis, 0, 0, tiled=False)  17.2 us
    ppermute x12, waiting for transfers between devices, passed_along(): return lax.ppermute(value, axis, pairs)  13 us
    unnamed x34, local copies, waits for them, and re-layouts  6.41 us
    sub x45, other arithmetic, df_add(): return (high, error - (high - total))  3.92 us
  transfers between devices with their start and end apart: 13, of which 8 were waited for; matrix products, arithmetic and copies ran while one was open for 1% of the time, Pallas kernels for 0%

profile of v8, /device:TPU:1, one launch (start us, length us, event | category | flops | bytes accessed | tf_op | source)
XLA Modules:
  0.0 187.5 jit_solution(8603282896969950484)
XLA Ops:
  1.5 1.3 fusion.206
  4.1 0.7 convert_bitcast_fusion
  5.8 3.9 %collective-permute-start.1 = (f32[2,1,1,16,68]{4,3,2,1,0:T(8,128)S(1)}, f32[2,1,1,16,68]{4,3,2,1,0:T(8,128)S(1)}, u32[]{:S(2)}, u32[]{:S(2)}) collective-permute-start(f32[2,1,1,16,68]{4,3,2,1,0:T(8,128)S(1)} %pad_maximum_fusion.1), channel_id=1, source_target_pairs={{0,16},{16,32},{32,48},{48,64},{64,80},{80,96},{96,112},{112,128},... | collective-permute-start | bytes 26120 | tf_op jit(solution)/shard_map/ppermute | solution.py:14
  9.8 4.8 %collective-permute-start = (f32[2,1,1,16,68]{4,3,2,1,0:T(8,128)S(1)}, f32[2,1,1,16,68]{4,3,2,1,0:T(8,128)S(1)}, u32[]{:S(2)}, u32[]{:S(2)}) collective-permute-start(f32[2,1,1,16,68]{4,3,2,1,0:T(8,128)S(1)} %pad_maximum_fusion), channel_id=1, source_target_pairs={{0,1},{1,2},{2,3},{3,4},{4,5},{5,6},{6,7},{7,8},{8,9},{9,10},{10,1... | collective-permute-start | bytes 26120 | tf_op jit(solution)/shard_map/ppermute | solution.py:14
  14.7 1.3 collective-permute-done
  16.0 0.2 fusion.2
  16.3 2.1 %collective-permute-start.2 = (f32[1,1,16,68]{3,2,1,0:T(8,128)S(1)}, f32[1,1,16,68]{3,2,1,0:T(8,128)S(1)}, u32[]{:S(2)}, u32[]{:S(2)}) collective-permute-start(f32[1,1,16,68]{3,2,1,0:T(8,128)S(1)} %get-tuple-element.26), channel_id=1, source_target_pairs={{1,0},{2,1},{3,2},{4,3},{5,4},{6,5},{7,6},{8,7},{9,8},{10,9},{11,1... | collective-permute-start | bytes 13064 | tf_op jit(solution)/shard_map/ppermute | solution.py:14
  18.3 1.3 collective-permute-start.3
  20.0 1.3 collective-permute-done.2
  21.3 1.6 collective-permute-done.3
  23.3 3.2 %collective-permute-start.5 = (f32[2,1,1,16,68]{4,3,2,1,0:T(8,128)S(1)}, f32[2,1,1,16,68]{4,3,2,1,0:T(8,128)S(1)}, u32[]{:S(2)}, u32[]{:S(2)}) collective-permute-start(f32[2,1,1,16,68]{4,3,2,1,0:T(8,128)S(1)} %stack.45), channel_id=1, source_target_pairs={{0,16},{16,32},{32,48},{48,64},{64,80},{80,96},{96,112},{112,128},... | collective-permute-start | bytes 26120 | tf_op jit(solution)/shard_map/ppermute | solution.py:14
  26.6 4.7 %collective-permute-start.4 = (f32[2,1,1,16,68]{4,3,2,1,0:T(8,128)S(1)}, f32[2,1,1,16,68]{4,3,2,1,0:T(8,128)S(1)}, u32[]{:S(2)}, u32[]{:S(2)}) collective-permute-start(f32[2,1,1,16,68]{4,3,2,1,0:T(8,128)S(1)} %stack.43), channel_id=1, source_target_pairs={{0,1},{1,2},{2,3},{3,4},{4,5},{5,6},{6,7},{7,8},{8,9},{9,10},{10,1... | collective-permute-start | bytes 26120 | tf_op jit(solution)/shard_map/ppermute | solution.py:14
  31.5 0.8 broadcast_in_dim.106
  32.4 22.2 %all-to-all-start.1 = ((f32[512,1,16]{2,1,0:T(1,128)}), f32[512,1,16]{2,1,0:T(1,128)S(1)}, u32[]{:S(2)}, u32[]{:S(2)}) async-start(f32[512,1,16]{2,1,0:T(1,128)} %broadcast_in_dim.106), calls=%async_computation.1 | async-start | bytes 524288 | tf_op jit(solution)/shard_map/all_to_all | solution.py:51
  54.6 17.2 %all-to-all-done.1 = f32[512,1,16]{2,1,0:T(1,128)S(1)} async-done(((f32[512,1,16]{2,1,0:T(1,128)}), f32[512,1,16]{2,1,0:T(1,128)S(1)}, u32[]{:S(2)}, u32[]{:S(2)}) %all-to-all-start.1) | async-done | bytes 32800 | tf_op jit(solution)/shard_map/all_to_all | solution.py:51
  71.9 0.6 reduce_sum.55
  72.5 0.4 copy-done.6
  72.9 0.2 convolution_multiply_fusion.2
  73.3 2.9 %collective-permute-start.6 = (f32[1,1,132]{2,1,0:T(1,128)S(1)}, f32[1,1,132]{2,1,0:T(1,128)S(1)}, u32[]{:S(2)}, u32[]{:S(2)}) collective-permute-start(f32[1,1,132]{2,1,0:T(1,128)S(1)} %constant_dynamic-update-slice_fusion), channel_id=1, source_target_pairs={{0,1},{1,2},{2,3},{3,4},{4,5},{5,6},{6,7},{7,8},{8,9},{9,10},{10,1... | collective-permute-start | bytes 1592 | tf_op jit(solution)/shard_map/ppermute | solution.py:14
  76.3 1.9 %collective-permute-start.7 = (f32[1,1,132]{2,1,0:T(1,128)S(1)}, f32[1,1,132]{2,1,0:T(1,128)S(1)}, u32[]{:S(2)}, u32[]{:S(2)}) collective-permute-start(f32[1,1,132]{2,1,0:T(1,128)S(1)} %constant_dynamic-update-slice_fusion), channel_id=1, source_target_pairs={{1,0},{2,1},{3,2},{4,3},{5,4},{6,5},{7,6},{8,7},{9,8},{10,9},{11,1... | collective-permute-start | bytes 1592 | tf_op jit(solution)/shard_map/ppermute | solution.py:14
  78.3 2.9 %collective-permute-done.7 = f32[1,1,132]{2,1,0:T(1,128)S(1)} collective-permute-done((f32[1,1,132]{2,1,0:T(1,128)S(1)}, f32[1,1,132]{2,1,0:T(1,128)S(1)}, u32[]{:S(2)}, u32[]{:S(2)}) %collective-permute-start.7) | collective-permute-done | bytes 560 | tf_op jit(solution)/shard_map/ppermute | solution.py:14
  81.2 2.1 %collective-permute-start.8 = (f32[1,3,132]{2,1,0:T(4,128)S(1)}, f32[1,3,132]{2,1,0:T(4,128)S(1)}, u32[]{:S(2)}, u32[]{:S(2)}) collective-permute-start(f32[1,3,132]{2,1,0:T(4,128)S(1)} %pad_maximum_fusion.4), channel_id=1, source_target_pairs={{0,16},{16,32},{32,48},{48,64},{64,80},{80,96},{96,112},{112,128},... | collective-permute-start | bytes 4760 | tf_op jit(solution)/shard_map/ppermute | solution.py:14
  83.2 1.3 collective-permute-start.9
  84.6 0.2 convolution_multiply_fusion
  84.8 2.8 %collective-permute-done.9 = f32[1,3,132]{2,1,0:T(4,128)S(1)} collective-permute-done((f32[1,3,132]{2,1,0:T(4,128)S(1)}, f32[1,3,132]{2,1,0:T(4,128)S(1)}, u32[]{:S(2)}, u32[]{:S(2)}) %collective-permute-start.9) | collective-permute-done | bytes 1616 | tf_op jit(solution)/shard_map/ppermute | solution.py:14
  88.0 0.3 fusion.6
  88.3 0.2 fusion.1
  88.6 1.9 %collective-permute-start.10 = (f32[1,1,16,68]{3,2,1,0:T(8,128)S(1)}, f32[1,1,16,68]{3,2,1,0:T(8,128)S(1)}, u32[]{:S(2)}, u32[]{:S(2)}) collective-permute-start(f32[1,1,16,68]{3,2,1,0:T(8,128)S(1)} %get-tuple-element.38), channel_id=1, source_target_pairs={{1,0},{2,1},{3,2},{4,3},{5,4},{6,5},{7,6},{8,7},{9,8},{10,9},{11,1... | collective-permute-start | bytes 13064 | tf_op jit(solution)/shard_map/ppermute | solution.py:14
  90.5 1.3 collective-permute-start.11
  91.8 1.7 collective-permute-done.10
  93.6 1.4 collective-permute-done.11
  96.3 0.2 subtract_reduce_fusion.3
  97.1 0.2 subtract_reduce_fusion.4
  97.9 0.2 subtract_reduce_fusion.5
  98.2 74.9 %all_to_all.17 = f32[512,7,16]{2,1,0:T(8,128)S(1)} all-to-all(f32[512,7,16]{2,1,0:T(8,128)S(1)} %broadcast_in_dim.107), channel_id=1, replica_groups=mesh['px'=32,'py'=16] {'px','py'}, dimensions={0} | all-to-all | bytes 458752 | tf_op jit(solution)/shard_map/all_to_all | solution.py:51
  173.2 2.1 %fusion.200 = (f32[256,1,16]{2,1,0:T(1,128)}, f32[256,1,16]{2,1,0:T(1,128)}, f32[256,1,16]{2,1,0:T(1,128)}, f32[256,1,16]{2,1,0:T(1,128)S(1)}, f32[256,1,16]{2,1...) fusion(f32[512,7,16]{2,1,0:T(8,128)S(1)} %all_to_all.17), kind=kLoop, calls=%fused_computation.406 | loop fusion | bytes 393216 | tf_op jit(solution)/shard_map/slice | solution.py:111
  175.3 1.0 copy.229
  176.3 1.6 copy.228
  177.9 1.6 copy.227
  179.4 0.7 copy.226
  180.7 0.8 fusion.22
  182.0 0.2 add_reduce_fusion
  182.7 0.2 add_reduce_fusion.1
  183.5 0.2 add_reduce_fusion.2
  183.7 0.6 slice_reduce_fusion
  184.3 1.3 and_reduce_fusion
  186.3 0.7 multiply_subtract_fusion
  187.0 0.5 copy-done.7
  (143 shorter events, 7.9 us)
Async XLA Ops:
  0.6 15.3 %copy-start = (bf16[1,1,272,272]{3,2,1,0:T(8,128)(2,1)S(1)}, bf16[1,1,272,272]{3,2,1,0:T(8,128)(2,1)}, u32[]{:S(2)}) copy-start(bf16[1,1,272,272]{3,2,1,0:T(8,128)(2,1)} %param.17) | copy-start | bytes 443908
  0.6 30.7 %copy-start.1 = (f32[1,1,16,136]{3,2,1,0:T(8,128)S(1)}, f32[1,1,16,136]{3,2,1,0:T(8,128)}, u32[]{:S(2)}) copy-start(f32[1,1,16,136]{3,2,1,0:T(8,128)} %param.13) | copy-start | bytes 26116
  0.7 53.9 %copy-start.8 = (f32[1,1,2,2]{3,2,1,0:T(2,128)S(1)}, f32[1,1,2,2]{3,2,1,0:T(2,128)}, u32[]{:S(2)}) copy-start(f32[1,1,2,2]{3,2,1,0:T(2,128)} %param.19) | copy-start | bytes 52
  0.7 71.7 %copy-start.9 = (f32[16]{0:T(128)S(1)}, f32[16]{0:T(128)}, u32[]{:S(2)}) copy-start(f32[16]{0:T(128)} %param.15) | copy-start | bytes 196
  0.7 72.2 %copy-start.5 = (bf16[1,1,8,272]{3,2,1,0:T(8,128)(2,1)S(1)}, bf16[1,1,8,272]{3,2,1,0:T(8,128)(2,1)}, u32[]{:S(2)}) copy-start(bf16[1,1,8,272]{3,2,1,0:T(8,128)(2,1)} %param.18) | copy-start | bytes 13060
  0.7 83.9 %copy-start.2 = (bf16[1,1,272,272]{3,2,1,0:T(8,128)(2,1)S(1)}, bf16[1,1,272,272]{3,2,1,0:T(8,128)(2,1)}, u32[]{:S(2)}) copy-start(bf16[1,1,272,272]{3,2,1,0:T(8,128)(2,1)} %param.16) | copy-start | bytes 443908
  5.8 8.8 %collective-permute-start.1 = (f32[2,1,1,16,68]{4,3,2,1,0:T(8,128)S(1)}, f32[2,1,1,16,68]{4,3,2,1,0:T(8,128)S(1)}, u32[]{:S(2)}, u32[]{:S(2)}) collective-permute-start(f32[2,1,1,16,68]{4,3,2,1,0:T(8,128)S(1)} %pad_maximum_fusion.1), channel_id=1, source_target_pairs={{0,16},{16,32},{32,48},{48,64},{64,80},{80,96},{96,112},{112,128},... | collective-permute-start | bytes 26120 | tf_op jit(solution)/shard_map/ppermute | solution.py:14
  9.8 6.2 %collective-permute-start = (f32[2,1,1,16,68]{4,3,2,1,0:T(8,128)S(1)}, f32[2,1,1,16,68]{4,3,2,1,0:T(8,128)S(1)}, u32[]{:S(2)}, u32[]{:S(2)}) collective-permute-start(f32[2,1,1,16,68]{4,3,2,1,0:T(8,128)S(1)} %pad_maximum_fusion), channel_id=1, source_target_pairs={{0,1},{1,2},{2,3},{3,4},{4,5},{5,6},{6,7},{7,8},{8,9},{9,10},{10,1... | collective-permute-start | bytes 26120 | tf_op jit(solution)/shard_map/ppermute | solution.py:14
  16.3 5.0 %collective-permute-start.2 = (f32[1,1,16,68]{3,2,1,0:T(8,128)S(1)}, f32[1,1,16,68]{3,2,1,0:T(8,128)S(1)}, u32[]{:S(2)}, u32[]{:S(2)}) collective-permute-start(f32[1,1,16,68]{3,2,1,0:T(8,128)S(1)} %get-tuple-element.26), channel_id=1, source_target_pairs={{1,0},{2,1},{3,2},{4,3},{5,4},{6,5},{7,6},{8,7},{9,8},{10,9},{11,1... | collective-permute-start | bytes 13064 | tf_op jit(solution)/shard_map/ppermute | solution.py:14
  18.3 4.5 %collective-permute-start.3 = (f32[1,1,16,68]{3,2,1,0:T(8,128)S(1)}, f32[1,1,16,68]{3,2,1,0:T(8,128)S(1)}, u32[]{:S(2)}, u32[]{:S(2)}) collective-permute-start(f32[1,1,16,68]{3,2,1,0:T(8,128)S(1)} %get-tuple-element.27), channel_id=1, source_target_pairs={{16,0},{32,16},{48,32},{64,48},{80,64},{96,80},{112,96},{128,112},... | collective-permute-start | bytes 13064 | tf_op jit(solution)/shard_map/ppermute | solution.py:14
  23.3 49.1 %collective-permute-start.5 = (f32[2,1,1,16,68]{4,3,2,1,0:T(8,128)S(1)}, f32[2,1,1,16,68]{4,3,2,1,0:T(8,128)S(1)}, u32[]{:S(2)}, u32[]{:S(2)}) collective-permute-start(f32[2,1,1,16,68]{4,3,2,1,0:T(8,128)S(1)} %stack.45), channel_id=1, source_target_pairs={{0,16},{16,32},{32,48},{48,64},{64,80},{80,96},{96,112},{112,128},... | collective-permute-start | bytes 26120 | tf_op jit(solution)/shard_map/ppermute | solution.py:14
  26.6 45.9 %collective-permute-start.4 = (f32[2,1,1,16,68]{4,3,2,1,0:T(8,128)S(1)}, f32[2,1,1,16,68]{4,3,2,1,0:T(8,128)S(1)}, u32[]{:S(2)}, u32[]{:S(2)}) collective-permute-start(f32[2,1,1,16,68]{4,3,2,1,0:T(8,128)S(1)} %stack.43), channel_id=1, source_target_pairs={{0,1},{1,2},{2,3},{3,4},{4,5},{5,6},{6,7},{7,8},{8,9},{9,10},{10,1... | collective-permute-start | bytes 26120 | tf_op jit(solution)/shard_map/ppermute | solution.py:14
  32.4 39.5 %all-to-all-start.1 = ((f32[512,1,16]{2,1,0:T(1,128)}), f32[512,1,16]{2,1,0:T(1,128)S(1)}, u32[]{:S(2)}, u32[]{:S(2)}) async-start(f32[512,1,16]{2,1,0:T(1,128)} %broadcast_in_dim.106), calls=%async_computation.1 | async-start | bytes 524288 | tf_op jit(solution)/shard_map/all_to_all | solution.py:51
  72.4 0.5 copy-start.6
  73.3 5.0 %collective-permute-start.6 = (f32[1,1,132]{2,1,0:T(1,128)S(1)}, f32[1,1,132]{2,1,0:T(1,128)S(1)}, u32[]{:S(2)}, u32[]{:S(2)}) collective-permute-start(f32[1,1,132]{2,1,0:T(1,128)S(1)} %constant_dynamic-update-slice_fusion), channel_id=1, source_target_pairs={{0,1},{1,2},{2,3},{3,4},{4,5},{5,6},{6,7},{7,8},{8,9},{9,10},{10,1... | collective-permute-start | bytes 1592 | tf_op jit(solution)/shard_map/ppermute | solution.py:14
  76.3 4.9 %collective-permute-start.7 = (f32[1,1,132]{2,1,0:T(1,128)S(1)}, f32[1,1,132]{2,1,0:T(1,128)S(1)}, u32[]{:S(2)}, u32[]{:S(2)}) collective-permute-start(f32[1,1,132]{2,1,0:T(1,128)S(1)} %constant_dynamic-update-slice_fusion), channel_id=1, source_target_pairs={{1,0},{2,1},{3,2},{4,3},{5,4},{6,5},{7,6},{8,7},{9,8},{10,9},{11,1... | collective-permute-start | bytes 1592 | tf_op jit(solution)/shard_map/ppermute | solution.py:14
  81.2 3.6 %collective-permute-start.8 = (f32[1,3,132]{2,1,0:T(4,128)S(1)}, f32[1,3,132]{2,1,0:T(4,128)S(1)}, u32[]{:S(2)}, u32[]{:S(2)}) collective-permute-start(f32[1,3,132]{2,1,0:T(4,128)S(1)} %pad_maximum_fusion.4), channel_id=1, source_target_pairs={{0,16},{16,32},{32,48},{48,64},{64,80},{80,96},{96,112},{112,128},... | collective-permute-start | bytes 4760 | tf_op jit(solution)/shard_map/ppermute | solution.py:14
  83.2 4.4 %collective-permute-start.9 = (f32[1,3,132]{2,1,0:T(4,128)S(1)}, f32[1,3,132]{2,1,0:T(4,128)S(1)}, u32[]{:S(2)}, u32[]{:S(2)}) collective-permute-start(f32[1,3,132]{2,1,0:T(4,128)S(1)} %pad_maximum_fusion.4), channel_id=1, source_target_pairs={{16,0},{32,16},{48,32},{64,48},{80,64},{96,80},{112,96},{128,112},... | collective-permute-start | bytes 4760 | tf_op jit(solution)/shard_map/ppermute | solution.py:14
  88.6 5.0 %collective-permute-start.10 = (f32[1,1,16,68]{3,2,1,0:T(8,128)S(1)}, f32[1,1,16,68]{3,2,1,0:T(8,128)S(1)}, u32[]{:S(2)}, u32[]{:S(2)}) collective-permute-start(f32[1,1,16,68]{3,2,1,0:T(8,128)S(1)} %get-tuple-element.38), channel_id=1, source_target_pairs={{1,0},{2,1},{3,2},{4,3},{5,4},{6,5},{7,6},{8,7},{9,8},{10,9},{11,1... | collective-permute-start | bytes 13064 | tf_op jit(solution)/shard_map/ppermute | solution.py:14
  90.5 4.4 %collective-permute-start.11 = (f32[1,1,16,68]{3,2,1,0:T(8,128)S(1)}, f32[1,1,16,68]{3,2,1,0:T(8,128)S(1)}, u32[]{:S(2)}, u32[]{:S(2)}) collective-permute-start(f32[1,1,16,68]{3,2,1,0:T(8,128)S(1)} %get-tuple-element.39), channel_id=1, source_target_pairs={{16,0},{32,16},{48,32},{64,48},{80,64},{96,80},{112,96},{128,112},... | collective-permute-start | bytes 13064 | tf_op jit(solution)/shard_map/ppermute | solution.py:14
  95.6 90.7 %copy-start.3 = (f32[1,1,16,136]{3,2,1,0:T(8,128)}, f32[1,1,16,136]{3,2,1,0:T(8,128)S(1)}, u32[]{:S(2)}) copy-start(f32[1,1,16,136]{3,2,1,0:T(8,128)S(1)} %get-tuple-element.142) | copy-start | bytes 26116
  180.2 6.1 %copy-start.4 = (f32[1,1,16,136]{3,2,1,0:T(8,128)S(1)}, f32[1,1,16,136]{3,2,1,0:T(8,128)}, u32[]{:S(2)}) copy-start(f32[1,1,16,136]{3,2,1,0:T(8,128)} %param.12) | copy-start | bytes 26116
  187.0 0.5 copy-start.7

commit v9 on v7

--- a/solution.py
+++ b/solution.py
@@ -220,15 +220,18 @@
         west_side = side_values[..., 2 * SIDE : 3 * SIDE]
         south_side = side_values[..., 3 * SIDE :]
         ones = jnp.broadcast_to(active, east_side.shape)
-        east_edge, north_edge = exchanged_together(
-            [(west_side, "py", -1), (south_side, "px", -1)]
+        east_perm_side = permute_side(east_side, east_flip)
+        north_perm_side = permute_side(north_side, north_flip)
+        east_edge, north_edge, west_sent, south_sent = exchanged_together(
+            [
+                (west_side, "py", -1),
+                (south_side, "px", -1),
+                (jnp.stack([east_perm_side, ones]), "py", 1),
+                (jnp.stack([north_perm_side, ones]), "px", 1),
+            ]
         )
         from_east = jnp.concatenate([west_side[:, 1:], east_edge], 1)
         from_north = jnp.concatenate([south_side[1:], north_edge], 0)
-        east_perm_side = permute_side(east_side, east_flip)
-        north_perm_side = permute_side(north_side, north_flip)
-        west_sent = passed_along(jnp.stack([east_perm_side, ones]), "py", 1)
-        south_sent = passed_along(jnp.stack([north_perm_side, ones]), "px", 1)
         east_term = permute_side(from_east, east_flip)
         north_term = permute_side(from_north, north_flip)
         joined = jnp.concatenate([east_side - east_term, north_side - north_term], 3)

time: 133 us -> 138 us (1.038)
  blocking collectives: 38.2 us -> 55.5 us
  starting transfers between devices: 55.7 us -> 43.3 us
    all_to_all x2 -> x3, blocking collectives: 38.2 us -> 55.5 us  [gathered(): return lax.all_to_all(copies, axis, 0, 0, tiled=False)]
    all_to_all x2 -> x1, starting transfers between devices: 23.9 us -> 11.7 us  [gathered(): return lax.all_to_all(copies, axis, 0, 0, tiled=False)]
    all_to_all x2 -> x1, waiting for transfers between devices: 8.4 us -> 7.74 us  [gathered(): return lax.all_to_all(copies, axis, 0, 0, tiled=False)]
  transfers between devices with their start and end apart: 14 -> 13, of which waited for: 8 -> 8; matrix products, arithmetic and copies ran while one was open for 1% -> 0% of each run, Pallas kernels for 0% -> 0%
where the time goes in v9:
time: 138 us; the launch traced here: 137 us
  blocking collectives  55.5 us (40%)
  starting transfers between devices  43.3 us (31%)
  waiting for transfers between devices  21 us (15%)
  local copies, waits for them, and re-layouts  7.11 us (5%)
  other arithmetic  5.37 us (4%)
  between operations  3.97 us (3%)
    all_to_all x3, blocking collectives, gathered(): return lax.all_to_all(copies, axis, 0, 0, tiled=False)  55.5 us
    ppermute x12, starting transfers between devices, passed_along(): return lax.ppermute(value, axis, pairs)  31.6 us
    ppermute x12, waiting for transfers between devices, passed_along(): return lax.ppermute(value, axis, pairs)  13.2 us
    all_to_all x1, starting transfers between devices, gathered(): return lax.all_to_all(copies, axis, 0, 0, tiled=False)  11.7 us
    all_to_all x1, waiting for transfers between devices, gathered(): return lax.all_to_all(copies, axis, 0, 0, tiled=False)  7.74 us
  transfers between devices with their start and end apart: 13, of which 8 were waited for; matrix products, arithmetic and copies ran while one was open for 0% of the time, Pallas kernels for 0%

profile of v9, /device:TPU:1, one launch (start us, length us, event | category | flops | bytes accessed | tf_op | source)
XLA Modules:
  0.0 137.3 jit_solution(5196136142915519253)
XLA Ops:
  1.4 0.5 fusion.181
  3.6 0.1 copy.132
  4.3 3.9 %collective-permute-start.1 = (f32[2,1,1,16,68]{4,3,2,1,0:T(8,128)S(1)}, f32[2,1,1,16,68]{4,3,2,1,0:T(8,128)S(1)}, u32[]{:S(2)}, u32[]{:S(2)}) collective-permute-start(f32[2,1,1,16,68]{4,3,2,1,0:T(8,128)S(1)} %pad_maximum_fusion.1), channel_id=1, source_target_pairs={{0,16},{16,32},{32,48},{48,64},{64,80},{80,96},{96,112},{112,128},... | collective-permute-start | bytes 26120 | tf_op jit(solution)/shard_map/ppermute | solution.py:12
  8.2 4.8 %collective-permute-start = (f32[2,1,1,16,68]{4,3,2,1,0:T(8,128)S(1)}, f32[2,1,1,16,68]{4,3,2,1,0:T(8,128)S(1)}, u32[]{:S(2)}, u32[]{:S(2)}) collective-permute-start(f32[2,1,1,16,68]{4,3,2,1,0:T(8,128)S(1)} %pad_maximum_fusion), channel_id=1, source_target_pairs={{0,1},{1,2},{2,3},{3,4},{4,5},{5,6},{6,7},{7,8},{8,9},{9,10},{10,1... | collective-permute-start | bytes 26120 | tf_op jit(solution)/shard_map/ppermute | solution.py:12
  13.1 1.3 collective-permute-done
  14.4 0.2 fusion.2
  14.7 0.1 copy.142
  15.2 3.7 %collective-permute-start.4 = (f32[2,1,1,16,68]{4,3,2,1,0:T(8,128)S(1)}, f32[2,1,1,16,68]{4,3,2,1,0:T(8,128)S(1)}, u32[]{:S(2)}, u32[]{:S(2)}) collective-permute-start(f32[2,1,1,16,68]{4,3,2,1,0:T(8,128)S(1)} %stack.49), channel_id=1, source_target_pairs={{0,1},{1,2},{2,3},{3,4},{4,5},{5,6},{6,7},{7,8},{8,9},{9,10},{10,1... | collective-permute-start | bytes 26120 | tf_op jit(solution)/shard_map/ppermute | solution.py:12
  18.9 3.1 %collective-permute-start.5 = (f32[2,1,1,16,68]{4,3,2,1,0:T(8,128)S(1)}, f32[2,1,1,16,68]{4,3,2,1,0:T(8,128)S(1)}, u32[]{:S(2)}, u32[]{:S(2)}) collective-permute-start(f32[2,1,1,16,68]{4,3,2,1,0:T(8,128)S(1)} %stack.51), channel_id=1, source_target_pairs={{0,16},{16,32},{32,48},{48,64},{64,80},{80,96},{96,112},{112,128},... | collective-permute-start | bytes 26120 | tf_op jit(solution)/shard_map/ppermute | solution.py:12
  22.0 1.9 %collective-permute-start.2 = (f32[1,1,16,68]{3,2,1,0:T(8,128)S(1)}, f32[1,1,16,68]{3,2,1,0:T(8,128)S(1)}, u32[]{:S(2)}, u32[]{:S(2)}) collective-permute-start(f32[1,1,16,68]{3,2,1,0:T(8,128)S(1)} %get-tuple-element.30), channel_id=1, source_target_pairs={{1,0},{2,1},{3,2},{4,3},{5,4},{6,5},{7,6},{8,7},{9,8},{10,9},{11,1... | collective-permute-start | bytes 13064 | tf_op jit(solution)/shard_map/ppermute | solution.py:12
  24.0 1.3 collective-permute-start.3
  25.3 1.7 %collective-permute-done.2 = f32[1,1,16,68]{3,2,1,0:T(8,128)S(1)} collective-permute-done((f32[1,1,16,68]{3,2,1,0:T(8,128)S(1)}, f32[1,1,16,68]{3,2,1,0:T(8,128)S(1)}, u32[]{:S(2)}, u32[]{:S(2)}) %collective-permute-start.2) | collective-permute-done | bytes 4384 | tf_op jit(solution)/shard_map/ppermute | solution.py:12
  27.0 1.4 collective-permute-done.3
  28.8 0.2 multiply_reduce_fusion.2
  29.0 20.4 %all_to_all.34 = f32[16,1,16]{2,1,0:T(1,128)S(1)} all-to-all(f32[16,1,16]{2,1,0:T(1,128)S(1)} %broadcast_in_dim.124), channel_id=1, replica_groups=mesh['px'=32,'py'=16] {'py'}, dimensions={0} | all-to-all | bytes 2048 | tf_op jit(solution)/shard_map/all_to_all | solution.py:49
  49.5 0.6 broadcast_in_dim.125
  50.1 11.7 %all-to-all-start.3 = ((f32[32,1,16]{2,1,0:T(1,128)}), f32[32,1,16]{2,1,0:T(1,128)S(1)}, u32[]{:S(2)}, u32[]{:S(2)}) async-start(f32[32,1,16]{2,1,0:T(1,128)} %broadcast_in_dim.125), calls=%async_computation.3 | async-start | bytes 32768 | tf_op jit(solution)/shard_map/all_to_all | solution.py:49
  61.9 0.7 copy-done.11
  62.6 7.7 %all-to-all-done.3 = f32[32,1,16]{2,1,0:T(1,128)S(1)} async-done(((f32[32,1,16]{2,1,0:T(1,128)}), f32[32,1,16]{2,1,0:T(1,128)S(1)}, u32[]{:S(2)}, u32[]{:S(2)}) %all-to-all-start.3) | async-done | bytes 2080 | tf_op jit(solution)/shard_map/all_to_all | solution.py:49
  70.5 0.7 copy-done.7
  71.2 0.2 convolution_multiply_fusion.2
  71.6 4.1 %collective-permute-start.6 = (f32[1,1,132]{2,1,0:T(1,128)S(1)}, f32[1,1,132]{2,1,0:T(1,128)S(1)}, u32[]{:S(2)}, u32[]{:S(2)}) collective-permute-start(f32[1,1,132]{2,1,0:T(1,128)S(1)} %constant_dynamic-update-slice_fusion), channel_id=1, source_target_pairs={{0,1},{1,2},{2,3},{3,4},{4,5},{5,6},{6,7},{7,8},{8,9},{9,10},{10,1... | collective-permute-start | bytes 1592 | tf_op jit(solution)/shard_map/ppermute | solution.py:12
  75.7 1.9 %collective-permute-start.7 = (f32[1,1,132]{2,1,0:T(1,128)S(1)}, f32[1,1,132]{2,1,0:T(1,128)S(1)}, u32[]{:S(2)}, u32[]{:S(2)}) collective-permute-start(f32[1,1,132]{2,1,0:T(1,128)S(1)} %constant_dynamic-update-slice_fusion), channel_id=1, source_target_pairs={{1,0},{2,1},{3,2},{4,3},{5,4},{6,5},{7,6},{8,7},{9,8},{10,9},{11,1... | collective-permute-start | bytes 1592 | tf_op jit(solution)/shard_map/ppermute | solution.py:12
  77.7 2.9 %collective-permute-done.7 = f32[1,1,132]{2,1,0:T(1,128)S(1)} collective-permute-done((f32[1,1,132]{2,1,0:T(1,128)S(1)}, f32[1,1,132]{2,1,0:T(1,128)S(1)}, u32[]{:S(2)}, u32[]{:S(2)}) %collective-permute-start.7) | collective-permute-done | bytes 560 | tf_op jit(solution)/shard_map/ppermute | solution.py:12
  80.6 2.2 %collective-permute-start.8 = (f32[1,3,132]{2,1,0:T(4,128)S(1)}, f32[1,3,132]{2,1,0:T(4,128)S(1)}, u32[]{:S(2)}, u32[]{:S(2)}) collective-permute-start(f32[1,3,132]{2,1,0:T(4,128)S(1)} %pad_maximum_fusion.4), channel_id=1, source_target_pairs={{0,16},{16,32},{32,48},{48,64},{64,80},{80,96},{96,112},{112,128},... | collective-permute-start | bytes 4760 | tf_op jit(solution)/shard_map/ppermute | solution.py:12
  82.9 1.3 collective-permute-start.9
  84.2 0.2 convolution_multiply_fusion
  84.4 2.8 %collective-permute-done.9 = f32[1,3,132]{2,1,0:T(4,128)S(1)} collective-permute-done((f32[1,3,132]{2,1,0:T(4,128)S(1)}, f32[1,3,132]{2,1,0:T(4,128)S(1)}, u32[]{:S(2)}, u32[]{:S(2)}) %collective-permute-start.9) | collective-permute-done | bytes 1616 | tf_op jit(solution)/shard_map/ppermute | solution.py:12
  87.2 0.6 copy-done.4
  87.8 0.1 copy.151
  88.0 0.1 copy.179
  88.1 0.6 slice-done
  88.7 0.1 reshape.580
  88.8 0.3 fusion.6
  89.1 0.2 fusion.1
  89.4 1.9 %collective-permute-start.10 = (f32[1,1,16,68]{3,2,1,0:T(8,128)S(1)}, f32[1,1,16,68]{3,2,1,0:T(8,128)S(1)}, u32[]{:S(2)}, u32[]{:S(2)}) collective-permute-start(f32[1,1,16,68]{3,2,1,0:T(8,128)S(1)} %get-tuple-element.46), channel_id=1, source_target_pairs={{1,0},{2,1},{3,2},{4,3},{5,4},{6,5},{7,6},{8,7},{9,8},{10,9},{11,1... | collective-permute-start | bytes 13064 | tf_op jit(solution)/shard_map/ppermute | solution.py:12
  91.3 1.3 collective-permute-start.11
  92.6 1.7 %collective-permute-done.10 = f32[1,1,16,68]{3,2,1,0:T(8,128)S(1)} collective-permute-done((f32[1,1,16,68]{3,2,1,0:T(8,128)S(1)}, f32[1,1,16,68]{3,2,1,0:T(8,128)S(1)}, u32[]{:S(2)}, u32[]{:S(2)}) %collective-permute-start.10) | collective-permute-done | bytes 4384 | tf_op jit(solution)/shard_map/ppermute | solution.py:12
  94.3 1.4 collective-permute-done.11
  96.1 0.2 multiply_reduce_fusion.1
  97.0 0.2 subtract_reduce_fusion
  97.8 0.2 subtract_reduce_fusion.1
  98.6 0.2 subtract_reduce_fusion.2
  98.9 14.7 %all_to_all.35 = f32[16,7,16]{2,1,0:T(8,128)S(1)} all-to-all(f32[16,7,16]{2,1,0:T(8,128)S(1)} %broadcast_in_dim.126), channel_id=1, replica_groups=mesh['px'=32,'py'=16] {'py'}, dimensions={0} | all-to-all | bytes 14336 | tf_op jit(solution)/shard_map/all_to_all | solution.py:49
  113.9 20.5 %all_to_all.36 = f32[32,7,16]{2,1,0:T(8,128)S(1)} all-to-all(f32[32,7,16]{2,1,0:T(8,128)S(1)} %broadcast_in_dim.127), channel_id=1, replica_groups=mesh['px'=32,'py'=16] {'px'}, dimensions={0} | all-to-all | bytes 28672 | tf_op jit(solution)/shard_map/all_to_all | solution.py:49
  134.8 0.7 and_reduce_fusion
  136.1 0.7 multiply_subtract_fusion
  136.8 0.5 copy-done.10
  (150 shorter events, 5.5 us)
Async XLA Ops:
  0.6 13.8 %copy-start = (bf16[1,1,272,272]{3,2,1,0:T(8,128)(2,1)S(1)}, bf16[1,1,272,272]{3,2,1,0:T(8,128)(2,1)}, u32[]{:S(2)}) copy-start(bf16[1,1,272,272]{3,2,1,0:T(8,128)(2,1)} %param.17) | copy-start | bytes 443908
  0.7 0.7 copy-start.9
  0.7 2.6 %copy-start.1 = (f32[1,1,16,136]{3,2,1,0:T(8,128)S(1)}, f32[1,1,16,136]{3,2,1,0:T(8,128)}, u32[]{:S(2)}) copy-start(f32[1,1,16,136]{3,2,1,0:T(8,128)} %param.13) | copy-start | bytes 26116
  0.7 2.6 %copy-start.6 = (f32[1,1,16,136]{3,2,1,0:T(8,128)S(1)}, f32[1,1,16,136]{3,2,1,0:T(8,128)}, u32[]{:S(2)}) copy-start(f32[1,1,16,136]{3,2,1,0:T(8,128)} %param.14) | copy-start | bytes 26116
  4.3 8.8 %collective-permute-start.1 = (f32[2,1,1,16,68]{4,3,2,1,0:T(8,128)S(1)}, f32[2,1,1,16,68]{4,3,2,1,0:T(8,128)S(1)}, u32[]{:S(2)}, u32[]{:S(2)}) collective-permute-start(f32[2,1,1,16,68]{4,3,2,1,0:T(8,128)S(1)} %pad_maximum_fusion.1), channel_id=1, source_target_pairs={{0,16},{16,32},{32,48},{48,64},{64,80},{80,96},{96,112},{112,128},... | collective-permute-start | bytes 26120 | tf_op jit(solution)/shard_map/ppermute | solution.py:12
  8.2 6.2 %collective-permute-start = (f32[2,1,1,16,68]{4,3,2,1,0:T(8,128)S(1)}, f32[2,1,1,16,68]{4,3,2,1,0:T(8,128)S(1)}, u32[]{:S(2)}, u32[]{:S(2)}) collective-permute-start(f32[2,1,1,16,68]{4,3,2,1,0:T(8,128)S(1)} %pad_maximum_fusion), channel_id=1, source_target_pairs={{0,1},{1,2},{2,3},{3,4},{4,5},{5,6},{6,7},{7,8},{8,9},{9,10},{10,1... | collective-permute-start | bytes 26120 | tf_op jit(solution)/shard_map/ppermute | solution.py:12
  15.2 13.2 %collective-permute-start.4 = (f32[2,1,1,16,68]{4,3,2,1,0:T(8,128)S(1)}, f32[2,1,1,16,68]{4,3,2,1,0:T(8,128)S(1)}, u32[]{:S(2)}, u32[]{:S(2)}) collective-permute-start(f32[2,1,1,16,68]{4,3,2,1,0:T(8,128)S(1)} %stack.49), channel_id=1, source_target_pairs={{0,1},{1,2},{2,3},{3,4},{4,5},{5,6},{6,7},{7,8},{8,9},{9,10},{10,1... | collective-permute-start | bytes 26120 | tf_op jit(solution)/shard_map/ppermute | solution.py:12
  18.9 9.5 %collective-permute-start.5 = (f32[2,1,1,16,68]{4,3,2,1,0:T(8,128)S(1)}, f32[2,1,1,16,68]{4,3,2,1,0:T(8,128)S(1)}, u32[]{:S(2)}, u32[]{:S(2)}) collective-permute-start(f32[2,1,1,16,68]{4,3,2,1,0:T(8,128)S(1)} %stack.51), channel_id=1, source_target_pairs={{0,16},{16,32},{32,48},{48,64},{64,80},{80,96},{96,112},{112,128},... | collective-permute-start | bytes 26120 | tf_op jit(solution)/shard_map/ppermute | solution.py:12
  22.0 5.0 %collective-permute-start.2 = (f32[1,1,16,68]{3,2,1,0:T(8,128)S(1)}, f32[1,1,16,68]{3,2,1,0:T(8,128)S(1)}, u32[]{:S(2)}, u32[]{:S(2)}) collective-permute-start(f32[1,1,16,68]{3,2,1,0:T(8,128)S(1)} %get-tuple-element.30), channel_id=1, source_target_pairs={{1,0},{2,1},{3,2},{4,3},{5,4},{6,5},{7,6},{8,7},{9,8},{10,9},{11,1... | collective-permute-start | bytes 13064 | tf_op jit(solution)/shard_map/ppermute | solution.py:12
  24.0 4.4 %collective-permute-start.3 = (f32[1,1,16,68]{3,2,1,0:T(8,128)S(1)}, f32[1,1,16,68]{3,2,1,0:T(8,128)S(1)}, u32[]{:S(2)}, u32[]{:S(2)}) collective-permute-start(f32[1,1,16,68]{3,2,1,0:T(8,128)S(1)} %get-tuple-element.31), channel_id=1, source_target_pairs={{16,0},{32,16},{48,32},{64,48},{80,64},{96,80},{112,96},{128,112},... | collective-permute-start | bytes 13064 | tf_op jit(solution)/shard_map/ppermute | solution.py:12
  28.7 55.4 %copy-start.2 = (bf16[1,1,272,272]{3,2,1,0:T(8,128)(2,1)S(1)}, bf16[1,1,272,272]{3,2,1,0:T(8,128)(2,1)}, u32[]{:S(2)}) copy-start(bf16[1,1,272,272]{3,2,1,0:T(8,128)(2,1)} %param.16) | copy-start | bytes 443908
  50.1 20.2 %all-to-all-start.3 = ((f32[32,1,16]{2,1,0:T(1,128)}), f32[32,1,16]{2,1,0:T(1,128)S(1)}, u32[]{:S(2)}, u32[]{:S(2)}) async-start(f32[32,1,16]{2,1,0:T(1,128)} %broadcast_in_dim.125), calls=%async_computation.3 | async-start | bytes 32768 | tf_op jit(solution)/shard_map/all_to_all | solution.py:49
  61.8 0.7 copy-start.11
  62.6 7.8 %copy-start.12 = (f32[16]{0:T(128)S(1)}, f32[16]{0:T(128)}, u32[]{:S(2)}) copy-start(f32[16]{0:T(128)} %param.15) | copy-start | bytes 196
  70.4 64.4 %copy-start.8 = (f32[16]{0:T(128)}, f32[16]{0:T(128)S(1)}, u32[]{:S(2)}) copy-start(f32[16]{0:T(128)S(1)} %reduce_sum.83) | copy-start | bytes 196
  70.5 0.7 copy-start.7
  71.6 6.2 %collective-permute-start.6 = (f32[1,1,132]{2,1,0:T(1,128)S(1)}, f32[1,1,132]{2,1,0:T(1,128)S(1)}, u32[]{:S(2)}, u32[]{:S(2)}) collective-permute-start(f32[1,1,132]{2,1,0:T(1,128)S(1)} %constant_dynamic-update-slice_fusion), channel_id=1, source_target_pairs={{0,1},{1,2},{2,3},{3,4},{4,5},{5,6},{6,7},{7,8},{8,9},{9,10},{10,1... | collective-permute-start | bytes 1592 | tf_op jit(solution)/shard_map/ppermute | solution.py:12
  75.7 4.9 %collective-permute-start.7 = (f32[1,1,132]{2,1,0:T(1,128)S(1)}, f32[1,1,132]{2,1,0:T(1,128)S(1)}, u32[]{:S(2)}, u32[]{:S(2)}) collective-permute-start(f32[1,1,132]{2,1,0:T(1,128)S(1)} %constant_dynamic-update-slice_fusion), channel_id=1, source_target_pairs={{1,0},{2,1},{3,2},{4,3},{5,4},{6,5},{7,6},{8,7},{9,8},{10,9},{11,1... | collective-permute-start | bytes 1592 | tf_op jit(solution)/shard_map/ppermute | solution.py:12
  80.6 3.7 %collective-permute-start.8 = (f32[1,3,132]{2,1,0:T(4,128)S(1)}, f32[1,3,132]{2,1,0:T(4,128)S(1)}, u32[]{:S(2)}, u32[]{:S(2)}) collective-permute-start(f32[1,3,132]{2,1,0:T(4,128)S(1)} %pad_maximum_fusion.4), channel_id=1, source_target_pairs={{0,16},{16,32},{32,48},{48,64},{64,80},{80,96},{96,112},{112,128},... | collective-permute-start | bytes 4760 | tf_op jit(solution)/shard_map/ppermute | solution.py:12
  82.9 4.4 %collective-permute-start.9 = (f32[1,3,132]{2,1,0:T(4,128)S(1)}, f32[1,3,132]{2,1,0:T(4,128)S(1)}, u32[]{:S(2)}, u32[]{:S(2)}) collective-permute-start(f32[1,3,132]{2,1,0:T(4,128)S(1)} %pad_maximum_fusion.4), channel_id=1, source_target_pairs={{16,0},{32,16},{48,32},{64,48},{80,64},{96,80},{112,96},{128,112},... | collective-permute-start | bytes 4760 | tf_op jit(solution)/shard_map/ppermute | solution.py:12
  87.2 0.6 copy-start.4
  88.0 0.7 slice-start
  89.4 5.0 %collective-permute-start.10 = (f32[1,1,16,68]{3,2,1,0:T(8,128)S(1)}, f32[1,1,16,68]{3,2,1,0:T(8,128)S(1)}, u32[]{:S(2)}, u32[]{:S(2)}) collective-permute-start(f32[1,1,16,68]{3,2,1,0:T(8,128)S(1)} %get-tuple-element.46), channel_id=1, source_target_pairs={{1,0},{2,1},{3,2},{4,3},{5,4},{6,5},{7,6},{8,7},{9,8},{10,9},{11,1... | collective-permute-start | bytes 13064 | tf_op jit(solution)/shard_map/ppermute | solution.py:12
  91.3 4.4 %collective-permute-start.11 = (f32[1,1,16,68]{3,2,1,0:T(8,128)S(1)}, f32[1,1,16,68]{3,2,1,0:T(8,128)S(1)}, u32[]{:S(2)}, u32[]{:S(2)}) collective-permute-start(f32[1,1,16,68]{3,2,1,0:T(8,128)S(1)} %get-tuple-element.47), channel_id=1, source_target_pairs={{16,0},{32,16},{48,32},{64,48},{80,64},{96,80},{112,96},{128,112},... | collective-permute-start | bytes 13064 | tf_op jit(solution)/shard_map/ppermute | solution.py:12
  96.3 39.8 %copy-start.3 = (f32[1,1,16,136]{3,2,1,0:T(8,128)}, f32[1,1,16,136]{3,2,1,0:T(8,128)S(1)}, u32[]{:S(2)}) copy-start(f32[1,1,16,136]{3,2,1,0:T(8,128)S(1)} %get-tuple-element.150) | copy-start | bytes 26116
  134.8 1.4 copy-start.5
  136.8 0.5 copy-start.10

commit v10 on v7

--- a/solution.py
+++ b/solution.py
@@ -114,10 +114,12 @@
 
 def all_sum_mixed(plain, pairs):
     for axis in ("py", "px"):
-        packed = jnp.stack([plain] + [part for pair in pairs for part in pair])
-        every = gathered(packed, axis)
-        plain = jnp.sum(every[:, 0], axis=0)
-        pairs = [df_tree_sum(every[:, 1 + 2 * k], every[:, 2 + 2 * k]) for k in range(len(pairs))]
+        rows = [plain] + [part for pair in pairs for part in pair]
+        width = plain.shape[0]
+        every = gathered(jnp.concatenate(rows), axis)
+        row = lambda k: every[:, k * width : (k + 1) * width]
+        plain = jnp.sum(row(0), axis=0)
+        pairs = [df_tree_sum(row(1 + 2 * k), row(2 + 2 * k)) for k in range(len(pairs))]
     return plain, pairs
 
 

time: 133 us -> 132 us (level)
  blocking collectives: 38.2 us -> 36.2 us
    all_to_all x2, blocking collectives: 38.2 us -> 36.2 us  [gathered(): return lax.all_to_all(copies, axis, 0, 0, tiled=False)]
    sub x48 -> x43, other arithmetic: 2.69 us -> 2.9 us  [df_add(): return (high, error - (high - total))]
where the time goes in v10:
time: 132 us
  starting transfers between devices  55.7 us (42%)
  blocking collectives  36.2 us (27%)
  waiting for transfers between devices  21.4 us (16%)
  local copies, waits for them, and re-layouts  7.79 us (6%)
  other arithmetic  5.53 us (4%)
  between operations  3.9 us (3%)
    all_to_all x2, blocking collectives, gathered(): return lax.all_to_all(copies, axis, 0, 0, tiled=False)  36.2 us
    ppermute x12, starting transfers between devices, passed_along(): return lax.ppermute(value, axis, pairs)  31.8 us
    all_to_all x2, starting transfers between devices, gathered(): return lax.all_to_all(copies, axis, 0, 0, tiled=False)  23.9 us
    ppermute x12, waiting for transfers between devices, passed_along(): return lax.ppermute(value, axis, pairs)  13 us
    all_to_all x2, waiting for transfers between devices, gathered(): return lax.all_to_all(copies, axis, 0, 0, tiled=False)  8.4 us
    sub x43, other arithmetic, df_add(): return (high, error - (high - total))  2.9 us
  transfers between devices with their start and end apart: 14, of which 8 were waited for; matrix products, arithmetic and copies ran while one was open for 1% of the time, Pallas kernels for 0%

profile of v10, /device:TPU:1, one launch (start us, length us, event | category | flops | bytes accessed | tf_op | source)
XLA Modules:
  0.0 131.5 jit_solution(7843356277170829722)
XLA Ops:
  1.7 0.6 copy-done.9
  2.3 0.5 fusion.189
  4.4 0.1 copy.100
  4.9 3.9 %collective-permute-start.1 = (f32[2,1,1,16,68]{4,3,2,1,0:T(8,128)S(1)}, f32[2,1,1,16,68]{4,3,2,1,0:T(8,128)S(1)}, u32[]{:S(2)}, u32[]{:S(2)}) collective-permute-start(f32[2,1,1,16,68]{4,3,2,1,0:T(8,128)S(1)} %pad_maximum_fusion.1), channel_id=1, source_target_pairs={{0,16},{16,32},{32,48},{48,64},{64,80},{80,96},{96,112},{112,128},... | collective-permute-start | bytes 26120 | tf_op jit(solution)/shard_map/ppermute | solution.py:12
  8.8 4.8 %collective-permute-start = (f32[2,1,1,16,68]{4,3,2,1,0:T(8,128)S(1)}, f32[2,1,1,16,68]{4,3,2,1,0:T(8,128)S(1)}, u32[]{:S(2)}, u32[]{:S(2)}) collective-permute-start(f32[2,1,1,16,68]{4,3,2,1,0:T(8,128)S(1)} %pad_maximum_fusion), channel_id=1, source_target_pairs={{0,1},{1,2},{2,3},{3,4},{4,5},{5,6},{6,7},{7,8},{8,9},{9,10},{10,1... | collective-permute-start | bytes 26120 | tf_op jit(solution)/shard_map/ppermute | solution.py:12
  13.7 1.3 collective-permute-done
  15.0 0.2 fusion.2
  15.3 2.1 %collective-permute-start.2 = (f32[1,1,16,68]{3,2,1,0:T(8,128)S(1)}, f32[1,1,16,68]{3,2,1,0:T(8,128)S(1)}, u32[]{:S(2)}, u32[]{:S(2)}) collective-permute-start(f32[1,1,16,68]{3,2,1,0:T(8,128)S(1)} %get-tuple-element.26), channel_id=1, source_target_pairs={{1,0},{2,1},{3,2},{4,3},{5,4},{6,5},{7,6},{8,7},{9,8},{10,9},{11,1... | collective-permute-start | bytes 13064 | tf_op jit(solution)/shard_map/ppermute | solution.py:12
  17.4 1.3 collective-permute-start.3
  19.1 1.3 collective-permute-done.2
  20.3 1.6 %collective-permute-done.3 = f32[1,1,16,68]{3,2,1,0:T(8,128)S(1)} collective-permute-done((f32[1,1,16,68]{3,2,1,0:T(8,128)S(1)}, f32[1,1,16,68]{3,2,1,0:T(8,128)S(1)}, u32[]{:S(2)}, u32[]{:S(2)}) %collective-permute-start.3) | collective-permute-done | bytes 4384 | tf_op jit(solution)/shard_map/ppermute | solution.py:12
  22.4 0.2 multiply_reduce_fusion.2
  22.6 0.6 broadcast_in_dim.124
  23.2 12.2 %all-to-all-start.2 = ((f32[16,1,16]{2,1,0:T(1,128)}), f32[16,1,16]{2,1,0:T(1,128)S(1)}, u32[]{:S(2)}, u32[]{:S(2)}) async-start(f32[16,1,16]{2,1,0:T(1,128)} %broadcast_in_dim.124), calls=%async_computation.2 | async-start | bytes 16384 | tf_op jit(solution)/shard_map/all_to_all | solution.py:49
  35.4 3.1 %collective-permute-start.5 = (f32[2,1,1,16,68]{4,3,2,1,0:T(8,128)S(1)}, f32[2,1,1,16,68]{4,3,2,1,0:T(8,128)S(1)}, u32[]{:S(2)}, u32[]{:S(2)}) collective-permute-start(f32[2,1,1,16,68]{4,3,2,1,0:T(8,128)S(1)} %stack.39), channel_id=1, source_target_pairs={{0,16},{16,32},{32,48},{48,64},{64,80},{80,96},{96,112},{112,128},... | collective-permute-start | bytes 26120 | tf_op jit(solution)/shard_map/ppermute | solution.py:12
  38.5 3.8 %collective-permute-start.4 = (f32[2,1,1,16,68]{4,3,2,1,0:T(8,128)S(1)}, f32[2,1,1,16,68]{4,3,2,1,0:T(8,128)S(1)}, u32[]{:S(2)}, u32[]{:S(2)}) collective-permute-start(f32[2,1,1,16,68]{4,3,2,1,0:T(8,128)S(1)} %stack.37), channel_id=1, source_target_pairs={{0,1},{1,2},{2,3},{3,4},{4,5},{5,6},{6,7},{7,8},{8,9},{9,10},{10,1... | collective-permute-start | bytes 26120 | tf_op jit(solution)/shard_map/ppermute | solution.py:12
  42.4 0.6 broadcast_in_dim.125
  43.0 11.7 %all-to-all-start.3 = ((f32[32,1,16]{2,1,0:T(1,128)}), f32[32,1,16]{2,1,0:T(1,128)S(1)}, u32[]{:S(2)}, u32[]{:S(2)}) async-start(f32[32,1,16]{2,1,0:T(1,128)} %broadcast_in_dim.125), calls=%async_computation.3 | async-start | bytes 32768 | tf_op jit(solution)/shard_map/all_to_all | solution.py:49
  54.8 8.4 %all-to-all-done.3 = f32[32,1,16]{2,1,0:T(1,128)S(1)} async-done(((f32[32,1,16]{2,1,0:T(1,128)}), f32[32,1,16]{2,1,0:T(1,128)S(1)}, u32[]{:S(2)}, u32[]{:S(2)}) %all-to-all-start.3) | async-done | bytes 2080 | tf_op jit(solution)/shard_map/all_to_all | solution.py:49
  63.4 0.7 copy-done.7
  64.1 0.2 convolution_multiply_fusion.2
  64.5 4.1 %collective-permute-start.6 = (f32[1,1,132]{2,1,0:T(1,128)S(1)}, f32[1,1,132]{2,1,0:T(1,128)S(1)}, u32[]{:S(2)}, u32[]{:S(2)}) collective-permute-start(f32[1,1,132]{2,1,0:T(1,128)S(1)} %constant_dynamic-update-slice_fusion), channel_id=1, source_target_pairs={{0,1},{1,2},{2,3},{3,4},{4,5},{5,6},{6,7},{7,8},{8,9},{9,10},{10,1... | collective-permute-start | bytes 1592 | tf_op jit(solution)/shard_map/ppermute | solution.py:12
  68.6 1.9 %collective-permute-start.7 = (f32[1,1,132]{2,1,0:T(1,128)S(1)}, f32[1,1,132]{2,1,0:T(1,128)S(1)}, u32[]{:S(2)}, u32[]{:S(2)}) collective-permute-start(f32[1,1,132]{2,1,0:T(1,128)S(1)} %constant_dynamic-update-slice_fusion), channel_id=1, source_target_pairs={{1,0},{2,1},{3,2},{4,3},{5,4},{6,5},{7,6},{8,7},{9,8},{10,9},{11,1... | collective-permute-start | bytes 1592 | tf_op jit(solution)/shard_map/ppermute | solution.py:12
  70.6 2.9 %collective-permute-done.7 = f32[1,1,132]{2,1,0:T(1,128)S(1)} collective-permute-done((f32[1,1,132]{2,1,0:T(1,128)S(1)}, f32[1,1,132]{2,1,0:T(1,128)S(1)}, u32[]{:S(2)}, u32[]{:S(2)}) %collective-permute-start.7) | collective-permute-done | bytes 560 | tf_op jit(solution)/shard_map/ppermute | solution.py:12
  73.5 2.2 %collective-permute-start.8 = (f32[1,3,132]{2,1,0:T(4,128)S(1)}, f32[1,3,132]{2,1,0:T(4,128)S(1)}, u32[]{:S(2)}, u32[]{:S(2)}) collective-permute-start(f32[1,3,132]{2,1,0:T(4,128)S(1)} %pad_maximum_fusion.4), channel_id=1, source_target_pairs={{0,16},{16,32},{32,48},{48,64},{64,80},{80,96},{96,112},{112,128},... | collective-permute-start | bytes 4760 | tf_op jit(solution)/shard_map/ppermute | solution.py:12
  75.7 1.3 collective-permute-start.9
  77.0 0.2 convolution_multiply_fusion
  77.3 2.8 %collective-permute-done.9 = f32[1,3,132]{2,1,0:T(4,128)S(1)} collective-permute-done((f32[1,3,132]{2,1,0:T(4,128)S(1)}, f32[1,3,132]{2,1,0:T(4,128)S(1)}, u32[]{:S(2)}, u32[]{:S(2)}) %collective-permute-start.9) | collective-permute-done | bytes 1616 | tf_op jit(solution)/shard_map/ppermute | solution.py:12
  80.1 0.6 copy-done.4
  80.7 0.1 copy.115
  80.9 0.1 copy.125
  81.0 0.6 slice-done
  81.6 0.1 reshape.560
  81.7 0.3 fusion.6
  81.9 0.2 fusion.1
  82.2 1.9 %collective-permute-start.10 = (f32[1,1,16,68]{3,2,1,0:T(8,128)S(1)}, f32[1,1,16,68]{3,2,1,0:T(8,128)S(1)}, u32[]{:S(2)}, u32[]{:S(2)}) collective-permute-start(f32[1,1,16,68]{3,2,1,0:T(8,128)S(1)} %get-tuple-element.38), channel_id=1, source_target_pairs={{1,0},{2,1},{3,2},{4,3},{5,4},{6,5},{7,6},{8,7},{9,8},{10,9},{11,1... | collective-permute-start | bytes 13064 | tf_op jit(solution)/shard_map/ppermute | solution.py:12
  84.2 1.3 collective-permute-start.11
  85.5 1.7 %collective-permute-done.10 = f32[1,1,16,68]{3,2,1,0:T(8,128)S(1)} collective-permute-done((f32[1,1,16,68]{3,2,1,0:T(8,128)S(1)}, f32[1,1,16,68]{3,2,1,0:T(8,128)S(1)}, u32[]{:S(2)}, u32[]{:S(2)}) %collective-permute-start.10) | collective-permute-done | bytes 4384 | tf_op jit(solution)/shard_map/ppermute | solution.py:12
  87.2 1.4 %collective-permute-done.11 = f32[1,1,16,68]{3,2,1,0:T(8,128)S(1)} collective-permute-done((f32[1,1,16,68]{3,2,1,0:T(8,128)S(1)}, f32[1,1,16,68]{3,2,1,0:T(8,128)S(1)}, u32[]{:S(2)}, u32[]{:S(2)}) %collective-permute-start.11) | collective-permute-done | bytes 4384 | tf_op jit(solution)/shard_map/ppermute | solution.py:12
  89.0 0.2 multiply_reduce_fusion.1
  89.9 0.2 subtract_reduce_fusion.2
  90.7 0.2 subtract_reduce_fusion.1
  91.5 0.2 subtract_reduce_fusion
  91.8 17.0 %all_to_all.42 = f32[16,1,112]{2,1,0:T(1,128)S(1)} all-to-all(f32[16,1,112]{2,1,0:T(1,128)S(1)} %broadcast_in_dim.126), channel_id=1, replica_groups=mesh['px'=32,'py'=16] {'py'}, dimensions={0} | all-to-all | bytes 14336 | tf_op jit(solution)/shard_map/all_to_all | solution.py:49
  109.3 19.2 %all_to_all.43 = f32[32,1,112]{2,1,0:T(1,128)S(1)} all-to-all(f32[32,1,112]{2,1,0:T(1,128)S(1)} %broadcast_in_dim.127), channel_id=1, replica_groups=mesh['px'=32,'py'=16] {'px'}, dimensions={0} | all-to-all | bytes 28672 | tf_op jit(solution)/shard_map/all_to_all | solution.py:49
  129.0 0.7 and_reduce_fusion
  130.3 0.7 multiply_subtract_fusion
  131.0 0.5 copy-done.10
  (145 shorter events, 5.9 us)
Async XLA Ops:
  0.6 14.4 %copy-start = (bf16[1,1,272,272]{3,2,1,0:T(8,128)(2,1)S(1)}, bf16[1,1,272,272]{3,2,1,0:T(8,128)(2,1)}, u32[]{:S(2)}) copy-start(bf16[1,1,272,272]{3,2,1,0:T(8,128)(2,1)} %param.17) | copy-start | bytes 443908
  0.6 0.8 copy-start.1
  0.7 0.8 copy-start.6
  1.6 0.7 copy-start.9
  4.9 8.8 %collective-permute-start.1 = (f32[2,1,1,16,68]{4,3,2,1,0:T(8,128)S(1)}, f32[2,1,1,16,68]{4,3,2,1,0:T(8,128)S(1)}, u32[]{:S(2)}, u32[]{:S(2)}) collective-permute-start(f32[2,1,1,16,68]{4,3,2,1,0:T(8,128)S(1)} %pad_maximum_fusion.1), channel_id=1, source_target_pairs={{0,16},{16,32},{32,48},{48,64},{64,80},{80,96},{96,112},{112,128},... | collective-permute-start | bytes 26120 | tf_op jit(solution)/shard_map/ppermute | solution.py:12
  8.8 6.2 %collective-permute-start = (f32[2,1,1,16,68]{4,3,2,1,0:T(8,128)S(1)}, f32[2,1,1,16,68]{4,3,2,1,0:T(8,128)S(1)}, u32[]{:S(2)}, u32[]{:S(2)}) collective-permute-start(f32[2,1,1,16,68]{4,3,2,1,0:T(8,128)S(1)} %pad_maximum_fusion), channel_id=1, source_target_pairs={{0,1},{1,2},{2,3},{3,4},{4,5},{5,6},{6,7},{7,8},{8,9},{9,10},{10,1... | collective-permute-start | bytes 26120 | tf_op jit(solution)/shard_map/ppermute | solution.py:12
  15.3 5.0 %collective-permute-start.2 = (f32[1,1,16,68]{3,2,1,0:T(8,128)S(1)}, f32[1,1,16,68]{3,2,1,0:T(8,128)S(1)}, u32[]{:S(2)}, u32[]{:S(2)}) collective-permute-start(f32[1,1,16,68]{3,2,1,0:T(8,128)S(1)} %get-tuple-element.26), channel_id=1, source_target_pairs={{1,0},{2,1},{3,2},{4,3},{5,4},{6,5},{7,6},{8,7},{9,8},{10,9},{11,1... | collective-permute-start | bytes 13064 | tf_op jit(solution)/shard_map/ppermute | solution.py:12
  17.4 4.5 %collective-permute-start.3 = (f32[1,1,16,68]{3,2,1,0:T(8,128)S(1)}, f32[1,1,16,68]{3,2,1,0:T(8,128)S(1)}, u32[]{:S(2)}, u32[]{:S(2)}) collective-permute-start(f32[1,1,16,68]{3,2,1,0:T(8,128)S(1)} %get-tuple-element.27), channel_id=1, source_target_pairs={{16,0},{32,16},{48,32},{64,48},{80,64},{96,80},{112,96},{128,112},... | collective-permute-start | bytes 13064 | tf_op jit(solution)/shard_map/ppermute | solution.py:12
  22.3 32.4 %copy-start.11 = (f32[1,1,2,2]{3,2,1,0:T(2,128)S(1)}, f32[1,1,2,2]{3,2,1,0:T(2,128)}, u32[]{:S(2)}) copy-start(f32[1,1,2,2]{3,2,1,0:T(2,128)} %param.19) | copy-start | bytes 52
  22.4 54.7 %copy-start.2 = (bf16[1,1,272,272]{3,2,1,0:T(8,128)(2,1)S(1)}, bf16[1,1,272,272]{3,2,1,0:T(8,128)(2,1)}, u32[]{:S(2)}) copy-start(bf16[1,1,272,272]{3,2,1,0:T(8,128)(2,1)} %param.16) | copy-start | bytes 443908
  23.2 19.2 %all-to-all-start.2 = ((f32[16,1,16]{2,1,0:T(1,128)}), f32[16,1,16]{2,1,0:T(1,128)S(1)}, u32[]{:S(2)}, u32[]{:S(2)}) async-start(f32[16,1,16]{2,1,0:T(1,128)} %broadcast_in_dim.124), calls=%async_computation.2 | async-start | bytes 16384 | tf_op jit(solution)/shard_map/all_to_all | solution.py:49
  35.4 27.9 %collective-permute-start.5 = (f32[2,1,1,16,68]{4,3,2,1,0:T(8,128)S(1)}, f32[2,1,1,16,68]{4,3,2,1,0:T(8,128)S(1)}, u32[]{:S(2)}, u32[]{:S(2)}) collective-permute-start(f32[2,1,1,16,68]{4,3,2,1,0:T(8,128)S(1)} %stack.39), channel_id=1, source_target_pairs={{0,16},{16,32},{32,48},{48,64},{64,80},{80,96},{96,112},{112,128},... | collective-permute-start | bytes 26120 | tf_op jit(solution)/shard_map/ppermute | solution.py:12
  38.5 24.7 %collective-permute-start.4 = (f32[2,1,1,16,68]{4,3,2,1,0:T(8,128)S(1)}, f32[2,1,1,16,68]{4,3,2,1,0:T(8,128)S(1)}, u32[]{:S(2)}, u32[]{:S(2)}) collective-permute-start(f32[2,1,1,16,68]{4,3,2,1,0:T(8,128)S(1)} %stack.37), channel_id=1, source_target_pairs={{0,1},{1,2},{2,3},{3,4},{4,5},{5,6},{6,7},{7,8},{8,9},{9,10},{10,1... | collective-permute-start | bytes 26120 | tf_op jit(solution)/shard_map/ppermute | solution.py:12
  43.0 20.2 %all-to-all-start.3 = ((f32[32,1,16]{2,1,0:T(1,128)}), f32[32,1,16]{2,1,0:T(1,128)S(1)}, u32[]{:S(2)}, u32[]{:S(2)}) async-start(f32[32,1,16]{2,1,0:T(1,128)} %broadcast_in_dim.125), calls=%async_computation.3 | async-start | bytes 32768 | tf_op jit(solution)/shard_map/all_to_all | solution.py:49
  54.8 8.5 %copy-start.12 = (f32[16]{0:T(128)S(1)}, f32[16]{0:T(128)}, u32[]{:S(2)}) copy-start(f32[16]{0:T(128)} %param.15) | copy-start | bytes 196
  63.3 65.7 %copy-start.8 = (f32[16]{0:T(128)}, f32[16]{0:T(128)S(1)}, u32[]{:S(2)}) copy-start(f32[16]{0:T(128)S(1)} %reduce_sum.83) | copy-start | bytes 196
  63.4 0.7 copy-start.7
  64.5 6.1 %collective-permute-start.6 = (f32[1,1,132]{2,1,0:T(1,128)S(1)}, f32[1,1,132]{2,1,0:T(1,128)S(1)}, u32[]{:S(2)}, u32[]{:S(2)}) collective-permute-start(f32[1,1,132]{2,1,0:T(1,128)S(1)} %constant_dynamic-update-slice_fusion), channel_id=1, source_target_pairs={{0,1},{1,2},{2,3},{3,4},{4,5},{5,6},{6,7},{7,8},{8,9},{9,10},{10,1... | collective-permute-start | bytes 1592 | tf_op jit(solution)/shard_map/ppermute | solution.py:12
  68.6 4.9 %collective-permute-start.7 = (f32[1,1,132]{2,1,0:T(1,128)S(1)}, f32[1,1,132]{2,1,0:T(1,128)S(1)}, u32[]{:S(2)}, u32[]{:S(2)}) collective-permute-start(f32[1,1,132]{2,1,0:T(1,128)S(1)} %constant_dynamic-update-slice_fusion), channel_id=1, source_target_pairs={{1,0},{2,1},{3,2},{4,3},{5,4},{6,5},{7,6},{8,7},{9,8},{10,9},{11,1... | collective-permute-start | bytes 1592 | tf_op jit(solution)/shard_map/ppermute | solution.py:12
  73.5 3.7 %collective-permute-start.8 = (f32[1,3,132]{2,1,0:T(4,128)S(1)}, f32[1,3,132]{2,1,0:T(4,128)S(1)}, u32[]{:S(2)}, u32[]{:S(2)}) collective-permute-start(f32[1,3,132]{2,1,0:T(4,128)S(1)} %pad_maximum_fusion.4), channel_id=1, source_target_pairs={{0,16},{16,32},{32,48},{48,64},{64,80},{80,96},{96,112},{112,128},... | collective-permute-start | bytes 4760 | tf_op jit(solution)/shard_map/ppermute | solution.py:12
  75.7 4.4 %collective-permute-start.9 = (f32[1,3,132]{2,1,0:T(4,128)S(1)}, f32[1,3,132]{2,1,0:T(4,128)S(1)}, u32[]{:S(2)}, u32[]{:S(2)}) collective-permute-start(f32[1,3,132]{2,1,0:T(4,128)S(1)} %pad_maximum_fusion.4), channel_id=1, source_target_pairs={{16,0},{32,16},{48,32},{64,48},{80,64},{96,80},{112,96},{128,112},... | collective-permute-start | bytes 4760 | tf_op jit(solution)/shard_map/ppermute | solution.py:12
  80.1 0.6 copy-start.4
  80.9 0.7 slice-start
  82.2 5.0 %collective-permute-start.10 = (f32[1,1,16,68]{3,2,1,0:T(8,128)S(1)}, f32[1,1,16,68]{3,2,1,0:T(8,128)S(1)}, u32[]{:S(2)}, u32[]{:S(2)}) collective-permute-start(f32[1,1,16,68]{3,2,1,0:T(8,128)S(1)} %get-tuple-element.38), channel_id=1, source_target_pairs={{1,0},{2,1},{3,2},{4,3},{5,4},{6,5},{7,6},{8,7},{9,8},{10,9},{11,1... | collective-permute-start | bytes 13064 | tf_op jit(solution)/shard_map/ppermute | solution.py:12
  84.2 4.4 %collective-permute-start.11 = (f32[1,1,16,68]{3,2,1,0:T(8,128)S(1)}, f32[1,1,16,68]{3,2,1,0:T(8,128)S(1)}, u32[]{:S(2)}, u32[]{:S(2)}) collective-permute-start(f32[1,1,16,68]{3,2,1,0:T(8,128)S(1)} %get-tuple-element.39), channel_id=1, source_target_pairs={{16,0},{32,16},{48,32},{64,48},{80,64},{96,80},{112,96},{128,112},... | collective-permute-start | bytes 13064 | tf_op jit(solution)/shard_map/ppermute | solution.py:12
  89.2 41.1 %copy-start.3 = (f32[1,1,16,136]{3,2,1,0:T(8,128)}, f32[1,1,16,136]{3,2,1,0:T(8,128)S(1)}, u32[]{:S(2)}) copy-start(f32[1,1,16,136]{3,2,1,0:T(8,128)S(1)} %get-tuple-element.142) | copy-start | bytes 26116
  128.9 1.4 %copy-start.5 = (f32[1,1,16,136]{3,2,1,0:T(8,128)S(1)}, f32[1,1,16,136]{3,2,1,0:T(8,128)}, u32[]{:S(2)}) copy-start(f32[1,1,16,136]{3,2,1,0:T(8,128)} %param.12) | copy-start | bytes 26116
  131.0 0.5 copy-start.10

commit v11 on v10

--- a/solution.py
+++ b/solution.py
@@ -50,7 +50,7 @@
 
 
 def all_sum(value):
-    for axis in ("py", "px"):
+    for axis in ("px", "py"):
         value = jnp.sum(gathered(value, axis), axis=0)
     return value
 
@@ -113,7 +113,7 @@
 
 
 def all_sum_mixed(plain, pairs):
-    for axis in ("py", "px"):
+    for axis in ("px", "py"):
         rows = [plain] + [part for pair in pairs for part in pair]
         width = plain.shape[0]
         every = gathered(jnp.concatenate(rows), axis)

time: 132 us -> 132 us (level)
  waiting for transfers between devices: 21.4 us -> 19.8 us
  starting transfers between devices: 55.7 us -> 57.3 us
    all_to_all x2, waiting for transfers between devices: 8.4 us -> 6.84 us  [gathered(): return lax.all_to_all(copies, axis, 0, 0, tiled=False)]
where the time goes in v11:
time: 132 us; the launch traced here: 131 us
  starting transfers between devices  57.3 us (43%)
  blocking collectives  35.5 us (27%)
  waiting for transfers between devices  19.8 us (15%)
  local copies, waits for them, and re-layouts  8.42 us (6%)
  other arithmetic  5.52 us (4%)
  between operations  3.89 us (3%)
    all_to_all x2, blocking collectives, gathered(): return lax.all_to_all(copies, axis, 0, 0, tiled=False)  35.5 us
    ppermute x12, starting transfers between devices, passed_along(): return lax.ppermute(value, axis, pairs)  32.8 us
    all_to_all x2, starting transfers between devices, gathered(): return lax.all_to_all(copies, axis, 0, 0, tiled=False)  24.5 us
    ppermute x12, waiting for transfers between devices, passed_along(): return lax.ppermute(value, axis, pairs)  13 us
    all_to_all x2, waiting for transfers between devices, gathered(): return lax.all_to_all(copies, axis, 0, 0, tiled=False)  6.84 us
    unnamed x28, local copies, waits for them, and re-layouts  3.23 us
    sub x43, other arithmetic, df_add(): return (high, error - (high - total))  2.9 us
  transfers between devices with their start and end apart: 14, of which 8 were waited for; matrix products, arithmetic and copies ran while one was open for 1% of the time, Pallas kernels for 0%

profile of v11, /device:TPU:1, one launch (start us, length us, event | category | flops | bytes accessed | tf_op | source)
XLA Modules:
  0.0 131.5 jit_solution(16624964180010118364)
XLA Ops:
  1.7 0.6 copy-done.9
  2.3 0.5 fusion.189
  4.9 3.9 %collective-permute-start.1 = (f32[2,1,1,16,68]{4,3,2,1,0:T(8,128)S(1)}, f32[2,1,1,16,68]{4,3,2,1,0:T(8,128)S(1)}, u32[]{:S(2)}, u32[]{:S(2)}) collective-permute-start(f32[2,1,1,16,68]{4,3,2,1,0:T(8,128)S(1)} %pad_maximum_fusion.1), channel_id=1, source_target_pairs={{0,16},{16,32},{32,48},{48,64},{64,80},{80,96},{96,112},{112,128},... | collective-permute-start | bytes 26120 | tf_op jit(solution)/shard_map/ppermute | solution.py:12
  8.8 4.8 %collective-permute-start = (f32[2,1,1,16,68]{4,3,2,1,0:T(8,128)S(1)}, f32[2,1,1,16,68]{4,3,2,1,0:T(8,128)S(1)}, u32[]{:S(2)}, u32[]{:S(2)}) collective-permute-start(f32[2,1,1,16,68]{4,3,2,1,0:T(8,128)S(1)} %pad_maximum_fusion), channel_id=1, source_target_pairs={{0,1},{1,2},{2,3},{3,4},{4,5},{5,6},{6,7},{7,8},{8,9},{9,10},{10,1... | collective-permute-start | bytes 26120 | tf_op jit(solution)/shard_map/ppermute | solution.py:12
  13.7 1.3 collective-permute-done
  15.0 0.2 fusion.2
  15.3 2.1 %collective-permute-start.2 = (f32[1,1,16,68]{3,2,1,0:T(8,128)S(1)}, f32[1,1,16,68]{3,2,1,0:T(8,128)S(1)}, u32[]{:S(2)}, u32[]{:S(2)}) collective-permute-start(f32[1,1,16,68]{3,2,1,0:T(8,128)S(1)} %get-tuple-element.26), channel_id=1, source_target_pairs={{1,0},{2,1},{3,2},{4,3},{5,4},{6,5},{7,6},{8,7},{9,8},{10,9},{11,1... | collective-permute-start | bytes 13064 | tf_op jit(solution)/shard_map/ppermute | solution.py:12
  17.4 1.3 collective-permute-start.3
  19.1 1.3 collective-permute-done.2
  20.3 1.6 %collective-permute-done.3 = f32[1,1,16,68]{3,2,1,0:T(8,128)S(1)} collective-permute-done((f32[1,1,16,68]{3,2,1,0:T(8,128)S(1)}, f32[1,1,16,68]{3,2,1,0:T(8,128)S(1)}, u32[]{:S(2)}, u32[]{:S(2)}) %collective-permute-start.3) | collective-permute-done | bytes 4384 | tf_op jit(solution)/shard_map/ppermute | solution.py:12
  22.4 0.2 multiply_reduce_fusion.2
  22.6 0.6 broadcast_in_dim.124
  23.2 10.9 %all-to-all-start.2 = ((f32[32,1,16]{2,1,0:T(1,128)}), f32[32,1,16]{2,1,0:T(1,128)S(1)}, u32[]{:S(2)}, u32[]{:S(2)}) async-start(f32[32,1,16]{2,1,0:T(1,128)} %broadcast_in_dim.124), calls=%async_computation.2 | async-start | bytes 32768 | tf_op jit(solution)/shard_map/all_to_all | solution.py:49
  34.1 3.1 %collective-permute-start.5 = (f32[2,1,1,16,68]{4,3,2,1,0:T(8,128)S(1)}, f32[2,1,1,16,68]{4,3,2,1,0:T(8,128)S(1)}, u32[]{:S(2)}, u32[]{:S(2)}) collective-permute-start(f32[2,1,1,16,68]{4,3,2,1,0:T(8,128)S(1)} %stack.39), channel_id=1, source_target_pairs={{0,16},{16,32},{32,48},{48,64},{64,80},{80,96},{96,112},{112,128},... | collective-permute-start | bytes 26120 | tf_op jit(solution)/shard_map/ppermute | solution.py:12
  37.3 6.2 %collective-permute-start.4 = (f32[2,1,1,16,68]{4,3,2,1,0:T(8,128)S(1)}, f32[2,1,1,16,68]{4,3,2,1,0:T(8,128)S(1)}, u32[]{:S(2)}, u32[]{:S(2)}) collective-permute-start(f32[2,1,1,16,68]{4,3,2,1,0:T(8,128)S(1)} %stack.37), channel_id=1, source_target_pairs={{0,1},{1,2},{2,3},{3,4},{4,5},{5,6},{6,7},{7,8},{8,9},{9,10},{10,1... | collective-permute-start | bytes 26120 | tf_op jit(solution)/shard_map/ppermute | solution.py:12
  43.6 0.6 broadcast_in_dim.125
  44.2 13.5 %all-to-all-start.3 = ((f32[16,1,16]{2,1,0:T(1,128)}), f32[16,1,16]{2,1,0:T(1,128)S(1)}, u32[]{:S(2)}, u32[]{:S(2)}) async-start(f32[16,1,16]{2,1,0:T(1,128)} %broadcast_in_dim.125), calls=%async_computation.3 | async-start | bytes 16384 | tf_op jit(solution)/shard_map/all_to_all | solution.py:49
  57.8 6.8 %all-to-all-done.3 = f32[16,1,16]{2,1,0:T(1,128)S(1)} async-done(((f32[16,1,16]{2,1,0:T(1,128)}), f32[16,1,16]{2,1,0:T(1,128)S(1)}, u32[]{:S(2)}, u32[]{:S(2)}) %all-to-all-start.3) | async-done | bytes 1056 | tf_op jit(solution)/shard_map/all_to_all | solution.py:49
  64.7 0.6 copy-done.12
  65.4 0.7 copy-done.7
  66.1 0.2 convolution_multiply_fusion.2
  66.5 2.7 %collective-permute-start.6 = (f32[1,1,132]{2,1,0:T(1,128)S(1)}, f32[1,1,132]{2,1,0:T(1,128)S(1)}, u32[]{:S(2)}, u32[]{:S(2)}) collective-permute-start(f32[1,1,132]{2,1,0:T(1,128)S(1)} %constant_dynamic-update-slice_fusion), channel_id=1, source_target_pairs={{0,1},{1,2},{2,3},{3,4},{4,5},{5,6},{6,7},{7,8},{8,9},{9,10},{10,1... | collective-permute-start | bytes 1592 | tf_op jit(solution)/shard_map/ppermute | solution.py:12
  69.2 1.9 %collective-permute-start.7 = (f32[1,1,132]{2,1,0:T(1,128)S(1)}, f32[1,1,132]{2,1,0:T(1,128)S(1)}, u32[]{:S(2)}, u32[]{:S(2)}) collective-permute-start(f32[1,1,132]{2,1,0:T(1,128)S(1)} %constant_dynamic-update-slice_fusion), channel_id=1, source_target_pairs={{1,0},{2,1},{3,2},{4,3},{5,4},{6,5},{7,6},{8,7},{9,8},{10,9},{11,1... | collective-permute-start | bytes 1592 | tf_op jit(solution)/shard_map/ppermute | solution.py:12
  71.2 2.9 %collective-permute-done.7 = f32[1,1,132]{2,1,0:T(1,128)S(1)} collective-permute-done((f32[1,1,132]{2,1,0:T(1,128)S(1)}, f32[1,1,132]{2,1,0:T(1,128)S(1)}, u32[]{:S(2)}, u32[]{:S(2)}) %collective-permute-start.7) | collective-permute-done | bytes 560 | tf_op jit(solution)/shard_map/ppermute | solution.py:12
  74.1 2.2 %collective-permute-start.8 = (f32[1,3,132]{2,1,0:T(4,128)S(1)}, f32[1,3,132]{2,1,0:T(4,128)S(1)}, u32[]{:S(2)}, u32[]{:S(2)}) collective-permute-start(f32[1,3,132]{2,1,0:T(4,128)S(1)} %pad_maximum_fusion.4), channel_id=1, source_target_pairs={{0,16},{16,32},{32,48},{48,64},{64,80},{80,96},{96,112},{112,128},... | collective-permute-start | bytes 4760 | tf_op jit(solution)/shard_map/ppermute | solution.py:12
  76.3 1.3 collective-permute-start.9
  77.6 0.2 convolution_multiply_fusion
  77.9 2.8 %collective-permute-done.9 = f32[1,3,132]{2,1,0:T(4,128)S(1)} collective-permute-done((f32[1,3,132]{2,1,0:T(4,128)S(1)}, f32[1,3,132]{2,1,0:T(4,128)S(1)}, u32[]{:S(2)}, u32[]{:S(2)}) %collective-permute-start.9) | collective-permute-done | bytes 1616 | tf_op jit(solution)/shard_map/ppermute | solution.py:12
  80.7 0.6 copy-done.4
  81.3 0.1 copy.115
  81.5 0.1 copy.125
  81.6 0.6 slice-done
  82.2 0.1 reshape.560
  82.3 0.3 fusion.6
  82.6 0.2 fusion.1
  82.9 1.9 %collective-permute-start.10 = (f32[1,1,16,68]{3,2,1,0:T(8,128)S(1)}, f32[1,1,16,68]{3,2,1,0:T(8,128)S(1)}, u32[]{:S(2)}, u32[]{:S(2)}) collective-permute-start(f32[1,1,16,68]{3,2,1,0:T(8,128)S(1)} %get-tuple-element.38), channel_id=1, source_target_pairs={{1,0},{2,1},{3,2},{4,3},{5,4},{6,5},{7,6},{8,7},{9,8},{10,9},{11,1... | collective-permute-start | bytes 13064 | tf_op jit(solution)/shard_map/ppermute | solution.py:12
  84.8 1.3 collective-permute-start.11
  86.1 1.7 %collective-permute-done.10 = f32[1,1,16,68]{3,2,1,0:T(8,128)S(1)} collective-permute-done((f32[1,1,16,68]{3,2,1,0:T(8,128)S(1)}, f32[1,1,16,68]{3,2,1,0:T(8,128)S(1)}, u32[]{:S(2)}, u32[]{:S(2)}) %collective-permute-start.10) | collective-permute-done | bytes 4384 | tf_op jit(solution)/shard_map/ppermute | solution.py:12
  87.8 1.4 %collective-permute-done.11 = f32[1,1,16,68]{3,2,1,0:T(8,128)S(1)} collective-permute-done((f32[1,1,16,68]{3,2,1,0:T(8,128)S(1)}, f32[1,1,16,68]{3,2,1,0:T(8,128)S(1)}, u32[]{:S(2)}, u32[]{:S(2)}) %collective-permute-start.11) | collective-permute-done | bytes 4384 | tf_op jit(solution)/shard_map/ppermute | solution.py:12
  89.6 0.2 multiply_reduce_fusion.1
  90.5 0.2 subtract_reduce_fusion.2
  91.3 0.2 subtract_reduce_fusion.1
  92.1 0.2 subtract_reduce_fusion
  92.4 20.2 %all_to_all.42 = f32[32,1,112]{2,1,0:T(1,128)S(1)} all-to-all(f32[32,1,112]{2,1,0:T(1,128)S(1)} %broadcast_in_dim.126), channel_id=1, replica_groups=mesh['px'=32,'py'=16] {'px'}, dimensions={0} | all-to-all | bytes 28672 | tf_op jit(solution)/shard_map/all_to_all | solution.py:49
  113.2 15.3 %all_to_all.43 = f32[16,1,112]{2,1,0:T(1,128)S(1)} all-to-all(f32[16,1,112]{2,1,0:T(1,128)S(1)} %broadcast_in_dim.127), channel_id=1, replica_groups=mesh['px'=32,'py'=16] {'py'}, dimensions={0} | all-to-all | bytes 14336 | tf_op jit(solution)/shard_map/all_to_all | solution.py:49
  128.9 0.7 and_reduce_fusion
  130.2 0.7 multiply_subtract_fusion
  130.9 0.5 copy-done.10
  (145 shorter events, 6.0 us)
Async XLA Ops:
  0.6 14.4 %copy-start = (bf16[1,1,272,272]{3,2,1,0:T(8,128)(2,1)S(1)}, bf16[1,1,272,272]{3,2,1,0:T(8,128)(2,1)}, u32[]{:S(2)}) copy-start(bf16[1,1,272,272]{3,2,1,0:T(8,128)(2,1)} %param.17) | copy-start | bytes 443908
  0.6 0.8 copy-start.1
  0.7 0.8 copy-start.6
  1.6 0.7 copy-start.9
  4.9 8.8 %collective-permute-start.1 = (f32[2,1,1,16,68]{4,3,2,1,0:T(8,128)S(1)}, f32[2,1,1,16,68]{4,3,2,1,0:T(8,128)S(1)}, u32[]{:S(2)}, u32[]{:S(2)}) collective-permute-start(f32[2,1,1,16,68]{4,3,2,1,0:T(8,128)S(1)} %pad_maximum_fusion.1), channel_id=1, source_target_pairs={{0,16},{16,32},{32,48},{48,64},{64,80},{80,96},{96,112},{112,128},... | collective-permute-start | bytes 26120 | tf_op jit(solution)/shard_map/ppermute | solution.py:12
  8.8 6.2 %collective-permute-start = (f32[2,1,1,16,68]{4,3,2,1,0:T(8,128)S(1)}, f32[2,1,1,16,68]{4,3,2,1,0:T(8,128)S(1)}, u32[]{:S(2)}, u32[]{:S(2)}) collective-permute-start(f32[2,1,1,16,68]{4,3,2,1,0:T(8,128)S(1)} %pad_maximum_fusion), channel_id=1, source_target_pairs={{0,1},{1,2},{2,3},{3,4},{4,5},{5,6},{6,7},{7,8},{8,9},{9,10},{10,1... | collective-permute-start | bytes 26120 | tf_op jit(solution)/shard_map/ppermute | solution.py:12
  15.3 5.0 %collective-permute-start.2 = (f32[1,1,16,68]{3,2,1,0:T(8,128)S(1)}, f32[1,1,16,68]{3,2,1,0:T(8,128)S(1)}, u32[]{:S(2)}, u32[]{:S(2)}) collective-permute-start(f32[1,1,16,68]{3,2,1,0:T(8,128)S(1)} %get-tuple-element.26), channel_id=1, source_target_pairs={{1,0},{2,1},{3,2},{4,3},{5,4},{6,5},{7,6},{8,7},{9,8},{10,9},{11,1... | collective-permute-start | bytes 13064 | tf_op jit(solution)/shard_map/ppermute | solution.py:12
  17.4 4.5 %collective-permute-start.3 = (f32[1,1,16,68]{3,2,1,0:T(8,128)S(1)}, f32[1,1,16,68]{3,2,1,0:T(8,128)S(1)}, u32[]{:S(2)}, u32[]{:S(2)}) collective-permute-start(f32[1,1,16,68]{3,2,1,0:T(8,128)S(1)} %get-tuple-element.27), channel_id=1, source_target_pairs={{16,0},{32,16},{48,32},{64,48},{80,64},{96,80},{112,96},{128,112},... | collective-permute-start | bytes 13064 | tf_op jit(solution)/shard_map/ppermute | solution.py:12
  22.3 35.4 %copy-start.11 = (f32[1,1,2,2]{3,2,1,0:T(2,128)S(1)}, f32[1,1,2,2]{3,2,1,0:T(2,128)}, u32[]{:S(2)}) copy-start(f32[1,1,2,2]{3,2,1,0:T(2,128)} %param.19) | copy-start | bytes 52
  22.4 55.3 %copy-start.2 = (bf16[1,1,272,272]{3,2,1,0:T(8,128)(2,1)S(1)}, bf16[1,1,272,272]{3,2,1,0:T(8,128)(2,1)}, u32[]{:S(2)}) copy-start(bf16[1,1,272,272]{3,2,1,0:T(8,128)(2,1)} %param.16) | copy-start | bytes 443908
  23.2 20.3 %all-to-all-start.2 = ((f32[32,1,16]{2,1,0:T(1,128)}), f32[32,1,16]{2,1,0:T(1,128)S(1)}, u32[]{:S(2)}, u32[]{:S(2)}) async-start(f32[32,1,16]{2,1,0:T(1,128)} %broadcast_in_dim.124), calls=%async_computation.2 | async-start | bytes 32768 | tf_op jit(solution)/shard_map/all_to_all | solution.py:49
  34.1 31.2 %collective-permute-start.5 = (f32[2,1,1,16,68]{4,3,2,1,0:T(8,128)S(1)}, f32[2,1,1,16,68]{4,3,2,1,0:T(8,128)S(1)}, u32[]{:S(2)}, u32[]{:S(2)}) collective-permute-start(f32[2,1,1,16,68]{4,3,2,1,0:T(8,128)S(1)} %stack.39), channel_id=1, source_target_pairs={{0,16},{16,32},{32,48},{48,64},{64,80},{80,96},{96,112},{112,128},... | collective-permute-start | bytes 26120 | tf_op jit(solution)/shard_map/ppermute | solution.py:12
  37.3 28.0 %collective-permute-start.4 = (f32[2,1,1,16,68]{4,3,2,1,0:T(8,128)S(1)}, f32[2,1,1,16,68]{4,3,2,1,0:T(8,128)S(1)}, u32[]{:S(2)}, u32[]{:S(2)}) collective-permute-start(f32[2,1,1,16,68]{4,3,2,1,0:T(8,128)S(1)} %stack.37), channel_id=1, source_target_pairs={{0,1},{1,2},{2,3},{3,4},{4,5},{5,6},{6,7},{7,8},{8,9},{9,10},{10,1... | collective-permute-start | bytes 26120 | tf_op jit(solution)/shard_map/ppermute | solution.py:12
  44.2 20.5 %all-to-all-start.3 = ((f32[16,1,16]{2,1,0:T(1,128)}), f32[16,1,16]{2,1,0:T(1,128)S(1)}, u32[]{:S(2)}, u32[]{:S(2)}) async-start(f32[16,1,16]{2,1,0:T(1,128)} %broadcast_in_dim.125), calls=%async_computation.3 | async-start | bytes 16384 | tf_op jit(solution)/shard_map/all_to_all | solution.py:49
  64.6 0.7 copy-start.12
  65.3 63.6 %copy-start.8 = (f32[16]{0:T(128)}, f32[16]{0:T(128)S(1)}, u32[]{:S(2)}) copy-start(f32[16]{0:T(128)S(1)} %reduce_sum.83) | copy-start | bytes 196
  65.4 0.7 copy-start.7
  66.5 4.7 %collective-permute-start.6 = (f32[1,1,132]{2,1,0:T(1,128)S(1)}, f32[1,1,132]{2,1,0:T(1,128)S(1)}, u32[]{:S(2)}, u32[]{:S(2)}) collective-permute-start(f32[1,1,132]{2,1,0:T(1,128)S(1)} %constant_dynamic-update-slice_fusion), channel_id=1, source_target_pairs={{0,1},{1,2},{2,3},{3,4},{4,5},{5,6},{6,7},{7,8},{8,9},{9,10},{10,1... | collective-permute-start | bytes 1592 | tf_op jit(solution)/shard_map/ppermute | solution.py:12
  69.2 4.9 %collective-permute-start.7 = (f32[1,1,132]{2,1,0:T(1,128)S(1)}, f32[1,1,132]{2,1,0:T(1,128)S(1)}, u32[]{:S(2)}, u32[]{:S(2)}) collective-permute-start(f32[1,1,132]{2,1,0:T(1,128)S(1)} %constant_dynamic-update-slice_fusion), channel_id=1, source_target_pairs={{1,0},{2,1},{3,2},{4,3},{5,4},{6,5},{7,6},{8,7},{9,8},{10,9},{11,1... | collective-permute-start | bytes 1592 | tf_op jit(solution)/shard_map/ppermute | solution.py:12
  74.1 3.7 %collective-permute-start.8 = (f32[1,3,132]{2,1,0:T(4,128)S(1)}, f32[1,3,132]{2,1,0:T(4,128)S(1)}, u32[]{:S(2)}, u32[]{:S(2)}) collective-permute-start(f32[1,3,132]{2,1,0:T(4,128)S(1)} %pad_maximum_fusion.4), channel_id=1, source_target_pairs={{0,16},{16,32},{32,48},{48,64},{64,80},{80,96},{96,112},{112,128},... | collective-permute-start | bytes 4760 | tf_op jit(solution)/shard_map/ppermute | solution.py:12
  76.3 4.4 %collective-permute-start.9 = (f32[1,3,132]{2,1,0:T(4,128)S(1)}, f32[1,3,132]{2,1,0:T(4,128)S(1)}, u32[]{:S(2)}, u32[]{:S(2)}) collective-permute-start(f32[1,3,132]{2,1,0:T(4,128)S(1)} %pad_maximum_fusion.4), channel_id=1, source_target_pairs={{16,0},{32,16},{48,32},{64,48},{80,64},{96,80},{112,96},{128,112},... | collective-permute-start | bytes 4760 | tf_op jit(solution)/shard_map/ppermute | solution.py:12
  80.7 0.6 copy-start.4
  81.5 0.7 slice-start
  82.9 5.0 %collective-permute-start.10 = (f32[1,1,16,68]{3,2,1,0:T(8,128)S(1)}, f32[1,1,16,68]{3,2,1,0:T(8,128)S(1)}, u32[]{:S(2)}, u32[]{:S(2)}) collective-permute-start(f32[1,1,16,68]{3,2,1,0:T(8,128)S(1)} %get-tuple-element.38), channel_id=1, source_target_pairs={{1,0},{2,1},{3,2},{4,3},{5,4},{6,5},{7,6},{8,7},{9,8},{10,9},{11,1... | collective-permute-start | bytes 13064 | tf_op jit(solution)/shard_map/ppermute | solution.py:12
  84.8 4.4 %collective-permute-start.11 = (f32[1,1,16,68]{3,2,1,0:T(8,128)S(1)}, f32[1,1,16,68]{3,2,1,0:T(8,128)S(1)}, u32[]{:S(2)}, u32[]{:S(2)}) collective-permute-start(f32[1,1,16,68]{3,2,1,0:T(8,128)S(1)} %get-tuple-element.39), channel_id=1, source_target_pairs={{16,0},{32,16},{48,32},{64,48},{80,64},{96,80},{112,96},{128,112},... | collective-permute-start | bytes 13064 | tf_op jit(solution)/shard_map/ppermute | solution.py:12
  89.8 40.4 %copy-start.3 = (f32[1,1,16,136]{3,2,1,0:T(8,128)}, f32[1,1,16,136]{3,2,1,0:T(8,128)S(1)}, u32[]{:S(2)}) copy-start(f32[1,1,16,136]{3,2,1,0:T(8,128)S(1)} %get-tuple-element.142) | copy-start | bytes 26116
  128.9 1.4 %copy-start.5 = (f32[1,1,16,136]{3,2,1,0:T(8,128)S(1)}, f32[1,1,16,136]{3,2,1,0:T(8,128)}, u32[]{:S(2)}) copy-start(f32[1,1,16,136]{3,2,1,0:T(8,128)} %param.12) | copy-start | bytes 26116
  130.9 0.5 copy-start.10

commit v12 on v10

--- a/solution.py
+++ b/solution.py
@@ -53,6 +53,18 @@
     for axis in ("py", "px"):
         value = jnp.sum(gathered(value, axis), axis=0)
     return value
+
+
+def all_sum_carrying(value, sends):
+    received = []
+    for axis, extra in zip(("py", "px"), sends):
+        width = value.shape[0]
+        every = gathered(jnp.concatenate([value, extra.reshape(-1)]), axis)
+        value = jnp.sum(every[:, :width], axis=0)
+        here = lax.axis_index(axis)
+        got = lax.dynamic_index_in_dim(every[:, width:], jnp.maximum(here - 1, 0), 0, keepdims=False)
+        received.append(jnp.where(here >= 1, got, 0.0).reshape(extra.shape))
+    return value, received
 
 
 def two_sum(a, b):
@@ -229,19 +241,21 @@
         from_north = jnp.concatenate([south_side[1:], north_edge], 0)
         east_perm_side = permute_side(east_side, east_flip)
         north_perm_side = permute_side(north_side, north_flip)
-        west_sent = passed_along(jnp.stack([east_perm_side, ones]), "py", 1)
-        south_sent = passed_along(jnp.stack([north_perm_side, ones]), "px", 1)
         east_term = permute_side(from_east, east_flip)
         north_term = permute_side(from_north, north_flip)
         joined = jnp.concatenate([east_side - east_term, north_side - north_term], 3)
         half_jump = 0.5 * (joined * edge_mask)
-        west_edge = 0.5 * ((west_sent[0] - west_side[:, :1]) * west_sent[1])
-        south_edge = 0.5 * ((south_sent[0] - south_side[:1]) * south_sent[1])
-        local_east = permute_side(half_jump[..., :SIDE], east_flip)
-        local_north = permute_side(half_jump[..., SIDE:], north_flip)
-        from_west = jnp.concatenate([west_edge, local_east[:, :-1]], 1)
-        from_south = jnp.concatenate([south_edge, local_north[:-1]], 0)
-        return half_jump, (half_jump[..., :SIDE], half_jump[..., SIDE:], from_west, from_south)
+        def finish(west_sent, south_sent):
+            west_edge = 0.5 * ((west_sent[0] - west_side[:, :1]) * west_sent[1])
+            south_edge = 0.5 * ((south_sent[0] - south_side[:1]) * south_sent[1])
+            local_east = permute_side(half_jump[..., :SIDE], east_flip)
+            local_north = permute_side(half_jump[..., SIDE:], north_flip)
+            from_west = jnp.concatenate([west_edge, local_east[:, :-1]], 1)
+            from_south = jnp.concatenate([south_edge, local_north[:-1]], 0)
+            return (half_jump[..., :SIDE], half_jump[..., SIDE:], from_west, from_south)
+
+        sends = (jnp.stack([east_perm_side, ones]), jnp.stack([north_perm_side, ones]))
+        return half_jump, finish, sends
 
     start_sol = solution * edge_mask
     start_res = residual * edge_mask
@@ -249,8 +263,9 @@
     res_parts, dir_parts = spread_pair(0.5 * start_res, start_dir)
     spread = spread_of(res_parts).astype(jnp.bfloat16)
     side_values = patch_products(dual_schur, spread)
-    precond, precond_parts = jump_and_spread(side_values)
-    rz_current = all_sum(jnp.sum(start_res * precond, axis=(0, 1, 3)))
+    precond, finish_parts, sends = jump_and_spread(side_values)
+    rz_current, received = all_sum_carrying(jnp.sum(start_res * precond, axis=(0, 1, 3)), sends)
+    precond_parts = finish_parts(*received)
     step_ratio = rz_current / rz_previous
     ratio = step_ratio[None, None, :, None]
     new_direction = precond + ratio * start_dir

time: 132 us -> 137 us (1.038)
  waiting for transfers between devices: 21.4 us -> 34 us
  starting transfers between devices: 55.7 us -> 47.9 us
  blocking collectives: 36.2 us -> 34.7 us
    all_to_all x2, waiting for transfers between devices: 8.4 us -> 20.9 us  [gathered(): return lax.all_to_all(copies, axis, 0, 0, tiled=False)]
    ppermute x12 -> x10, starting transfers between devices: 31.8 us -> 24 us  [passed_along(): return lax.ppermute(value, axis, pairs)]
    all_to_all x2, blocking collectives: 36.2 us -> 34.7 us  [gathered(): return lax.all_to_all(copies, axis, 0, 0, tiled=False)]
    ppermute x12 -> x10, waiting for transfers between devices: 13 us -> 13.2 us  [passed_along(): return lax.ppermute(value, axis, pairs)]
  transfers between devices with their start and end apart: 14 -> 12, of which waited for: 8 -> 9; matrix products, arithmetic and copies ran while one was open for 1% -> 1% of each run, Pallas kernels for 0% -> 0%
where the time goes in v12:
time: 137 us; the launch traced here: 136 us
  starting transfers between devices  47.9 us (35%)
  blocking collectives  34.7 us (25%)
  waiting for transfers between devices  34 us (25%)
  local copies, waits for them, and re-layouts  8.64 us (6%)
  other arithmetic  5.7 us (4%)
  between operations  3.99 us (3%)
    all_to_all x2, blocking collectives, gathered(): return lax.all_to_all(copies, axis, 0, 0, tiled=False)  34.7 us
    ppermute x10, starting transfers between devices, passed_along(): return lax.ppermute(value, axis, pairs)  24 us
    all_to_all x2, starting transfers between devices, gathered(): return lax.all_to_all(copies, axis, 0, 0, tiled=False)  23.9 us
    all_to_all x2, waiting for transfers between devices, gathered(): return lax.all_to_all(copies, axis, 0, 0, tiled=False)  20.9 us
    ppermute x10, waiting for transfers between devices, passed_along(): return lax.ppermute(value, axis, pairs)  13.2 us
    sub x43, other arithmetic, df_add(): return (high, error - (high - total))  2.89 us
  transfers between devices with their start and end apart: 12, of which 9 were waited for; matrix products, arithmetic and copies ran while one was open for 1% of the time, Pallas kernels for 0%

profile of v12, /device:TPU:1, one launch (start us, length us, event | category | flops | bytes accessed | tf_op | source)
XLA Modules:
  0.0 136.1 jit_solution(2168547468492449132)
XLA Ops:
  1.4 0.5 fusion.183
  4.3 3.9 %collective-permute-start.1 = (f32[2,1,1,16,68]{4,3,2,1,0:T(8,128)S(1)}, f32[2,1,1,16,68]{4,3,2,1,0:T(8,128)S(1)}, u32[]{:S(2)}, u32[]{:S(2)}) collective-permute-start(f32[2,1,1,16,68]{4,3,2,1,0:T(8,128)S(1)} %pad_maximum_fusion.1), channel_id=1, source_target_pairs={{0,16},{16,32},{32,48},{48,64},{64,80},{80,96},{96,112},{112,128},... | collective-permute-start | bytes 26120 | tf_op jit(solution)/shard_map/ppermute | solution.py:12
  8.2 4.8 %collective-permute-start = (f32[2,1,1,16,68]{4,3,2,1,0:T(8,128)S(1)}, f32[2,1,1,16,68]{4,3,2,1,0:T(8,128)S(1)}, u32[]{:S(2)}, u32[]{:S(2)}) collective-permute-start(f32[2,1,1,16,68]{4,3,2,1,0:T(8,128)S(1)} %pad_maximum_fusion), channel_id=1, source_target_pairs={{0,1},{1,2},{2,3},{3,4},{4,5},{5,6},{6,7},{7,8},{8,9},{9,10},{10,1... | collective-permute-start | bytes 26120 | tf_op jit(solution)/shard_map/ppermute | solution.py:12
  13.1 1.3 collective-permute-done
  14.4 0.2 fusion.2
  14.7 2.1 %collective-permute-start.2 = (f32[1,1,16,68]{3,2,1,0:T(8,128)S(1)}, f32[1,1,16,68]{3,2,1,0:T(8,128)S(1)}, u32[]{:S(2)}, u32[]{:S(2)}) collective-permute-start(f32[1,1,16,68]{3,2,1,0:T(8,128)S(1)} %get-tuple-element.26), channel_id=1, source_target_pairs={{1,0},{2,1},{3,2},{4,3},{5,4},{6,5},{7,6},{8,7},{9,8},{10,9},{11,1... | collective-permute-start | bytes 13064 | tf_op jit(solution)/shard_map/ppermute | solution.py:12
  16.8 1.3 collective-permute-start.3
  18.2 1.5 %collective-permute-done.2 = f32[1,1,16,68]{3,2,1,0:T(8,128)S(1)} collective-permute-done((f32[1,1,16,68]{3,2,1,0:T(8,128)S(1)}, f32[1,1,16,68]{3,2,1,0:T(8,128)S(1)}, u32[]{:S(2)}, u32[]{:S(2)}) %collective-permute-start.2) | collective-permute-done | bytes 4384 | tf_op jit(solution)/shard_map/ppermute | solution.py:12
  19.7 1.6 %collective-permute-done.3 = f32[1,1,16,68]{3,2,1,0:T(8,128)S(1)} collective-permute-done((f32[1,1,16,68]{3,2,1,0:T(8,128)S(1)}, f32[1,1,16,68]{3,2,1,0:T(8,128)S(1)}, u32[]{:S(2)}, u32[]{:S(2)}) %collective-permute-start.3) | collective-permute-done | bytes 4384 | tf_op jit(solution)/shard_map/ppermute | solution.py:12
  22.0 0.1 reshape.606
  22.1 0.2 multiply_reduce_fusion.2
  22.3 0.7 broadcast_in_dim.129
  23.1 12.2 %all-to-all-start.2 = ((f32[16,1,2192]{2,1,0:T(1,128)}), f32[16,1,2192]{2,1,0:T(1,128)S(1)}, u32[]{:S(2)}, u32[]{:S(2)}) async-start(f32[16,1,2192]{2,1,0:T(1,128)} %broadcast_in_dim.129), calls=%async_computation.2 | async-start | bytes 294912 | tf_op jit(solution)/shard_map/all_to_all | solution.py:49
  35.3 0.7 copy-done.11
  36.1 8.5 %all-to-all-done.2 = f32[16,1,2192]{2,1,0:T(1,128)S(1)} async-done(((f32[16,1,2192]{2,1,0:T(1,128)}), f32[16,1,2192]{2,1,0:T(1,128)S(1)}, u32[]{:S(2)}, u32[]{:S(2)}) %all-to-all-start.2) | async-done | bytes 140320 | tf_op jit(solution)/shard_map/all_to_all | solution.py:49
  44.7 0.9 broadcast_in_dim.130
  45.6 11.7 %all-to-all-start.3 = ((f32[32,1,2192]{2,1,0:T(1,128)}), f32[32,1,2192]{2,1,0:T(1,128)S(1)}, u32[]{:S(2)}, u32[]{:S(2)}) async-start(f32[32,1,2192]{2,1,0:T(1,128)} %broadcast_in_dim.130), calls=%async_computation.3 | async-start | bytes 589824 | tf_op jit(solution)/shard_map/all_to_all | solution.py:49
  57.7 12.4 %all-to-all-done.3 = f32[32,1,2192]{2,1,0:T(1,128)S(1)} async-done(((f32[32,1,2192]{2,1,0:T(1,128)}), f32[32,1,2192]{2,1,0:T(1,128)S(1)}, u32[]{:S(2)}, u32[]{:S(2)}) %all-to-all-start.3) | async-done | bytes 280608 | tf_op jit(solution)/shard_map/all_to_all | solution.py:49
  70.2 0.1 slice.1089
  70.6 0.2 copy-done.12
  70.9 0.2 convolution_multiply_fusion.2
  71.3 3.7 %collective-permute-start.4 = (f32[1,1,132]{2,1,0:T(1,128)S(1)}, f32[1,1,132]{2,1,0:T(1,128)S(1)}, u32[]{:S(2)}, u32[]{:S(2)}) collective-permute-start(f32[1,1,132]{2,1,0:T(1,128)S(1)} %constant_dynamic-update-slice_fusion), channel_id=1, source_target_pairs={{0,1},{1,2},{2,3},{3,4},{4,5},{5,6},{6,7},{7,8},{8,9},{9,10},{10,1... | collective-permute-start | bytes 1592 | tf_op jit(solution)/shard_map/ppermute | solution.py:12
  75.1 1.9 %collective-permute-start.5 = (f32[1,1,132]{2,1,0:T(1,128)S(1)}, f32[1,1,132]{2,1,0:T(1,128)S(1)}, u32[]{:S(2)}, u32[]{:S(2)}) collective-permute-start(f32[1,1,132]{2,1,0:T(1,128)S(1)} %constant_dynamic-update-slice_fusion), channel_id=1, source_target_pairs={{1,0},{2,1},{3,2},{4,3},{5,4},{6,5},{7,6},{8,7},{9,8},{10,9},{11,1... | collective-permute-start | bytes 1592 | tf_op jit(solution)/shard_map/ppermute | solution.py:12
  77.1 2.9 %collective-permute-done.5 = f32[1,1,132]{2,1,0:T(1,128)S(1)} collective-permute-done((f32[1,1,132]{2,1,0:T(1,128)S(1)}, f32[1,1,132]{2,1,0:T(1,128)S(1)}, u32[]{:S(2)}, u32[]{:S(2)}) %collective-permute-start.5) | collective-permute-done | bytes 560 | tf_op jit(solution)/shard_map/ppermute | solution.py:12
  80.0 1.7 %collective-permute-start.6 = (f32[1,3,132]{2,1,0:T(4,128)S(1)}, f32[1,3,132]{2,1,0:T(4,128)S(1)}, u32[]{:S(2)}, u32[]{:S(2)}) collective-permute-start(f32[1,3,132]{2,1,0:T(4,128)S(1)} %pad_maximum_fusion.6), channel_id=1, source_target_pairs={{0,16},{16,32},{32,48},{48,64},{64,80},{80,96},{96,112},{112,128},... | collective-permute-start | bytes 4760 | tf_op jit(solution)/shard_map/ppermute | solution.py:12
  81.7 1.3 collective-permute-start.7
  83.0 0.2 convolution_multiply_fusion
  83.2 2.8 %collective-permute-done.7 = f32[1,3,132]{2,1,0:T(4,128)S(1)} collective-permute-done((f32[1,3,132]{2,1,0:T(4,128)S(1)}, f32[1,3,132]{2,1,0:T(4,128)S(1)}, u32[]{:S(2)}, u32[]{:S(2)}) %collective-permute-start.7) | collective-permute-done | bytes 1616 | tf_op jit(solution)/shard_map/ppermute | solution.py:12
  86.0 0.6 copy-done.4
  86.6 0.1 copy.113
  86.8 0.1 copy.124
  86.9 0.6 slice-done
  87.5 0.1 reshape.614
  87.6 0.3 fusion.6
  87.9 0.2 fusion.1
  88.2 1.9 %collective-permute-start.8 = (f32[1,1,16,68]{3,2,1,0:T(8,128)S(1)}, f32[1,1,16,68]{3,2,1,0:T(8,128)S(1)}, u32[]{:S(2)}, u32[]{:S(2)}) collective-permute-start(f32[1,1,16,68]{3,2,1,0:T(8,128)S(1)} %get-tuple-element.38), channel_id=1, source_target_pairs={{1,0},{2,1},{3,2},{4,3},{5,4},{6,5},{7,6},{8,7},{9,8},{10,9},{11,1... | collective-permute-start | bytes 13064 | tf_op jit(solution)/shard_map/ppermute | solution.py:12
  90.1 1.3 collective-permute-start.9
  91.4 1.7 %collective-permute-done.8 = f32[1,1,16,68]{3,2,1,0:T(8,128)S(1)} collective-permute-done((f32[1,1,16,68]{3,2,1,0:T(8,128)S(1)}, f32[1,1,16,68]{3,2,1,0:T(8,128)S(1)}, u32[]{:S(2)}, u32[]{:S(2)}) %collective-permute-start.8) | collective-permute-done | bytes 4384 | tf_op jit(solution)/shard_map/ppermute | solution.py:12
  93.1 1.4 collective-permute-done.9
  95.0 0.2 multiply_reduce_fusion.1
  95.8 0.2 subtract_reduce_fusion
  96.6 0.2 subtract_reduce_fusion.1
  97.4 0.2 subtract_reduce_fusion.2
  97.7 14.5 %all_to_all.48 = f32[16,1,112]{2,1,0:T(1,128)S(1)} all-to-all(f32[16,1,112]{2,1,0:T(1,128)S(1)} %broadcast_in_dim.132), channel_id=1, replica_groups=mesh['px'=32,'py'=16] {'py'}, dimensions={0} | all-to-all | bytes 14336 | tf_op jit(solution)/shard_map/all_to_all | solution.py:49
  112.8 20.2 %all_to_all.49 = f32[32,1,112]{2,1,0:T(1,128)S(1)} all-to-all(f32[32,1,112]{2,1,0:T(1,128)S(1)} %broadcast_in_dim.133), channel_id=1, replica_groups=mesh['px'=32,'py'=16] {'px'}, dimensions={0} | all-to-all | bytes 28672 | tf_op jit(solution)/shard_map/all_to_all | solution.py:49
  133.5 0.7 and_reduce_fusion
  134.8 0.7 multiply_subtract_fusion
  135.5 0.5 copy-done.10
  (158 shorter events, 6.8 us)
Async XLA Ops:
  0.6 13.8 %copy-start = (bf16[1,1,272,272]{3,2,1,0:T(8,128)(2,1)S(1)}, bf16[1,1,272,272]{3,2,1,0:T(8,128)(2,1)}, u32[]{:S(2)}) copy-start(bf16[1,1,272,272]{3,2,1,0:T(8,128)(2,1)} %param.17) | copy-start | bytes 443908
  0.7 0.7 copy-start.9
  0.7 2.6 %copy-start.1 = (f32[1,1,16,136]{3,2,1,0:T(8,128)S(1)}, f32[1,1,16,136]{3,2,1,0:T(8,128)}, u32[]{:S(2)}) copy-start(f32[1,1,16,136]{3,2,1,0:T(8,128)} %param.13) | copy-start | bytes 26116
  0.7 2.6 %copy-start.6 = (f32[1,1,16,136]{3,2,1,0:T(8,128)S(1)}, f32[1,1,16,136]{3,2,1,0:T(8,128)}, u32[]{:S(2)}) copy-start(f32[1,1,16,136]{3,2,1,0:T(8,128)} %param.14) | copy-start | bytes 26116
  4.3 8.8 %collective-permute-start.1 = (f32[2,1,1,16,68]{4,3,2,1,0:T(8,128)S(1)}, f32[2,1,1,16,68]{4,3,2,1,0:T(8,128)S(1)}, u32[]{:S(2)}, u32[]{:S(2)}) collective-permute-start(f32[2,1,1,16,68]{4,3,2,1,0:T(8,128)S(1)} %pad_maximum_fusion.1), channel_id=1, source_target_pairs={{0,16},{16,32},{32,48},{48,64},{64,80},{80,96},{96,112},{112,128},... | collective-permute-start | bytes 26120 | tf_op jit(solution)/shard_map/ppermute | solution.py:12
  8.2 6.2 %collective-permute-start = (f32[2,1,1,16,68]{4,3,2,1,0:T(8,128)S(1)}, f32[2,1,1,16,68]{4,3,2,1,0:T(8,128)S(1)}, u32[]{:S(2)}, u32[]{:S(2)}) collective-permute-start(f32[2,1,1,16,68]{4,3,2,1,0:T(8,128)S(1)} %pad_maximum_fusion), channel_id=1, source_target_pairs={{0,1},{1,2},{2,3},{3,4},{4,5},{5,6},{6,7},{7,8},{8,9},{9,10},{10,1... | collective-permute-start | bytes 26120 | tf_op jit(solution)/shard_map/ppermute | solution.py:12
  14.7 5.0 %collective-permute-start.2 = (f32[1,1,16,68]{3,2,1,0:T(8,128)S(1)}, f32[1,1,16,68]{3,2,1,0:T(8,128)S(1)}, u32[]{:S(2)}, u32[]{:S(2)}) collective-permute-start(f32[1,1,16,68]{3,2,1,0:T(8,128)S(1)} %get-tuple-element.26), channel_id=1, source_target_pairs={{1,0},{2,1},{3,2},{4,3},{5,4},{6,5},{7,6},{8,7},{9,8},{10,9},{11,1... | collective-permute-start | bytes 13064 | tf_op jit(solution)/shard_map/ppermute | solution.py:12
  16.8 4.5 %collective-permute-start.3 = (f32[1,1,16,68]{3,2,1,0:T(8,128)S(1)}, f32[1,1,16,68]{3,2,1,0:T(8,128)S(1)}, u32[]{:S(2)}, u32[]{:S(2)}) collective-permute-start(f32[1,1,16,68]{3,2,1,0:T(8,128)S(1)} %get-tuple-element.27), channel_id=1, source_target_pairs={{16,0},{32,16},{48,32},{64,48},{80,64},{96,80},{112,96},{128,112},... | collective-permute-start | bytes 13064 | tf_op jit(solution)/shard_map/ppermute | solution.py:12
  23.1 21.5 %all-to-all-start.2 = ((f32[16,1,2192]{2,1,0:T(1,128)}), f32[16,1,2192]{2,1,0:T(1,128)S(1)}, u32[]{:S(2)}, u32[]{:S(2)}) async-start(f32[16,1,2192]{2,1,0:T(1,128)} %broadcast_in_dim.129), calls=%async_computation.2 | async-start | bytes 294912 | tf_op jit(solution)/shard_map/all_to_all | solution.py:49
  35.3 0.7 copy-start.11
  45.6 24.5 %all-to-all-start.3 = ((f32[32,1,2192]{2,1,0:T(1,128)}), f32[32,1,2192]{2,1,0:T(1,128)S(1)}, u32[]{:S(2)}, u32[]{:S(2)}) async-start(f32[32,1,2192]{2,1,0:T(1,128)} %broadcast_in_dim.130), calls=%async_computation.3 | async-start | bytes 589824 | tf_op jit(solution)/shard_map/all_to_all | solution.py:49
  70.2 63.3 %copy-start.8 = (f32[16]{0:T(128)}, f32[16]{0:T(128)S(1)}, u32[]{:S(2)}) copy-start(f32[16]{0:T(128)S(1)} %slice_reduce_fusion.1) | copy-start | bytes 196
  70.2 0.7 copy-start.12
  70.2 0.7 copy-start.7
  70.3 12.6 %copy-start.2 = (bf16[1,1,272,272]{3,2,1,0:T(8,128)(2,1)S(1)}, bf16[1,1,272,272]{3,2,1,0:T(8,128)(2,1)}, u32[]{:S(2)}) copy-start(bf16[1,1,272,272]{3,2,1,0:T(8,128)(2,1)} %param.16) | copy-start | bytes 443908
  71.3 5.8 %collective-permute-start.4 = (f32[1,1,132]{2,1,0:T(1,128)S(1)}, f32[1,1,132]{2,1,0:T(1,128)S(1)}, u32[]{:S(2)}, u32[]{:S(2)}) collective-permute-start(f32[1,1,132]{2,1,0:T(1,128)S(1)} %constant_dynamic-update-slice_fusion), channel_id=1, source_target_pairs={{0,1},{1,2},{2,3},{3,4},{4,5},{5,6},{6,7},{7,8},{8,9},{9,10},{10,1... | collective-permute-start | bytes 1592 | tf_op jit(solution)/shard_map/ppermute | solution.py:12
  75.1 4.9 %collective-permute-start.5 = (f32[1,1,132]{2,1,0:T(1,128)S(1)}, f32[1,1,132]{2,1,0:T(1,128)S(1)}, u32[]{:S(2)}, u32[]{:S(2)}) collective-permute-start(f32[1,1,132]{2,1,0:T(1,128)S(1)} %constant_dynamic-update-slice_fusion), channel_id=1, source_target_pairs={{1,0},{2,1},{3,2},{4,3},{5,4},{6,5},{7,6},{8,7},{9,8},{10,9},{11,1... | collective-permute-start | bytes 1592 | tf_op jit(solution)/shard_map/ppermute | solution.py:12
  80.0 3.2 %collective-permute-start.6 = (f32[1,3,132]{2,1,0:T(4,128)S(1)}, f32[1,3,132]{2,1,0:T(4,128)S(1)}, u32[]{:S(2)}, u32[]{:S(2)}) collective-permute-start(f32[1,3,132]{2,1,0:T(4,128)S(1)} %pad_maximum_fusion.6), channel_id=1, source_target_pairs={{0,16},{16,32},{32,48},{48,64},{64,80},{80,96},{96,112},{112,128},... | collective-permute-start | bytes 4760 | tf_op jit(solution)/shard_map/ppermute | solution.py:12
  81.7 4.4 %collective-permute-start.7 = (f32[1,3,132]{2,1,0:T(4,128)S(1)}, f32[1,3,132]{2,1,0:T(4,128)S(1)}, u32[]{:S(2)}, u32[]{:S(2)}) collective-permute-start(f32[1,3,132]{2,1,0:T(4,128)S(1)} %pad_maximum_fusion.6), channel_id=1, source_target_pairs={{16,0},{32,16},{48,32},{64,48},{80,64},{96,80},{112,96},{128,112},... | collective-permute-start | bytes 4760 | tf_op jit(solution)/shard_map/ppermute | solution.py:12
  86.0 0.6 copy-start.4
  86.8 0.7 slice-start
  88.2 5.0 %collective-permute-start.8 = (f32[1,1,16,68]{3,2,1,0:T(8,128)S(1)}, f32[1,1,16,68]{3,2,1,0:T(8,128)S(1)}, u32[]{:S(2)}, u32[]{:S(2)}) collective-permute-start(f32[1,1,16,68]{3,2,1,0:T(8,128)S(1)} %get-tuple-element.38), channel_id=1, source_target_pairs={{1,0},{2,1},{3,2},{4,3},{5,4},{6,5},{7,6},{8,7},{9,8},{10,9},{11,1... | collective-permute-start | bytes 13064 | tf_op jit(solution)/shard_map/ppermute | solution.py:12
  90.1 4.4 %collective-permute-start.9 = (f32[1,1,16,68]{3,2,1,0:T(8,128)S(1)}, f32[1,1,16,68]{3,2,1,0:T(8,128)S(1)}, u32[]{:S(2)}, u32[]{:S(2)}) collective-permute-start(f32[1,1,16,68]{3,2,1,0:T(8,128)S(1)} %get-tuple-element.39), channel_id=1, source_target_pairs={{16,0},{32,16},{48,32},{64,48},{80,64},{96,80},{112,96},{128,112},... | collective-permute-start | bytes 13064 | tf_op jit(solution)/shard_map/ppermute | solution.py:12
  95.1 39.7 %copy-start.3 = (f32[1,1,16,136]{3,2,1,0:T(8,128)}, f32[1,1,16,136]{3,2,1,0:T(8,128)S(1)}, u32[]{:S(2)}) copy-start(f32[1,1,16,136]{3,2,1,0:T(8,128)S(1)} %get-tuple-element.146) | copy-start | bytes 26116
  133.5 1.4 %copy-start.5 = (f32[1,1,16,136]{3,2,1,0:T(8,128)S(1)}, f32[1,1,16,136]{3,2,1,0:T(8,128)}, u32[]{:S(2)}) copy-start(f32[1,1,16,136]{3,2,1,0:T(8,128)} %param.12) | copy-start | bytes 26116
  135.5 0.5 copy-start.10

commit v13 on v10

--- a/solution.py
+++ b/solution.py
@@ -100,6 +100,22 @@
         half = high.shape[1] // 2
         high, low = df_add((high[:, :half], low[:, :half]), (high[:, half:], low[:, half:]))
     return high[:, 0], low[:, 0]
+
+
+def df_case_sums_stacked(a, b):
+    count, cases = a.shape[0], a.shape[3]
+    a = jnp.moveaxis(a, 3, 1).reshape(count, cases, -1)
+    b = jnp.moveaxis(b, 3, 1).reshape(count, cases, -1)
+    high, low = two_prod(a, b)
+    while high.shape[2] > 1:
+        if high.shape[2] % 2:
+            high = jnp.pad(high, ((0, 0), (0, 0), (0, 1)))
+            low = jnp.pad(low, ((0, 0), (0, 0), (0, 1)))
+        half = high.shape[2] // 2
+        high, low = df_add(
+            (high[:, :, :half], low[:, :, :half]), (high[:, :, half:], low[:, :, half:])
+        )
+    return [(high[k, :, 0], low[k, :, 0]) for k in range(count)]
 
 
 def df_tree_sum(high, low):
@@ -303,7 +319,9 @@
     image = jump_b((inner_part + correction) * active)
     curvature, (res_res, res_img, img_img) = all_sum_mixed(
         jnp.sum(new_direction * image, axis=(0, 1, 3)),
-        [df_case_sums(start_res, start_res), df_case_sums(start_res, image), df_case_sums(image, image)],
+        df_case_sums_stacked(
+            jnp.stack([start_res, start_res, image]), jnp.stack([start_res, image, image])
+        ),
     )
     step_length = rz_current / curvature
     new_solution = start_sol + step_length[None, None, :, None] * new_direction

time: 132 us -> 131 us (level)
  other arithmetic: 5.53 us -> 3.91 us
    sub x43 -> x27, other arithmetic: 2.9 us -> 1.25 us  [df_add(): return (high, error - (high - total))]
where the time goes in v13:
time: 131 us; the launch traced here: 130 us
  starting transfers between devices  55.7 us (43%)
  blocking collectives  36.2 us (28%)
  waiting for transfers between devices  21.4 us (16%)
  local copies, waits for them, and re-layouts  8.07 us (6%)
  between operations  3.94 us (3%)
  other arithmetic  3.91 us (3%)
    all_to_all x2, blocking collectives, gathered(): return lax.all_to_all(copies, axis, 0, 0, tiled=False)  36.2 us
    ppermute x12, starting transfers between devices, passed_along(): return lax.ppermute(value, axis, pairs)  31.8 us
    all_to_all x2, starting transfers between devices, gathered(): return lax.all_to_all(copies, axis, 0, 0, tiled=False)  23.9 us
    ppermute x12, waiting for transfers between devices, passed_along(): return lax.ppermute(value, axis, pairs)  13 us
    all_to_all x2, waiting for transfers between devices, gathered(): return lax.all_to_all(copies, axis, 0, 0, tiled=False)  8.4 us
  transfers between devices with their start and end apart: 14, of which 8 were waited for; matrix products, arithmetic and copies ran while one was open for 1% of the time, Pallas kernels for 0%

profile of v13, /device:TPU:1, one launch (start us, length us, event | category | flops | bytes accessed | tf_op | source)
XLA Modules:
  0.0 130.2 jit_solution(14095477006818820413)
XLA Ops:
  1.7 0.6 copy-done.9
  2.3 0.5 fusion.150
  4.4 0.1 copy.108
  4.9 3.9 %collective-permute-start.1 = (f32[2,1,1,16,68]{4,3,2,1,0:T(8,128)S(1)}, f32[2,1,1,16,68]{4,3,2,1,0:T(8,128)S(1)}, u32[]{:S(2)}, u32[]{:S(2)}) collective-permute-start(f32[2,1,1,16,68]{4,3,2,1,0:T(8,128)S(1)} %pad_maximum_fusion.1), channel_id=1, source_target_pairs={{0,16},{16,32},{32,48},{48,64},{64,80},{80,96},{96,112},{112,128},... | collective-permute-start | bytes 26120 | tf_op jit(solution)/shard_map/ppermute | solution.py:12
  8.8 4.8 %collective-permute-start = (f32[2,1,1,16,68]{4,3,2,1,0:T(8,128)S(1)}, f32[2,1,1,16,68]{4,3,2,1,0:T(8,128)S(1)}, u32[]{:S(2)}, u32[]{:S(2)}) collective-permute-start(f32[2,1,1,16,68]{4,3,2,1,0:T(8,128)S(1)} %pad_maximum_fusion), channel_id=1, source_target_pairs={{0,1},{1,2},{2,3},{3,4},{4,5},{5,6},{6,7},{7,8},{8,9},{9,10},{10,1... | collective-permute-start | bytes 26120 | tf_op jit(solution)/shard_map/ppermute | solution.py:12
  13.7 1.3 %collective-permute-done = f32[2,1,1,16,68]{4,3,2,1,0:T(8,128)S(1)} collective-permute-done((f32[2,1,1,16,68]{4,3,2,1,0:T(8,128)S(1)}, f32[2,1,1,16,68]{4,3,2,1,0:T(8,128)S(1)}, u32[]{:S(2)}, u32[]{:S(2)}) %collective-permute-start) | collective-permute-done | bytes 8736 | tf_op jit(solution)/shard_map/ppermute | solution.py:12
  15.0 0.2 fusion.2
  15.3 2.1 %collective-permute-start.2 = (f32[1,1,16,68]{3,2,1,0:T(8,128)S(1)}, f32[1,1,16,68]{3,2,1,0:T(8,128)S(1)}, u32[]{:S(2)}, u32[]{:S(2)}) collective-permute-start(f32[1,1,16,68]{3,2,1,0:T(8,128)S(1)} %get-tuple-element.26), channel_id=1, source_target_pairs={{1,0},{2,1},{3,2},{4,3},{5,4},{6,5},{7,6},{8,7},{9,8},{10,9},{11,1... | collective-permute-start | bytes 13064 | tf_op jit(solution)/shard_map/ppermute | solution.py:12
  17.4 1.3 collective-permute-start.3
  18.7 0.1 copy.118
  19.1 1.3 collective-permute-done.2
  20.3 1.6 %collective-permute-done.3 = f32[1,1,16,68]{3,2,1,0:T(8,128)S(1)} collective-permute-done((f32[1,1,16,68]{3,2,1,0:T(8,128)S(1)}, f32[1,1,16,68]{3,2,1,0:T(8,128)S(1)}, u32[]{:S(2)}, u32[]{:S(2)}) %collective-permute-start.3) | collective-permute-done | bytes 4384 | tf_op jit(solution)/shard_map/ppermute | solution.py:12
  22.4 0.2 multiply_reduce_fusion.2
  22.6 0.6 broadcast_in_dim.124
  23.2 12.2 %all-to-all-start.2 = ((f32[16,1,16]{2,1,0:T(1,128)}), f32[16,1,16]{2,1,0:T(1,128)S(1)}, u32[]{:S(2)}, u32[]{:S(2)}) async-start(f32[16,1,16]{2,1,0:T(1,128)} %broadcast_in_dim.124), calls=%async_computation.2 | async-start | bytes 16384 | tf_op jit(solution)/shard_map/all_to_all | solution.py:49
  35.4 3.1 %collective-permute-start.5 = (f32[2,1,1,16,68]{4,3,2,1,0:T(8,128)S(1)}, f32[2,1,1,16,68]{4,3,2,1,0:T(8,128)S(1)}, u32[]{:S(2)}, u32[]{:S(2)}) collective-permute-start(f32[2,1,1,16,68]{4,3,2,1,0:T(8,128)S(1)} %stack.53), channel_id=1, source_target_pairs={{0,16},{16,32},{32,48},{48,64},{64,80},{80,96},{96,112},{112,128},... | collective-permute-start | bytes 26120 | tf_op jit(solution)/shard_map/ppermute | solution.py:12
  38.5 3.8 %collective-permute-start.4 = (f32[2,1,1,16,68]{4,3,2,1,0:T(8,128)S(1)}, f32[2,1,1,16,68]{4,3,2,1,0:T(8,128)S(1)}, u32[]{:S(2)}, u32[]{:S(2)}) collective-permute-start(f32[2,1,1,16,68]{4,3,2,1,0:T(8,128)S(1)} %stack.51), channel_id=1, source_target_pairs={{0,1},{1,2},{2,3},{3,4},{4,5},{5,6},{6,7},{7,8},{8,9},{9,10},{10,1... | collective-permute-start | bytes 26120 | tf_op jit(solution)/shard_map/ppermute | solution.py:12
  42.4 0.6 broadcast_in_dim.125
  43.0 11.7 %all-to-all-start.3 = ((f32[32,1,16]{2,1,0:T(1,128)}), f32[32,1,16]{2,1,0:T(1,128)S(1)}, u32[]{:S(2)}, u32[]{:S(2)}) async-start(f32[32,1,16]{2,1,0:T(1,128)} %broadcast_in_dim.125), calls=%async_computation.3 | async-start | bytes 32768 | tf_op jit(solution)/shard_map/all_to_all | solution.py:49
  54.8 8.4 %all-to-all-done.3 = f32[32,1,16]{2,1,0:T(1,128)S(1)} async-done(((f32[32,1,16]{2,1,0:T(1,128)}), f32[32,1,16]{2,1,0:T(1,128)S(1)}, u32[]{:S(2)}, u32[]{:S(2)}) %all-to-all-start.3) | async-done | bytes 2080 | tf_op jit(solution)/shard_map/all_to_all | solution.py:49
  63.4 0.7 copy-done.7
  64.1 0.2 convolution_multiply_fusion.2
  64.5 4.1 %collective-permute-start.6 = (f32[1,1,132]{2,1,0:T(1,128)S(1)}, f32[1,1,132]{2,1,0:T(1,128)S(1)}, u32[]{:S(2)}, u32[]{:S(2)}) collective-permute-start(f32[1,1,132]{2,1,0:T(1,128)S(1)} %constant_dynamic-update-slice_fusion), channel_id=1, source_target_pairs={{0,1},{1,2},{2,3},{3,4},{4,5},{5,6},{6,7},{7,8},{8,9},{9,10},{10,1... | collective-permute-start | bytes 1592 | tf_op jit(solution)/shard_map/ppermute | solution.py:12
  68.6 1.9 %collective-permute-start.7 = (f32[1,1,132]{2,1,0:T(1,128)S(1)}, f32[1,1,132]{2,1,0:T(1,128)S(1)}, u32[]{:S(2)}, u32[]{:S(2)}) collective-permute-start(f32[1,1,132]{2,1,0:T(1,128)S(1)} %constant_dynamic-update-slice_fusion), channel_id=1, source_target_pairs={{1,0},{2,1},{3,2},{4,3},{5,4},{6,5},{7,6},{8,7},{9,8},{10,9},{11,1... | collective-permute-start | bytes 1592 | tf_op jit(solution)/shard_map/ppermute | solution.py:12
  70.6 2.9 %collective-permute-done.7 = f32[1,1,132]{2,1,0:T(1,128)S(1)} collective-permute-done((f32[1,1,132]{2,1,0:T(1,128)S(1)}, f32[1,1,132]{2,1,0:T(1,128)S(1)}, u32[]{:S(2)}, u32[]{:S(2)}) %collective-permute-start.7) | collective-permute-done | bytes 560 | tf_op jit(solution)/shard_map/ppermute | solution.py:12
  73.5 2.2 %collective-permute-start.8 = (f32[1,3,132]{2,1,0:T(4,128)S(1)}, f32[1,3,132]{2,1,0:T(4,128)S(1)}, u32[]{:S(2)}, u32[]{:S(2)}) collective-permute-start(f32[1,3,132]{2,1,0:T(4,128)S(1)} %pad_maximum_fusion.4), channel_id=1, source_target_pairs={{0,16},{16,32},{32,48},{48,64},{64,80},{80,96},{96,112},{112,128},... | collective-permute-start | bytes 4760 | tf_op jit(solution)/shard_map/ppermute | solution.py:12
  75.7 1.3 collective-permute-start.9
  77.0 0.2 convolution_multiply_fusion
  77.3 2.8 %collective-permute-done.9 = f32[1,3,132]{2,1,0:T(4,128)S(1)} collective-permute-done((f32[1,3,132]{2,1,0:T(4,128)S(1)}, f32[1,3,132]{2,1,0:T(4,128)S(1)}, u32[]{:S(2)}, u32[]{:S(2)}) %collective-permute-start.9) | collective-permute-done | bytes 1616 | tf_op jit(solution)/shard_map/ppermute | solution.py:12
  80.1 0.6 copy-done.4
  80.7 0.1 copy.123
  80.9 0.1 copy.135
  81.0 0.6 slice-done
  81.6 0.1 reshape.603
  81.7 0.3 fusion.16
  82.0 0.2 fusion.1
  82.2 1.9 %collective-permute-start.10 = (f32[1,1,16,68]{3,2,1,0:T(8,128)S(1)}, f32[1,1,16,68]{3,2,1,0:T(8,128)S(1)}, u32[]{:S(2)}, u32[]{:S(2)}) collective-permute-start(f32[1,1,16,68]{3,2,1,0:T(8,128)S(1)} %get-tuple-element.38), channel_id=1, source_target_pairs={{1,0},{2,1},{3,2},{4,3},{5,4},{6,5},{7,6},{8,7},{9,8},{10,9},{11,1... | collective-permute-start | bytes 13064 | tf_op jit(solution)/shard_map/ppermute | solution.py:12
  84.2 1.3 collective-permute-start.11
  85.5 1.7 %collective-permute-done.10 = f32[1,1,16,68]{3,2,1,0:T(8,128)S(1)} collective-permute-done((f32[1,1,16,68]{3,2,1,0:T(8,128)S(1)}, f32[1,1,16,68]{3,2,1,0:T(8,128)S(1)}, u32[]{:S(2)}, u32[]{:S(2)}) %collective-permute-start.10) | collective-permute-done | bytes 4384 | tf_op jit(solution)/shard_map/ppermute | solution.py:12
  87.2 1.4 %collective-permute-done.11 = f32[1,1,16,68]{3,2,1,0:T(8,128)S(1)} collective-permute-done((f32[1,1,16,68]{3,2,1,0:T(8,128)S(1)}, f32[1,1,16,68]{3,2,1,0:T(8,128)S(1)}, u32[]{:S(2)}, u32[]{:S(2)}) %collective-permute-start.11) | collective-permute-done | bytes 4384 | tf_op jit(solution)/shard_map/ppermute | solution.py:12
  89.0 0.2 multiply_reduce_fusion.1
  90.1 0.1 slice_reduce_fusion.3
  90.3 0.2 slice_reduce_fusion.2
  90.5 17.0 %all_to_all.42 = f32[16,1,112]{2,1,0:T(1,128)S(1)} all-to-all(f32[16,1,112]{2,1,0:T(1,128)S(1)} %broadcast_in_dim.126), channel_id=1, replica_groups=mesh['px'=32,'py'=16] {'py'}, dimensions={0} | all-to-all | bytes 14336 | tf_op jit(solution)/shard_map/all_to_all | solution.py:49
  108.0 19.2 %all_to_all.43 = f32[32,1,112]{2,1,0:T(1,128)S(1)} all-to-all(f32[32,1,112]{2,1,0:T(1,128)S(1)} %broadcast_in_dim.127), channel_id=1, replica_groups=mesh['px'=32,'py'=16] {'px'}, dimensions={0} | all-to-all | bytes 28672 | tf_op jit(solution)/shard_map/all_to_all | solution.py:49
  127.7 0.7 and_reduce_fusion
  129.0 0.7 multiply_subtract_fusion
  129.7 0.5 copy-done.10
  (132 shorter events, 4.7 us)
Async XLA Ops:
  0.6 14.4 %copy-start = (bf16[1,1,272,272]{3,2,1,0:T(8,128)(2,1)S(1)}, bf16[1,1,272,272]{3,2,1,0:T(8,128)(2,1)}, u32[]{:S(2)}) copy-start(bf16[1,1,272,272]{3,2,1,0:T(8,128)(2,1)} %param.17) | copy-start | bytes 443908
  0.6 0.8 copy-start.2
  0.7 0.8 copy-start.6
  1.6 0.7 copy-start.9
  4.9 8.8 %collective-permute-start.1 = (f32[2,1,1,16,68]{4,3,2,1,0:T(8,128)S(1)}, f32[2,1,1,16,68]{4,3,2,1,0:T(8,128)S(1)}, u32[]{:S(2)}, u32[]{:S(2)}) collective-permute-start(f32[2,1,1,16,68]{4,3,2,1,0:T(8,128)S(1)} %pad_maximum_fusion.1), channel_id=1, source_target_pairs={{0,16},{16,32},{32,48},{48,64},{64,80},{80,96},{96,112},{112,128},... | collective-permute-start | bytes 26120 | tf_op jit(solution)/shard_map/ppermute | solution.py:12
  8.8 6.2 %collective-permute-start = (f32[2,1,1,16,68]{4,3,2,1,0:T(8,128)S(1)}, f32[2,1,1,16,68]{4,3,2,1,0:T(8,128)S(1)}, u32[]{:S(2)}, u32[]{:S(2)}) collective-permute-start(f32[2,1,1,16,68]{4,3,2,1,0:T(8,128)S(1)} %pad_maximum_fusion), channel_id=1, source_target_pairs={{0,1},{1,2},{2,3},{3,4},{4,5},{5,6},{6,7},{7,8},{8,9},{9,10},{10,1... | collective-permute-start | bytes 26120 | tf_op jit(solution)/shard_map/ppermute | solution.py:12
  15.3 5.0 %collective-permute-start.2 = (f32[1,1,16,68]{3,2,1,0:T(8,128)S(1)}, f32[1,1,16,68]{3,2,1,0:T(8,128)S(1)}, u32[]{:S(2)}, u32[]{:S(2)}) collective-permute-start(f32[1,1,16,68]{3,2,1,0:T(8,128)S(1)} %get-tuple-element.26), channel_id=1, source_target_pairs={{1,0},{2,1},{3,2},{4,3},{5,4},{6,5},{7,6},{8,7},{9,8},{10,9},{11,1... | collective-permute-start | bytes 13064 | tf_op jit(solution)/shard_map/ppermute | solution.py:12
  17.4 4.5 %collective-permute-start.3 = (f32[1,1,16,68]{3,2,1,0:T(8,128)S(1)}, f32[1,1,16,68]{3,2,1,0:T(8,128)S(1)}, u32[]{:S(2)}, u32[]{:S(2)}) collective-permute-start(f32[1,1,16,68]{3,2,1,0:T(8,128)S(1)} %get-tuple-element.27), channel_id=1, source_target_pairs={{16,0},{32,16},{48,32},{64,48},{80,64},{96,80},{112,96},{128,112},... | collective-permute-start | bytes 13064 | tf_op jit(solution)/shard_map/ppermute | solution.py:12
  22.4 32.4 %copy-start.11 = (f32[1,1,2,2]{3,2,1,0:T(2,128)S(1)}, f32[1,1,2,2]{3,2,1,0:T(2,128)}, u32[]{:S(2)}) copy-start(f32[1,1,2,2]{3,2,1,0:T(2,128)} %param.19) | copy-start | bytes 52
  22.4 40.9 %copy-start.12 = (f32[16]{0:T(128)S(1)}, f32[16]{0:T(128)}, u32[]{:S(2)}) copy-start(f32[16]{0:T(128)} %param.15) | copy-start | bytes 196
  22.6 54.5 %copy-start.1 = (bf16[1,1,272,272]{3,2,1,0:T(8,128)(2,1)S(1)}, bf16[1,1,272,272]{3,2,1,0:T(8,128)(2,1)}, u32[]{:S(2)}) copy-start(bf16[1,1,272,272]{3,2,1,0:T(8,128)(2,1)} %param.16) | copy-start | bytes 443908
  23.2 19.2 %all-to-all-start.2 = ((f32[16,1,16]{2,1,0:T(1,128)}), f32[16,1,16]{2,1,0:T(1,128)S(1)}, u32[]{:S(2)}, u32[]{:S(2)}) async-start(f32[16,1,16]{2,1,0:T(1,128)} %broadcast_in_dim.124), calls=%async_computation.2 | async-start | bytes 16384 | tf_op jit(solution)/shard_map/all_to_all | solution.py:49
  35.4 27.9 %collective-permute-start.5 = (f32[2,1,1,16,68]{4,3,2,1,0:T(8,128)S(1)}, f32[2,1,1,16,68]{4,3,2,1,0:T(8,128)S(1)}, u32[]{:S(2)}, u32[]{:S(2)}) collective-permute-start(f32[2,1,1,16,68]{4,3,2,1,0:T(8,128)S(1)} %stack.53), channel_id=1, source_target_pairs={{0,16},{16,32},{32,48},{48,64},{64,80},{80,96},{96,112},{112,128},... | collective-permute-start | bytes 26120 | tf_op jit(solution)/shard_map/ppermute | solution.py:12
  38.5 24.7 %collective-permute-start.4 = (f32[2,1,1,16,68]{4,3,2,1,0:T(8,128)S(1)}, f32[2,1,1,16,68]{4,3,2,1,0:T(8,128)S(1)}, u32[]{:S(2)}, u32[]{:S(2)}) collective-permute-start(f32[2,1,1,16,68]{4,3,2,1,0:T(8,128)S(1)} %stack.51), channel_id=1, source_target_pairs={{0,1},{1,2},{2,3},{3,4},{4,5},{5,6},{6,7},{7,8},{8,9},{9,10},{10,1... | collective-permute-start | bytes 26120 | tf_op jit(solution)/shard_map/ppermute | solution.py:12
  43.0 20.2 %all-to-all-start.3 = ((f32[32,1,16]{2,1,0:T(1,128)}), f32[32,1,16]{2,1,0:T(1,128)S(1)}, u32[]{:S(2)}, u32[]{:S(2)}) async-start(f32[32,1,16]{2,1,0:T(1,128)} %broadcast_in_dim.125), calls=%async_computation.3 | async-start | bytes 32768 | tf_op jit(solution)/shard_map/all_to_all | solution.py:49
  63.3 64.4 %copy-start.8 = (f32[16]{0:T(128)}, f32[16]{0:T(128)S(1)}, u32[]{:S(2)}) copy-start(f32[16]{0:T(128)S(1)} %reduce_sum.83) | copy-start | bytes 196
  63.4 0.7 copy-start.7
  64.5 6.1 %collective-permute-start.6 = (f32[1,1,132]{2,1,0:T(1,128)S(1)}, f32[1,1,132]{2,1,0:T(1,128)S(1)}, u32[]{:S(2)}, u32[]{:S(2)}) collective-permute-start(f32[1,1,132]{2,1,0:T(1,128)S(1)} %constant_dynamic-update-slice_fusion), channel_id=1, source_target_pairs={{0,1},{1,2},{2,3},{3,4},{4,5},{5,6},{6,7},{7,8},{8,9},{9,10},{10,1... | collective-permute-start | bytes 1592 | tf_op jit(solution)/shard_map/ppermute | solution.py:12
  68.6 4.9 %collective-permute-start.7 = (f32[1,1,132]{2,1,0:T(1,128)S(1)}, f32[1,1,132]{2,1,0:T(1,128)S(1)}, u32[]{:S(2)}, u32[]{:S(2)}) collective-permute-start(f32[1,1,132]{2,1,0:T(1,128)S(1)} %constant_dynamic-update-slice_fusion), channel_id=1, source_target_pairs={{1,0},{2,1},{3,2},{4,3},{5,4},{6,5},{7,6},{8,7},{9,8},{10,9},{11,1... | collective-permute-start | bytes 1592 | tf_op jit(solution)/shard_map/ppermute | solution.py:12
  73.5 3.7 %collective-permute-start.8 = (f32[1,3,132]{2,1,0:T(4,128)S(1)}, f32[1,3,132]{2,1,0:T(4,128)S(1)}, u32[]{:S(2)}, u32[]{:S(2)}) collective-permute-start(f32[1,3,132]{2,1,0:T(4,128)S(1)} %pad_maximum_fusion.4), channel_id=1, source_target_pairs={{0,16},{16,32},{32,48},{48,64},{64,80},{80,96},{96,112},{112,128},... | collective-permute-start | bytes 4760 | tf_op jit(solution)/shard_map/ppermute | solution.py:12
  75.7 4.4 %collective-permute-start.9 = (f32[1,3,132]{2,1,0:T(4,128)S(1)}, f32[1,3,132]{2,1,0:T(4,128)S(1)}, u32[]{:S(2)}, u32[]{:S(2)}) collective-permute-start(f32[1,3,132]{2,1,0:T(4,128)S(1)} %pad_maximum_fusion.4), channel_id=1, source_target_pairs={{16,0},{32,16},{48,32},{64,48},{80,64},{96,80},{112,96},{128,112},... | collective-permute-start | bytes 4760 | tf_op jit(solution)/shard_map/ppermute | solution.py:12
  80.1 0.6 copy-start.4
  80.9 0.7 slice-start
  82.2 5.0 %collective-permute-start.10 = (f32[1,1,16,68]{3,2,1,0:T(8,128)S(1)}, f32[1,1,16,68]{3,2,1,0:T(8,128)S(1)}, u32[]{:S(2)}, u32[]{:S(2)}) collective-permute-start(f32[1,1,16,68]{3,2,1,0:T(8,128)S(1)} %get-tuple-element.38), channel_id=1, source_target_pairs={{1,0},{2,1},{3,2},{4,3},{5,4},{6,5},{7,6},{8,7},{9,8},{10,9},{11,1... | collective-permute-start | bytes 13064 | tf_op jit(solution)/shard_map/ppermute | solution.py:12
  84.2 4.4 %collective-permute-start.11 = (f32[1,1,16,68]{3,2,1,0:T(8,128)S(1)}, f32[1,1,16,68]{3,2,1,0:T(8,128)S(1)}, u32[]{:S(2)}, u32[]{:S(2)}) collective-permute-start(f32[1,1,16,68]{3,2,1,0:T(8,128)S(1)} %get-tuple-element.39), channel_id=1, source_target_pairs={{16,0},{32,16},{48,32},{64,48},{80,64},{96,80},{112,96},{128,112},... | collective-permute-start | bytes 13064 | tf_op jit(solution)/shard_map/ppermute | solution.py:12
  89.2 39.8 %copy-start.3 = (f32[1,1,16,136]{3,2,1,0:T(8,128)}, f32[1,1,16,136]{3,2,1,0:T(8,128)S(1)}, u32[]{:S(2)}) copy-start(f32[1,1,16,136]{3,2,1,0:T(8,128)S(1)} %get-tuple-element.116) | copy-start | bytes 26116
  127.6 1.4 %copy-start.5 = (f32[1,1,16,136]{3,2,1,0:T(8,128)S(1)}, f32[1,1,16,136]{3,2,1,0:T(8,128)}, u32[]{:S(2)}) copy-start(f32[1,1,16,136]{3,2,1,0:T(8,128)} %param.12) | copy-start | bytes 26116
  129.7 0.5 copy-start.10

commit v14 on v13

--- a/solution.py
+++ b/solution.py
@@ -135,7 +135,11 @@
         every = gathered(jnp.concatenate(rows), axis)
         row = lambda k: every[:, k * width : (k + 1) * width]
         plain = jnp.sum(row(0), axis=0)
-        pairs = [df_tree_sum(row(1 + 2 * k), row(2 + 2 * k)) for k in range(len(pairs))]
+        high, low = df_tree_sum(
+            jnp.stack([row(1 + 2 * k) for k in range(len(pairs))], 1),
+            jnp.stack([row(2 + 2 * k) for k in range(len(pairs))], 1),
+        )
+        pairs = [(high[k], low[k]) for k in range(len(pairs))]
     return plain, pairs
 
 

time: 131 us -> 130 us (level)
  no operation moved by 1% of the time
where the time goes in v14:
time: 130 us
  starting transfers between devices  55.7 us (43%)
  blocking collectives  36.2 us (28%)
  waiting for transfers between devices  21.4 us (16%)
  local copies, waits for them, and re-layouts  8.08 us (6%)
  between operations  3.94 us (3%)
  other arithmetic  3.45 us (3%)
    all_to_all x2, blocking collectives, gathered(): return lax.all_to_all(copies, axis, 0, 0, tiled=False)  36.2 us
    ppermute x12, starting transfers between devices, passed_along(): return lax.ppermute(value, axis, pairs)  31.8 us
    all_to_all x2, starting transfers between devices, gathered(): return lax.all_to_all(copies, axis, 0, 0, tiled=False)  23.9 us
    ppermute x12, waiting for transfers between devices, passed_along(): return lax.ppermute(value, axis, pairs)  13 us
    all_to_all x2, waiting for transfers between devices, gathered(): return lax.all_to_all(copies, axis, 0, 0, tiled=False)  8.4 us
  transfers between devices with their start and end apart: 14, of which 8 were waited for; matrix products, arithmetic and copies ran while one was open for 1% of the time, Pallas kernels for 0%

profile of v14, /device:TPU:1, one launch (start us, length us, event | category | flops | bytes accessed | tf_op | source)
XLA Modules:
  0.0 129.8 jit_solution(408423896121876422)
XLA Ops:
  1.7 0.6 copy-done.9
  2.3 0.5 fusion.127
  4.4 0.1 copy.141
  4.9 3.9 %collective-permute-start.1 = (f32[2,1,1,16,68]{4,3,2,1,0:T(8,128)S(1)}, f32[2,1,1,16,68]{4,3,2,1,0:T(8,128)S(1)}, u32[]{:S(2)}, u32[]{:S(2)}) collective-permute-start(f32[2,1,1,16,68]{4,3,2,1,0:T(8,128)S(1)} %pad_maximum_fusion.5), channel_id=1, source_target_pairs={{0,16},{16,32},{32,48},{48,64},{64,80},{80,96},{96,112},{112,128},... | collective-permute-start | bytes 26120 | tf_op jit(solution)/shard_map/ppermute | solution.py:12
  8.8 4.8 %collective-permute-start = (f32[2,1,1,16,68]{4,3,2,1,0:T(8,128)S(1)}, f32[2,1,1,16,68]{4,3,2,1,0:T(8,128)S(1)}, u32[]{:S(2)}, u32[]{:S(2)}) collective-permute-start(f32[2,1,1,16,68]{4,3,2,1,0:T(8,128)S(1)} %pad_maximum_fusion.4), channel_id=1, source_target_pairs={{0,1},{1,2},{2,3},{3,4},{4,5},{5,6},{6,7},{7,8},{8,9},{9,10},{10,1... | collective-permute-start | bytes 26120 | tf_op jit(solution)/shard_map/ppermute | solution.py:12
  13.7 1.3 %collective-permute-done = f32[2,1,1,16,68]{4,3,2,1,0:T(8,128)S(1)} collective-permute-done((f32[2,1,1,16,68]{4,3,2,1,0:T(8,128)S(1)}, f32[2,1,1,16,68]{4,3,2,1,0:T(8,128)S(1)}, u32[]{:S(2)}, u32[]{:S(2)}) %collective-permute-start) | collective-permute-done | bytes 8736 | tf_op jit(solution)/shard_map/ppermute | solution.py:12
  15.0 0.2 fusion.2
  15.3 2.1 %collective-permute-start.2 = (f32[1,1,16,68]{3,2,1,0:T(8,128)S(1)}, f32[1,1,16,68]{3,2,1,0:T(8,128)S(1)}, u32[]{:S(2)}, u32[]{:S(2)}) collective-permute-start(f32[1,1,16,68]{3,2,1,0:T(8,128)S(1)} %get-tuple-element.26), channel_id=1, source_target_pairs={{1,0},{2,1},{3,2},{4,3},{5,4},{6,5},{7,6},{8,7},{9,8},{10,9},{11,1... | collective-permute-start | bytes 13064 | tf_op jit(solution)/shard_map/ppermute | solution.py:12
  17.4 1.3 collective-permute-start.3
  18.7 0.1 copy.151
  19.1 1.3 collective-permute-done.2
  20.3 1.6 %collective-permute-done.3 = f32[1,1,16,68]{3,2,1,0:T(8,128)S(1)} collective-permute-done((f32[1,1,16,68]{3,2,1,0:T(8,128)S(1)}, f32[1,1,16,68]{3,2,1,0:T(8,128)S(1)}, u32[]{:S(2)}, u32[]{:S(2)}) %collective-permute-start.3) | collective-permute-done | bytes 4384 | tf_op jit(solution)/shard_map/ppermute | solution.py:12
  22.4 0.2 multiply_reduce_fusion.2
  22.6 0.6 broadcast_in_dim.124
  23.2 12.2 %all-to-all-start.2 = ((f32[16,1,16]{2,1,0:T(1,128)}), f32[16,1,16]{2,1,0:T(1,128)S(1)}, u32[]{:S(2)}, u32[]{:S(2)}) async-start(f32[16,1,16]{2,1,0:T(1,128)} %broadcast_in_dim.124), calls=%async_computation.2 | async-start | bytes 16384 | tf_op jit(solution)/shard_map/all_to_all | solution.py:49
  35.4 3.1 %collective-permute-start.5 = (f32[2,1,1,16,68]{4,3,2,1,0:T(8,128)S(1)}, f32[2,1,1,16,68]{4,3,2,1,0:T(8,128)S(1)}, u32[]{:S(2)}, u32[]{:S(2)}) collective-permute-start(f32[2,1,1,16,68]{4,3,2,1,0:T(8,128)S(1)} %stack.101), channel_id=1, source_target_pairs={{0,16},{16,32},{32,48},{48,64},{64,80},{80,96},{96,112},{112,128},... | collective-permute-start | bytes 26120 | tf_op jit(solution)/shard_map/ppermute | solution.py:12
  38.5 3.8 %collective-permute-start.4 = (f32[2,1,1,16,68]{4,3,2,1,0:T(8,128)S(1)}, f32[2,1,1,16,68]{4,3,2,1,0:T(8,128)S(1)}, u32[]{:S(2)}, u32[]{:S(2)}) collective-permute-start(f32[2,1,1,16,68]{4,3,2,1,0:T(8,128)S(1)} %stack.99), channel_id=1, source_target_pairs={{0,1},{1,2},{2,3},{3,4},{4,5},{5,6},{6,7},{7,8},{8,9},{9,10},{10,1... | collective-permute-start | bytes 26120 | tf_op jit(solution)/shard_map/ppermute | solution.py:12
  42.4 0.6 broadcast_in_dim.125
  43.0 11.7 %all-to-all-start.3 = ((f32[32,1,16]{2,1,0:T(1,128)}), f32[32,1,16]{2,1,0:T(1,128)S(1)}, u32[]{:S(2)}, u32[]{:S(2)}) async-start(f32[32,1,16]{2,1,0:T(1,128)} %broadcast_in_dim.125), calls=%async_computation.3 | async-start | bytes 32768 | tf_op jit(solution)/shard_map/all_to_all | solution.py:49
  54.8 8.4 %all-to-all-done.3 = f32[32,1,16]{2,1,0:T(1,128)S(1)} async-done(((f32[32,1,16]{2,1,0:T(1,128)}), f32[32,1,16]{2,1,0:T(1,128)S(1)}, u32[]{:S(2)}, u32[]{:S(2)}) %all-to-all-start.3) | async-done | bytes 2080 | tf_op jit(solution)/shard_map/all_to_all | solution.py:49
  63.4 0.7 copy-done.7
  64.1 0.2 convolution_multiply_fusion.2
  64.5 4.1 %collective-permute-start.6 = (f32[1,1,132]{2,1,0:T(1,128)S(1)}, f32[1,1,132]{2,1,0:T(1,128)S(1)}, u32[]{:S(2)}, u32[]{:S(2)}) collective-permute-start(f32[1,1,132]{2,1,0:T(1,128)S(1)} %constant_dynamic-update-slice_fusion), channel_id=1, source_target_pairs={{0,1},{1,2},{2,3},{3,4},{4,5},{5,6},{6,7},{7,8},{8,9},{9,10},{10,1... | collective-permute-start | bytes 1592 | tf_op jit(solution)/shard_map/ppermute | solution.py:12
  68.6 1.9 %collective-permute-start.7 = (f32[1,1,132]{2,1,0:T(1,128)S(1)}, f32[1,1,132]{2,1,0:T(1,128)S(1)}, u32[]{:S(2)}, u32[]{:S(2)}) collective-permute-start(f32[1,1,132]{2,1,0:T(1,128)S(1)} %constant_dynamic-update-slice_fusion), channel_id=1, source_target_pairs={{1,0},{2,1},{3,2},{4,3},{5,4},{6,5},{7,6},{8,7},{9,8},{10,9},{11,1... | collective-permute-start | bytes 1592 | tf_op jit(solution)/shard_map/ppermute | solution.py:12
  70.6 2.9 %collective-permute-done.7 = f32[1,1,132]{2,1,0:T(1,128)S(1)} collective-permute-done((f32[1,1,132]{2,1,0:T(1,128)S(1)}, f32[1,1,132]{2,1,0:T(1,128)S(1)}, u32[]{:S(2)}, u32[]{:S(2)}) %collective-permute-start.7) | collective-permute-done | bytes 560 | tf_op jit(solution)/shard_map/ppermute | solution.py:12
  73.5 2.2 %collective-permute-start.8 = (f32[1,3,132]{2,1,0:T(4,128)S(1)}, f32[1,3,132]{2,1,0:T(4,128)S(1)}, u32[]{:S(2)}, u32[]{:S(2)}) collective-permute-start(f32[1,3,132]{2,1,0:T(4,128)S(1)} %pad_maximum_fusion.8), channel_id=1, source_target_pairs={{0,16},{16,32},{32,48},{48,64},{64,80},{80,96},{96,112},{112,128},... | collective-permute-start | bytes 4760 | tf_op jit(solution)/shard_map/ppermute | solution.py:12
  75.7 1.3 collective-permute-start.9
  77.0 0.2 convolution_multiply_fusion
  77.3 2.8 %collective-permute-done.9 = f32[1,3,132]{2,1,0:T(4,128)S(1)} collective-permute-done((f32[1,3,132]{2,1,0:T(4,128)S(1)}, f32[1,3,132]{2,1,0:T(4,128)S(1)}, u32[]{:S(2)}, u32[]{:S(2)}) %collective-permute-start.9) | collective-permute-done | bytes 1616 | tf_op jit(solution)/shard_map/ppermute | solution.py:12
  80.1 0.6 copy-done.4
  80.7 0.1 copy.156
  80.9 0.1 copy.168
  81.0 0.6 slice-done
  81.6 0.1 reshape.627
  81.7 0.3 fusion.16
  82.0 0.2 fusion.1
  82.2 1.9 %collective-permute-start.10 = (f32[1,1,16,68]{3,2,1,0:T(8,128)S(1)}, f32[1,1,16,68]{3,2,1,0:T(8,128)S(1)}, u32[]{:S(2)}, u32[]{:S(2)}) collective-permute-start(f32[1,1,16,68]{3,2,1,0:T(8,128)S(1)} %get-tuple-element.38), channel_id=1, source_target_pairs={{1,0},{2,1},{3,2},{4,3},{5,4},{6,5},{7,6},{8,7},{9,8},{10,9},{11,1... | collective-permute-start | bytes 13064 | tf_op jit(solution)/shard_map/ppermute | solution.py:12
  84.2 1.3 collective-permute-start.11
  85.5 1.7 %collective-permute-done.10 = f32[1,1,16,68]{3,2,1,0:T(8,128)S(1)} collective-permute-done((f32[1,1,16,68]{3,2,1,0:T(8,128)S(1)}, f32[1,1,16,68]{3,2,1,0:T(8,128)S(1)}, u32[]{:S(2)}, u32[]{:S(2)}) %collective-permute-start.10) | collective-permute-done | bytes 4384 | tf_op jit(solution)/shard_map/ppermute | solution.py:12
  87.2 1.4 %collective-permute-done.11 = f32[1,1,16,68]{3,2,1,0:T(8,128)S(1)} collective-permute-done((f32[1,1,16,68]{3,2,1,0:T(8,128)S(1)}, f32[1,1,16,68]{3,2,1,0:T(8,128)S(1)}, u32[]{:S(2)}, u32[]{:S(2)}) %collective-permute-start.11) | collective-permute-done | bytes 4384 | tf_op jit(solution)/shard_map/ppermute | solution.py:12
  89.0 0.2 multiply_reduce_fusion.1
  90.1 0.1 slice_reduce_fusion.3
  90.3 0.2 slice_reduce_fusion.2
  90.5 17.0 %all_to_all.42 = f32[16,1,112]{2,1,0:T(1,128)S(1)} all-to-all(f32[16,1,112]{2,1,0:T(1,128)S(1)} %broadcast_in_dim.126), channel_id=1, replica_groups=mesh['px'=32,'py'=16] {'py'}, dimensions={0} | all-to-all | bytes 14336 | tf_op jit(solution)/shard_map/all_to_all | solution.py:49
  107.8 19.2 %all_to_all.43 = f32[32,1,112]{2,1,0:T(1,128)S(1)} all-to-all(f32[32,1,112]{2,1,0:T(1,128)S(1)} %broadcast_in_dim.127), channel_id=1, replica_groups=mesh['px'=32,'py'=16] {'px'}, dimensions={0} | all-to-all | bytes 28672 | tf_op jit(solution)/shard_map/all_to_all | solution.py:49
  127.2 0.7 and_reduce_fusion
  128.6 0.7 multiply_subtract_fusion
  129.3 0.5 copy-done.10
  (120 shorter events, 4.3 us)
Async XLA Ops:
  0.6 14.4 %copy-start = (bf16[1,1,272,272]{3,2,1,0:T(8,128)(2,1)S(1)}, bf16[1,1,272,272]{3,2,1,0:T(8,128)(2,1)}, u32[]{:S(2)}) copy-start(bf16[1,1,272,272]{3,2,1,0:T(8,128)(2,1)} %param.17) | copy-start | bytes 443908
  0.6 0.8 copy-start.2
  0.7 0.8 copy-start.6
  1.6 0.7 copy-start.9
  4.9 8.8 %collective-permute-start.1 = (f32[2,1,1,16,68]{4,3,2,1,0:T(8,128)S(1)}, f32[2,1,1,16,68]{4,3,2,1,0:T(8,128)S(1)}, u32[]{:S(2)}, u32[]{:S(2)}) collective-permute-start(f32[2,1,1,16,68]{4,3,2,1,0:T(8,128)S(1)} %pad_maximum_fusion.5), channel_id=1, source_target_pairs={{0,16},{16,32},{32,48},{48,64},{64,80},{80,96},{96,112},{112,128},... | collective-permute-start | bytes 26120 | tf_op jit(solution)/shard_map/ppermute | solution.py:12
  8.8 6.2 %collective-permute-start = (f32[2,1,1,16,68]{4,3,2,1,0:T(8,128)S(1)}, f32[2,1,1,16,68]{4,3,2,1,0:T(8,128)S(1)}, u32[]{:S(2)}, u32[]{:S(2)}) collective-permute-start(f32[2,1,1,16,68]{4,3,2,1,0:T(8,128)S(1)} %pad_maximum_fusion.4), channel_id=1, source_target_pairs={{0,1},{1,2},{2,3},{3,4},{4,5},{5,6},{6,7},{7,8},{8,9},{9,10},{10,1... | collective-permute-start | bytes 26120 | tf_op jit(solution)/shard_map/ppermute | solution.py:12
  15.3 5.0 %collective-permute-start.2 = (f32[1,1,16,68]{3,2,1,0:T(8,128)S(1)}, f32[1,1,16,68]{3,2,1,0:T(8,128)S(1)}, u32[]{:S(2)}, u32[]{:S(2)}) collective-permute-start(f32[1,1,16,68]{3,2,1,0:T(8,128)S(1)} %get-tuple-element.26), channel_id=1, source_target_pairs={{1,0},{2,1},{3,2},{4,3},{5,4},{6,5},{7,6},{8,7},{9,8},{10,9},{11,1... | collective-permute-start | bytes 13064 | tf_op jit(solution)/shard_map/ppermute | solution.py:12
  17.4 4.5 %collective-permute-start.3 = (f32[1,1,16,68]{3,2,1,0:T(8,128)S(1)}, f32[1,1,16,68]{3,2,1,0:T(8,128)S(1)}, u32[]{:S(2)}, u32[]{:S(2)}) collective-permute-start(f32[1,1,16,68]{3,2,1,0:T(8,128)S(1)} %get-tuple-element.27), channel_id=1, source_target_pairs={{16,0},{32,16},{48,32},{64,48},{80,64},{96,80},{112,96},{128,112},... | collective-permute-start | bytes 13064 | tf_op jit(solution)/shard_map/ppermute | solution.py:12
  22.4 32.4 %copy-start.11 = (f32[1,1,2,2]{3,2,1,0:T(2,128)S(1)}, f32[1,1,2,2]{3,2,1,0:T(2,128)}, u32[]{:S(2)}) copy-start(f32[1,1,2,2]{3,2,1,0:T(2,128)} %param.19) | copy-start | bytes 52
  22.4 40.9 %copy-start.12 = (f32[16]{0:T(128)S(1)}, f32[16]{0:T(128)}, u32[]{:S(2)}) copy-start(f32[16]{0:T(128)} %param.15) | copy-start | bytes 196
  22.6 54.5 %copy-start.1 = (bf16[1,1,272,272]{3,2,1,0:T(8,128)(2,1)S(1)}, bf16[1,1,272,272]{3,2,1,0:T(8,128)(2,1)}, u32[]{:S(2)}) copy-start(bf16[1,1,272,272]{3,2,1,0:T(8,128)(2,1)} %param.16) | copy-start | bytes 443908
  23.2 19.2 %all-to-all-start.2 = ((f32[16,1,16]{2,1,0:T(1,128)}), f32[16,1,16]{2,1,0:T(1,128)S(1)}, u32[]{:S(2)}, u32[]{:S(2)}) async-start(f32[16,1,16]{2,1,0:T(1,128)} %broadcast_in_dim.124), calls=%async_computation.2 | async-start | bytes 16384 | tf_op jit(solution)/shard_map/all_to_all | solution.py:49
  35.4 27.9 %collective-permute-start.5 = (f32[2,1,1,16,68]{4,3,2,1,0:T(8,128)S(1)}, f32[2,1,1,16,68]{4,3,2,1,0:T(8,128)S(1)}, u32[]{:S(2)}, u32[]{:S(2)}) collective-permute-start(f32[2,1,1,16,68]{4,3,2,1,0:T(8,128)S(1)} %stack.101), channel_id=1, source_target_pairs={{0,16},{16,32},{32,48},{48,64},{64,80},{80,96},{96,112},{112,128},... | collective-permute-start | bytes 26120 | tf_op jit(solution)/shard_map/ppermute | solution.py:12
  38.5 24.7 %collective-permute-start.4 = (f32[2,1,1,16,68]{4,3,2,1,0:T(8,128)S(1)}, f32[2,1,1,16,68]{4,3,2,1,0:T(8,128)S(1)}, u32[]{:S(2)}, u32[]{:S(2)}) collective-permute-start(f32[2,1,1,16,68]{4,3,2,1,0:T(8,128)S(1)} %stack.99), channel_id=1, source_target_pairs={{0,1},{1,2},{2,3},{3,4},{4,5},{5,6},{6,7},{7,8},{8,9},{9,10},{10,1... | collective-permute-start | bytes 26120 | tf_op jit(solution)/shard_map/ppermute | solution.py:12
  43.0 20.2 %all-to-all-start.3 = ((f32[32,1,16]{2,1,0:T(1,128)}), f32[32,1,16]{2,1,0:T(1,128)S(1)}, u32[]{:S(2)}, u32[]{:S(2)}) async-start(f32[32,1,16]{2,1,0:T(1,128)} %broadcast_in_dim.125), calls=%async_computation.3 | async-start | bytes 32768 | tf_op jit(solution)/shard_map/all_to_all | solution.py:49
  63.3 64.0 %copy-start.8 = (f32[16]{0:T(128)}, f32[16]{0:T(128)S(1)}, u32[]{:S(2)}) copy-start(f32[16]{0:T(128)S(1)} %reduce_sum.83) | copy-start | bytes 196
  63.4 0.7 copy-start.7
  64.5 6.1 %collective-permute-start.6 = (f32[1,1,132]{2,1,0:T(1,128)S(1)}, f32[1,1,132]{2,1,0:T(1,128)S(1)}, u32[]{:S(2)}, u32[]{:S(2)}) collective-permute-start(f32[1,1,132]{2,1,0:T(1,128)S(1)} %constant_dynamic-update-slice_fusion), channel_id=1, source_target_pairs={{0,1},{1,2},{2,3},{3,4},{4,5},{5,6},{6,7},{7,8},{8,9},{9,10},{10,1... | collective-permute-start | bytes 1592 | tf_op jit(solution)/shard_map/ppermute | solution.py:12
  68.6 4.9 %collective-permute-start.7 = (f32[1,1,132]{2,1,0:T(1,128)S(1)}, f32[1,1,132]{2,1,0:T(1,128)S(1)}, u32[]{:S(2)}, u32[]{:S(2)}) collective-permute-start(f32[1,1,132]{2,1,0:T(1,128)S(1)} %constant_dynamic-update-slice_fusion), channel_id=1, source_target_pairs={{1,0},{2,1},{3,2},{4,3},{5,4},{6,5},{7,6},{8,7},{9,8},{10,9},{11,1... | collective-permute-start | bytes 1592 | tf_op jit(solution)/shard_map/ppermute | solution.py:12
  73.5 3.7 %collective-permute-start.8 = (f32[1,3,132]{2,1,0:T(4,128)S(1)}, f32[1,3,132]{2,1,0:T(4,128)S(1)}, u32[]{:S(2)}, u32[]{:S(2)}) collective-permute-start(f32[1,3,132]{2,1,0:T(4,128)S(1)} %pad_maximum_fusion.8), channel_id=1, source_target_pairs={{0,16},{16,32},{32,48},{48,64},{64,80},{80,96},{96,112},{112,128},... | collective-permute-start | bytes 4760 | tf_op jit(solution)/shard_map/ppermute | solution.py:12
  75.7 4.4 %collective-permute-start.9 = (f32[1,3,132]{2,1,0:T(4,128)S(1)}, f32[1,3,132]{2,1,0:T(4,128)S(1)}, u32[]{:S(2)}, u32[]{:S(2)}) collective-permute-start(f32[1,3,132]{2,1,0:T(4,128)S(1)} %pad_maximum_fusion.8), channel_id=1, source_target_pairs={{16,0},{32,16},{48,32},{64,48},{80,64},{96,80},{112,96},{128,112},... | collective-permute-start | bytes 4760 | tf_op jit(solution)/shard_map/ppermute | solution.py:12
  80.1 0.6 copy-start.4
  80.9 0.7 slice-start
  82.2 5.0 %collective-permute-start.10 = (f32[1,1,16,68]{3,2,1,0:T(8,128)S(1)}, f32[1,1,16,68]{3,2,1,0:T(8,128)S(1)}, u32[]{:S(2)}, u32[]{:S(2)}) collective-permute-start(f32[1,1,16,68]{3,2,1,0:T(8,128)S(1)} %get-tuple-element.38), channel_id=1, source_target_pairs={{1,0},{2,1},{3,2},{4,3},{5,4},{6,5},{7,6},{8,7},{9,8},{10,9},{11,1... | collective-permute-start | bytes 13064 | tf_op jit(solution)/shard_map/ppermute | solution.py:12
  84.2 4.4 %collective-permute-start.11 = (f32[1,1,16,68]{3,2,1,0:T(8,128)S(1)}, f32[1,1,16,68]{3,2,1,0:T(8,128)S(1)}, u32[]{:S(2)}, u32[]{:S(2)}) collective-permute-start(f32[1,1,16,68]{3,2,1,0:T(8,128)S(1)} %get-tuple-element.39), channel_id=1, source_target_pairs={{16,0},{32,16},{48,32},{64,48},{80,64},{96,80},{112,96},{128,112},... | collective-permute-start | bytes 13064 | tf_op jit(solution)/shard_map/ppermute | solution.py:12
  89.2 39.4 %copy-start.3 = (f32[1,1,16,136]{3,2,1,0:T(8,128)}, f32[1,1,16,136]{3,2,1,0:T(8,128)S(1)}, u32[]{:S(2)}) copy-start(f32[1,1,16,136]{3,2,1,0:T(8,128)S(1)} %get-tuple-element.86) | copy-start | bytes 26116
  127.2 1.4 %copy-start.5 = (f32[1,1,16,136]{3,2,1,0:T(8,128)S(1)}, f32[1,1,16,136]{3,2,1,0:T(8,128)}, u32[]{:S(2)}) copy-start(f32[1,1,16,136]{3,2,1,0:T(8,128)} %param.12) | copy-start | bytes 26116
  129.3 0.5 copy-start.10

commit v15 on v14

--- a/solution.py
+++ b/solution.py
@@ -249,19 +249,24 @@
         from_north = jnp.concatenate([south_side[1:], north_edge], 0)
         east_perm_side = permute_side(east_side, east_flip)
         north_perm_side = permute_side(north_side, north_flip)
-        west_sent = passed_along(jnp.stack([east_perm_side, ones]), "py", 1)
-        south_sent = passed_along(jnp.stack([north_perm_side, ones]), "px", 1)
         east_term = permute_side(from_east, east_flip)
         north_term = permute_side(from_north, north_flip)
         joined = jnp.concatenate([east_side - east_term, north_side - north_term], 3)
         half_jump = 0.5 * (joined * edge_mask)
+        rz_partial = jnp.sum(start_res * half_jump, axis=(0, 1, 3))
+        rz_py = jnp.sum(gathered(rz_partial, "py"), axis=0)
+        rz_py, west_load, south_load = lax.optimization_barrier(
+            (rz_py, jnp.stack([east_perm_side, ones]), jnp.stack([north_perm_side, ones]))
+        )
+        west_sent = passed_along(west_load, "py", 1)
+        south_sent = passed_along(south_load, "px", 1)
         west_edge = 0.5 * ((west_sent[0] - west_side[:, :1]) * west_sent[1])
         south_edge = 0.5 * ((south_sent[0] - south_side[:1]) * south_sent[1])
         local_east = permute_side(half_jump[..., :SIDE], east_flip)
         local_north = permute_side(half_jump[..., SIDE:], north_flip)
         from_west = jnp.concatenate([west_edge, local_east[:, :-1]], 1)
         from_south = jnp.concatenate([south_edge, local_north[:-1]], 0)
-        return half_jump, (half_jump[..., :SIDE], half_jump[..., SIDE:], from_west, from_south)
+        return half_jump, (half_jump[..., :SIDE], half_jump[..., SIDE:], from_west, from_south), rz_py
 
     start_sol = solution * edge_mask
     start_res = residual * edge_mask
@@ -269,8 +274,8 @@
     res_parts, dir_parts = spread_pair(0.5 * start_res, start_dir)
     spread = spread_of(res_parts).astype(jnp.bfloat16)
     side_values = patch_products(dual_schur, spread)
-    precond, precond_parts = jump_and_spread(side_values)
-    rz_current = all_sum(jnp.sum(start_res * precond, axis=(0, 1, 3)))
+    precond, precond_parts, rz_py = jump_and_spread(side_values)
+    rz_current = jnp.sum(gathered(rz_py, "px"), axis=0)
     step_ratio = rz_current / rz_previous
     ratio = step_ratio[None, None, :, None]
     new_direction = precond + ratio * start_dir

time: 130 us -> 133 us (1.023)
  blocking collectives: 36.2 us -> 39.2 us
    all_to_all x2, blocking collectives: 36.2 us -> 39.2 us  [gathered(): return lax.all_to_all(copies, axis, 0, 0, tiled=False)]
    all_to_all x2, starting transfers between devices: 23.9 us -> 22.4 us  [gathered(): return lax.all_to_all(copies, axis, 0, 0, tiled=False)]
  transfers between devices with their start and end apart: 14 -> 14, of which waited for: 8 -> 9; matrix products, arithmetic and copies ran while one was open for 1% -> 1% of each run, Pallas kernels for 0% -> 0%
where the time goes in v15:
time: 133 us; the launch traced here: 132 us
  starting transfers between devices  54.8 us (41%)
  blocking collectives  39.2 us (29%)
  waiting for transfers between devices  21.8 us (16%)
  local copies, waits for them, and re-layouts  8.09 us (6%)
  between operations  3.92 us (3%)
  other arithmetic  3.44 us (3%)
    all_to_all x2, blocking collectives, gathered(): return lax.all_to_all(copies, axis, 0, 0, tiled=False)  39.2 us
    ppermute x12, starting transfers between devices, passed_along(): return lax.ppermute(value, axis, pairs)  32.4 us
    all_to_all x2, starting transfers between devices, gathered(): return lax.all_to_all(copies, axis, 0, 0, tiled=False)  22.4 us
    ppermute x12, waiting for transfers between devices, passed_along(): return lax.ppermute(value, axis, pairs)  12.9 us
    all_to_all x2, waiting for transfers between devices, gathered(): return lax.all_to_all(copies, axis, 0, 0, tiled=False)  8.89 us
  transfers between devices with their start and end apart: 14, of which 9 were waited for; matrix products, arithmetic and copies ran while one was open for 1% of the time, Pallas kernels for 0%

profile of v15, /device:TPU:1, one launch (start us, length us, event | category | flops | bytes accessed | tf_op | source)
XLA Modules:
  0.0 132.3 jit_solution(14624105942588542663)
XLA Ops:
  2.4 0.6 copy-done.9
  3.0 0.5 fusion.127
  4.9 5.4 %collective-permute-start = (f32[2,1,1,16,68]{4,3,2,1,0:T(8,128)S(1)}, f32[2,1,1,16,68]{4,3,2,1,0:T(8,128)S(1)}, u32[]{:S(2)}, u32[]{:S(2)}) collective-permute-start(f32[2,1,1,16,68]{4,3,2,1,0:T(8,128)S(1)} %pad_maximum_fusion.4), channel_id=1, source_target_pairs={{0,1},{1,2},{2,3},{3,4},{4,5},{5,6},{6,7},{7,8},{8,9},{9,10},{10,1... | collective-permute-start | bytes 26120 | tf_op jit(solution)/shard_map/ppermute | solution.py:12
  10.3 3.1 %collective-permute-start.1 = (f32[2,1,1,16,68]{4,3,2,1,0:T(8,128)S(1)}, f32[2,1,1,16,68]{4,3,2,1,0:T(8,128)S(1)}, u32[]{:S(2)}, u32[]{:S(2)}) collective-permute-start(f32[2,1,1,16,68]{4,3,2,1,0:T(8,128)S(1)} %pad_maximum_fusion.5), channel_id=1, source_target_pairs={{0,16},{16,32},{32,48},{48,64},{64,80},{80,96},{96,112},{112,128},... | collective-permute-start | bytes 26120 | tf_op jit(solution)/shard_map/ppermute | solution.py:12
  13.4 0.3 collective-permute-done
  13.7 0.6 collective-permute-done.1
  14.3 0.2 fusion.2
  14.5 3.4 %collective-permute-start.2 = (f32[1,1,16,68]{3,2,1,0:T(8,128)S(1)}, f32[1,1,16,68]{3,2,1,0:T(8,128)S(1)}, u32[]{:S(2)}, u32[]{:S(2)}) collective-permute-start(f32[1,1,16,68]{3,2,1,0:T(8,128)S(1)} %get-tuple-element.29), channel_id=1, source_target_pairs={{1,0},{2,1},{3,2},{4,3},{5,4},{6,5},{7,6},{8,7},{9,8},{10,9},{11,1... | collective-permute-start | bytes 13064 | tf_op jit(solution)/shard_map/ppermute | solution.py:12
  18.0 1.3 collective-permute-start.3
  19.3 0.1 copy.150
  19.7 3.3 %collective-permute-done.3 = f32[1,1,16,68]{3,2,1,0:T(8,128)S(1)} collective-permute-done((f32[1,1,16,68]{3,2,1,0:T(8,128)S(1)}, f32[1,1,16,68]{3,2,1,0:T(8,128)S(1)}, u32[]{:S(2)}, u32[]{:S(2)}) %collective-permute-start.3) | collective-permute-done | bytes 4384 | tf_op jit(solution)/shard_map/ppermute | solution.py:12
  23.4 0.2 multiply_reduce_fusion.2
  23.6 0.6 broadcast_in_dim.124
  24.2 10.3 %all-to-all-start.2 = ((f32[16,1,16]{2,1,0:T(1,128)}), f32[16,1,16]{2,1,0:T(1,128)S(1)}, u32[]{:S(2)}, u32[]{:S(2)}) async-start(f32[16,1,16]{2,1,0:T(1,128)} %broadcast_in_dim.124), calls=%async_computation.2 | async-start | bytes 16384 | tf_op jit(solution)/shard_map/all_to_all | solution.py:49
  34.6 6.9 %all-to-all-done.2 = f32[16,1,16]{2,1,0:T(1,128)S(1)} async-done(((f32[16,1,16]{2,1,0:T(1,128)}), f32[16,1,16]{2,1,0:T(1,128)S(1)}, u32[]{:S(2)}, u32[]{:S(2)}) %all-to-all-start.2) | async-done | bytes 1056 | tf_op jit(solution)/shard_map/all_to_all | solution.py:49
  41.5 0.6 broadcast_in_dim.125
  42.1 12.0 %all-to-all-start.3 = ((f32[32,1,16]{2,1,0:T(1,128)}), f32[32,1,16]{2,1,0:T(1,128)S(1)}, u32[]{:S(2)}, u32[]{:S(2)}) async-start(f32[32,1,16]{2,1,0:T(1,128)} %broadcast_in_dim.125), calls=%async_computation.3 | async-start | bytes 32768 | tf_op jit(solution)/shard_map/all_to_all | solution.py:49
  54.1 3.0 %collective-permute-start.4 = (f32[2,1,1,16,68]{4,3,2,1,0:T(8,128)S(1)}, f32[2,1,1,16,68]{4,3,2,1,0:T(8,128)S(1)}, u32[]{:S(2)}, u32[]{:S(2)}) collective-permute-start(f32[2,1,1,16,68]{4,3,2,1,0:T(8,128)S(1)} %stack.99), channel_id=1, source_target_pairs={{0,1},{1,2},{2,3},{3,4},{4,5},{5,6},{6,7},{7,8},{8,9},{9,10},{10,1... | collective-permute-start | bytes 26120 | tf_op jit(solution)/shard_map/ppermute | solution.py:12
  57.1 3.4 %collective-permute-start.5 = (f32[2,1,1,16,68]{4,3,2,1,0:T(8,128)S(1)}, f32[2,1,1,16,68]{4,3,2,1,0:T(8,128)S(1)}, u32[]{:S(2)}, u32[]{:S(2)}) collective-permute-start(f32[2,1,1,16,68]{4,3,2,1,0:T(8,128)S(1)} %stack.101), channel_id=1, source_target_pairs={{0,16},{16,32},{32,48},{48,64},{64,80},{80,96},{96,112},{112,128},... | collective-permute-start | bytes 26120 | tf_op jit(solution)/shard_map/ppermute | solution.py:12
  60.7 2.0 %all-to-all-done.3 = f32[32,1,16]{2,1,0:T(1,128)S(1)} async-done(((f32[32,1,16]{2,1,0:T(1,128)}), f32[32,1,16]{2,1,0:T(1,128)S(1)}, u32[]{:S(2)}, u32[]{:S(2)}) %all-to-all-start.3) | async-done | bytes 2080 | tf_op jit(solution)/shard_map/all_to_all | solution.py:49
  62.8 0.7 copy-done.7
  63.5 0.2 convolution_multiply_fusion.2
  63.9 4.2 %collective-permute-start.6 = (f32[1,1,132]{2,1,0:T(1,128)S(1)}, f32[1,1,132]{2,1,0:T(1,128)S(1)}, u32[]{:S(2)}, u32[]{:S(2)}) collective-permute-start(f32[1,1,132]{2,1,0:T(1,128)S(1)} %constant_dynamic-update-slice_fusion), channel_id=1, source_target_pairs={{0,1},{1,2},{2,3},{3,4},{4,5},{5,6},{6,7},{7,8},{8,9},{9,10},{10,1... | collective-permute-start | bytes 1592 | tf_op jit(solution)/shard_map/ppermute | solution.py:12
  68.1 1.9 %collective-permute-start.7 = (f32[1,1,132]{2,1,0:T(1,128)S(1)}, f32[1,1,132]{2,1,0:T(1,128)S(1)}, u32[]{:S(2)}, u32[]{:S(2)}) collective-permute-start(f32[1,1,132]{2,1,0:T(1,128)S(1)} %constant_dynamic-update-slice_fusion), channel_id=1, source_target_pairs={{1,0},{2,1},{3,2},{4,3},{5,4},{6,5},{7,6},{8,7},{9,8},{10,9},{11,1... | collective-permute-start | bytes 1592 | tf_op jit(solution)/shard_map/ppermute | solution.py:12
  70.1 2.9 %collective-permute-done.7 = f32[1,1,132]{2,1,0:T(1,128)S(1)} collective-permute-done((f32[1,1,132]{2,1,0:T(1,128)S(1)}, f32[1,1,132]{2,1,0:T(1,128)S(1)}, u32[]{:S(2)}, u32[]{:S(2)}) %collective-permute-start.7) | collective-permute-done | bytes 560 | tf_op jit(solution)/shard_map/ppermute | solution.py:12
  73.0 2.2 %collective-permute-start.8 = (f32[1,3,132]{2,1,0:T(4,128)S(1)}, f32[1,3,132]{2,1,0:T(4,128)S(1)}, u32[]{:S(2)}, u32[]{:S(2)}) collective-permute-start(f32[1,3,132]{2,1,0:T(4,128)S(1)} %pad_maximum_fusion.8), channel_id=1, source_target_pairs={{0,16},{16,32},{32,48},{48,64},{64,80},{80,96},{96,112},{112,128},... | collective-permute-start | bytes 4760 | tf_op jit(solution)/shard_map/ppermute | solution.py:12
  75.2 1.3 collective-permute-start.9
  76.5 0.2 convolution_multiply_fusion
  76.7 2.8 %collective-permute-done.9 = f32[1,3,132]{2,1,0:T(4,128)S(1)} collective-permute-done((f32[1,3,132]{2,1,0:T(4,128)S(1)}, f32[1,3,132]{2,1,0:T(4,128)S(1)}, u32[]{:S(2)}, u32[]{:S(2)}) %collective-permute-start.9) | collective-permute-done | bytes 1616 | tf_op jit(solution)/shard_map/ppermute | solution.py:12
  79.6 0.6 copy-done.4
  80.2 0.1 reshape.627
  80.3 0.6 slice-done
  80.8 0.1 copy.156
  81.0 0.1 copy.168
  81.1 0.3 fusion.16
  81.4 0.2 fusion.1
  81.7 1.9 %collective-permute-start.10 = (f32[1,1,16,68]{3,2,1,0:T(8,128)S(1)}, f32[1,1,16,68]{3,2,1,0:T(8,128)S(1)}, u32[]{:S(2)}, u32[]{:S(2)}) collective-permute-start(f32[1,1,16,68]{3,2,1,0:T(8,128)S(1)} %get-tuple-element.44), channel_id=1, source_target_pairs={{1,0},{2,1},{3,2},{4,3},{5,4},{6,5},{7,6},{8,7},{9,8},{10,9},{11,1... | collective-permute-start | bytes 13064 | tf_op jit(solution)/shard_map/ppermute | solution.py:12
  83.6 1.3 collective-permute-start.11
  84.9 1.7 %collective-permute-done.10 = f32[1,1,16,68]{3,2,1,0:T(8,128)S(1)} collective-permute-done((f32[1,1,16,68]{3,2,1,0:T(8,128)S(1)}, f32[1,1,16,68]{3,2,1,0:T(8,128)S(1)}, u32[]{:S(2)}, u32[]{:S(2)}) %collective-permute-start.10) | collective-permute-done | bytes 4384 | tf_op jit(solution)/shard_map/ppermute | solution.py:12
  86.7 1.4 %collective-permute-done.11 = f32[1,1,16,68]{3,2,1,0:T(8,128)S(1)} collective-permute-done((f32[1,1,16,68]{3,2,1,0:T(8,128)S(1)}, f32[1,1,16,68]{3,2,1,0:T(8,128)S(1)}, u32[]{:S(2)}, u32[]{:S(2)}) %collective-permute-start.11) | collective-permute-done | bytes 4384 | tf_op jit(solution)/shard_map/ppermute | solution.py:12
  88.5 0.2 multiply_reduce_fusion.1
  89.6 0.1 slice_reduce_fusion.2
  89.7 0.2 slice_reduce_fusion.3
  90.0 13.9 %all_to_all.42 = f32[16,1,112]{2,1,0:T(1,128)S(1)} all-to-all(f32[16,1,112]{2,1,0:T(1,128)S(1)} %broadcast_in_dim.126), channel_id=1, replica_groups=mesh['px'=32,'py'=16] {'py'}, dimensions={0} | all-to-all | bytes 14336 | tf_op jit(solution)/shard_map/all_to_all | solution.py:49
  104.1 25.3 %all_to_all.43 = f32[32,1,112]{2,1,0:T(1,128)S(1)} all-to-all(f32[32,1,112]{2,1,0:T(1,128)S(1)} %broadcast_in_dim.127), channel_id=1, replica_groups=mesh['px'=32,'py'=16] {'px'}, dimensions={0} | all-to-all | bytes 28672 | tf_op jit(solution)/shard_map/all_to_all | solution.py:49
  129.7 0.7 and_reduce_fusion
  131.1 0.7 multiply_subtract_fusion
  131.8 0.5 copy-done.10
  (120 shorter events, 4.4 us)
Async XLA Ops:
  0.6 13.6 %copy-start = (bf16[1,1,272,272]{3,2,1,0:T(8,128)(2,1)S(1)}, bf16[1,1,272,272]{3,2,1,0:T(8,128)(2,1)}, u32[]{:S(2)}) copy-start(bf16[1,1,272,272]{3,2,1,0:T(8,128)(2,1)} %param.17) | copy-start | bytes 443908
  0.6 0.8 copy-start.2
  0.7 0.8 copy-start.6
  2.3 0.7 copy-start.9
  4.9 8.8 %collective-permute-start = (f32[2,1,1,16,68]{4,3,2,1,0:T(8,128)S(1)}, f32[2,1,1,16,68]{4,3,2,1,0:T(8,128)S(1)}, u32[]{:S(2)}, u32[]{:S(2)}) collective-permute-start(f32[2,1,1,16,68]{4,3,2,1,0:T(8,128)S(1)} %pad_maximum_fusion.4), channel_id=1, source_target_pairs={{0,1},{1,2},{2,3},{3,4},{4,5},{5,6},{6,7},{7,8},{8,9},{9,10},{10,1... | collective-permute-start | bytes 26120 | tf_op jit(solution)/shard_map/ppermute | solution.py:12
  10.3 4.0 %collective-permute-start.1 = (f32[2,1,1,16,68]{4,3,2,1,0:T(8,128)S(1)}, f32[2,1,1,16,68]{4,3,2,1,0:T(8,128)S(1)}, u32[]{:S(2)}, u32[]{:S(2)}) collective-permute-start(f32[2,1,1,16,68]{4,3,2,1,0:T(8,128)S(1)} %pad_maximum_fusion.5), channel_id=1, source_target_pairs={{0,16},{16,32},{32,48},{48,64},{64,80},{80,96},{96,112},{112,128},... | collective-permute-start | bytes 26120 | tf_op jit(solution)/shard_map/ppermute | solution.py:12
  14.5 5.1 %collective-permute-start.2 = (f32[1,1,16,68]{3,2,1,0:T(8,128)S(1)}, f32[1,1,16,68]{3,2,1,0:T(8,128)S(1)}, u32[]{:S(2)}, u32[]{:S(2)}) collective-permute-start(f32[1,1,16,68]{3,2,1,0:T(8,128)S(1)} %get-tuple-element.29), channel_id=1, source_target_pairs={{1,0},{2,1},{3,2},{4,3},{5,4},{6,5},{7,6},{8,7},{9,8},{10,9},{11,1... | collective-permute-start | bytes 13064 | tf_op jit(solution)/shard_map/ppermute | solution.py:12
  18.0 5.0 %collective-permute-start.3 = (f32[1,1,16,68]{3,2,1,0:T(8,128)S(1)}, f32[1,1,16,68]{3,2,1,0:T(8,128)S(1)}, u32[]{:S(2)}, u32[]{:S(2)}) collective-permute-start(f32[1,1,16,68]{3,2,1,0:T(8,128)S(1)} %get-tuple-element.30), channel_id=1, source_target_pairs={{16,0},{32,16},{48,32},{64,48},{80,64},{96,80},{112,96},{128,112},... | collective-permute-start | bytes 13064 | tf_op jit(solution)/shard_map/ppermute | solution.py:12
  23.4 37.2 %copy-start.11 = (f32[1,1,2,2]{3,2,1,0:T(2,128)S(1)}, f32[1,1,2,2]{3,2,1,0:T(2,128)}, u32[]{:S(2)}) copy-start(f32[1,1,2,2]{3,2,1,0:T(2,128)} %param.19) | copy-start | bytes 52
  23.4 39.3 %copy-start.12 = (f32[16]{0:T(128)S(1)}, f32[16]{0:T(128)}, u32[]{:S(2)}) copy-start(f32[16]{0:T(128)} %param.15) | copy-start | bytes 196
  23.6 52.9 %copy-start.1 = (bf16[1,1,272,272]{3,2,1,0:T(8,128)(2,1)S(1)}, bf16[1,1,272,272]{3,2,1,0:T(8,128)(2,1)}, u32[]{:S(2)}) copy-start(bf16[1,1,272,272]{3,2,1,0:T(8,128)(2,1)} %param.16) | copy-start | bytes 443908
  24.2 17.3 %all-to-all-start.2 = ((f32[16,1,16]{2,1,0:T(1,128)}), f32[16,1,16]{2,1,0:T(1,128)S(1)}, u32[]{:S(2)}, u32[]{:S(2)}) async-start(f32[16,1,16]{2,1,0:T(1,128)} %broadcast_in_dim.124), calls=%async_computation.2 | async-start | bytes 16384 | tf_op jit(solution)/shard_map/all_to_all | solution.py:49
  42.1 20.5 %all-to-all-start.3 = ((f32[32,1,16]{2,1,0:T(1,128)}), f32[32,1,16]{2,1,0:T(1,128)S(1)}, u32[]{:S(2)}, u32[]{:S(2)}) async-start(f32[32,1,16]{2,1,0:T(1,128)} %broadcast_in_dim.125), calls=%async_computation.3 | async-start | bytes 32768 | tf_op jit(solution)/shard_map/all_to_all | solution.py:49
  54.1 8.6 %collective-permute-start.4 = (f32[2,1,1,16,68]{4,3,2,1,0:T(8,128)S(1)}, f32[2,1,1,16,68]{4,3,2,1,0:T(8,128)S(1)}, u32[]{:S(2)}, u32[]{:S(2)}) collective-permute-start(f32[2,1,1,16,68]{4,3,2,1,0:T(8,128)S(1)} %stack.99), channel_id=1, source_target_pairs={{0,1},{1,2},{2,3},{3,4},{4,5},{5,6},{6,7},{7,8},{8,9},{9,10},{10,1... | collective-permute-start | bytes 26120 | tf_op jit(solution)/shard_map/ppermute | solution.py:12
  57.1 5.6 %collective-permute-start.5 = (f32[2,1,1,16,68]{4,3,2,1,0:T(8,128)S(1)}, f32[2,1,1,16,68]{4,3,2,1,0:T(8,128)S(1)}, u32[]{:S(2)}, u32[]{:S(2)}) collective-permute-start(f32[2,1,1,16,68]{4,3,2,1,0:T(8,128)S(1)} %stack.101), channel_id=1, source_target_pairs={{0,16},{16,32},{32,48},{48,64},{64,80},{80,96},{96,112},{112,128},... | collective-permute-start | bytes 26120 | tf_op jit(solution)/shard_map/ppermute | solution.py:12
  62.7 67.0 %copy-start.8 = (f32[16]{0:T(128)}, f32[16]{0:T(128)S(1)}, u32[]{:S(2)}) copy-start(f32[16]{0:T(128)S(1)} %reduce_sum.83) | copy-start | bytes 196
  62.8 0.7 copy-start.7
  63.9 6.2 %collective-permute-start.6 = (f32[1,1,132]{2,1,0:T(1,128)S(1)}, f32[1,1,132]{2,1,0:T(1,128)S(1)}, u32[]{:S(2)}, u32[]{:S(2)}) collective-permute-start(f32[1,1,132]{2,1,0:T(1,128)S(1)} %constant_dynamic-update-slice_fusion), channel_id=1, source_target_pairs={{0,1},{1,2},{2,3},{3,4},{4,5},{5,6},{6,7},{7,8},{8,9},{9,10},{10,1... | collective-permute-start | bytes 1592 | tf_op jit(solution)/shard_map/ppermute | solution.py:12
  68.1 4.9 %collective-permute-start.7 = (f32[1,1,132]{2,1,0:T(1,128)S(1)}, f32[1,1,132]{2,1,0:T(1,128)S(1)}, u32[]{:S(2)}, u32[]{:S(2)}) collective-permute-start(f32[1,1,132]{2,1,0:T(1,128)S(1)} %constant_dynamic-update-slice_fusion), channel_id=1, source_target_pairs={{1,0},{2,1},{3,2},{4,3},{5,4},{6,5},{7,6},{8,7},{9,8},{10,9},{11,1... | collective-permute-start | bytes 1592 | tf_op jit(solution)/shard_map/ppermute | solution.py:12
  73.0 3.7 %collective-permute-start.8 = (f32[1,3,132]{2,1,0:T(4,128)S(1)}, f32[1,3,132]{2,1,0:T(4,128)S(1)}, u32[]{:S(2)}, u32[]{:S(2)}) collective-permute-start(f32[1,3,132]{2,1,0:T(4,128)S(1)} %pad_maximum_fusion.8), channel_id=1, source_target_pairs={{0,16},{16,32},{32,48},{48,64},{64,80},{80,96},{96,112},{112,128},... | collective-permute-start | bytes 4760 | tf_op jit(solution)/shard_map/ppermute | solution.py:12
  75.2 4.4 %collective-permute-start.9 = (f32[1,3,132]{2,1,0:T(4,128)S(1)}, f32[1,3,132]{2,1,0:T(4,128)S(1)}, u32[]{:S(2)}, u32[]{:S(2)}) collective-permute-start(f32[1,3,132]{2,1,0:T(4,128)S(1)} %pad_maximum_fusion.8), channel_id=1, source_target_pairs={{16,0},{32,16},{48,32},{64,48},{80,64},{96,80},{112,96},{128,112},... | collective-permute-start | bytes 4760 | tf_op jit(solution)/shard_map/ppermute | solution.py:12
  79.6 0.6 copy-start.4
  80.2 0.7 slice-start
  81.7 5.0 %collective-permute-start.10 = (f32[1,1,16,68]{3,2,1,0:T(8,128)S(1)}, f32[1,1,16,68]{3,2,1,0:T(8,128)S(1)}, u32[]{:S(2)}, u32[]{:S(2)}) collective-permute-start(f32[1,1,16,68]{3,2,1,0:T(8,128)S(1)} %get-tuple-element.44), channel_id=1, source_target_pairs={{1,0},{2,1},{3,2},{4,3},{5,4},{6,5},{7,6},{8,7},{9,8},{10,9},{11,1... | collective-permute-start | bytes 13064 | tf_op jit(solution)/shard_map/ppermute | solution.py:12
  83.6 4.4 %collective-permute-start.11 = (f32[1,1,16,68]{3,2,1,0:T(8,128)S(1)}, f32[1,1,16,68]{3,2,1,0:T(8,128)S(1)}, u32[]{:S(2)}, u32[]{:S(2)}) collective-permute-start(f32[1,1,16,68]{3,2,1,0:T(8,128)S(1)} %get-tuple-element.45), channel_id=1, source_target_pairs={{16,0},{32,16},{48,32},{64,48},{80,64},{96,80},{112,96},{128,112},... | collective-permute-start | bytes 13064 | tf_op jit(solution)/shard_map/ppermute | solution.py:12
  88.7 42.4 %copy-start.3 = (f32[1,1,16,136]{3,2,1,0:T(8,128)}, f32[1,1,16,136]{3,2,1,0:T(8,128)S(1)}, u32[]{:S(2)}) copy-start(f32[1,1,16,136]{3,2,1,0:T(8,128)S(1)} %get-tuple-element.92) | copy-start | bytes 26116
  129.7 1.4 %copy-start.5 = (f32[1,1,16,136]{3,2,1,0:T(8,128)S(1)}, f32[1,1,16,136]{3,2,1,0:T(8,128)}, u32[]{:S(2)}) copy-start(f32[1,1,16,136]{3,2,1,0:T(8,128)} %param.12) | copy-start | bytes 26116
  131.8 0.5 copy-start.10
